TPU v7x, 128 devices: a whole 4x4x4 slice. The times are simulated.
128 devices in a mesh: gx: 16 (over z, x), gy: 8 (over y, core).
Axes of the slice: x: 4, y: 4, z: 4, core: 2. Of those that a mesh axis runs over, the one named last changes fastest.
Arguments:
- velocity: float32 [3, 128, 128, 128], P(None, 'gx', 'gy'), may hold values from -6 to 6
- stress: float32 [6, 128, 128, 128], P(None, 'gx', 'gy'), may hold values from -6 to 6
- lame_first: float32 [128, 128, 128], P('gx', 'gy'), may hold values from 0.5 to 1.5
- shear_modulus: float32 [128, 128, 128], P('gx', 'gy'), may hold values from 0.3 to 1
- buoyancy: float32 [128, 128, 128], P('gx', 'gy'), may hold values from 0.5 to 1
- forward_strain: bfloat16 [12, 128, 128, 128], P(None, 'gx', 'gy'), may hold values from -6 to 6
- lame_accum: float32 [128, 128, 128], P('gx', 'gy'), may hold values from -6 to 6
- shear_accum: float32 [128, 128, 128], P('gx', 'gy'), may hold values from -6 to 6
- residuals: bfloat16 [4096, 4096], P(('gx', 'gy')), may hold values from -24 to 24
- station_cell: int32 [4096], P(('gx', 'gy')), may hold values from 0 to 127
- station_pairs: int32 [16384, 2], replicated, may hold values from 0 to 4095, as said below
Outputs:
- new_velocity: float32 [3, 128, 128, 128], P(None, 'gx', 'gy')
- new_stress: float32 [6, 128, 128, 128], P(None, 'gx', 'gy')
- lame_kernel: float32 [128, 128, 128], P('gx', 'gy')
- shear_kernel: float32 [128, 128, 128], P('gx', 'gy')
- adjoint_source: float32 [4096, 4096], P(('gx', 'gy'))
Inputs may be any that keep to these rules, and one draw needn't show every extreme that they name: station_cell[s] numbers the surface cell x * 16 + y of station s within the block of the device that holds station s. `station_pairs`: stations s * 32 to (s + 1) * 32 - 1 are held by device s of gx+gy. The first station of pair p is held by device p // 128. Among the 128 pairs of one device, at most 2 have a second station held by any one device; some may have none. Some device's stations are the second station of exactly 2 pairs of every device.
All inputs are finite; a program needn't handle non-finite values.
Results may differ from a plain program's by a relative error of at most 0.0017.
Values may be sent and summed in bfloat16 or wider, within the bound.
No kernel may reach another device: no remote copies, remote signals or barrier semaphores. Data moves between devices by JAX's collectives and lax.ppermute only.
A program may use at most 64 MiB of HBM per device.

v0:
```python
import jax
import jax.numpy as jnp
from jax import lax
from jax.sharding import PartitionSpec as P

near_weight = 9.0 / 8.0
far_weight = -1.0 / 24.0
time_step = 0.25
epsilon = 1e-06


def with_halo(block, sides, width):
    for axis, dim in sides:
        count = lax.axis_size(axis)
        forward = [(i, i + 1) for i in range(count - 1)]
        backward = [(target, source) for source, target in forward]
        low = lax.ppermute(
            lax.slice_in_dim(block, block.shape[dim] - width, None, axis=dim), axis, forward
        )
        high = lax.ppermute(lax.slice_in_dim(block, 0, width, axis=dim), axis, backward)
        block = jnp.concatenate([low, block, high], axis=dim)
    return block


def shifted(padded, start, length, axis):
    return lax.slice_in_dim(padded, start, start + length, axis=axis)


def backward_diff(padded, length, axis):
    return near_weight * (
        shifted(padded, 2, length, axis) - shifted(padded, 1, length, axis)
    ) + far_weight * (shifted(padded, 3, length, axis) - shifted(padded, 0, length, axis))


def forward_diff(padded, length, axis):
    return near_weight * (
        shifted(padded, 3, length, axis) - shifted(padded, 2, length, axis)
    ) + far_weight * (shifted(padded, 4, length, axis) - shifted(padded, 1, length, axis))


def pair_terms(first_rows, second_rows):
    first_vals = first_rows.astype(jnp.float32)
    second_vals = second_rows.astype(jnp.float32)
    first_vals = first_vals / jnp.sqrt(
        jnp.mean(first_vals * first_vals, axis=1, keepdims=True) + epsilon
    )
    second_vals = second_vals / jnp.sqrt(
        jnp.mean(second_vals * second_vals, axis=1, keepdims=True) + epsilon
    )
    corr = jnp.mean(first_vals * second_vals, axis=1, keepdims=True)
    return (
        (second_vals - corr * first_vals).astype(jnp.bfloat16),
        (first_vals - corr * second_vals).astype(jnp.bfloat16),
    )


def contract(hits, rows):
    return lax.dot_general(hits, rows, (((0,), (0,)), ((), ())), preferred_element_type=jnp.float32)


def route_slots(rows):
    return lax.all_to_all(rows, ("gx", "gy"), split_axis=0, concat_axis=0, tiled=True)


def stress_sides(stress):
    cells_first = stress.shape[1]
    cells_second = stress.shape[2]
    wide_stress = with_halo(stress, (("gx", 1), ("gy", 2)), 2)
    first_part = wide_stress[:, :, 2 : 2 + cells_second, :]
    second_part = wide_stress[:, 2 : 2 + cells_first, :, :]
    return (
        (first_part[0], first_part[3], first_part[4]),
        (second_part[1], second_part[3], second_part[5]),
    )


def motion_sides(moved):
    cells_first = moved.shape[1]
    cells_second = moved.shape[2]
    wide_motion = with_halo(moved, (("gx", 1), ("gy", 2)), 2)
    return (wide_motion[:, :, 2 : 2 + cells_second, :], wide_motion[:, 2 : 2 + cells_first, :, :])


def advance(
    velocity,
    stress,
    lame_first,
    shear_modulus,
    buoyancy,
    strain_now,
    surface,
    lame_kernel,
    shear_kernel,
):
    cells_first = velocity.shape[1]
    cells_second = velocity.shape[2]
    cells_third = velocity.shape[3]
    across_stress, along_stress = stress_sides(stress)
    stress_third = jnp.pad(stress, ((0, 0), (0, 0), (0, 0), (2, 2)))
    force_first = (
        forward_diff(across_stress[0], cells_first, 0)
        + backward_diff(along_stress[1], cells_second, 1)
        + backward_diff(stress_third[4], cells_third, 2)
    )
    force_second = (
        backward_diff(across_stress[1], cells_first, 0)
        + forward_diff(along_stress[0], cells_second, 1)
        + backward_diff(stress_third[5], cells_third, 2)
    )
    force_third = (
        backward_diff(across_stress[2], cells_first, 0)
        + backward_diff(along_stress[2], cells_second, 1)
        + forward_diff(stress_third[2], cells_third, 2)
    )
    force_third = force_third.at[:, :, 0].add(surface)
    moved = velocity + time_step * buoyancy[None] * jnp.stack(
        [force_first, force_second, force_third]
    )
    motion_first, motion_second = motion_sides(moved)
    motion_third = jnp.pad(moved, ((0, 0), (0, 0), (0, 0), (2, 2)))
    rate_first = backward_diff(motion_first[0], cells_first, 0)
    rate_second = backward_diff(motion_second[1], cells_second, 1)
    rate_third = backward_diff(motion_third[2], cells_third, 2)
    shear_one = forward_diff(motion_second[0], cells_second, 1) + forward_diff(
        motion_first[1], cells_first, 0
    )
    shear_two = forward_diff(motion_third[0], cells_third, 2) + forward_diff(
        motion_first[2], cells_first, 0
    )
    shear_three = forward_diff(motion_third[1], cells_third, 2) + forward_diff(
        motion_second[2], cells_second, 1
    )
    dilation = rate_first + rate_second + rate_third
    grown = stress + time_step * jnp.stack(
        [
            lame_first * dilation + 2.0 * shear_modulus * rate_first,
            lame_first * dilation + 2.0 * shear_modulus * rate_second,
            lame_first * dilation + 2.0 * shear_modulus * rate_third,
            shear_modulus * shear_one,
            shear_modulus * shear_two,
            shear_modulus * shear_three,
        ]
    )
    strain_vals = strain_now.astype(jnp.float32)
    lame_kernel = (
        lame_kernel + time_step * (strain_vals[0] + strain_vals[1] + strain_vals[2]) * dilation
    )
    shear_kernel = shear_kernel + 2.0 * time_step * (
        strain_vals[0] * rate_first
        + strain_vals[1] * rate_second
        + strain_vals[2] * rate_third
        + strain_vals[3] * shear_one
        + strain_vals[4] * shear_two
        + strain_vals[5] * shear_three
    )
    return (moved, grown, lame_kernel, shear_kernel)


def shards(
    velocity,
    stress,
    lame_first,
    shear_modulus,
    buoyancy,
    forward_strain,
    lame_accum,
    shear_accum,
    residuals,
    station_cell,
    station_pairs,
):
    stations_here = residuals.shape[0]
    samples = residuals.shape[1]
    devices = lax.axis_size(("gx", "gy"))
    pair_rows = station_pairs.shape[0] // devices
    slot_count = 2 * pair_rows
    capacity = slot_count // devices
    device_index = lax.axis_index(("gx", "gy"))
    own_pairs = lax.dynamic_slice_in_dim(station_pairs, device_index * pair_rows, pair_rows, 0)
    first_local = own_pairs[:, 0] - device_index * stations_here
    owner_device = own_pairs[:, 1] // stations_here
    order_index = jnp.arange(pair_rows)
    earlier = (owner_device[:, None] == owner_device[None, :]) & (
        order_index[None, :] < order_index[:, None]
    )
    slot_index = owner_device * capacity + jnp.sum(earlier.astype(jnp.int32), axis=1)
    blocks = station_pairs.reshape(devices, pair_rows, 2)
    mine_mask = (blocks[:, :, 1] // stations_here == device_index).astype(jnp.int32)
    before = jnp.cumsum(mine_mask, axis=1) - mine_mask
    matches = (
        (mine_mask[:, :, None] > 0) & (before[:, :, None] == jnp.arange(capacity)[None, None, :])
    ).astype(jnp.int32)
    wanted = (blocks[:, :, 1] % stations_here)[:, :, None]
    found = jnp.sum(matches, axis=1)
    picked = jnp.sum(matches * wanted, axis=1)
    asked_ids = jnp.where(found > 0, picked, -1).reshape(slot_count)
    station_ids = jnp.arange(stations_here)
    first_hits = (first_local[:, None] == station_ids[None, :]).astype(jnp.bfloat16)
    asked_hits = (asked_ids[:, None] == station_ids[None, :]).astype(jnp.bfloat16)
    first_rows = residuals[first_local]
    local_rows = jnp.where(
        asked_ids[:, None] >= 0, residuals[jnp.maximum(asked_ids, 0)], jnp.zeros((), jnp.bfloat16)
    )
    fetched = route_slots(local_rows)
    toward_first, toward_second = pair_terms(first_rows, fetched[slot_index])
    outgoing = jnp.zeros((slot_count, samples), jnp.bfloat16).at[slot_index].set(toward_second)
    returned = route_slots(outgoing)
    adjoint = contract(first_hits, toward_first) + contract(asked_hits, returned)
    cells_first = velocity.shape[1]
    cells_second = velocity.shape[2]
    step_count = forward_strain.shape[0] // 6
    cells_hit = (station_cell[:, None] == jnp.arange(cells_first * cells_second)[None, :]).astype(
        jnp.float32
    )
    surfaces = jnp.stack(
        [
            jnp.sum(cells_hit * adjoint[:, samples - 1 - window_step][:, None], axis=0).reshape(
                cells_first, cells_second
            )
            for window_step in range(step_count)
        ]
    )
    for window_step in range(step_count):
        strain_now = forward_strain[6 * window_step : 6 * window_step + 6]
        velocity, stress, lame_accum, shear_accum = advance(
            velocity,
            stress,
            lame_first,
            shear_modulus,
            buoyancy,
            strain_now,
            surfaces[window_step],
            lame_accum,
            shear_accum,
        )
    return (velocity, stress, lame_accum, shear_accum, adjoint)


def solution(mesh):
    return jax.shard_map(
        shards,
        mesh=mesh,
        in_specs=(
            P(None, "gx", "gy", None),
            P(None, "gx", "gy", None),
            P("gx", "gy", None),
            P("gx", "gy", None),
            P("gx", "gy", None),
            P(None, "gx", "gy", None),
            P("gx", "gy", None),
            P("gx", "gy", None),
            P(("gx", "gy"), None),
            P(("gx", "gy")),
            P(),
        ),
        out_specs=(
            P(None, "gx", "gy", None),
            P(None, "gx", "gy", None),
            P("gx", "gy", None),
            P("gx", "gy", None),
            P(("gx", "gy"), None),
        ),
        check_vma=False,
    )
```

profile of v0, /device:TPU:14, one launch (start us, length us, event | category | flops | bytes accessed | tf_op | source)
XLA Modules:
  0.0 182.7 jit_solution(13370661635664374671)
XLA Ops:
  4.6 2.6 %gather.12 = bf16[128,2,4096]{2,1,0:T(2,128)(2,1)} reshape(bf16[256,4096]{1,0:T(8,128)(2,1)S(1)} %gather_fusion) | data formatting | bytes 4194304 | tf_op jit(solution)/shard_map/gather | solution.py:202
  7.4 4.8 %broadcast_select_fusion = bf16[128,2,4096]{2,1,0:T(2,128)(2,1)} fusion(bf16[128,2,4096]{2,1,0:T(2,128)(2,1)} %gather.12, pred[128,2]{1,0:T(8,128)(4,1)S(1)} %copy.345), kind=kLoop, calls=%fused_computation.5 | loop fusion | flops 1048576 | bytes 4194560 | tf_op jit(solution)/shard_map/jit(_where)/select_n | solution.py:201
  12.2 10.8 %all-to-all-start = ((bf16[128,2,4096]{2,1,0:T(2,128)(2,1)}), bf16[128,2,4096]{2,1,0:T(2,128)(2,1)}, u32[]{:S(2)}, u32[]{:S(2)}) async-start(bf16[128,2,4096]{2,1,0:T(2,128)(2,1)} %broadcast_select_fusion), calls=%async_computation | async-start | bytes 4194304 | tf_op jit(solution)/shard_map/all_to_all | solution.py:62
  25.5 24.6 %all-to-all-done = bf16[128,2,4096]{2,1,0:T(2,128)(2,1)} async-done(((bf16[128,2,4096]{2,1,0:T(2,128)(2,1)}), bf16[128,2,4096]{2,1,0:T(2,128)(2,1)}, u32[]{:S(2)}, u32[]{:S(2)}) %all-to-all-start) | async-done | bytes 2097184 | tf_op jit(solution)/shard_map/all_to_all | solution.py:62
  50.1 2.7 %all_to_all.15 = bf16[256,4096]{1,0:T(8,128)(2,1)S(1)} reshape(bf16[128,2,4096]{2,1,0:T(2,128)(2,1)} %all-to-all-done) | data formatting | bytes 4194304 | tf_op jit(solution)/shard_map/all_to_all | solution.py:62
  52.8 2.2 %gather_fusion.1 = bf16[128,4096]{1,0:T(8,128)(2,1)} fusion(bf16[256,4096]{1,0:T(8,128)(2,1)S(1)} %all_to_all.15, s32[1024]{0:T(1024)S(1)} %get-tuple-element.132), kind=kCustom, calls=%fused_computation.1 | custom fusion | bytes 2097664 | tf_op jit(solution)/shard_map/gather | solution.py:205
  58.4 4.0 %scatter_custom_fusion = bf16[256,4096]{1,0:T(8,128)(2,1)} fusion(s32[128]{0:T(128)S(1)} %fusion.221, bf16[]{:T(256)} %constant.138.clone.1, f32[128]{0:T(128)S(1)} %broadcast_multiply_fusion.1, bf16[128,4096]{1,0:T(8,128)(2,1)S(1)} %copy-done.1, f32[128]{0:T(128)S(1)} %add_sqrt_fusion.1, bf16[128,4096]{1,0:T(8,128)(2,1)S(1)} %gather_fusion.2, ...), kind=kCustom, calls=%fused_computation.21 | custom fusion | flops 3670016 | bytes 4195842 | tf_op jit(solution)/shard_map/scatter | solution.py:206
  62.4 4.4 %all_to_all.16 = bf16[128,2,4096]{2,1,0:T(2,128)(2,1)} reshape(bf16[256,4096]{1,0:T(8,128)(2,1)} %scatter_custom_fusion) | data formatting | bytes 4194304 | tf_op jit(solution)/shard_map/all_to_all | solution.py:62
  66.8 8.8 %all-to-all-start.1 = ((bf16[128,2,4096]{2,1,0:T(2,128)(2,1)}), bf16[128,2,4096]{2,1,0:T(2,128)(2,1)}, u32[]{:S(2)}, u32[]{:S(2)}) async-start(bf16[128,2,4096]{2,1,0:T(2,128)(2,1)} %all_to_all.16), calls=%async_computation.1 | async-start | bytes 4194304 | tf_op jit(solution)/shard_map/all_to_all | solution.py:62
  75.6 3.6 %collective-permute-start.1 = (f32[6,2,16,128]{3,2,1,0:T(8,128)S(1)}, f32[6,2,16,128]{3,2,1,0:T(8,128)S(1)}, u32[]{:S(2)}, u32[]{:S(2)}) collective-permute-start(f32[6,2,16,128]{3,2,1,0:T(8,128)S(1)} %get-tuple-element.103), channel_id=1, source_target_pairs={{0,8},{8,16},{16,24},{24,32},{32,40},{40,48},{48,56},{56,64},{64,7... | collective-permute-start | bytes 294920 | tf_op jit(solution)/shard_map/ppermute | solution.py:17
  79.2 2.4 %collective-permute-start = (f32[6,2,16,128]{3,2,1,0:T(8,128)S(1)}, f32[6,2,16,128]{3,2,1,0:T(8,128)S(1)}, u32[]{:S(2)}, u32[]{:S(2)}) collective-permute-start(f32[6,2,16,128]{3,2,1,0:T(8,128)S(1)} %get-tuple-element.102), channel_id=1, source_target_pairs={{8,0},{16,8},{24,16},{32,24},{40,32},{48,40},{56,48},{64,56},{72,6... | collective-permute-start | bytes 294920 | tf_op jit(solution)/shard_map/ppermute | solution.py:20
  82.0 18.9 %collective-permute-done.1 = f32[6,2,16,128]{3,2,1,0:T(8,128)S(1)} collective-permute-done((f32[6,2,16,128]{3,2,1,0:T(8,128)S(1)}, f32[6,2,16,128]{3,2,1,0:T(8,128)S(1)}, u32[]{:S(2)}, u32[]{:S(2)}) %collective-permute-start.1) | collective-permute-done | bytes 98336 | tf_op jit(solution)/shard_map/ppermute | solution.py:17
  104.9 3.6 %collective-permute-start.3 = (f32[6,12,2,128]{3,2,1,0:T(2,128)S(1)}, f32[6,12,2,128]{3,2,1,0:T(2,128)S(1)}, u32[]{:S(2)}, u32[]{:S(2)}) collective-permute-start(f32[6,12,2,128]{3,2,1,0:T(2,128)S(1)} %get-tuple-element.88), channel_id=1, source_target_pairs={{1,0},{2,1},{3,2},{4,3},{5,4},{6,5},{7,6},{9,8},{10,9},{11,10},{12... | collective-permute-start | bytes 221192 | tf_op jit(solution)/shard_map/ppermute | solution.py:20
  111.0 4.1 %all_to_all.18 = bf16[256,4096]{1,0:T(8,128)(2,1)} reshape(bf16[128,2,4096]{2,1,0:T(2,128)(2,1)} %all-to-all-done.1) | data formatting | bytes 4194304 | tf_op jit(solution)/shard_map/all_to_all | solution.py:62
  119.2 3.5 %collective-permute-start.4 = (f32[3,2,16,128]{3,2,1,0:T(8,128)S(1)}, f32[3,2,16,128]{3,2,1,0:T(8,128)S(1)}, u32[]{:S(2)}, u32[]{:S(2)}) collective-permute-start(f32[3,2,16,128]{3,2,1,0:T(8,128)S(1)} %get-tuple-element.122), channel_id=1, source_target_pairs={{0,8},{8,16},{16,24},{24,32},{32,40},{40,48},{48,56},{56,64},{64,7... | collective-permute-start | bytes 147464 | tf_op jit(solution)/shard_map/ppermute | solution.py:17
  122.7 2.3 %collective-permute-start.5 = (f32[3,2,16,128]{3,2,1,0:T(8,128)S(1)}, f32[3,2,16,128]{3,2,1,0:T(8,128)S(1)}, u32[]{:S(2)}, u32[]{:S(2)}) collective-permute-start(f32[3,2,16,128]{3,2,1,0:T(8,128)S(1)} %get-tuple-element.123), channel_id=1, source_target_pairs={{8,0},{16,8},{24,16},{32,24},{40,32},{48,40},{56,48},{64,56},{72,6... | collective-permute-start | bytes 147464 | tf_op jit(solution)/shard_map/ppermute | solution.py:20
  125.4 5.7 %collective-permute-done.5 = f32[3,2,16,128]{3,2,1,0:T(8,128)S(1)} collective-permute-done((f32[3,2,16,128]{3,2,1,0:T(8,128)S(1)}, f32[3,2,16,128]{3,2,1,0:T(8,128)S(1)}, u32[]{:S(2)}, u32[]{:S(2)}) %collective-permute-start.5) | collective-permute-done | bytes 49184 | tf_op jit(solution)/shard_map/ppermute | solution.py:20
  133.1 3.5 %collective-permute-start.7 = (f32[3,12,2,128]{3,2,1,0:T(2,128)S(1)}, f32[3,12,2,128]{3,2,1,0:T(2,128)S(1)}, u32[]{:S(2)}, u32[]{:S(2)}) collective-permute-start(f32[3,12,2,128]{3,2,1,0:T(2,128)S(1)} %get-tuple-element.113), channel_id=1, source_target_pairs={{1,0},{2,1},{3,2},{4,3},{5,4},{6,5},{7,6},{9,8},{10,9},{11,10},{12... | collective-permute-start | bytes 110600 | tf_op jit(solution)/shard_map/ppermute | solution.py:20
  140.9 6.0 %collective-permute-start.9 = (f32[6,2,16,128]{3,2,1,0:T(8,128)S(1)}, f32[6,2,16,128]{3,2,1,0:T(8,128)S(1)}, u32[]{:S(2)}, u32[]{:S(2)}) collective-permute-start(f32[6,2,16,128]{3,2,1,0:T(8,128)S(1)} %get-tuple-element.94), channel_id=1, source_target_pairs={{0,8},{8,16},{16,24},{24,32},{32,40},{40,48},{48,56},{56,64},{64,7... | collective-permute-start | bytes 294920 | tf_op jit(solution)/shard_map/ppermute | solution.py:17
  149.8 2.3 %collective-permute-start.10 = (f32[6,12,2,128]{3,2,1,0:T(2,128)S(1)}, f32[6,12,2,128]{3,2,1,0:T(2,128)S(1)}, u32[]{:S(2)}, u32[]{:S(2)}) collective-permute-start(f32[6,12,2,128]{3,2,1,0:T(2,128)S(1)} %get-tuple-element.85), channel_id=1, source_target_pairs={{0,1},{1,2},{2,3},{3,4},{4,5},{5,6},{6,7},{8,9},{9,10},{10,11},{11... | collective-permute-start | bytes 221192 | tf_op jit(solution)/shard_map/ppermute | solution.py:17
  152.2 3.2 %collective-permute-start.11 = (f32[6,12,2,128]{3,2,1,0:T(2,128)S(1)}, f32[6,12,2,128]{3,2,1,0:T(2,128)S(1)}, u32[]{:S(2)}, u32[]{:S(2)}) collective-permute-start(f32[6,12,2,128]{3,2,1,0:T(2,128)S(1)} %get-tuple-element.86), channel_id=1, source_target_pairs={{1,0},{2,1},{3,2},{4,3},{5,4},{6,5},{7,6},{9,8},{10,9},{11,10},{12... | collective-permute-start | bytes 221192 | tf_op jit(solution)/shard_map/ppermute | solution.py:20
  158.1 6.5 %collective-permute-start.12 = (f32[3,2,16,128]{3,2,1,0:T(8,128)S(1)}, f32[3,2,16,128]{3,2,1,0:T(8,128)S(1)}, u32[]{:S(2)}, u32[]{:S(2)}) collective-permute-start(f32[3,2,16,128]{3,2,1,0:T(8,128)S(1)} %get-tuple-element.117), channel_id=1, source_target_pairs={{0,8},{8,16},{16,24},{24,32},{32,40},{40,48},{48,56},{56,64},{64,7... | collective-permute-start | bytes 147464 | tf_op jit(solution)/shard_map/ppermute | solution.py:17
  166.6 6.2 %collective-permute-done.13 = f32[3,2,16,128]{3,2,1,0:T(8,128)S(1)} collective-permute-done((f32[3,2,16,128]{3,2,1,0:T(8,128)S(1)}, f32[3,2,16,128]{3,2,1,0:T(8,128)S(1)}, u32[]{:S(2)}, u32[]{:S(2)}) %collective-permute-start.13) | collective-permute-done | bytes 49184 | tf_op jit(solution)/shard_map/ppermute | solution.py:20
  175.0 3.4 %collective-permute-start.15 = (f32[3,12,2,128]{3,2,1,0:T(2,128)S(1)}, f32[3,12,2,128]{3,2,1,0:T(2,128)S(1)}, u32[]{:S(2)}, u32[]{:S(2)}) collective-permute-start(f32[3,12,2,128]{3,2,1,0:T(2,128)S(1)} %get-tuple-element.111), channel_id=1, source_target_pairs={{1,0},{2,1},{3,2},{4,3},{5,4},{6,5},{7,6},{9,8},{10,9},{11,10},{12... | collective-permute-start | bytes 110600 | tf_op jit(solution)/shard_map/ppermute | solution.py:20
  (133 shorter events, 40.9 us)
Async XLA Ops:
  12.2 37.8 %all-to-all-start = ((bf16[128,2,4096]{2,1,0:T(2,128)(2,1)}), bf16[128,2,4096]{2,1,0:T(2,128)(2,1)}, u32[]{:S(2)}, u32[]{:S(2)}) async-start(bf16[128,2,4096]{2,1,0:T(2,128)(2,1)} %broadcast_select_fusion), calls=%async_computation | async-start | bytes 4194304 | tf_op jit(solution)/shard_map/all_to_all | solution.py:62
  66.8 14.9 %copy-start.10 = (f32[8,16,128]{2,1,0:T(8,128)S(1)}, f32[8,16,128]{2,1,0:T(8,128)}, u32[]{:S(2)}) copy-start(f32[8,16,128]{2,1,0:T(8,128)} %param.19) | copy-start | bytes 196612
  66.8 44.2 %all-to-all-start.1 = ((bf16[128,2,4096]{2,1,0:T(2,128)(2,1)}), bf16[128,2,4096]{2,1,0:T(2,128)(2,1)}, u32[]{:S(2)}, u32[]{:S(2)}) async-start(bf16[128,2,4096]{2,1,0:T(2,128)(2,1)} %all_to_all.16), calls=%async_computation.1 | async-start | bytes 4194304 | tf_op jit(solution)/shard_map/all_to_all | solution.py:62
  75.6 25.2 %collective-permute-start.1 = (f32[6,2,16,128]{3,2,1,0:T(8,128)S(1)}, f32[6,2,16,128]{3,2,1,0:T(8,128)S(1)}, u32[]{:S(2)}, u32[]{:S(2)}) collective-permute-start(f32[6,2,16,128]{3,2,1,0:T(8,128)S(1)} %get-tuple-element.103), channel_id=1, source_target_pairs={{0,8},{8,16},{16,24},{24,32},{32,40},{40,48},{48,56},{56,64},{64,7... | collective-permute-start | bytes 294920 | tf_op jit(solution)/shard_map/ppermute | solution.py:17
  79.2 23.7 %collective-permute-start = (f32[6,2,16,128]{3,2,1,0:T(8,128)S(1)}, f32[6,2,16,128]{3,2,1,0:T(8,128)S(1)}, u32[]{:S(2)}, u32[]{:S(2)}) collective-permute-start(f32[6,2,16,128]{3,2,1,0:T(8,128)S(1)} %get-tuple-element.102), channel_id=1, source_target_pairs={{8,0},{16,8},{24,16},{32,24},{40,32},{48,40},{56,48},{64,56},{72,6... | collective-permute-start | bytes 294920 | tf_op jit(solution)/shard_map/ppermute | solution.py:20
  103.0 5.7 %collective-permute-start.2 = (f32[6,12,2,128]{3,2,1,0:T(2,128)S(1)}, f32[6,12,2,128]{3,2,1,0:T(2,128)S(1)}, u32[]{:S(2)}, u32[]{:S(2)}) collective-permute-start(f32[6,12,2,128]{3,2,1,0:T(2,128)S(1)} %get-tuple-element.87), channel_id=1, source_target_pairs={{0,1},{1,2},{2,3},{3,4},{4,5},{5,6},{6,7},{8,9},{9,10},{10,11},{11... | collective-permute-start | bytes 221192 | tf_op jit(solution)/shard_map/ppermute | solution.py:17
  104.9 5.6 %collective-permute-start.3 = (f32[6,12,2,128]{3,2,1,0:T(2,128)S(1)}, f32[6,12,2,128]{3,2,1,0:T(2,128)S(1)}, u32[]{:S(2)}, u32[]{:S(2)}) collective-permute-start(f32[6,12,2,128]{3,2,1,0:T(2,128)S(1)} %get-tuple-element.88), channel_id=1, source_target_pairs={{1,0},{2,1},{3,2},{4,3},{5,4},{6,5},{7,6},{9,8},{10,9},{11,10},{12... | collective-permute-start | bytes 221192 | tf_op jit(solution)/shard_map/ppermute | solution.py:20
  118.0 20.4 %copy-start.2 = (f32[8,16,128]{2,1,0:T(8,128)S(1)}, f32[8,16,128]{2,1,0:T(8,128)}, u32[]{:S(2)}) copy-start(f32[8,16,128]{2,1,0:T(8,128)} %param.18) | copy-start | bytes 196612
  118.0 20.4 %copy-start.7 = (f32[8,16,128]{2,1,0:T(8,128)S(1)}, f32[8,16,128]{2,1,0:T(8,128)}, u32[]{:S(2)}) copy-start(f32[8,16,128]{2,1,0:T(8,128)} %param.17) | copy-start | bytes 196612
  119.2 6.2 %collective-permute-start.4 = (f32[3,2,16,128]{3,2,1,0:T(8,128)S(1)}, f32[3,2,16,128]{3,2,1,0:T(8,128)S(1)}, u32[]{:S(2)}, u32[]{:S(2)}) collective-permute-start(f32[3,2,16,128]{3,2,1,0:T(8,128)S(1)} %get-tuple-element.122), channel_id=1, source_target_pairs={{0,8},{8,16},{16,24},{24,32},{32,40},{40,48},{48,56},{56,64},{64,7... | collective-permute-start | bytes 147464 | tf_op jit(solution)/shard_map/ppermute | solution.py:17
  122.7 8.4 %collective-permute-start.5 = (f32[3,2,16,128]{3,2,1,0:T(8,128)S(1)}, f32[3,2,16,128]{3,2,1,0:T(8,128)S(1)}, u32[]{:S(2)}, u32[]{:S(2)}) collective-permute-start(f32[3,2,16,128]{3,2,1,0:T(8,128)S(1)} %get-tuple-element.123), channel_id=1, source_target_pairs={{8,0},{16,8},{24,16},{32,24},{40,32},{48,40},{56,48},{64,56},{72,6... | collective-permute-start | bytes 147464 | tf_op jit(solution)/shard_map/ppermute | solution.py:20
  131.1 5.7 %collective-permute-start.6 = (f32[3,12,2,128]{3,2,1,0:T(2,128)S(1)}, f32[3,12,2,128]{3,2,1,0:T(2,128)S(1)}, u32[]{:S(2)}, u32[]{:S(2)}) collective-permute-start(f32[3,12,2,128]{3,2,1,0:T(2,128)S(1)} %get-tuple-element.112), channel_id=1, source_target_pairs={{0,1},{1,2},{2,3},{3,4},{4,5},{5,6},{6,7},{8,9},{9,10},{10,11},{11... | collective-permute-start | bytes 110600 | tf_op jit(solution)/shard_map/ppermute | solution.py:17
  133.1 5.2 %collective-permute-start.7 = (f32[3,12,2,128]{3,2,1,0:T(2,128)S(1)}, f32[3,12,2,128]{3,2,1,0:T(2,128)S(1)}, u32[]{:S(2)}, u32[]{:S(2)}) collective-permute-start(f32[3,12,2,128]{3,2,1,0:T(2,128)S(1)} %get-tuple-element.113), channel_id=1, source_target_pairs={{1,0},{2,1},{3,2},{4,3},{5,4},{6,5},{7,6},{9,8},{10,9},{11,10},{12... | collective-permute-start | bytes 110600 | tf_op jit(solution)/shard_map/ppermute | solution.py:20
  139.0 9.1 %collective-permute-start.8 = (f32[6,2,16,128]{3,2,1,0:T(8,128)S(1)}, f32[6,2,16,128]{3,2,1,0:T(8,128)S(1)}, u32[]{:S(2)}, u32[]{:S(2)}) collective-permute-start(f32[6,2,16,128]{3,2,1,0:T(8,128)S(1)} %get-tuple-element.95), channel_id=1, source_target_pairs={{8,0},{16,8},{24,16},{32,24},{40,32},{48,40},{56,48},{64,56},{72,6... | collective-permute-start | bytes 294920 | tf_op jit(solution)/shard_map/ppermute | solution.py:20
  140.9 8.9 %collective-permute-start.9 = (f32[6,2,16,128]{3,2,1,0:T(8,128)S(1)}, f32[6,2,16,128]{3,2,1,0:T(8,128)S(1)}, u32[]{:S(2)}, u32[]{:S(2)}) collective-permute-start(f32[6,2,16,128]{3,2,1,0:T(8,128)S(1)} %get-tuple-element.94), channel_id=1, source_target_pairs={{0,8},{8,16},{16,24},{24,32},{32,40},{40,48},{48,56},{56,64},{64,7... | collective-permute-start | bytes 294920 | tf_op jit(solution)/shard_map/ppermute | solution.py:17
  149.8 5.7 %collective-permute-start.10 = (f32[6,12,2,128]{3,2,1,0:T(2,128)S(1)}, f32[6,12,2,128]{3,2,1,0:T(2,128)S(1)}, u32[]{:S(2)}, u32[]{:S(2)}) collective-permute-start(f32[6,12,2,128]{3,2,1,0:T(2,128)S(1)} %get-tuple-element.85), channel_id=1, source_target_pairs={{0,1},{1,2},{2,3},{3,4},{4,5},{5,6},{6,7},{8,9},{9,10},{10,11},{11... | collective-permute-start | bytes 221192 | tf_op jit(solution)/shard_map/ppermute | solution.py:17
  152.2 5.2 %collective-permute-start.11 = (f32[6,12,2,128]{3,2,1,0:T(2,128)S(1)}, f32[6,12,2,128]{3,2,1,0:T(2,128)S(1)}, u32[]{:S(2)}, u32[]{:S(2)}) collective-permute-start(f32[6,12,2,128]{3,2,1,0:T(2,128)S(1)} %get-tuple-element.86), channel_id=1, source_target_pairs={{1,0},{2,1},{3,2},{4,3},{5,4},{6,5},{7,6},{9,8},{10,9},{11,10},{12... | collective-permute-start | bytes 221192 | tf_op jit(solution)/shard_map/ppermute | solution.py:20
  157.6 8.9 %copy-start.6 = (bf16[12,8,16,128]{3,2,1,0:T(8,128)(2,1)S(1)}, bf16[12,8,16,128]{3,2,1,0:T(8,128)(2,1)}, u32[]{:S(2)}) copy-start(bf16[12,8,16,128]{3,2,1,0:T(8,128)(2,1)} %param.20) | copy-start | bytes 1179652
  158.0 22.1 %copy-start.8 = (f32[8,16,128]{2,1,0:T(8,128)S(1)}, f32[8,16,128]{2,1,0:T(8,128)}, u32[]{:S(2)}) copy-start(f32[8,16,128]{2,1,0:T(8,128)} %param.22) | copy-start | bytes 196612
  158.1 23.0 %copy-start.3 = (f32[3,8,16,128]{3,2,1,0:T(8,128)}, f32[3,8,16,128]{3,2,1,0:T(8,128)S(1)}, u32[]{:S(2)}) copy-start(f32[3,8,16,128]{3,2,1,0:T(8,128)S(1)} %fusion.7) | copy-start | bytes 589828
  158.1 8.5 %collective-permute-start.12 = (f32[3,2,16,128]{3,2,1,0:T(8,128)S(1)}, f32[3,2,16,128]{3,2,1,0:T(8,128)S(1)}, u32[]{:S(2)}, u32[]{:S(2)}) collective-permute-start(f32[3,2,16,128]{3,2,1,0:T(8,128)S(1)} %get-tuple-element.117), channel_id=1, source_target_pairs={{0,8},{8,16},{16,24},{24,32},{32,40},{40,48},{48,56},{56,64},{64,7... | collective-permute-start | bytes 147464 | tf_op jit(solution)/shard_map/ppermute | solution.py:17
  164.6 8.2 %collective-permute-start.13 = (f32[3,2,16,128]{3,2,1,0:T(8,128)S(1)}, f32[3,2,16,128]{3,2,1,0:T(8,128)S(1)}, u32[]{:S(2)}, u32[]{:S(2)}) collective-permute-start(f32[3,2,16,128]{3,2,1,0:T(8,128)S(1)} %get-tuple-element.118), channel_id=1, source_target_pairs={{8,0},{16,8},{24,16},{32,24},{40,32},{48,40},{56,48},{64,56},{72,6... | collective-permute-start | bytes 147464 | tf_op jit(solution)/shard_map/ppermute | solution.py:20
  172.8 5.7 %collective-permute-start.14 = (f32[3,12,2,128]{3,2,1,0:T(2,128)S(1)}, f32[3,12,2,128]{3,2,1,0:T(2,128)S(1)}, u32[]{:S(2)}, u32[]{:S(2)}) collective-permute-start(f32[3,12,2,128]{3,2,1,0:T(2,128)S(1)} %get-tuple-element.110), channel_id=1, source_target_pairs={{0,1},{1,2},{2,3},{3,4},{4,5},{5,6},{6,7},{8,9},{9,10},{10,11},{11... | collective-permute-start | bytes 110600 | tf_op jit(solution)/shard_map/ppermute | solution.py:17
  175.0 5.0 %collective-permute-start.15 = (f32[3,12,2,128]{3,2,1,0:T(2,128)S(1)}, f32[3,12,2,128]{3,2,1,0:T(2,128)S(1)}, u32[]{:S(2)}, u32[]{:S(2)}) collective-permute-start(f32[3,12,2,128]{3,2,1,0:T(2,128)S(1)} %get-tuple-element.111), channel_id=1, source_target_pairs={{1,0},{2,1},{3,2},{4,3},{5,4},{6,5},{7,6},{9,8},{10,9},{11,10},{12... | collective-permute-start | bytes 110600 | tf_op jit(solution)/shard_map/ppermute | solution.py:20
  (7 other events, 19.0 us)
where the time goes:
time: 186 us; the launch traced here: 183 us
  starting transfers between devices  70.1 us (38%)
  waiting for transfers between devices  66.7 us (36%)
  local copies, waits for them, and re-layouts  24 us (13%)
  other arithmetic  17.6 us (9%)
  matrix products  2.86 us (2%)
    ppermute x8, starting transfers between devices, with_halo(): lax.ppermute(lax.slice_in_dim(block, block.shape[dim] - width, None, axis...  28.1 us
    all_to_all x2, waiting for transfers between devices, route_slots(): lax.all_to_all(rows, ('gx', 'gy'), split_axis=0, concat_axis=0, tiled=True)  24.6 us
    ppermute x8, starting transfers between devices, with_halo(): lax.ppermute(lax.slice_in_dim(block, 0, width, axis=dim), axis, backward)  22.4 us
    ppermute x8, waiting for transfers between devices, with_halo(): lax.ppermute(lax.slice_in_dim(block, 0, width, axis=dim), axis, backward)  21.1 us
    ppermute x8, waiting for transfers between devices, with_halo(): lax.ppermute(lax.slice_in_dim(block, block.shape[dim] - width, None, axis...  21 us
    all_to_all x2, starting transfers between devices, route_slots(): lax.all_to_all(rows, ('gx', 'gy'), split_axis=0, concat_axis=0, tiled=True)  19.6 us
    all_to_all x3, local copies, waits for them, and re-layouts, route_slots(): lax.all_to_all(rows, ('gx', 'gy'), split_axis=0, concat_axis=0, tiled=True)  11.3 us
    select_n x1, other arithmetic, shards(): jnp.where(asked_ids[:, None] >= 0, residuals[jnp.maximum(asked_ids, 0)],...  4.79 us
  transfers between devices with their start and end apart: 18, of which 12 were waited for; matrix products, arithmetic and copies ran while one was open for 2% of the time, Pallas kernels for 0%

commit v1 on v0

v1 whole, which is shorter than its diff:
```python
import jax
import jax.numpy as jnp
from jax import lax
from jax.sharding import PartitionSpec as P

near_weight = 9.0 / 8.0
far_weight = -1.0 / 24.0
time_step = 0.25
epsilon = 1e-06


def shifted(padded, start, length, axis):
    return lax.slice_in_dim(padded, start, start + length, axis=axis)


def backward_diff(padded, length, axis):
    return near_weight * (
        shifted(padded, 2, length, axis) - shifted(padded, 1, length, axis)
    ) + far_weight * (shifted(padded, 3, length, axis) - shifted(padded, 0, length, axis))


def forward_diff(padded, length, axis):
    return near_weight * (
        shifted(padded, 3, length, axis) - shifted(padded, 2, length, axis)
    ) + far_weight * (shifted(padded, 4, length, axis) - shifted(padded, 1, length, axis))


def halo_pad(block, axis, dim, width=2):
    count = lax.axis_size(axis)
    forward = [(i, i + 1) for i in range(count - 1)]
    backward = [(i + 1, i) for i in range(count - 1)]
    size = block.shape[dim]
    low = lax.ppermute(lax.slice_in_dim(block, size - width, size, axis=dim), axis, forward)
    high = lax.ppermute(lax.slice_in_dim(block, 0, width, axis=dim), axis, backward)
    return jnp.concatenate([low, block, high], axis=dim)


def z_pad(block):
    pads = [(0, 0)] * (block.ndim - 1) + [(2, 2)]
    return jnp.pad(block, pads)


def advance(velocity, stress, lame_first, shear_modulus, buoyancy, strain_now, surface, lame_kernel, shear_kernel):
    nx = velocity.shape[1]
    ny = velocity.shape[2]
    nz = velocity.shape[3]
    sx = halo_pad(jnp.stack([stress[0], stress[3], stress[4]]), "gx", 1)
    sy = halo_pad(jnp.stack([stress[3], stress[1], stress[5]]), "gy", 2)
    sz = z_pad(jnp.stack([stress[4], stress[5], stress[2]]))
    force_first = forward_diff(sx[0], nx, 0) + backward_diff(sy[0], ny, 1) + backward_diff(sz[0], nz, 2)
    force_second = backward_diff(sx[1], nx, 0) + forward_diff(sy[1], ny, 1) + backward_diff(sz[1], nz, 2)
    force_third = backward_diff(sx[2], nx, 0) + backward_diff(sy[2], ny, 1) + forward_diff(sz[2], nz, 2)
    force_third = force_third.at[:, :, 0].add(surface)
    moved = velocity + time_step * buoyancy[None] * jnp.stack([force_first, force_second, force_third])
    mx = halo_pad(moved, "gx", 1)
    my = halo_pad(moved, "gy", 2)
    mz = z_pad(moved)
    rate_first = backward_diff(mx[0], nx, 0)
    rate_second = backward_diff(my[1], ny, 1)
    rate_third = backward_diff(mz[2], nz, 2)
    shear_one = forward_diff(my[0], ny, 1) + forward_diff(mx[1], nx, 0)
    shear_two = forward_diff(mz[0], nz, 2) + forward_diff(mx[2], nx, 0)
    shear_three = forward_diff(mz[1], nz, 2) + forward_diff(my[2], ny, 1)
    dilation = rate_first + rate_second + rate_third
    grown = stress + time_step * jnp.stack(
        [
            lame_first * dilation + 2.0 * shear_modulus * rate_first,
            lame_first * dilation + 2.0 * shear_modulus * rate_second,
            lame_first * dilation + 2.0 * shear_modulus * rate_third,
            shear_modulus * shear_one,
            shear_modulus * shear_two,
            shear_modulus * shear_three,
        ]
    )
    strain_vals = strain_now.astype(jnp.float32)
    lame_kernel = lame_kernel + time_step * (strain_vals[0] + strain_vals[1] + strain_vals[2]) * dilation
    shear_kernel = shear_kernel + 2.0 * time_step * (
        strain_vals[0] * rate_first
        + strain_vals[1] * rate_second
        + strain_vals[2] * rate_third
        + strain_vals[3] * shear_one
        + strain_vals[4] * shear_two
        + strain_vals[5] * shear_three
    )
    return (moved, grown, lame_kernel, shear_kernel)


def station_part(residuals, station_cell, station_pairs, cells_first, cells_second, step_count):
    stations_here = residuals.shape[0]
    samples = residuals.shape[1]
    devices = lax.axis_size(("gx", "gy"))
    pair_rows = station_pairs.shape[0] // devices
    me = lax.axis_index(("gx", "gy"))
    own = lax.dynamic_slice_in_dim(station_pairs, me * pair_rows, pair_rows, 0)
    first_local = own[:, 0] - me * stations_here
    dest = own[:, 1] // stations_here
    order = jnp.arange(pair_rows)
    same = (dest[:, None] == dest[None, :]) & (order[None, :] < order[:, None])
    rank = jnp.sum(same.astype(jnp.int32), axis=1)
    device_ids = jnp.arange(devices)
    pick_own = (dest[None, :, None] == device_ids[:, None, None]) & (rank[None, :, None] == jnp.arange(2)[None, None, :])
    own_station = jnp.sum(jnp.where(pick_own, first_local[None, :, None] + 1, 0), axis=1) - 1
    blocks = station_pairs.reshape(devices, pair_rows, 2)
    hit = (blocks[:, :, 1] // stations_here == me).astype(jnp.int32)
    before = jnp.cumsum(hit, axis=1) - hit
    pick_in = (hit[:, :, None] > 0) & (before[:, :, None] == jnp.arange(2)[None, None, :])
    in_station = jnp.sum(jnp.where(pick_in, (blocks[:, :, 1] % stations_here)[:, :, None] + 1, 0), axis=1) - 1
    slot_station = jnp.concatenate([own_station, in_station], axis=1)
    hits = (slot_station[:, :, None] == jnp.arange(stations_here)[None, None, :]).astype(jnp.bfloat16)
    lanes = 128
    rows = residuals.reshape(stations_here, samples // lanes, lanes)
    send = jnp.einsum("xjs,sab->xjab", hits, rows)
    recv = lax.all_to_all(send, ("gx", "gy"), split_axis=0, concat_axis=0, tiled=True)
    partner = jnp.concatenate([recv[:, 2:4], recv[:, 0:2]], axis=1)
    mine_vals = send.astype(jnp.float32)
    other_vals = partner.astype(jnp.float32)
    mine_norm = jnp.sqrt(jnp.mean(mine_vals * mine_vals, axis=(2, 3), keepdims=True) + epsilon)
    other_norm = jnp.sqrt(jnp.mean(other_vals * other_vals, axis=(2, 3), keepdims=True) + epsilon)
    corr = jnp.mean(mine_vals * other_vals, axis=(2, 3), keepdims=True) / (mine_norm * other_norm)
    toward = (other_vals / other_norm - corr * (mine_vals / mine_norm)).astype(jnp.bfloat16)
    adjoint3 = jnp.einsum("xjs,xjab->sab", hits, toward, preferred_element_type=jnp.float32)
    adjoint = adjoint3.reshape(stations_here, samples)
    tail = jnp.einsum(
        "xjs,xjk->sk", hits, toward[:, :, -1, lanes - step_count :], preferred_element_type=jnp.float32
    )
    cells_hit = (station_cell[:, None] == jnp.arange(cells_first * cells_second)[None, :]).astype(jnp.float32)
    surfaces = jnp.stack(
        [
            jnp.sum(cells_hit * tail[:, step_count - 1 - window_step][:, None], axis=0).reshape(cells_first, cells_second)
            for window_step in range(step_count)
        ]
    )
    return adjoint, surfaces


def shards(velocity, stress, lame_first, shear_modulus, buoyancy, forward_strain, lame_accum, shear_accum, residuals, station_cell, station_pairs):
    step_count = forward_strain.shape[0] // 6
    adjoint, surfaces = station_part(residuals, station_cell, station_pairs, velocity.shape[1], velocity.shape[2], step_count)
    for window_step in range(step_count):
        strain_now = forward_strain[6 * window_step : 6 * window_step + 6]
        velocity, stress, lame_accum, shear_accum = advance(
            velocity, stress, lame_first, shear_modulus, buoyancy, strain_now, surfaces[window_step], lame_accum, shear_accum
        )
    return (velocity, stress, lame_accum, shear_accum, adjoint)


def solution(mesh):
    return jax.shard_map(
        shards,
        mesh=mesh,
        in_specs=(
            P(None, "gx", "gy", None),
            P(None, "gx", "gy", None),
            P("gx", "gy", None),
            P("gx", "gy", None),
            P("gx", "gy", None),
            P(None, "gx", "gy", None),
            P("gx", "gy", None),
            P("gx", "gy", None),
            P(("gx", "gy"), None),
            P(("gx", "gy")),
            P(),
        ),
        out_specs=(
            P(None, "gx", "gy", None),
            P(None, "gx", "gy", None),
            P("gx", "gy", None),
            P("gx", "gy", None),
            P(("gx", "gy"), None),
        ),
        check_vma=False,
    )
```

time: 186 us -> 167 us (0.90); the launches traced: 183 us -> 166 us
  waiting for transfers between devices: 66.7 us -> 43.2 us
  starting transfers between devices: 70.1 us -> 60.8 us
  local copies, waits for them, and re-layouts: 24 us -> 29.9 us
  other arithmetic: 17.6 us -> 23.2 us
  matrix products: 2.86 us -> 6.87 us
    all_to_all x2 -> x1, waiting for transfers between devices: 24.6 us -> 0.01 us  [station_part(): lax.all_to_all(send, ('gx', 'gy'), split_axis=0, concat_axis=0, tiled=True)]
    all_to_all x3 -> x0, local copies, waits for them, and re-layouts: 11.3 us -> none  [route_slots(): lax.all_to_all(rows, ('gx', 'gy'), split_axis=0, concat_axis=0, tiled=True)]
    unnamed x30 -> x38, local copies, waits for them, and re-layouts: 1.72 us -> 11.6 us
    all_to_all x2 -> x1, starting transfers between devices: 19.6 us -> 10.8 us  [station_part(): lax.all_to_all(send, ('gx', 'gy'), split_axis=0, concat_axis=0, tiled=True)]
    dot_general x0 -> x1, local copies, waits for them, and re-layouts: none -> 7.9 us  [station_part(): send = jnp.einsum('xjs,sab->xjab', hits, rows)]
    gather x4 -> x0, local copies, waits for them, and re-layouts: 7.86 us -> none  [the longest x2 4.49 us: shards(): residuals[jnp.maximum(asked_ids, 0)]]
    slice x7 -> x18, local copies, waits for them, and re-layouts: 0.29 us -> 5.42 us  [the longest x1 5.23 us: station_part(): partner = jnp.concatenate([recv[:, 2:4], recv[:, 0:2]], axis=1)]
    select_n x3 -> x1, other arithmetic: 4.81 us -> 0.01 us  [station_part(): dest = own[:, 1] // stations_here]
  transfers between devices with their start and end apart: 18 -> 17, of which waited for: 12 -> 5; matrix products, arithmetic and copies ran while one was open for 2% -> 4% of each run, Pallas kernels for 0% -> 0%
where the time goes in v1:
time: 167 us; the launch traced here: 166 us
  starting transfers between devices  60.8 us (36%)
  waiting for transfers between devices  43.2 us (26%)
  local copies, waits for them, and re-layouts  29.9 us (18%)
  other arithmetic  23.2 us (14%)
  matrix products  6.87 us (4%)
    ppermute x8, waiting for transfers between devices, halo_pad(): lax.ppermute(lax.slice_in_dim(block, size - width, size, axis=dim), axis,...  30.4 us
    ppermute x8, starting transfers between devices, halo_pad(): lax.ppermute(lax.slice_in_dim(block, size - width, size, axis=dim), axis,...  25.7 us
    ppermute x8, starting transfers between devices, halo_pad(): lax.ppermute(lax.slice_in_dim(block, 0, width, axis=dim), axis, backward)  24.2 us
    ppermute x8, waiting for transfers between devices, halo_pad(): lax.ppermute(lax.slice_in_dim(block, 0, width, axis=dim), axis, backward)  12.8 us
    unnamed x38, local copies, waits for them, and re-layouts  11.6 us
    all_to_all x1, starting transfers between devices, station_part(): lax.all_to_all(send, ('gx', 'gy'), split_axis=0, concat_axis=0, tiled=True)  10.8 us
    dot_general x1, local copies, waits for them, and re-layouts, station_part(): send = jnp.einsum('xjs,sab->xjab', hits, rows)  7.9 us
    slice x1, local copies, waits for them, and re-layouts, station_part(): partner = jnp.concatenate([recv[:, 2:4], recv[:, 0:2]], axis=1)  5.23 us
  transfers between devices with their start and end apart: 17, of which 5 were waited for; matrix products, arithmetic and copies ran while one was open for 4% of the time, Pallas kernels for 0%

profile of v1, /device:TPU:14, one launch (start us, length us, event | category | flops | bytes accessed | tf_op | source)
XLA Modules:
  0.0 165.5 jit_solution(2149860440912727112)
XLA Ops:
  3.5 3.3 %fusion.7 = bf16[128,4,32,128]{0,3,2,1:T(8,128)(2,1)} fusion(s32[128,4]{0,1:T(4,128)S(1)} %pad_add_fusion, bf16[32,4096]{1,0:T(8,128)(2,1)S(1)} %copy-done), kind=kOutput, calls=%fused_computation.61 | convolution fusion | flops 134234112 | bytes 4458496 | tf_op jit(solution)/shard_map/xjs,sab->xjab/dot_general | solution.py:112
  6.8 7.9 %copy.390 = bf16[128,4,32,128]{3,2,1,0:T(8,128)(2,1)} copy(bf16[128,4,32,128]{0,3,2,1:T(8,128)(2,1)} %fusion.7) | data formatting | bytes 8388608 | tf_op jit(solution)/shard_map/xjs,sab->xjab/dot_general | solution.py:112
  14.7 10.8 %all-to-all-start = ((bf16[128,4,32,128]{3,2,1,0:T(8,128)(2,1)}), bf16[128,4,32,128]{3,2,1,0:T(8,128)(2,1)}, u32[]{:S(2)}, u32[]{:S(2)}) async-start(bf16[128,4,32,128]{3,2,1,0:T(8,128)(2,1)} %copy.390), calls=%async_computation | async-start | bytes 8388608 | tf_op jit(solution)/shard_map/all_to_all | solution.py:113
  27.7 3.5 %collective-permute-start.3 = (f32[3,8,2,128]{3,1,2,0:T(8,128)S(1)}, f32[3,8,2,128]{3,1,2,0:T(8,128)S(1)}, u32[]{:S(2)}, u32[]{:S(2)}) collective-permute-start(f32[3,8,2,128]{3,1,2,0:T(8,128)S(1)} %copy.382), channel_id=1, source_target_pairs={{1,0},{2,1},{3,2},{4,3},{5,4},{6,5},{7,6},{9,8},{10,9},{11,10},{12... | collective-permute-start | bytes 73736 | tf_op jit(solution)/shard_map/ppermute | solution.py:34
  31.3 2.8 %collective-permute-start = (f32[3,2,16,128]{3,2,1,0:T(8,128)S(1)}, f32[3,2,16,128]{3,2,1,0:T(8,128)S(1)}, u32[]{:S(2)}, u32[]{:S(2)}) collective-permute-start(f32[3,2,16,128]{3,2,1,0:T(8,128)S(1)} %get-tuple-element.134), channel_id=1, source_target_pairs={{8,0},{16,8},{24,16},{32,24},{40,32},{48,40},{56,48},{64,56},{72,6... | collective-permute-start | bytes 147464 | tf_op jit(solution)/shard_map/ppermute | solution.py:34
  34.0 5.2 %collective-permute-start.1 = (f32[3,2,16,128]{3,2,1,0:T(8,128)S(1)}, f32[3,2,16,128]{3,2,1,0:T(8,128)S(1)}, u32[]{:S(2)}, u32[]{:S(2)}) collective-permute-start(f32[3,2,16,128]{3,2,1,0:T(8,128)S(1)} %get-tuple-element.135), channel_id=1, source_target_pairs={{0,8},{8,16},{16,24},{24,32},{32,40},{40,48},{48,56},{56,64},{64,7... | collective-permute-start | bytes 147464 | tf_op jit(solution)/shard_map/ppermute | solution.py:33
  40.2 30.4 %collective-permute-done.2 = f32[3,8,2,128]{3,1,2,0:T(8,128)S(1)} collective-permute-done((f32[3,8,2,128]{3,1,2,0:T(8,128)S(1)}, f32[3,8,2,128]{3,1,2,0:T(8,128)S(1)}, u32[]{:S(2)}, u32[]{:S(2)}) %collective-permute-start.2) | collective-permute-done | bytes 24608 | tf_op jit(solution)/shard_map/ppermute | solution.py:33
  70.7 3.5 %collective-permute-done = f32[3,2,16,128]{3,2,1,0:T(8,128)S(1)} collective-permute-done((f32[3,2,16,128]{3,2,1,0:T(8,128)S(1)}, f32[3,2,16,128]{3,2,1,0:T(8,128)S(1)}, u32[]{:S(2)}, u32[]{:S(2)}) %collective-permute-start) | collective-permute-done | bytes 49184 | tf_op jit(solution)/shard_map/ppermute | solution.py:34
  76.5 5.2 %fusion.235 = (bf16[128,2,32,128]{3,2,1,0:T(8,128)(2,1)}, bf16[128,2,32,128]{3,2,1,0:T(8,128)(2,1)}) fusion(bf16[128,4,32,128]{3,2,1,0:T(8,128)(2,1)} %all-to-all-done), kind=kLoop, calls=%fused_computation.442 | loop fusion | bytes 8388608 | tf_op jit(solution)/shard_map/slice | solution.py:114
  81.8 3.5 %copy.416 = bf16[128,2,32,128]{0,3,2,1:T(8,128)(2,1)S(1)} copy(bf16[128,2,32,128]{3,2,1,0:T(8,128)(2,1)} %get-tuple-element.76) | data formatting | bytes 4194304
  85.3 4.6 %copy.417 = bf16[128,2,32,128]{0,3,2,1:T(8,128)(2,1)} copy(bf16[128,2,32,128]{3,2,1,0:T(8,128)(2,1)} %get-tuple-element.77) | data formatting | bytes 4194304
  89.8 4.3 %fusion = (f32[128,4]{0,1:T(4,128)S(1)}, f32[128,4]{0,1:T(4,128)S(1)}, f32[128,4]{0,1:T(4,128)S(1)}) fusion(bf16[128,2,32,128]{0,3,2,1:T(8,128)(2,1)} %copy.417, bf16[128,2,32,128]{0,3,2,1:T(8,128)(2,1)S(1)} %copy.416, bf16[128,4,32,128]{0,3,2,1:T(8,128)(2,1)} %fusion.7), kind=kLoop, calls=%fused_computation.5 | loop fusion | flops 18872832 | bytes 8394752 | tf_op jit(solution)/shard_map/reduce_sum | solution.py:118
  94.6 2.3 %fusion.2 = bf16[128,4,32,128]{0,3,2,1:T(8,128)(2,1)S(1)} fusion(bf16[128,4,32,128]{0,3,2,1:T(8,128)(2,1)S(1)} %copy-done.1, f32[128,4]{0,1:T(4,128)S(1)} %get-tuple-element.140, f32[128,4]{0,1:T(4,128)S(1)} %get-tuple-element.139, f32[128,4]{0,1:T(4,128)S(1)} %get-tuple-element.138, bf16[128,2,32,128]{0,3,2,1:T(8,128)(2,1)S(1)} %copy-done.2, ...), kind=kLoop, calls=%fused_computation.7 | loop fusion | flops 16777216 | bytes 12589056 | tf_op jit(solution)/shard_map/convert_element_type | solution.py:120
  102.8 3.5 %convolution_bitcast_fusion = f32[32,4,8,128]{3,2,1,0:T(8,128)S(1)} fusion(bf16[128,4,32,128]{0,3,2,1:T(8,128)(2,1)} %copy-done.3, s32[128,4]{0,1:T(4,128)S(1)} %pad_add_fusion), kind=kOutput, calls=%fused_computation.12 | convolution fusion | flops 134234112 | bytes 4720640 | tf_op jit(solution)/shard_map/xjs,xjab->sab/dot_general | solution.py:121
  108.2 3.6 %collective-permute-start.7 = (f32[3,8,2,128]{3,1,2,0:T(8,128)S(1)}, f32[3,8,2,128]{3,1,2,0:T(8,128)S(1)}, u32[]{:S(2)}, u32[]{:S(2)}) collective-permute-start(f32[3,8,2,128]{3,1,2,0:T(8,128)S(1)} %copy.396), channel_id=1, source_target_pairs={{1,0},{2,1},{3,2},{4,3},{5,4},{6,5},{7,6},{9,8},{10,9},{11,10},{12... | collective-permute-start | bytes 73736 | tf_op jit(solution)/shard_map/ppermute | solution.py:34
  112.0 3.6 %collective-permute-start.4 = (f32[3,2,16,128]{3,2,1,0:T(8,128)S(1)}, f32[3,2,16,128]{3,2,1,0:T(8,128)S(1)}, u32[]{:S(2)}, u32[]{:S(2)}) collective-permute-start(f32[3,2,16,128]{3,2,1,0:T(8,128)S(1)} %get-tuple-element.128), channel_id=1, source_target_pairs={{0,8},{8,16},{16,24},{24,32},{32,40},{40,48},{48,56},{56,64},{64,7... | collective-permute-start | bytes 147464 | tf_op jit(solution)/shard_map/ppermute | solution.py:33
  115.6 2.3 %collective-permute-start.5 = (f32[3,2,16,128]{3,2,1,0:T(8,128)S(1)}, f32[3,2,16,128]{3,2,1,0:T(8,128)S(1)}, u32[]{:S(2)}, u32[]{:S(2)}) collective-permute-start(f32[3,2,16,128]{3,2,1,0:T(8,128)S(1)} %get-tuple-element.129), channel_id=1, source_target_pairs={{8,0},{16,8},{24,16},{32,24},{40,32},{48,40},{56,48},{64,56},{72,6... | collective-permute-start | bytes 147464 | tf_op jit(solution)/shard_map/ppermute | solution.py:34
  119.7 4.0 %collective-permute-done.5 = f32[3,2,16,128]{3,2,1,0:T(8,128)S(1)} collective-permute-done((f32[3,2,16,128]{3,2,1,0:T(8,128)S(1)}, f32[3,2,16,128]{3,2,1,0:T(8,128)S(1)}, u32[]{:S(2)}, u32[]{:S(2)}) %collective-permute-start.5) | collective-permute-done | bytes 49184 | tf_op jit(solution)/shard_map/ppermute | solution.py:34
  129.7 6.0 %collective-permute-start.9 = (f32[3,2,16,128]{3,2,1,0:T(8,128)S(1)}, f32[3,2,16,128]{3,2,1,0:T(8,128)S(1)}, u32[]{:S(2)}, u32[]{:S(2)}) collective-permute-start(f32[3,2,16,128]{3,2,1,0:T(8,128)S(1)} %get-tuple-element.122), channel_id=1, source_target_pairs={{0,8},{8,16},{16,24},{24,32},{32,40},{40,48},{48,56},{56,64},{64,7... | collective-permute-start | bytes 147464 | tf_op jit(solution)/shard_map/ppermute | solution.py:33
  137.7 3.6 %collective-permute-start.11 = (f32[3,8,2,128]{3,1,2,0:T(8,128)S(1)}, f32[3,8,2,128]{3,1,2,0:T(8,128)S(1)}, u32[]{:S(2)}, u32[]{:S(2)}) collective-permute-start(f32[3,8,2,128]{3,1,2,0:T(8,128)S(1)} %copy.400), channel_id=1, source_target_pairs={{1,0},{2,1},{3,2},{4,3},{5,4},{6,5},{7,6},{9,8},{10,9},{11,10},{12... | collective-permute-start | bytes 73736 | tf_op jit(solution)/shard_map/ppermute | solution.py:34
  144.6 3.1 %collective-permute-start.14 = (f32[3,8,2,128]{3,1,2,0:T(8,128)S(1)}, f32[3,8,2,128]{3,1,2,0:T(8,128)S(1)}, u32[]{:S(2)}, u32[]{:S(2)}) collective-permute-start(f32[3,8,2,128]{3,1,2,0:T(8,128)S(1)} %copy.405), channel_id=1, source_target_pairs={{0,1},{1,2},{2,3},{3,4},{4,5},{5,6},{6,7},{8,9},{9,10},{10,11},{11... | collective-permute-start | bytes 73736 | tf_op jit(solution)/shard_map/ppermute | solution.py:33
  147.8 2.4 %collective-permute-start.15 = (f32[3,8,2,128]{3,1,2,0:T(8,128)S(1)}, f32[3,8,2,128]{3,1,2,0:T(8,128)S(1)}, u32[]{:S(2)}, u32[]{:S(2)}) collective-permute-start(f32[3,8,2,128]{3,1,2,0:T(8,128)S(1)} %copy.406), channel_id=1, source_target_pairs={{1,0},{2,1},{3,2},{4,3},{5,4},{6,5},{7,6},{9,8},{10,9},{11,10},{12... | collective-permute-start | bytes 73736 | tf_op jit(solution)/shard_map/ppermute | solution.py:34
  152.3 3.9 %collective-permute-start.13 = (f32[3,2,16,128]{3,2,1,0:T(8,128)S(1)}, f32[3,2,16,128]{3,2,1,0:T(8,128)S(1)}, u32[]{:S(2)}, u32[]{:S(2)}) collective-permute-start(f32[3,2,16,128]{3,2,1,0:T(8,128)S(1)} %get-tuple-element.115), channel_id=1, source_target_pairs={{8,0},{16,8},{24,16},{32,24},{40,32},{48,40},{56,48},{64,56},{72,6... | collective-permute-start | bytes 147464 | tf_op jit(solution)/shard_map/ppermute | solution.py:34
  156.4 4.0 %collective-permute-done.13 = f32[3,2,16,128]{3,2,1,0:T(8,128)S(1)} collective-permute-done((f32[3,2,16,128]{3,2,1,0:T(8,128)S(1)}, f32[3,2,16,128]{3,2,1,0:T(8,128)S(1)}, u32[]{:S(2)}, u32[]{:S(2)}) %collective-permute-start.13) | collective-permute-done | bytes 49184 | tf_op jit(solution)/shard_map/ppermute | solution.py:34
  (153 shorter events, 36.6 us)
Async XLA Ops:
  14.7 24.7 %copy-start.13 = (bf16[12,8,16,128]{3,2,1,0:T(8,128)(2,1)S(1)}, bf16[12,8,16,128]{3,2,1,0:T(8,128)(2,1)}, u32[]{:S(2)}) copy-start(bf16[12,8,16,128]{3,2,1,0:T(8,128)(2,1)} %param.20) | copy-start | bytes 1179652
  14.7 61.8 %all-to-all-start = ((bf16[128,4,32,128]{3,2,1,0:T(8,128)(2,1)}), bf16[128,4,32,128]{3,2,1,0:T(8,128)(2,1)}, u32[]{:S(2)}, u32[]{:S(2)}) async-start(bf16[128,4,32,128]{3,2,1,0:T(8,128)(2,1)} %copy.390), calls=%async_computation | async-start | bytes 8388608 | tf_op jit(solution)/shard_map/all_to_all | solution.py:113
  25.6 44.9 %collective-permute-start.2 = (f32[3,8,2,128]{3,1,2,0:T(8,128)S(1)}, f32[3,8,2,128]{3,1,2,0:T(8,128)S(1)}, u32[]{:S(2)}, u32[]{:S(2)}) collective-permute-start(f32[3,8,2,128]{3,1,2,0:T(8,128)S(1)} %copy.381), channel_id=1, source_target_pairs={{0,1},{1,2},{2,3},{3,4},{4,5},{5,6},{6,7},{8,9},{9,10},{10,11},{11... | collective-permute-start | bytes 73736 | tf_op jit(solution)/shard_map/ppermute | solution.py:33
  27.7 42.9 %collective-permute-start.3 = (f32[3,8,2,128]{3,1,2,0:T(8,128)S(1)}, f32[3,8,2,128]{3,1,2,0:T(8,128)S(1)}, u32[]{:S(2)}, u32[]{:S(2)}) collective-permute-start(f32[3,8,2,128]{3,1,2,0:T(8,128)S(1)} %copy.382), channel_id=1, source_target_pairs={{1,0},{2,1},{3,2},{4,3},{5,4},{6,5},{7,6},{9,8},{10,9},{11,10},{12... | collective-permute-start | bytes 73736 | tf_op jit(solution)/shard_map/ppermute | solution.py:34
  31.3 42.9 %collective-permute-start = (f32[3,2,16,128]{3,2,1,0:T(8,128)S(1)}, f32[3,2,16,128]{3,2,1,0:T(8,128)S(1)}, u32[]{:S(2)}, u32[]{:S(2)}) collective-permute-start(f32[3,2,16,128]{3,2,1,0:T(8,128)S(1)} %get-tuple-element.134), channel_id=1, source_target_pairs={{8,0},{16,8},{24,16},{32,24},{40,32},{48,40},{56,48},{64,56},{72,6... | collective-permute-start | bytes 147464 | tf_op jit(solution)/shard_map/ppermute | solution.py:34
  34.0 40.2 %collective-permute-start.1 = (f32[3,2,16,128]{3,2,1,0:T(8,128)S(1)}, f32[3,2,16,128]{3,2,1,0:T(8,128)S(1)}, u32[]{:S(2)}, u32[]{:S(2)}) collective-permute-start(f32[3,2,16,128]{3,2,1,0:T(8,128)S(1)} %get-tuple-element.135), channel_id=1, source_target_pairs={{0,8},{8,16},{16,24},{24,32},{32,40},{40,48},{48,56},{56,64},{64,7... | collective-permute-start | bytes 147464 | tf_op jit(solution)/shard_map/ppermute | solution.py:33
  101.6 22.1 %copy-start.4 = (f32[8,16,128]{2,1,0:T(8,128)S(1)}, f32[8,16,128]{2,1,0:T(8,128)}, u32[]{:S(2)}) copy-start(f32[8,16,128]{2,1,0:T(8,128)} %param.18) | copy-start | bytes 196612
  106.3 13.3 %collective-permute-start.6 = (f32[3,8,2,128]{3,1,2,0:T(8,128)S(1)}, f32[3,8,2,128]{3,1,2,0:T(8,128)S(1)}, u32[]{:S(2)}, u32[]{:S(2)}) collective-permute-start(f32[3,8,2,128]{3,1,2,0:T(8,128)S(1)} %copy.395), channel_id=1, source_target_pairs={{0,1},{1,2},{2,3},{3,4},{4,5},{5,6},{6,7},{8,9},{9,10},{10,11},{11... | collective-permute-start | bytes 73736 | tf_op jit(solution)/shard_map/ppermute | solution.py:33
  108.2 11.3 %collective-permute-start.7 = (f32[3,8,2,128]{3,1,2,0:T(8,128)S(1)}, f32[3,8,2,128]{3,1,2,0:T(8,128)S(1)}, u32[]{:S(2)}, u32[]{:S(2)}) collective-permute-start(f32[3,8,2,128]{3,1,2,0:T(8,128)S(1)} %copy.396), channel_id=1, source_target_pairs={{1,0},{2,1},{3,2},{4,3},{5,4},{6,5},{7,6},{9,8},{10,9},{11,10},{12... | collective-permute-start | bytes 73736 | tf_op jit(solution)/shard_map/ppermute | solution.py:34
  112.0 7.6 %collective-permute-start.4 = (f32[3,2,16,128]{3,2,1,0:T(8,128)S(1)}, f32[3,2,16,128]{3,2,1,0:T(8,128)S(1)}, u32[]{:S(2)}, u32[]{:S(2)}) collective-permute-start(f32[3,2,16,128]{3,2,1,0:T(8,128)S(1)} %get-tuple-element.128), channel_id=1, source_target_pairs={{0,8},{8,16},{16,24},{24,32},{32,40},{40,48},{48,56},{56,64},{64,7... | collective-permute-start | bytes 147464 | tf_op jit(solution)/shard_map/ppermute | solution.py:33
  115.6 8.1 %collective-permute-start.5 = (f32[3,2,16,128]{3,2,1,0:T(8,128)S(1)}, f32[3,2,16,128]{3,2,1,0:T(8,128)S(1)}, u32[]{:S(2)}, u32[]{:S(2)}) collective-permute-start(f32[3,2,16,128]{3,2,1,0:T(8,128)S(1)} %get-tuple-element.129), channel_id=1, source_target_pairs={{8,0},{16,8},{24,16},{32,24},{40,32},{48,40},{56,48},{64,56},{72,6... | collective-permute-start | bytes 147464 | tf_op jit(solution)/shard_map/ppermute | solution.py:34
  127.5 16.1 %copy-start.9 = (f32[1,8,16,128]{3,2,1,0:T(8,128)S(1)}, f32[1,8,16,128]{3,2,1,0:T(8,128)}, u32[]{:S(2)}) copy-start(f32[1,8,16,128]{3,2,1,0:T(8,128)} %scatter-add.6) | copy-start | bytes 196612
  127.5 16.1 %copy-start.10 = (f32[3,8,16,128]{3,2,1,0:T(8,128)S(1)}, f32[3,8,16,128]{3,2,1,0:T(8,128)}, u32[]{:S(2)}) copy-start(f32[3,8,16,128]{3,2,1,0:T(8,128)} %param.15) | copy-start | bytes 589828
  127.6 15.3 %collective-permute-start.8 = (f32[3,2,16,128]{3,2,1,0:T(8,128)S(1)}, f32[3,2,16,128]{3,2,1,0:T(8,128)S(1)}, u32[]{:S(2)}, u32[]{:S(2)}) collective-permute-start(f32[3,2,16,128]{3,2,1,0:T(8,128)S(1)} %get-tuple-element.121), channel_id=1, source_target_pairs={{8,0},{16,8},{24,16},{32,24},{40,32},{48,40},{56,48},{64,56},{72,6... | collective-permute-start | bytes 147464 | tf_op jit(solution)/shard_map/ppermute | solution.py:34
  129.7 13.3 %collective-permute-start.9 = (f32[3,2,16,128]{3,2,1,0:T(8,128)S(1)}, f32[3,2,16,128]{3,2,1,0:T(8,128)S(1)}, u32[]{:S(2)}, u32[]{:S(2)}) collective-permute-start(f32[3,2,16,128]{3,2,1,0:T(8,128)S(1)} %get-tuple-element.122), channel_id=1, source_target_pairs={{0,8},{8,16},{16,24},{24,32},{32,40},{40,48},{48,56},{56,64},{64,7... | collective-permute-start | bytes 147464 | tf_op jit(solution)/shard_map/ppermute | solution.py:33
  135.8 5.8 %collective-permute-start.10 = (f32[3,8,2,128]{3,1,2,0:T(8,128)S(1)}, f32[3,8,2,128]{3,1,2,0:T(8,128)S(1)}, u32[]{:S(2)}, u32[]{:S(2)}) collective-permute-start(f32[3,8,2,128]{3,1,2,0:T(8,128)S(1)} %copy.399), channel_id=1, source_target_pairs={{0,1},{1,2},{2,3},{3,4},{4,5},{5,6},{6,7},{8,9},{9,10},{10,11},{11... | collective-permute-start | bytes 73736 | tf_op jit(solution)/shard_map/ppermute | solution.py:33
  137.7 5.1 %collective-permute-start.11 = (f32[3,8,2,128]{3,1,2,0:T(8,128)S(1)}, f32[3,8,2,128]{3,1,2,0:T(8,128)S(1)}, u32[]{:S(2)}, u32[]{:S(2)}) collective-permute-start(f32[3,8,2,128]{3,1,2,0:T(8,128)S(1)} %copy.400), channel_id=1, source_target_pairs={{1,0},{2,1},{3,2},{4,3},{5,4},{6,5},{7,6},{9,8},{10,9},{11,10},{12... | collective-permute-start | bytes 73736 | tf_op jit(solution)/shard_map/ppermute | solution.py:34
  141.6 18.8 %copy-start.8 = (f32[8,16,128]{2,1,0:T(8,128)S(1)}, f32[8,16,128]{2,1,0:T(8,128)}, u32[]{:S(2)}) copy-start(f32[8,16,128]{2,1,0:T(8,128)} %copy-done.7) | copy-start | bytes 196612
  141.6 18.8 %copy-start.11 = (f32[8,16,128]{2,1,0:T(8,128)S(1)}, f32[8,16,128]{2,1,0:T(8,128)}, u32[]{:S(2)}) copy-start(f32[8,16,128]{2,1,0:T(8,128)} %get-tuple-element.72) | copy-start | bytes 196612
  144.5 20.2 %copy-start.5 = (f32[3,8,16,128]{3,2,1,0:T(8,128)}, f32[3,8,16,128]{3,2,1,0:T(8,128)S(1)}, u32[]{:S(2)}) copy-start(f32[3,8,16,128]{3,2,1,0:T(8,128)S(1)} %fusion.10) | copy-start | bytes 589828
  144.6 11.6 %collective-permute-start.14 = (f32[3,8,2,128]{3,1,2,0:T(8,128)S(1)}, f32[3,8,2,128]{3,1,2,0:T(8,128)S(1)}, u32[]{:S(2)}, u32[]{:S(2)}) collective-permute-start(f32[3,8,2,128]{3,1,2,0:T(8,128)S(1)} %copy.405), channel_id=1, source_target_pairs={{0,1},{1,2},{2,3},{3,4},{4,5},{5,6},{6,7},{8,9},{9,10},{10,11},{11... | collective-permute-start | bytes 73736 | tf_op jit(solution)/shard_map/ppermute | solution.py:33
  147.8 8.5 %collective-permute-start.15 = (f32[3,8,2,128]{3,1,2,0:T(8,128)S(1)}, f32[3,8,2,128]{3,1,2,0:T(8,128)S(1)}, u32[]{:S(2)}, u32[]{:S(2)}) collective-permute-start(f32[3,8,2,128]{3,1,2,0:T(8,128)S(1)} %copy.406), channel_id=1, source_target_pairs={{1,0},{2,1},{3,2},{4,3},{5,4},{6,5},{7,6},{9,8},{10,9},{11,10},{12... | collective-permute-start | bytes 73736 | tf_op jit(solution)/shard_map/ppermute | solution.py:34
  150.4 6.0 %collective-permute-start.12 = (f32[3,2,16,128]{3,2,1,0:T(8,128)S(1)}, f32[3,2,16,128]{3,2,1,0:T(8,128)S(1)}, u32[]{:S(2)}, u32[]{:S(2)}) collective-permute-start(f32[3,2,16,128]{3,2,1,0:T(8,128)S(1)} %get-tuple-element.116), channel_id=1, source_target_pairs={{0,8},{8,16},{16,24},{24,32},{32,40},{40,48},{48,56},{56,64},{64,7... | collective-permute-start | bytes 147464 | tf_op jit(solution)/shard_map/ppermute | solution.py:33
  152.3 8.1 %collective-permute-start.13 = (f32[3,2,16,128]{3,2,1,0:T(8,128)S(1)}, f32[3,2,16,128]{3,2,1,0:T(8,128)S(1)}, u32[]{:S(2)}, u32[]{:S(2)}) collective-permute-start(f32[3,2,16,128]{3,2,1,0:T(8,128)S(1)} %get-tuple-element.115), channel_id=1, source_target_pairs={{8,0},{16,8},{24,16},{32,24},{40,32},{48,40},{56,48},{64,56},{72,6... | collective-permute-start | bytes 147464 | tf_op jit(solution)/shard_map/ppermute | solution.py:34
  (10 other events, 77.4 us)

commit v2 on v1

--- a/solution.py
+++ b/solution.py
@@ -106,22 +106,28 @@
     pick_in = (hit[:, :, None] > 0) & (before[:, :, None] == jnp.arange(2)[None, None, :])
     in_station = jnp.sum(jnp.where(pick_in, (blocks[:, :, 1] % stations_here)[:, :, None] + 1, 0), axis=1) - 1
     slot_station = jnp.concatenate([own_station, in_station], axis=1)
-    hits = (slot_station[:, :, None] == jnp.arange(stations_here)[None, None, :]).astype(jnp.bfloat16)
     lanes = 128
     rows = residuals.reshape(stations_here, samples // lanes, lanes)
-    send = jnp.einsum("xjs,sab->xjab", hits, rows)
+    send = jnp.where(
+        (slot_station >= 0)[:, :, None, None], rows[jnp.maximum(slot_station, 0)], jnp.zeros((), residuals.dtype)
+    )
     recv = lax.all_to_all(send, ("gx", "gy"), split_axis=0, concat_axis=0, tiled=True)
-    partner = jnp.concatenate([recv[:, 2:4], recv[:, 0:2]], axis=1)
-    mine_vals = send.astype(jnp.float32)
-    other_vals = partner.astype(jnp.float32)
+    mine_station = jnp.concatenate([slot_station[:, 2:4], slot_station[:, 0:2]], axis=1)
+    mine = jnp.where(
+        (mine_station >= 0)[:, :, None, None], rows[jnp.maximum(mine_station, 0)], jnp.zeros((), residuals.dtype)
+    )
+    mine_vals = mine.astype(jnp.float32)
+    other_vals = recv.astype(jnp.float32)
     mine_norm = jnp.sqrt(jnp.mean(mine_vals * mine_vals, axis=(2, 3), keepdims=True) + epsilon)
     other_norm = jnp.sqrt(jnp.mean(other_vals * other_vals, axis=(2, 3), keepdims=True) + epsilon)
     corr = jnp.mean(mine_vals * other_vals, axis=(2, 3), keepdims=True) / (mine_norm * other_norm)
     toward = (other_vals / other_norm - corr * (mine_vals / mine_norm)).astype(jnp.bfloat16)
-    adjoint3 = jnp.einsum("xjs,xjab->sab", hits, toward, preferred_element_type=jnp.float32)
-    adjoint = adjoint3.reshape(stations_here, samples)
-    tail = jnp.einsum(
-        "xjs,xjk->sk", hits, toward[:, :, -1, lanes - step_count :], preferred_element_type=jnp.float32
+    slots = devices * 4
+    hits = (mine_station.reshape(slots)[:, None] == jnp.arange(stations_here)[None, :]).astype(jnp.bfloat16)
+    flat = toward.reshape(slots, samples)
+    adjoint = lax.dot_general(hits, flat, (((0,), (0,)), ((), ())), preferred_element_type=jnp.float32)
+    tail = lax.dot_general(
+        hits, flat[:, samples - step_count :], (((0,), (0,)), ((), ())), preferred_element_type=jnp.float32
     )
     cells_hit = (station_cell[:, None] == jnp.arange(cells_first * cells_second)[None, :]).astype(jnp.float32)
     surfaces = jnp.stack(

time: 167 us -> 155 us (0.928)
  local copies, waits for them, and re-layouts: 29.9 us -> 17.3 us
  other arithmetic: 23.2 us -> 28 us
  matrix products: 6.87 us -> 4.77 us
  waiting for transfers between devices: 43.2 us -> 41.5 us
    dot_general x1 -> x0, local copies, waits for them, and re-layouts: 7.9 us -> none  [station_part(): send = jnp.einsum('xjs,sab->xjab', hits, rows)]
    reduce_sum x1, other arithmetic: 4.27 us -> 11.4 us  [station_part(): jnp.mean(mine_vals * other_vals, axis=(2, 3), keepdims=True)]
    gather x0 -> x2, local copies, waits for them, and re-layouts: none -> 7.06 us  [the longest x1 3.54 us: station_part(): rows[jnp.maximum(slot_station, 0)]]
    slice x1 -> x0, local copies, waits for them, and re-layouts: 5.23 us -> none  [station_part(): partner = jnp.concatenate([recv[:, 2:4], recv[:, 0:2]], axis=1)]
    unnamed x38 -> x26, local copies, waits for them, and re-layouts: 11.6 us -> 6.33 us
    convert_element_type x1, other arithmetic: 2.31 us -> 7.17 us  [station_part(): (other_vals / other_norm - corr * (mine_vals / mine_norm)).astype(jnp.bfl...]
    select_n x0 -> x1, other arithmetic: none -> 3.91 us  [station_part(): jnp.where((slot_station >= 0)[:, :, None, None], rows[jnp.maximum(slot_st...]
    ppermute x8, waiting for transfers between devices: 30.4 us -> 26.7 us  [halo_pad(): lax.ppermute(lax.slice_in_dim(block, size - width, size, axis=dim), axis,...]
  transfers between devices with their start and end apart: 17 -> 17, of which waited for: 5 -> 6; matrix products, arithmetic and copies ran while one was open for 4% -> 4% of each run, Pallas kernels for 0% -> 0%
where the time goes in v2:
time: 155 us; the launch traced here: 154 us
  starting transfers between devices  60.8 us (39%)
  waiting for transfers between devices  41.5 us (27%)
  other arithmetic  28 us (18%)
  local copies, waits for them, and re-layouts  17.3 us (11%)
  matrix products  4.77 us (3%)
  between operations  1.65 us (1%)
    ppermute x8, waiting for transfers between devices, halo_pad(): lax.ppermute(lax.slice_in_dim(block, size - width, size, axis=dim), axis,...  26.7 us
    ppermute x8, starting transfers between devices, halo_pad(): lax.ppermute(lax.slice_in_dim(block, size - width, size, axis=dim), axis,...  25.1 us
    ppermute x8, starting transfers between devices, halo_pad(): lax.ppermute(lax.slice_in_dim(block, 0, width, axis=dim), axis, backward)  24.9 us
    ppermute x8, waiting for transfers between devices, halo_pad(): lax.ppermute(lax.slice_in_dim(block, 0, width, axis=dim), axis, backward)  13.3 us
    reduce_sum x1, other arithmetic, station_part(): jnp.mean(mine_vals * other_vals, axis=(2, 3), keepdims=True)  11.4 us
    all_to_all x1, starting transfers between devices, station_part(): lax.all_to_all(send, ('gx', 'gy'), split_axis=0, concat_axis=0, tiled=True)  10.8 us
    convert_element_type x1, other arithmetic, station_part(): (other_vals / other_norm - corr * (mine_vals / mine_norm)).astype(jnp.bfl...  7.17 us
    unnamed x26, local copies, waits for them, and re-layouts  6.33 us
  transfers between devices with their start and end apart: 17, of which 6 were waited for; matrix products, arithmetic and copies ran while one was open for 4% of the time, Pallas kernels for 0%

profile of v2, /device:TPU:14, one launch (start us, length us, event | category | flops | bytes accessed | tf_op | source)
XLA Modules:
  0.0 154.0 jit_solution(8470656284652067938)
XLA Ops:
  4.9 3.5 %gather_fusion = bf16[512,32,128]{2,1,0:T(8,128)(2,1)} fusion(bf16[32,32,128]{2,1,0:T(8,128)(2,1)S(1)} %bitcast.273, s32[1024]{0:T(1024)S(1)} %pad_clamp_fusion.1), kind=kCustom, calls=%fused_computation | custom fusion | bytes 8390656 | tf_op jit(solution)/shard_map/gather | solution.py:112
  8.4 3.9 %broadcast_select_fusion.1 = bf16[128,4,32,128]{3,2,1,0:T(8,128)(2,1)} fusion(bf16[128,4,32,128]{3,2,1,0:T(8,128)(2,1)} %bitcast.278, pred[128,4]{1,0:T(8,128)(4,1)S(1)} %copy.417), kind=kLoop, calls=%fused_computation.15 | loop fusion | flops 2097152 | bytes 8389120 | tf_op jit(solution)/shard_map/jit(_where)/select_n | solution.py:111
  12.3 10.8 %all-to-all-start = ((bf16[128,4,32,128]{3,2,1,0:T(8,128)(2,1)}), bf16[128,4,32,128]{3,2,1,0:T(8,128)(2,1)}, u32[]{:S(2)}, u32[]{:S(2)}) async-start(bf16[128,4,32,128]{3,2,1,0:T(8,128)(2,1)} %broadcast_select_fusion.1), calls=%async_computation | async-start | bytes 8388608 | tf_op jit(solution)/shard_map/all_to_all | solution.py:114
  23.2 2.0 %collective-permute-start.2 = (f32[3,8,2,128]{3,1,2,0:T(8,128)S(1)}, f32[3,8,2,128]{3,1,2,0:T(8,128)S(1)}, u32[]{:S(2)}, u32[]{:S(2)}) collective-permute-start(f32[3,8,2,128]{3,1,2,0:T(8,128)S(1)} %copy.408), channel_id=1, source_target_pairs={{0,1},{1,2},{2,3},{3,4},{4,5},{5,6},{6,7},{8,9},{9,10},{10,11},{11... | collective-permute-start | bytes 73736 | tf_op jit(solution)/shard_map/ppermute | solution.py:33
  25.3 3.5 %collective-permute-start.3 = (f32[3,8,2,128]{3,1,2,0:T(8,128)S(1)}, f32[3,8,2,128]{3,1,2,0:T(8,128)S(1)}, u32[]{:S(2)}, u32[]{:S(2)}) collective-permute-start(f32[3,8,2,128]{3,1,2,0:T(8,128)S(1)} %copy.409), channel_id=1, source_target_pairs={{1,0},{2,1},{3,2},{4,3},{5,4},{6,5},{7,6},{9,8},{10,9},{11,10},{12... | collective-permute-start | bytes 73736 | tf_op jit(solution)/shard_map/ppermute | solution.py:34
  28.9 2.8 %collective-permute-start = (f32[3,2,16,128]{3,2,1,0:T(8,128)S(1)}, f32[3,2,16,128]{3,2,1,0:T(8,128)S(1)}, u32[]{:S(2)}, u32[]{:S(2)}) collective-permute-start(f32[3,2,16,128]{3,2,1,0:T(8,128)S(1)} %get-tuple-element.132), channel_id=1, source_target_pairs={{8,0},{16,8},{24,16},{32,24},{40,32},{48,40},{56,48},{64,56},{72,6... | collective-permute-start | bytes 147464 | tf_op jit(solution)/shard_map/ppermute | solution.py:34
  31.6 5.4 %collective-permute-start.1 = (f32[3,2,16,128]{3,2,1,0:T(8,128)S(1)}, f32[3,2,16,128]{3,2,1,0:T(8,128)S(1)}, u32[]{:S(2)}, u32[]{:S(2)}) collective-permute-start(f32[3,2,16,128]{3,2,1,0:T(8,128)S(1)} %get-tuple-element.133), channel_id=1, source_target_pairs={{0,8},{8,16},{16,24},{24,32},{32,40},{40,48},{48,56},{56,64},{64,7... | collective-permute-start | bytes 147464 | tf_op jit(solution)/shard_map/ppermute | solution.py:33
  37.7 3.5 %gather_fusion.1 = bf16[512,32,128]{2,1,0:T(8,128)(2,1)} fusion(bf16[32,32,128]{2,1,0:T(8,128)(2,1)S(1)} %bitcast.274, s32[1024]{0:T(1024)S(1)} %pad_clamp_fusion), kind=kCustom, calls=%fused_computation.1 | custom fusion | bytes 8390656 | tf_op jit(solution)/shard_map/gather | solution.py:117
  41.5 26.7 %collective-permute-done.2 = f32[3,8,2,128]{3,1,2,0:T(8,128)S(1)} collective-permute-done((f32[3,8,2,128]{3,1,2,0:T(8,128)S(1)}, f32[3,8,2,128]{3,1,2,0:T(8,128)S(1)}, u32[]{:S(2)}, u32[]{:S(2)}) %collective-permute-start.2) | collective-permute-done | bytes 24608 | tf_op jit(solution)/shard_map/ppermute | solution.py:33
  68.3 3.5 %collective-permute-done = f32[3,2,16,128]{3,2,1,0:T(8,128)S(1)} collective-permute-done((f32[3,2,16,128]{3,2,1,0:T(8,128)S(1)}, f32[3,2,16,128]{3,2,1,0:T(8,128)S(1)}, u32[]{:S(2)}, u32[]{:S(2)}) %collective-permute-start) | collective-permute-done | bytes 49184 | tf_op jit(solution)/shard_map/ppermute | solution.py:34
  73.7 11.4 %fusion.3 = (f32[128,4]{1,0:T(8,128)S(1)}, f32[128,4]{1,0:T(8,128)S(1)}, f32[128,4]{1,0:T(8,128)S(1)}) fusion(bf16[128,4,32,128]{3,2,1,0:T(8,128)(2,1)} %all-to-all-done, bf16[128,4,32,128]{3,2,1,0:T(8,128)(2,1)} %bitcast.275, pred[128,4]{1,0:T(8,128)(4,1)S(1)} %copy.421), kind=kLoop, calls=%fused_computation.10 | loop fusion | flops 18872832 | bytes 8395264 | tf_op jit(solution)/shard_map/reduce_sum | solution.py:123
  85.7 7.2 %fusion.2 = bf16[128,4,32,128]{3,2,1,0:T(8,128)(2,1)S(1)} fusion(bf16[128,4,32,128]{3,2,1,0:T(8,128)(2,1)} %all-to-all-done, f32[128,4]{1,0:T(8,128)S(1)} %copy.426, f32[128,4]{1,0:T(8,128)S(1)} %copy.425, f32[128,4]{1,0:T(8,128)S(1)} %copy.420, pred[128,4]{1,0:T(8,128)(4,1)S(1)} %copy.421, bf16[512,32,128]{2,1,0:T(8,128)(2,1)} %gather_fusion.1), kind=kLoop, calls=%fused_computation.9 | loop fusion | flops 16777216 | bytes 12589568 | tf_op jit(solution)/shard_map/convert_element_type | solution.py:124
  92.9 4.3 %copy.450 = bf16[64,8,32,128]{3,1,2,0:T(8,128)(2,1)S(1)} copy(bf16[64,8,32,128]{3,2,1,0:T(8,128)(2,1)S(1)} %bitcast.276) | data formatting | bytes 8388608
  98.1 4.4 %fusion.7 = f32[32,4096]{1,0:T(8,128)} fusion(s32[512]{0:T(512)S(1)} %eq.121, bf16[64,8,32,128]{3,2,1,0:T(8,128)(2,1)} %bitcast.277), kind=kOutput, calls=%fused_computation.62 | convolution fusion | flops 134234112 | bytes 4720640 | tf_op jit(solution)/shard_map/dot_general | solution.py:128
  104.4 3.6 %collective-permute-start.7 = (f32[3,8,2,128]{3,1,2,0:T(8,128)S(1)}, f32[3,8,2,128]{3,1,2,0:T(8,128)S(1)}, u32[]{:S(2)}, u32[]{:S(2)}) collective-permute-start(f32[3,8,2,128]{3,1,2,0:T(8,128)S(1)} %copy.430), channel_id=1, source_target_pairs={{1,0},{2,1},{3,2},{4,3},{5,4},{6,5},{7,6},{9,8},{10,9},{11,10},{12... | collective-permute-start | bytes 73736 | tf_op jit(solution)/shard_map/ppermute | solution.py:34
  108.3 2.7 %collective-permute-start.4 = (f32[3,2,16,128]{3,2,1,0:T(8,128)S(1)}, f32[3,2,16,128]{3,2,1,0:T(8,128)S(1)}, u32[]{:S(2)}, u32[]{:S(2)}) collective-permute-start(f32[3,2,16,128]{3,2,1,0:T(8,128)S(1)} %get-tuple-element.126), channel_id=1, source_target_pairs={{0,8},{8,16},{16,24},{24,32},{32,40},{40,48},{48,56},{56,64},{64,7... | collective-permute-start | bytes 147464 | tf_op jit(solution)/shard_map/ppermute | solution.py:33
  110.9 3.2 %collective-permute-start.5 = (f32[3,2,16,128]{3,2,1,0:T(8,128)S(1)}, f32[3,2,16,128]{3,2,1,0:T(8,128)S(1)}, u32[]{:S(2)}, u32[]{:S(2)}) collective-permute-start(f32[3,2,16,128]{3,2,1,0:T(8,128)S(1)} %get-tuple-element.127), channel_id=1, source_target_pairs={{8,0},{16,8},{24,16},{32,24},{40,32},{48,40},{56,48},{64,56},{72,6... | collective-permute-start | bytes 147464 | tf_op jit(solution)/shard_map/ppermute | solution.py:34
  114.5 4.5 %collective-permute-done.5 = f32[3,2,16,128]{3,2,1,0:T(8,128)S(1)} collective-permute-done((f32[3,2,16,128]{3,2,1,0:T(8,128)S(1)}, f32[3,2,16,128]{3,2,1,0:T(8,128)S(1)}, u32[]{:S(2)}, u32[]{:S(2)}) %collective-permute-start.5) | collective-permute-done | bytes 49184 | tf_op jit(solution)/shard_map/ppermute | solution.py:34
  121.6 6.0 %collective-permute-start.9 = (f32[3,2,16,128]{3,2,1,0:T(8,128)S(1)}, f32[3,2,16,128]{3,2,1,0:T(8,128)S(1)}, u32[]{:S(2)}, u32[]{:S(2)}) collective-permute-start(f32[3,2,16,128]{3,2,1,0:T(8,128)S(1)} %get-tuple-element.120), channel_id=1, source_target_pairs={{0,8},{8,16},{16,24},{24,32},{32,40},{40,48},{48,56},{56,64},{64,7... | collective-permute-start | bytes 147464 | tf_op jit(solution)/shard_map/ppermute | solution.py:33
  129.6 3.6 %collective-permute-start.11 = (f32[3,8,2,128]{3,1,2,0:T(8,128)S(1)}, f32[3,8,2,128]{3,1,2,0:T(8,128)S(1)}, u32[]{:S(2)}, u32[]{:S(2)}) collective-permute-start(f32[3,8,2,128]{3,1,2,0:T(8,128)S(1)} %copy.434), channel_id=1, source_target_pairs={{1,0},{2,1},{3,2},{4,3},{5,4},{6,5},{7,6},{9,8},{10,9},{11,10},{12... | collective-permute-start | bytes 73736 | tf_op jit(solution)/shard_map/ppermute | solution.py:34
  135.6 3.3 %collective-permute-start.14 = (f32[3,8,2,128]{3,1,2,0:T(8,128)S(1)}, f32[3,8,2,128]{3,1,2,0:T(8,128)S(1)}, u32[]{:S(2)}, u32[]{:S(2)}) collective-permute-start(f32[3,8,2,128]{3,1,2,0:T(8,128)S(1)} %copy.439), channel_id=1, source_target_pairs={{0,1},{1,2},{2,3},{3,4},{4,5},{5,6},{6,7},{8,9},{9,10},{10,11},{11... | collective-permute-start | bytes 73736 | tf_op jit(solution)/shard_map/ppermute | solution.py:33
  139.0 2.3 %collective-permute-start.15 = (f32[3,8,2,128]{3,1,2,0:T(8,128)S(1)}, f32[3,8,2,128]{3,1,2,0:T(8,128)S(1)}, u32[]{:S(2)}, u32[]{:S(2)}) collective-permute-start(f32[3,8,2,128]{3,1,2,0:T(8,128)S(1)} %copy.440), channel_id=1, source_target_pairs={{1,0},{2,1},{3,2},{4,3},{5,4},{6,5},{7,6},{9,8},{10,9},{11,10},{12... | collective-permute-start | bytes 73736 | tf_op jit(solution)/shard_map/ppermute | solution.py:34
  143.3 3.9 %collective-permute-start.13 = (f32[3,2,16,128]{3,2,1,0:T(8,128)S(1)}, f32[3,2,16,128]{3,2,1,0:T(8,128)S(1)}, u32[]{:S(2)}, u32[]{:S(2)}) collective-permute-start(f32[3,2,16,128]{3,2,1,0:T(8,128)S(1)} %get-tuple-element.113), channel_id=1, source_target_pairs={{8,0},{16,8},{24,16},{32,24},{40,32},{48,40},{56,48},{64,56},{72,6... | collective-permute-start | bytes 147464 | tf_op jit(solution)/shard_map/ppermute | solution.py:34
  147.4 4.0 %collective-permute-done.13 = f32[3,2,16,128]{3,2,1,0:T(8,128)S(1)} collective-permute-done((f32[3,2,16,128]{3,2,1,0:T(8,128)S(1)}, f32[3,2,16,128]{3,2,1,0:T(8,128)S(1)}, u32[]{:S(2)}, u32[]{:S(2)}) %collective-permute-start.13) | collective-permute-done | bytes 49184 | tf_op jit(solution)/shard_map/ppermute | solution.py:34
  (158 shorter events, 22.2 us)
Async XLA Ops:
  12.3 25.1 %copy-start.9 = (f32[8,16,128]{2,1,0:T(8,128)S(1)}, f32[8,16,128]{2,1,0:T(8,128)}, u32[]{:S(2)}) copy-start(f32[8,16,128]{2,1,0:T(8,128)} %param.19) | copy-start | bytes 196612
  12.3 25.2 %copy-start.5 = (bf16[12,8,16,128]{3,2,1,0:T(8,128)(2,1)S(1)}, bf16[12,8,16,128]{3,2,1,0:T(8,128)(2,1)}, u32[]{:S(2)}) copy-start(bf16[12,8,16,128]{3,2,1,0:T(8,128)(2,1)} %param.20) | copy-start | bytes 1179652
  12.3 61.4 %all-to-all-start = ((bf16[128,4,32,128]{3,2,1,0:T(8,128)(2,1)}), bf16[128,4,32,128]{3,2,1,0:T(8,128)(2,1)}, u32[]{:S(2)}, u32[]{:S(2)}) async-start(bf16[128,4,32,128]{3,2,1,0:T(8,128)(2,1)} %broadcast_select_fusion.1), calls=%async_computation | async-start | bytes 8388608 | tf_op jit(solution)/shard_map/all_to_all | solution.py:114
  23.2 44.9 %collective-permute-start.2 = (f32[3,8,2,128]{3,1,2,0:T(8,128)S(1)}, f32[3,8,2,128]{3,1,2,0:T(8,128)S(1)}, u32[]{:S(2)}, u32[]{:S(2)}) collective-permute-start(f32[3,8,2,128]{3,1,2,0:T(8,128)S(1)} %copy.408), channel_id=1, source_target_pairs={{0,1},{1,2},{2,3},{3,4},{4,5},{5,6},{6,7},{8,9},{9,10},{10,11},{11... | collective-permute-start | bytes 73736 | tf_op jit(solution)/shard_map/ppermute | solution.py:33
  25.3 42.9 %collective-permute-start.3 = (f32[3,8,2,128]{3,1,2,0:T(8,128)S(1)}, f32[3,8,2,128]{3,1,2,0:T(8,128)S(1)}, u32[]{:S(2)}, u32[]{:S(2)}) collective-permute-start(f32[3,8,2,128]{3,1,2,0:T(8,128)S(1)} %copy.409), channel_id=1, source_target_pairs={{1,0},{2,1},{3,2},{4,3},{5,4},{6,5},{7,6},{9,8},{10,9},{11,10},{12... | collective-permute-start | bytes 73736 | tf_op jit(solution)/shard_map/ppermute | solution.py:34
  28.9 42.9 %collective-permute-start = (f32[3,2,16,128]{3,2,1,0:T(8,128)S(1)}, f32[3,2,16,128]{3,2,1,0:T(8,128)S(1)}, u32[]{:S(2)}, u32[]{:S(2)}) collective-permute-start(f32[3,2,16,128]{3,2,1,0:T(8,128)S(1)} %get-tuple-element.132), channel_id=1, source_target_pairs={{8,0},{16,8},{24,16},{32,24},{40,32},{48,40},{56,48},{64,56},{72,6... | collective-permute-start | bytes 147464 | tf_op jit(solution)/shard_map/ppermute | solution.py:34
  31.6 40.2 %collective-permute-start.1 = (f32[3,2,16,128]{3,2,1,0:T(8,128)S(1)}, f32[3,2,16,128]{3,2,1,0:T(8,128)S(1)}, u32[]{:S(2)}, u32[]{:S(2)}) collective-permute-start(f32[3,2,16,128]{3,2,1,0:T(8,128)S(1)} %get-tuple-element.133), channel_id=1, source_target_pairs={{0,8},{8,16},{16,24},{24,32},{32,40},{40,48},{48,56},{56,64},{64,7... | collective-permute-start | bytes 147464 | tf_op jit(solution)/shard_map/ppermute | solution.py:33
  97.2 21.9 %copy-start.1 = (f32[8,16,128]{2,1,0:T(8,128)S(1)}, f32[8,16,128]{2,1,0:T(8,128)}, u32[]{:S(2)}) copy-start(f32[8,16,128]{2,1,0:T(8,128)} %param.18) | copy-start | bytes 196612
  97.2 21.9 %copy-start.6 = (f32[8,16,128]{2,1,0:T(8,128)S(1)}, f32[8,16,128]{2,1,0:T(8,128)}, u32[]{:S(2)}) copy-start(f32[8,16,128]{2,1,0:T(8,128)} %param.17) | copy-start | bytes 196612
  102.5 11.8 %collective-permute-start.6 = (f32[3,8,2,128]{3,1,2,0:T(8,128)S(1)}, f32[3,8,2,128]{3,1,2,0:T(8,128)S(1)}, u32[]{:S(2)}, u32[]{:S(2)}) collective-permute-start(f32[3,8,2,128]{3,1,2,0:T(8,128)S(1)} %copy.429), channel_id=1, source_target_pairs={{0,1},{1,2},{2,3},{3,4},{4,5},{5,6},{6,7},{8,9},{9,10},{10,11},{11... | collective-permute-start | bytes 73736 | tf_op jit(solution)/shard_map/ppermute | solution.py:33
  104.4 9.9 %collective-permute-start.7 = (f32[3,8,2,128]{3,1,2,0:T(8,128)S(1)}, f32[3,8,2,128]{3,1,2,0:T(8,128)S(1)}, u32[]{:S(2)}, u32[]{:S(2)}) collective-permute-start(f32[3,8,2,128]{3,1,2,0:T(8,128)S(1)} %copy.430), channel_id=1, source_target_pairs={{1,0},{2,1},{3,2},{4,3},{5,4},{6,5},{7,6},{9,8},{10,9},{11,10},{12... | collective-permute-start | bytes 73736 | tf_op jit(solution)/shard_map/ppermute | solution.py:34
  108.3 6.2 %collective-permute-start.4 = (f32[3,2,16,128]{3,2,1,0:T(8,128)S(1)}, f32[3,2,16,128]{3,2,1,0:T(8,128)S(1)}, u32[]{:S(2)}, u32[]{:S(2)}) collective-permute-start(f32[3,2,16,128]{3,2,1,0:T(8,128)S(1)} %get-tuple-element.126), channel_id=1, source_target_pairs={{0,8},{8,16},{16,24},{24,32},{32,40},{40,48},{48,56},{56,64},{64,7... | collective-permute-start | bytes 147464 | tf_op jit(solution)/shard_map/ppermute | solution.py:33
  110.9 8.1 %collective-permute-start.5 = (f32[3,2,16,128]{3,2,1,0:T(8,128)S(1)}, f32[3,2,16,128]{3,2,1,0:T(8,128)S(1)}, u32[]{:S(2)}, u32[]{:S(2)}) collective-permute-start(f32[3,2,16,128]{3,2,1,0:T(8,128)S(1)} %get-tuple-element.127), channel_id=1, source_target_pairs={{8,0},{16,8},{24,16},{32,24},{40,32},{48,40},{56,48},{64,56},{72,6... | collective-permute-start | bytes 147464 | tf_op jit(solution)/shard_map/ppermute | solution.py:34
  119.7 15.2 %collective-permute-start.8 = (f32[3,2,16,128]{3,2,1,0:T(8,128)S(1)}, f32[3,2,16,128]{3,2,1,0:T(8,128)S(1)}, u32[]{:S(2)}, u32[]{:S(2)}) collective-permute-start(f32[3,2,16,128]{3,2,1,0:T(8,128)S(1)} %get-tuple-element.119), channel_id=1, source_target_pairs={{8,0},{16,8},{24,16},{32,24},{40,32},{48,40},{56,48},{64,56},{72,6... | collective-permute-start | bytes 147464 | tf_op jit(solution)/shard_map/ppermute | solution.py:34
  121.6 13.3 %collective-permute-start.9 = (f32[3,2,16,128]{3,2,1,0:T(8,128)S(1)}, f32[3,2,16,128]{3,2,1,0:T(8,128)S(1)}, u32[]{:S(2)}, u32[]{:S(2)}) collective-permute-start(f32[3,2,16,128]{3,2,1,0:T(8,128)S(1)} %get-tuple-element.120), channel_id=1, source_target_pairs={{0,8},{8,16},{16,24},{24,32},{32,40},{40,48},{48,56},{56,64},{64,7... | collective-permute-start | bytes 147464 | tf_op jit(solution)/shard_map/ppermute | solution.py:33
  127.7 5.8 %collective-permute-start.10 = (f32[3,8,2,128]{3,1,2,0:T(8,128)S(1)}, f32[3,8,2,128]{3,1,2,0:T(8,128)S(1)}, u32[]{:S(2)}, u32[]{:S(2)}) collective-permute-start(f32[3,8,2,128]{3,1,2,0:T(8,128)S(1)} %copy.433), channel_id=1, source_target_pairs={{0,1},{1,2},{2,3},{3,4},{4,5},{5,6},{6,7},{8,9},{9,10},{10,11},{11... | collective-permute-start | bytes 73736 | tf_op jit(solution)/shard_map/ppermute | solution.py:33
  129.6 5.1 %collective-permute-start.11 = (f32[3,8,2,128]{3,1,2,0:T(8,128)S(1)}, f32[3,8,2,128]{3,1,2,0:T(8,128)S(1)}, u32[]{:S(2)}, u32[]{:S(2)}) collective-permute-start(f32[3,8,2,128]{3,1,2,0:T(8,128)S(1)} %copy.434), channel_id=1, source_target_pairs={{1,0},{2,1},{3,2},{4,3},{5,4},{6,5},{7,6},{9,8},{10,9},{11,10},{12... | collective-permute-start | bytes 73736 | tf_op jit(solution)/shard_map/ppermute | solution.py:34
  133.5 17.9 %copy-start.7 = (f32[8,16,128]{2,1,0:T(8,128)S(1)}, f32[8,16,128]{2,1,0:T(8,128)}, u32[]{:S(2)}) copy-start(f32[8,16,128]{2,1,0:T(8,128)} %param.22) | copy-start | bytes 196612
  135.2 17.2 %copy-start.8 = (f32[8,16,128]{2,1,0:T(8,128)S(1)}, f32[8,16,128]{2,1,0:T(8,128)}, u32[]{:S(2)}) copy-start(f32[8,16,128]{2,1,0:T(8,128)} %param.21) | copy-start | bytes 196612
  135.6 17.6 %copy-start.2 = (f32[3,8,16,128]{3,2,1,0:T(8,128)}, f32[3,8,16,128]{3,2,1,0:T(8,128)S(1)}, u32[]{:S(2)}) copy-start(f32[3,8,16,128]{3,2,1,0:T(8,128)S(1)} %fusion.10) | copy-start | bytes 589828
  135.6 11.6 %collective-permute-start.14 = (f32[3,8,2,128]{3,1,2,0:T(8,128)S(1)}, f32[3,8,2,128]{3,1,2,0:T(8,128)S(1)}, u32[]{:S(2)}, u32[]{:S(2)}) collective-permute-start(f32[3,8,2,128]{3,1,2,0:T(8,128)S(1)} %copy.439), channel_id=1, source_target_pairs={{0,1},{1,2},{2,3},{3,4},{4,5},{5,6},{6,7},{8,9},{9,10},{10,11},{11... | collective-permute-start | bytes 73736 | tf_op jit(solution)/shard_map/ppermute | solution.py:33
  139.0 8.3 %collective-permute-start.15 = (f32[3,8,2,128]{3,1,2,0:T(8,128)S(1)}, f32[3,8,2,128]{3,1,2,0:T(8,128)S(1)}, u32[]{:S(2)}, u32[]{:S(2)}) collective-permute-start(f32[3,8,2,128]{3,1,2,0:T(8,128)S(1)} %copy.440), channel_id=1, source_target_pairs={{1,0},{2,1},{3,2},{4,3},{5,4},{6,5},{7,6},{9,8},{10,9},{11,10},{12... | collective-permute-start | bytes 73736 | tf_op jit(solution)/shard_map/ppermute | solution.py:34
  141.4 6.0 %collective-permute-start.12 = (f32[3,2,16,128]{3,2,1,0:T(8,128)S(1)}, f32[3,2,16,128]{3,2,1,0:T(8,128)S(1)}, u32[]{:S(2)}, u32[]{:S(2)}) collective-permute-start(f32[3,2,16,128]{3,2,1,0:T(8,128)S(1)} %get-tuple-element.114), channel_id=1, source_target_pairs={{0,8},{8,16},{16,24},{24,32},{32,40},{40,48},{48,56},{56,64},{64,7... | collective-permute-start | bytes 147464 | tf_op jit(solution)/shard_map/ppermute | solution.py:33
  143.3 8.1 %collective-permute-start.13 = (f32[3,2,16,128]{3,2,1,0:T(8,128)S(1)}, f32[3,2,16,128]{3,2,1,0:T(8,128)S(1)}, u32[]{:S(2)}, u32[]{:S(2)}) collective-permute-start(f32[3,2,16,128]{3,2,1,0:T(8,128)S(1)} %get-tuple-element.113), channel_id=1, source_target_pairs={{8,0},{16,8},{24,16},{32,24},{40,32},{48,40},{56,48},{64,56},{72,6... | collective-permute-start | bytes 147464 | tf_op jit(solution)/shard_map/ppermute | solution.py:34
  (4 other events, 25.1 us)

commit v3 on v2

--- a/solution.py
+++ b/solution.py
@@ -40,20 +40,37 @@
     return jnp.pad(block, pads)
 
 
-def advance(velocity, stress, lame_first, shear_modulus, buoyancy, strain_now, surface, lame_kernel, shear_kernel):
+def halo_x(block):
+    return halo_pad(block, "gx", 1)
+
+
+def halo_y(block):
+    return halo_pad(block, "gy", 2)
+
+
+def zero_x(block):
+    return jnp.pad(block, ((0, 0), (2, 2), (0, 0), (0, 0)))
+
+
+def zero_y(block):
+    return jnp.pad(block, ((0, 0), (0, 0), (2, 2), (0, 0)))
+
+
+def advance(velocity, stress, lame_first, shear_modulus, buoyancy, strain_now, surface, lame_kernel, shear_kernel, pad_x, pad_y):
     nx = velocity.shape[1]
     ny = velocity.shape[2]
     nz = velocity.shape[3]
-    sx = halo_pad(jnp.stack([stress[0], stress[3], stress[4]]), "gx", 1)
-    sy = halo_pad(jnp.stack([stress[3], stress[1], stress[5]]), "gy", 2)
+    sx = pad_x(jnp.stack([stress[0], stress[3], stress[4]]))
+    sy = pad_y(jnp.stack([stress[3], stress[1], stress[5]]))
     sz = z_pad(jnp.stack([stress[4], stress[5], stress[2]]))
     force_first = forward_diff(sx[0], nx, 0) + backward_diff(sy[0], ny, 1) + backward_diff(sz[0], nz, 2)
     force_second = backward_diff(sx[1], nx, 0) + forward_diff(sy[1], ny, 1) + backward_diff(sz[1], nz, 2)
     force_third = backward_diff(sx[2], nx, 0) + backward_diff(sy[2], ny, 1) + forward_diff(sz[2], nz, 2)
-    force_third = force_third.at[:, :, 0].add(surface)
+    if surface is not None:
+        force_third = force_third.at[:, :, 0].add(surface)
     moved = velocity + time_step * buoyancy[None] * jnp.stack([force_first, force_second, force_third])
-    mx = halo_pad(moved, "gx", 1)
-    my = halo_pad(moved, "gy", 2)
+    mx = pad_x(moved)
+    my = pad_y(moved)
     mz = z_pad(moved)
     rate_first = backward_diff(mx[0], nx, 0)
     rate_second = backward_diff(my[1], ny, 1)
@@ -139,14 +156,50 @@
     return adjoint, surfaces
 
 
+def wide_halo(block, width):
+    return halo_pad(halo_pad(block, "gx", 1, width), "gy", 2, width)
+
+
 def shards(velocity, stress, lame_first, shear_modulus, buoyancy, forward_strain, lame_accum, shear_accum, residuals, station_cell, station_pairs):
     step_count = forward_strain.shape[0] // 6
-    adjoint, surfaces = station_part(residuals, station_cell, station_pairs, velocity.shape[1], velocity.shape[2], step_count)
+    nx = velocity.shape[1]
+    ny = velocity.shape[2]
+    reach = 6
+    depth = 8
+    adjoint, surfaces = station_part(residuals, station_cell, station_pairs, nx, ny, step_count)
+    free_v, free_s, free_l, free_k = velocity, stress, lame_accum, shear_accum
     for window_step in range(step_count):
         strain_now = forward_strain[6 * window_step : 6 * window_step + 6]
-        velocity, stress, lame_accum, shear_accum = advance(
-            velocity, stress, lame_first, shear_modulus, buoyancy, strain_now, surfaces[window_step], lame_accum, shear_accum
+        free_v, free_s, free_l, free_k = advance(
+            free_v, free_s, lame_first, shear_modulus, buoyancy, strain_now, None, free_l, free_k, halo_x, halo_y
         )
+    params = wide_halo(jnp.stack([lame_first, shear_modulus, buoyancy])[:, :, :, :depth], reach)
+    gathered = lax.all_gather(surfaces, ("gx", "gy"), tiled=False)
+    rows_x = lax.axis_size("gx")
+    rows_y = lax.axis_size("gy")
+    whole = gathered.reshape(rows_x, rows_y, step_count, nx, ny).transpose(2, 0, 3, 1, 4)
+    whole = whole.reshape(step_count, rows_x * nx, rows_y * ny)
+    whole = jnp.pad(whole, ((0, 0), (reach, reach), (reach, reach)))
+    near = lax.dynamic_slice(
+        whole, (0, lax.axis_index("gx") * nx, lax.axis_index("gy") * ny), (step_count, nx + 2 * reach, ny + 2 * reach)
+    )
+    wx = nx + 2 * reach
+    wy = ny + 2 * reach
+    src_v = jnp.zeros((3, wx, wy, depth), jnp.float32)
+    src_s = jnp.zeros((6, wx, wy, depth), jnp.float32)
+    src_l = jnp.zeros((wx, wy, depth), jnp.float32)
+    src_k = jnp.zeros((wx, wy, depth), jnp.float32)
+    for window_step in range(step_count):
+        strain_now = forward_strain[6 * window_step : 6 * window_step + 6, :, :, :depth]
+        strain_now = jnp.pad(strain_now, ((0, 0), (reach, reach), (reach, reach), (0, 0)))
+        src_v, src_s, src_l, src_k = advance(
+            src_v, src_s, params[0], params[1], params[2], strain_now, near[window_step], src_l, src_k, zero_x, zero_y
+        )
+    inner = (slice(reach, reach + nx), slice(reach, reach + ny))
+    velocity = free_v.at[:, :, :, :depth].add(src_v[(slice(None),) + inner])
+    stress = free_s.at[:, :, :, :depth].add(src_s[(slice(None),) + inner])
+    lame_accum = free_l.at[:, :, :depth].add(src_l[inner])
+    shear_accum = free_k.at[:, :, :depth].add(src_k[inner])
     return (velocity, stress, lame_accum, shear_accum, adjoint)
 
 

time: 155 us -> 254 us (1.64); the launches traced: 154 us -> 249 us
  blocking collectives: 0 us -> 34.8 us
  local copies, waits for them, and re-layouts: 17.3 us -> 51.5 us
  other arithmetic: 28 us -> 56.4 us
  waiting for transfers between devices: 41.5 us -> 30.8 us
  starting transfers between devices: 60.8 us -> 71 us
    all_gather x0 -> x1, blocking collectives: none -> 34.8 us  [shards(): gathered = lax.all_gather(surfaces, ('gx', 'gy'), tiled=False)]
    ppermute x8 -> x10, waiting for transfers between devices: 26.7 us -> 16.8 us  [halo_pad(): lax.ppermute(lax.slice_in_dim(block, size - width, size, axis=dim), axis,...]
    unnamed x26 -> x120, local copies, waits for them, and re-layouts: 6.33 us -> 13.3 us
    scatter-add x0 -> x4, local copies, waits for them, and re-layouts: none -> 5.64 us  [the longest x1 4.62 us: shards(): stress = free_s.at[:, :, :, :depth].add(src_s[(slice(None),) + inner])]
    ppermute x8 -> x10, starting transfers between devices: 24.9 us -> 30.2 us  [halo_pad(): lax.ppermute(lax.slice_in_dim(block, 0, width, axis=dim), axis, backward)]
    ppermute x8 -> x10, starting transfers between devices: 25.1 us -> 29.9 us  [halo_pad(): lax.ppermute(lax.slice_in_dim(block, size - width, size, axis=dim), axis,...]
    add x0 -> x4, other arithmetic: none -> 4.67 us  [the longest x1 1.49 us: shards(): shear_accum = free_k.at[:, :, :depth].add(src_k[inner])]
    scatter-add x2, local copies, waits for them, and re-layouts: 0.23 us -> 4.7 us  [advance(): force_third = force_third.at[:, :, 0].add(surface)]
  transfers between devices with their start and end apart: 17 -> 21, of which waited for: 6 -> 6; matrix products, arithmetic and copies ran while one was open for 4% -> 12% of each run, Pallas kernels for 0% -> 0%
where the time goes in v3:
time: 254 us; the launch traced here: 249 us
  starting transfers between devices  71 us (28%)
  other arithmetic  56.4 us (22%)
  local copies, waits for them, and re-layouts  51.5 us (20%)
  blocking collectives  34.8 us (14%)
  waiting for transfers between devices  30.8 us (12%)
  matrix products  2.6 us (1%)
    all_gather x1, blocking collectives, shards(): gathered = lax.all_gather(surfaces, ('gx', 'gy'), tiled=False)  34.8 us
    ppermute x10, starting transfers between devices, halo_pad(): lax.ppermute(lax.slice_in_dim(block, 0, width, axis=dim), axis, backward)  30.2 us
    ppermute x10, starting transfers between devices, halo_pad(): lax.ppermute(lax.slice_in_dim(block, size - width, size, axis=dim), axis,...  29.9 us
    ppermute x10, waiting for transfers between devices, halo_pad(): lax.ppermute(lax.slice_in_dim(block, size - width, size, axis=dim), axis,...  16.8 us
    ppermute x10, waiting for transfers between devices, halo_pad(): lax.ppermute(lax.slice_in_dim(block, 0, width, axis=dim), axis, backward)  14 us
    unnamed x120, local copies, waits for them, and re-layouts  13.3 us
    reduce_sum x1, other arithmetic, station_part(): jnp.mean(mine_vals * other_vals, axis=(2, 3), keepdims=True)  11.3 us
    all_to_all x1, starting transfers between devices, station_part(): lax.all_to_all(send, ('gx', 'gy'), split_axis=0, concat_axis=0, tiled=True)  10.8 us
  transfers between devices with their start and end apart: 21, of which 6 were waited for; matrix products, arithmetic and copies ran while one was open for 12% of the time, Pallas kernels for 0%

profile of v3, /device:TPU:14, one launch (start us, length us, event | category | flops | bytes accessed | tf_op | source)
XLA Modules:
  0.0 249.3 jit_solution(10267649325880405959)
XLA Ops:
  4.0 3.5 %gather_fusion = bf16[512,32,128]{2,1,0:T(8,128)(2,1)} fusion(bf16[32,32,128]{2,1,0:T(8,128)(2,1)S(1)} %bitcast.514, s32[1024]{0:T(1024)S(1)} %pad_clamp_fusion.1), kind=kCustom, calls=%fused_computation | custom fusion | bytes 8390656 | tf_op jit(solution)/shard_map/gather | solution.py:129
  7.5 4.0 %broadcast_select_fusion.1 = bf16[128,4,32,128]{3,2,1,0:T(8,128)(2,1)} fusion(bf16[128,4,32,128]{3,2,1,0:T(8,128)(2,1)} %bitcast.519, pred[128,4]{1,0:T(8,128)(4,1)S(1)} %copy.604), kind=kLoop, calls=%fused_computation.24 | loop fusion | flops 2097152 | bytes 8389120 | tf_op jit(solution)/shard_map/jit(_where)/select_n | solution.py:128
  11.5 10.8 %all-to-all-start = ((bf16[128,4,32,128]{3,2,1,0:T(8,128)(2,1)}), bf16[128,4,32,128]{3,2,1,0:T(8,128)(2,1)}, u32[]{:S(2)}, u32[]{:S(2)}) async-start(bf16[128,4,32,128]{3,2,1,0:T(8,128)(2,1)} %broadcast_select_fusion.1), calls=%async_computation | async-start | bytes 8388608 | tf_op jit(solution)/shard_map/all_to_all | solution.py:131
  23.1 3.5 %collective-permute-start.12 = (f32[3,6,16,8]{3,2,1,0:T(8,128)}, f32[3,6,16,8]{3,2,1,0:T(8,128)}, u32[]{:S(2)}, u32[]{:S(2)}) collective-permute-start(f32[3,6,16,8]{3,2,1,0:T(8,128)} %get-tuple-element.241), channel_id=1, source_target_pairs={{0,8},{8,16},{16,24},{24,32},{32,40},{40,48},{48,56},{56,64},{64,7... | collective-permute-start | bytes 27656 | tf_op jit(solution)/shard_map/ppermute | solution.py:33
  32.3 3.6 %collective-permute-start.3 = (f32[3,8,2,128]{3,1,2,0:T(8,128)}, f32[3,8,2,128]{3,1,2,0:T(8,128)}, u32[]{:S(2)}, u32[]{:S(2)}) collective-permute-start(f32[3,8,2,128]{3,1,2,0:T(8,128)} %copy.588), channel_id=1, source_target_pairs={{1,0},{2,1},{3,2},{4,3},{5,4},{6,5},{7,6},{9,8},{10,9},{11,10},{12... | collective-permute-start | bytes 73736 | tf_op jit(solution)/shard_map/ppermute | solution.py:34
  37.2 2.8 %collective-permute-start = (f32[3,2,16,128]{3,2,1,0:T(8,128)}, f32[3,2,16,128]{3,2,1,0:T(8,128)}, u32[]{:S(2)}, u32[]{:S(2)}) collective-permute-start(f32[3,2,16,128]{3,2,1,0:T(8,128)} %get-tuple-element.258), channel_id=1, source_target_pairs={{8,0},{16,8},{24,16},{32,24},{40,32},{48,40},{56,48},{64,56},{72,6... | collective-permute-start | bytes 147464 | tf_op jit(solution)/shard_map/ppermute | solution.py:34
  54.6 16.7 %collective-permute-done.12 = f32[3,6,16,8]{3,2,1,0:T(8,128)} collective-permute-done((f32[3,6,16,8]{3,2,1,0:T(8,128)}, f32[3,6,16,8]{3,2,1,0:T(8,128)}, u32[]{:S(2)}, u32[]{:S(2)}) %collective-permute-start.12) | collective-permute-done | bytes 9248 | tf_op jit(solution)/shard_map/ppermute | solution.py:33
  71.4 2.9 %collective-permute-done.13 = f32[3,6,16,8]{3,2,1,0:T(8,128)} collective-permute-done((f32[3,6,16,8]{3,2,1,0:T(8,128)}, f32[3,6,16,8]{3,2,1,0:T(8,128)}, u32[]{:S(2)}, u32[]{:S(2)}) %collective-permute-start.13) | collective-permute-done | bytes 9248 | tf_op jit(solution)/shard_map/ppermute | solution.py:34
  77.2 3.6 %collective-permute-start.15 = (f32[3,20,6,8]{3,2,1,0:T(8,128)S(1)}, f32[3,20,6,8]{3,2,1,0:T(8,128)S(1)}, u32[]{:S(2)}, u32[]{:S(2)}) collective-permute-start(f32[3,20,6,8]{3,2,1,0:T(8,128)S(1)} %get-tuple-element.197), channel_id=1, source_target_pairs={{1,0},{2,1},{3,2},{4,3},{5,4},{6,5},{7,6},{9,8},{10,9},{11,10},{12... | collective-permute-start | bytes 34568 | tf_op jit(solution)/shard_map/ppermute | solution.py:34
  81.0 3.6 %gather_fusion.1 = bf16[512,32,128]{2,1,0:T(8,128)(2,1)} fusion(bf16[32,32,128]{2,1,0:T(8,128)(2,1)S(1)} %bitcast.515, s32[1024]{0:T(1024)S(1)} %pad_clamp_fusion), kind=kCustom, calls=%fused_computation.1 | custom fusion | bytes 8390656 | tf_op jit(solution)/shard_map/gather | solution.py:134
  84.9 3.0 %collective-permute-start.1 = (f32[3,2,16,128]{3,2,1,0:T(8,128)S(1)}, f32[3,2,16,128]{3,2,1,0:T(8,128)S(1)}, u32[]{:S(2)}, u32[]{:S(2)}) collective-permute-start(f32[3,2,16,128]{3,2,1,0:T(8,128)S(1)} %copy-done.56), channel_id=1, source_target_pairs={{0,8},{8,16},{16,24},{24,32},{32,40},{40,48},{48,56},{56,64},{64,7... | collective-permute-start | bytes 147464 | tf_op jit(solution)/shard_map/ppermute | solution.py:33
  94.4 3.6 %collective-permute-start.7 = (f32[3,8,2,128]{3,1,2,0:T(8,128)S(1)}, f32[3,8,2,128]{3,1,2,0:T(8,128)S(1)}, u32[]{:S(2)}, u32[]{:S(2)}) collective-permute-start(f32[3,8,2,128]{3,1,2,0:T(8,128)S(1)} %copy.592), channel_id=1, source_target_pairs={{1,0},{2,1},{3,2},{4,3},{5,4},{6,5},{7,6},{9,8},{10,9},{11,10},{12... | collective-permute-start | bytes 73736 | tf_op jit(solution)/shard_map/ppermute | solution.py:34
  98.2 4.9 %collective-permute-start.4 = (f32[3,2,16,128]{3,2,1,0:T(8,128)S(1)}, f32[3,2,16,128]{3,2,1,0:T(8,128)S(1)}, u32[]{:S(2)}, u32[]{:S(2)}) collective-permute-start(f32[3,2,16,128]{3,2,1,0:T(8,128)S(1)} %get-tuple-element.252), channel_id=1, source_target_pairs={{0,8},{8,16},{16,24},{24,32},{32,40},{40,48},{48,56},{56,64},{64,7... | collective-permute-start | bytes 147464 | tf_op jit(solution)/shard_map/ppermute | solution.py:33
  105.2 6.0 %collective-permute-done.5 = f32[3,2,16,128]{3,2,1,0:T(8,128)S(1)} collective-permute-done((f32[3,2,16,128]{3,2,1,0:T(8,128)S(1)}, f32[3,2,16,128]{3,2,1,0:T(8,128)S(1)}, u32[]{:S(2)}, u32[]{:S(2)}) %collective-permute-start.5) | collective-permute-done | bytes 49184 | tf_op jit(solution)/shard_map/ppermute | solution.py:34
  113.8 6.0 %collective-permute-start.9 = (f32[3,2,16,128]{3,2,1,0:T(8,128)S(1)}, f32[3,2,16,128]{3,2,1,0:T(8,128)S(1)}, u32[]{:S(2)}, u32[]{:S(2)}) collective-permute-start(f32[3,2,16,128]{3,2,1,0:T(8,128)S(1)} %get-tuple-element.246), channel_id=1, source_target_pairs={{0,8},{8,16},{16,24},{24,32},{32,40},{40,48},{48,56},{56,64},{64,7... | collective-permute-start | bytes 147464 | tf_op jit(solution)/shard_map/ppermute | solution.py:33
  121.8 3.6 %collective-permute-start.11 = (f32[3,8,2,128]{3,1,2,0:T(8,128)S(1)}, f32[3,8,2,128]{3,1,2,0:T(8,128)S(1)}, u32[]{:S(2)}, u32[]{:S(2)}) collective-permute-start(f32[3,8,2,128]{3,1,2,0:T(8,128)S(1)} %copy.596), channel_id=1, source_target_pairs={{1,0},{2,1},{3,2},{4,3},{5,4},{6,5},{7,6},{9,8},{10,9},{11,10},{12... | collective-permute-start | bytes 73736 | tf_op jit(solution)/shard_map/ppermute | solution.py:34
  127.7 2.9 %collective-permute-start.18 = (f32[3,8,2,128]{3,1,2,0:T(8,128)S(1)}, f32[3,8,2,128]{3,1,2,0:T(8,128)S(1)}, u32[]{:S(2)}, u32[]{:S(2)}) collective-permute-start(f32[3,8,2,128]{3,1,2,0:T(8,128)S(1)} %copy.621), channel_id=1, source_target_pairs={{0,1},{1,2},{2,3},{3,4},{4,5},{5,6},{6,7},{8,9},{9,10},{10,11},{11... | collective-permute-start | bytes 73736 | tf_op jit(solution)/shard_map/ppermute | solution.py:33
  135.4 4.1 %collective-permute-start.17 = (f32[3,2,16,128]{3,2,1,0:T(8,128)S(1)}, f32[3,2,16,128]{3,2,1,0:T(8,128)S(1)}, u32[]{:S(2)}, u32[]{:S(2)}) collective-permute-start(f32[3,2,16,128]{3,2,1,0:T(8,128)S(1)} %get-tuple-element.237), channel_id=1, source_target_pairs={{8,0},{16,8},{24,16},{32,24},{40,32},{48,40},{56,48},{64,56},{72,6... | collective-permute-start | bytes 147464 | tf_op jit(solution)/shard_map/ppermute | solution.py:34
  139.6 3.8 %collective-permute-done.17 = f32[3,2,16,128]{3,2,1,0:T(8,128)S(1)} collective-permute-done((f32[3,2,16,128]{3,2,1,0:T(8,128)S(1)}, f32[3,2,16,128]{3,2,1,0:T(8,128)S(1)}, u32[]{:S(2)}, u32[]{:S(2)}) %collective-permute-start.17) | collective-permute-done | bytes 49184 | tf_op jit(solution)/shard_map/ppermute | solution.py:34
  146.1 11.3 %fusion.3 = (f32[128,4]{1,0:T(8,128)S(1)}, f32[128,4]{1,0:T(8,128)S(1)}, f32[128,4]{1,0:T(8,128)S(1)}) fusion(bf16[128,4,32,128]{3,2,1,0:T(8,128)(2,1)} %all-to-all-done, bf16[128,4,32,128]{3,2,1,0:T(8,128)(2,1)} %bitcast.516, pred[128,4]{1,0:T(8,128)(4,1)S(1)} %copy.608), kind=kLoop, calls=%fused_computation.10 | loop fusion | flops 18872832 | bytes 8395264 | tf_op jit(solution)/shard_map/reduce_sum | solution.py:140
  158.0 7.2 %fusion.2 = bf16[128,4,32,128]{3,2,1,0:T(8,128)(2,1)S(1)} fusion(bf16[128,4,32,128]{3,2,1,0:T(8,128)(2,1)} %all-to-all-done, f32[128,4]{1,0:T(8,128)S(1)} %copy.613, f32[128,4]{1,0:T(8,128)S(1)} %copy.612, f32[128,4]{1,0:T(8,128)S(1)} %copy.607, pred[128,4]{1,0:T(8,128)(4,1)S(1)} %copy.608, bf16[512,32,128]{2,1,0:T(8,128)(2,1)} %gather_fusion.1), kind=kLoop, calls=%fused_computation.9 | loop fusion | flops 16777216 | bytes 12589568 | tf_op jit(solution)/shard_map/convert_element_type | solution.py:141
  165.2 4.3 %copy.633 = bf16[64,8,32,128]{3,1,2,0:T(8,128)(2,1)S(1)} copy(bf16[64,8,32,128]{3,2,1,0:T(8,128)(2,1)S(1)} %bitcast.517) | data formatting | bytes 8388608
  170.1 34.8 %all-gather = f32[256,8,16]{2,1,0:T(8,128)S(1)} all-gather(f32[2,8,16]{2,1,0:T(8,128)S(1)} %pad_maximum_fusion.23), channel_id=2, replica_groups=mesh['gx'=16,'gy'=8] {'gx','gy'}, dimensions={0}, use_global_device_ids=true | all-gather | bytes 132096 | tf_op jit(solution)/shard_map/all_gather | solution.py:177
  243.2 4.6 %scatter-add.25 = f32[6,8,16,128]{3,2,1,0:T(8,128)S(1)} dynamic-update-slice(f32[6,8,16,128]{3,2,1,0:T(8,128)S(1)} %copy-done.25, f32[6,8,16,8]{3,2,1,0:T(8,128)S(1)} %fusion.10, s32[]{:T(128)} %constant.224.clone.1, s32[]{:T(128)} %constant.224.clone.1, s32[]{:T(128)} %constant.224.clone.1, s32[]{:T(128)} %constant.224.clone.1) | dynamic-update-slice | bytes 49156 | tf_op jit(solution)/shard_map/scatter-add | solution.py:200
  (321 shorter events, 91.8 us)
Async XLA Ops:
  11.5 134.6 %all-to-all-start = ((bf16[128,4,32,128]{3,2,1,0:T(8,128)(2,1)}), bf16[128,4,32,128]{3,2,1,0:T(8,128)(2,1)}, u32[]{:S(2)}, u32[]{:S(2)}) async-start(bf16[128,4,32,128]{3,2,1,0:T(8,128)(2,1)} %broadcast_select_fusion.1), calls=%async_computation | async-start | bytes 8388608 | tf_op jit(solution)/shard_map/all_to_all | solution.py:131
  23.1 48.2 %collective-permute-start.12 = (f32[3,6,16,8]{3,2,1,0:T(8,128)}, f32[3,6,16,8]{3,2,1,0:T(8,128)}, u32[]{:S(2)}, u32[]{:S(2)}) collective-permute-start(f32[3,6,16,8]{3,2,1,0:T(8,128)} %get-tuple-element.241), channel_id=1, source_target_pairs={{0,8},{8,16},{16,24},{24,32},{32,40},{40,48},{48,56},{56,64},{64,7... | collective-permute-start | bytes 27656 | tf_op jit(solution)/shard_map/ppermute | solution.py:33
  26.7 47.6 %collective-permute-start.13 = (f32[3,6,16,8]{3,2,1,0:T(8,128)}, f32[3,6,16,8]{3,2,1,0:T(8,128)}, u32[]{:S(2)}, u32[]{:S(2)}) collective-permute-start(f32[3,6,16,8]{3,2,1,0:T(8,128)} %get-tuple-element.242), channel_id=1, source_target_pairs={{8,0},{16,8},{24,16},{32,24},{40,32},{48,40},{56,48},{64,56},{72,6... | collective-permute-start | bytes 27656 | tf_op jit(solution)/shard_map/ppermute | solution.py:34
  29.7 59.4 %collective-permute-start.2 = (f32[3,8,2,128]{3,1,2,0:T(8,128)}, f32[3,8,2,128]{3,1,2,0:T(8,128)}, u32[]{:S(2)}, u32[]{:S(2)}) collective-permute-start(f32[3,8,2,128]{3,1,2,0:T(8,128)} %copy.587), channel_id=1, source_target_pairs={{0,1},{1,2},{2,3},{3,4},{4,5},{5,6},{6,7},{8,9},{9,10},{10,11},{11... | collective-permute-start | bytes 73736 | tf_op jit(solution)/shard_map/ppermute | solution.py:33
  32.3 57.8 %collective-permute-start.3 = (f32[3,8,2,128]{3,1,2,0:T(8,128)}, f32[3,8,2,128]{3,1,2,0:T(8,128)}, u32[]{:S(2)}, u32[]{:S(2)}) collective-permute-start(f32[3,8,2,128]{3,1,2,0:T(8,128)} %copy.588), channel_id=1, source_target_pairs={{1,0},{2,1},{3,2},{4,3},{5,4},{6,5},{7,6},{9,8},{10,9},{11,10},{12... | collective-permute-start | bytes 73736 | tf_op jit(solution)/shard_map/ppermute | solution.py:34
  37.2 53.7 %collective-permute-start = (f32[3,2,16,128]{3,2,1,0:T(8,128)}, f32[3,2,16,128]{3,2,1,0:T(8,128)}, u32[]{:S(2)}, u32[]{:S(2)}) collective-permute-start(f32[3,2,16,128]{3,2,1,0:T(8,128)} %get-tuple-element.258), channel_id=1, source_target_pairs={{8,0},{16,8},{24,16},{32,24},{40,32},{48,40},{56,48},{64,56},{72,6... | collective-permute-start | bytes 147464 | tf_op jit(solution)/shard_map/ppermute | solution.py:34
  54.6 154.2 %copy-start.20 = (f32[1,20,28,8]{3,2,1,0:T(8,128)}, f32[1,20,28,8]{3,2,1,0:T(8,128)S(1)}, u32[]{:S(2)}) copy-start(f32[1,20,28,8]{3,2,1,0:T(8,128)S(1)} %get-tuple-element.188) | copy-start | bytes 53764
  75.3 9.5 %collective-permute-start.14 = (f32[3,20,6,8]{3,2,1,0:T(8,128)S(1)}, f32[3,20,6,8]{3,2,1,0:T(8,128)S(1)}, u32[]{:S(2)}, u32[]{:S(2)}) collective-permute-start(f32[3,20,6,8]{3,2,1,0:T(8,128)S(1)} %get-tuple-element.196), channel_id=1, source_target_pairs={{0,1},{1,2},{2,3},{3,4},{4,5},{5,6},{6,7},{8,9},{9,10},{10,11},{11... | collective-permute-start | bytes 34568 | tf_op jit(solution)/shard_map/ppermute | solution.py:33
  77.2 10.6 %collective-permute-start.15 = (f32[3,20,6,8]{3,2,1,0:T(8,128)S(1)}, f32[3,20,6,8]{3,2,1,0:T(8,128)S(1)}, u32[]{:S(2)}, u32[]{:S(2)}) collective-permute-start(f32[3,20,6,8]{3,2,1,0:T(8,128)S(1)} %get-tuple-element.197), channel_id=1, source_target_pairs={{1,0},{2,1},{3,2},{4,3},{5,4},{6,5},{7,6},{9,8},{10,9},{11,10},{12... | collective-permute-start | bytes 34568 | tf_op jit(solution)/shard_map/ppermute | solution.py:34
  84.9 6.1 %collective-permute-start.1 = (f32[3,2,16,128]{3,2,1,0:T(8,128)S(1)}, f32[3,2,16,128]{3,2,1,0:T(8,128)S(1)}, u32[]{:S(2)}, u32[]{:S(2)}) collective-permute-start(f32[3,2,16,128]{3,2,1,0:T(8,128)S(1)} %copy-done.56), channel_id=1, source_target_pairs={{0,8},{8,16},{16,24},{24,32},{32,40},{40,48},{48,56},{56,64},{64,7... | collective-permute-start | bytes 147464 | tf_op jit(solution)/shard_map/ppermute | solution.py:33
  89.1 119.7 %copy-start.19 = (f32[20,28,8]{2,1,0:T(8,128)}, f32[20,28,8]{2,1,0:T(8,128)S(1)}, u32[]{:S(2)}) copy-start(f32[20,28,8]{2,1,0:T(8,128)S(1)} %fusion.191) | copy-start | bytes 53764
  92.1 19.1 %copy-start.45 = (f32[8,16,128]{2,1,0:T(8,128)S(1)}, f32[8,16,128]{2,1,0:T(8,128)}, u32[]{:S(2)}) copy-start(f32[8,16,128]{2,1,0:T(8,128)} %param.25) | copy-start | bytes 196612
  92.4 12.6 %collective-permute-start.6 = (f32[3,8,2,128]{3,1,2,0:T(8,128)S(1)}, f32[3,8,2,128]{3,1,2,0:T(8,128)S(1)}, u32[]{:S(2)}, u32[]{:S(2)}) collective-permute-start(f32[3,8,2,128]{3,1,2,0:T(8,128)S(1)} %copy.591), channel_id=1, source_target_pairs={{0,1},{1,2},{2,3},{3,4},{4,5},{5,6},{6,7},{8,9},{9,10},{10,11},{11... | collective-permute-start | bytes 73736 | tf_op jit(solution)/shard_map/ppermute | solution.py:33
  94.4 10.7 %collective-permute-start.7 = (f32[3,8,2,128]{3,1,2,0:T(8,128)S(1)}, f32[3,8,2,128]{3,1,2,0:T(8,128)S(1)}, u32[]{:S(2)}, u32[]{:S(2)}) collective-permute-start(f32[3,8,2,128]{3,1,2,0:T(8,128)S(1)} %copy.592), channel_id=1, source_target_pairs={{1,0},{2,1},{3,2},{4,3},{5,4},{6,5},{7,6},{9,8},{10,9},{11,10},{12... | collective-permute-start | bytes 73736 | tf_op jit(solution)/shard_map/ppermute | solution.py:34
  98.2 7.0 %collective-permute-start.4 = (f32[3,2,16,128]{3,2,1,0:T(8,128)S(1)}, f32[3,2,16,128]{3,2,1,0:T(8,128)S(1)}, u32[]{:S(2)}, u32[]{:S(2)}) collective-permute-start(f32[3,2,16,128]{3,2,1,0:T(8,128)S(1)} %get-tuple-element.252), channel_id=1, source_target_pairs={{0,8},{8,16},{16,24},{24,32},{32,40},{40,48},{48,56},{56,64},{64,7... | collective-permute-start | bytes 147464 | tf_op jit(solution)/shard_map/ppermute | solution.py:33
  103.1 8.1 %collective-permute-start.5 = (f32[3,2,16,128]{3,2,1,0:T(8,128)S(1)}, f32[3,2,16,128]{3,2,1,0:T(8,128)S(1)}, u32[]{:S(2)}, u32[]{:S(2)}) collective-permute-start(f32[3,2,16,128]{3,2,1,0:T(8,128)S(1)} %get-tuple-element.253), channel_id=1, source_target_pairs={{8,0},{16,8},{24,16},{32,24},{40,32},{48,40},{56,48},{64,56},{72,6... | collective-permute-start | bytes 147464 | tf_op jit(solution)/shard_map/ppermute | solution.py:34
  111.9 15.2 %collective-permute-start.8 = (f32[3,2,16,128]{3,2,1,0:T(8,128)S(1)}, f32[3,2,16,128]{3,2,1,0:T(8,128)S(1)}, u32[]{:S(2)}, u32[]{:S(2)}) collective-permute-start(f32[3,2,16,128]{3,2,1,0:T(8,128)S(1)} %get-tuple-element.245), channel_id=1, source_target_pairs={{8,0},{16,8},{24,16},{32,24},{40,32},{48,40},{56,48},{64,56},{72,6... | collective-permute-start | bytes 147464 | tf_op jit(solution)/shard_map/ppermute | solution.py:34
  113.8 13.3 %collective-permute-start.9 = (f32[3,2,16,128]{3,2,1,0:T(8,128)S(1)}, f32[3,2,16,128]{3,2,1,0:T(8,128)S(1)}, u32[]{:S(2)}, u32[]{:S(2)}) collective-permute-start(f32[3,2,16,128]{3,2,1,0:T(8,128)S(1)} %get-tuple-element.246), channel_id=1, source_target_pairs={{0,8},{8,16},{16,24},{24,32},{32,40},{40,48},{48,56},{56,64},{64,7... | collective-permute-start | bytes 147464 | tf_op jit(solution)/shard_map/ppermute | solution.py:33
  119.9 5.8 %collective-permute-start.10 = (f32[3,8,2,128]{3,1,2,0:T(8,128)S(1)}, f32[3,8,2,128]{3,1,2,0:T(8,128)S(1)}, u32[]{:S(2)}, u32[]{:S(2)}) collective-permute-start(f32[3,8,2,128]{3,1,2,0:T(8,128)S(1)} %copy.595), channel_id=1, source_target_pairs={{0,1},{1,2},{2,3},{3,4},{4,5},{5,6},{6,7},{8,9},{9,10},{10,11},{11... | collective-permute-start | bytes 73736 | tf_op jit(solution)/shard_map/ppermute | solution.py:33
  121.8 5.1 %collective-permute-start.11 = (f32[3,8,2,128]{3,1,2,0:T(8,128)S(1)}, f32[3,8,2,128]{3,1,2,0:T(8,128)S(1)}, u32[]{:S(2)}, u32[]{:S(2)}) collective-permute-start(f32[3,8,2,128]{3,1,2,0:T(8,128)S(1)} %copy.596), channel_id=1, source_target_pairs={{1,0},{2,1},{3,2},{4,3},{5,4},{6,5},{7,6},{9,8},{10,9},{11,10},{12... | collective-permute-start | bytes 73736 | tf_op jit(solution)/shard_map/ppermute | solution.py:34
  127.7 11.8 %collective-permute-start.18 = (f32[3,8,2,128]{3,1,2,0:T(8,128)S(1)}, f32[3,8,2,128]{3,1,2,0:T(8,128)S(1)}, u32[]{:S(2)}, u32[]{:S(2)}) collective-permute-start(f32[3,8,2,128]{3,1,2,0:T(8,128)S(1)} %copy.621), channel_id=1, source_target_pairs={{0,1},{1,2},{2,3},{3,4},{4,5},{5,6},{6,7},{8,9},{9,10},{10,11},{11... | collective-permute-start | bytes 73736 | tf_op jit(solution)/shard_map/ppermute | solution.py:33
  130.5 9.0 %collective-permute-start.19 = (f32[3,8,2,128]{3,1,2,0:T(8,128)S(1)}, f32[3,8,2,128]{3,1,2,0:T(8,128)S(1)}, u32[]{:S(2)}, u32[]{:S(2)}) collective-permute-start(f32[3,8,2,128]{3,1,2,0:T(8,128)S(1)} %copy.622), channel_id=1, source_target_pairs={{1,0},{2,1},{3,2},{4,3},{5,4},{6,5},{7,6},{9,8},{10,9},{11,10},{12... | collective-permute-start | bytes 73736 | tf_op jit(solution)/shard_map/ppermute | solution.py:34
  133.4 6.2 %collective-permute-start.16 = (f32[3,2,16,128]{3,2,1,0:T(8,128)S(1)}, f32[3,2,16,128]{3,2,1,0:T(8,128)S(1)}, u32[]{:S(2)}, u32[]{:S(2)}) collective-permute-start(f32[3,2,16,128]{3,2,1,0:T(8,128)S(1)} %get-tuple-element.238), channel_id=1, source_target_pairs={{0,8},{8,16},{16,24},{24,32},{32,40},{40,48},{48,56},{56,64},{64,7... | collective-permute-start | bytes 147464 | tf_op jit(solution)/shard_map/ppermute | solution.py:33
  135.4 8.1 %collective-permute-start.17 = (f32[3,2,16,128]{3,2,1,0:T(8,128)S(1)}, f32[3,2,16,128]{3,2,1,0:T(8,128)S(1)}, u32[]{:S(2)}, u32[]{:S(2)}) collective-permute-start(f32[3,2,16,128]{3,2,1,0:T(8,128)S(1)} %get-tuple-element.237), channel_id=1, source_target_pairs={{8,0},{16,8},{24,16},{32,24},{40,32},{48,40},{56,48},{64,56},{72,6... | collective-permute-start | bytes 147464 | tf_op jit(solution)/shard_map/ppermute | solution.py:34
  (55 other events, 260.6 us)

commit v4 on v2

--- a/solution.py
+++ b/solution.py
@@ -1,7 +1,11 @@
+import functools
+
 import jax
 import jax.numpy as jnp
 from jax import lax
 from jax.sharding import PartitionSpec as P
+from jax.experimental import pallas as pl
+from jax.experimental.pallas import tpu as pltpu
 
 near_weight = 9.0 / 8.0
 far_weight = -1.0 / 24.0
@@ -85,6 +89,59 @@
     return (moved, grown, lame_kernel, shear_kernel)
 
 
+def pair_kernel(block, samples, station_ref, mine_ref, other_ref, out_ref, acc_ref, toward_ref):
+    step = pl.program_id(0)
+
+    @pl.when(step == 0)
+    def _():
+        acc_ref[...] = jnp.zeros_like(acc_ref)
+
+    mine_vals = mine_ref[...].astype(jnp.float32)
+    other_vals = other_ref[...].astype(jnp.float32)
+    mine_sq = jnp.sum(jnp.sum(mine_vals * mine_vals, axis=2, keepdims=True), axis=1, keepdims=True)
+    other_sq = jnp.sum(jnp.sum(other_vals * other_vals, axis=2, keepdims=True), axis=1, keepdims=True)
+    cross = jnp.sum(jnp.sum(mine_vals * other_vals, axis=2, keepdims=True), axis=1, keepdims=True)
+    mine_norm = jnp.sqrt(mine_sq / samples + epsilon)
+    other_norm = jnp.sqrt(other_sq / samples + epsilon)
+    corr = (cross / samples) / (mine_norm * other_norm)
+    toward = other_vals / other_norm - corr * (mine_vals / mine_norm)
+    toward_ref[...] = toward.astype(jnp.bfloat16).astype(jnp.float32)
+
+    def add_one(i, carry):
+        target = station_ref[step * block + i]
+        acc_ref[target] = acc_ref[target] + toward_ref[i]
+        return carry
+
+    lax.fori_loop(0, block, add_one, 0)
+
+    @pl.when(step == pl.num_programs(0) - 1)
+    def _():
+        out_ref[...] = acc_ref[: out_ref.shape[0]]
+
+
+def pair_sums(targets, mine, other, stations):
+    slots, rows, lanes = mine.shape
+    block = 64
+    samples = rows * lanes
+    spec = pl.BlockSpec((block, rows, lanes), lambda g, t: (g, 0, 0))
+    return pl.pallas_call(
+        functools.partial(pair_kernel, block, float(samples)),
+        grid_spec=pltpu.PrefetchScalarGridSpec(
+            num_scalar_prefetch=1,
+            grid=(slots // block,),
+            in_specs=[spec, spec],
+            out_specs=pl.BlockSpec((stations, rows, lanes), lambda g, t: (0, 0, 0)),
+            scratch_shapes=[
+                pltpu.VMEM((stations + 1, rows, lanes), jnp.float32),
+                pltpu.VMEM((block, rows, lanes), jnp.float32),
+            ],
+        ),
+        out_shape=jax.ShapeDtypeStruct((stations, rows, lanes), jnp.float32),
+        compiler_params=pltpu.CompilerParams(dimension_semantics=("arbitrary",)),
+        cost_estimate=pl.CostEstimate(flops=20 * slots * samples, transcendentals=0, bytes_accessed=4 * slots * samples),
+    )(targets, mine, other)
+
+
 def station_part(residuals, station_cell, station_pairs, cells_first, cells_second, step_count):
     stations_here = residuals.shape[0]
     samples = residuals.shape[1]
@@ -116,19 +173,14 @@
     mine = jnp.where(
         (mine_station >= 0)[:, :, None, None], rows[jnp.maximum(mine_station, 0)], jnp.zeros((), residuals.dtype)
     )
-    mine_vals = mine.astype(jnp.float32)
-    other_vals = recv.astype(jnp.float32)
-    mine_norm = jnp.sqrt(jnp.mean(mine_vals * mine_vals, axis=(2, 3), keepdims=True) + epsilon)
-    other_norm = jnp.sqrt(jnp.mean(other_vals * other_vals, axis=(2, 3), keepdims=True) + epsilon)
-    corr = jnp.mean(mine_vals * other_vals, axis=(2, 3), keepdims=True) / (mine_norm * other_norm)
-    toward = (other_vals / other_norm - corr * (mine_vals / mine_norm)).astype(jnp.bfloat16)
     slots = devices * 4
-    hits = (mine_station.reshape(slots)[:, None] == jnp.arange(stations_here)[None, :]).astype(jnp.bfloat16)
-    flat = toward.reshape(slots, samples)
-    adjoint = lax.dot_general(hits, flat, (((0,), (0,)), ((), ())), preferred_element_type=jnp.float32)
-    tail = lax.dot_general(
-        hits, flat[:, samples - step_count :], (((0,), (0,)), ((), ())), preferred_element_type=jnp.float32
-    )
+    targets = jnp.where(mine_station >= 0, mine_station, stations_here).reshape(slots)
+    adjoint3 = pair_sums(
+        targets, mine.reshape(slots, samples // lanes, lanes), recv.reshape(slots, samples // lanes, lanes), stations_here
+    )
+    adjoint = adjoint3.reshape(stations_here, samples)
+    last = adjoint3[:, samples // lanes - 1, lanes - step_count :]
+    tail = last
     cells_hit = (station_cell[:, None] == jnp.arange(cells_first * cells_second)[None, :]).astype(jnp.float32)
     surfaces = jnp.stack(
         [

time: 155 us -> 142 us (0.916)
  Pallas kernels: 0 us -> 14.6 us
  other arithmetic: 28 us -> 14.8 us
  waiting for transfers between devices: 41.5 us -> 34.1 us
  matrix products: 4.77 us -> 0 us
  local copies, waits for them, and re-layouts: 17.3 us -> 15.7 us
    pallas_call x0 -> x1, Pallas kernels: none -> 14.6 us  [pair_sums(): pl.pallas_call(functools.partial(pair_kernel, block, float(samples)), gri...]
    reduce_sum x1 -> x0, other arithmetic: 11.4 us -> none  [station_part(): jnp.mean(mine_vals * other_vals, axis=(2, 3), keepdims=True)]
    convert_element_type x1 -> x0, other arithmetic: 7.17 us -> none  [station_part(): (other_vals / other_norm - corr * (mine_vals / mine_norm)).astype(jnp.bfl...]
    select_n x0 -> x2, other arithmetic: none -> 5.21 us  [the longest x1 4.64 us: station_part(): jnp.where((mine_station >= 0)[:, :, None, None], rows[jnp.maximum(mine_st...]
    ppermute x8, waiting for transfers between devices: 26.7 us -> 21.5 us  [halo_pad(): lax.ppermute(lax.slice_in_dim(block, size - width, size, axis=dim), axis,...]
    dot_general x2 -> x0, matrix products: 4.77 us -> none  [the longest x1 4.38 us: station_part(): lax.dot_general(hits, flat, (((0,), (0,)), ((), ())), preferred_element_t...]
    unnamed x26 -> x24, local copies, waits for them, and re-layouts: 6.33 us -> 4.19 us
    ppermute x8, waiting for transfers between devices: 13.3 us -> 11.2 us  [halo_pad(): lax.ppermute(lax.slice_in_dim(block, 0, width, axis=dim), axis, backward)]
  transfers between devices with their start and end apart: 17 -> 17, of which waited for: 6 -> 6; matrix products, arithmetic and copies ran while one was open for 4% -> 10% of each run, Pallas kernels for 0% -> 0%
where the time goes in v4:
time: 142 us; the launch traced here: 141 us
  starting transfers between devices  60.7 us (43%)
  waiting for transfers between devices  34.1 us (24%)
  local copies, waits for them, and re-layouts  15.7 us (11%)
  other arithmetic  14.8 us (10%)
  Pallas kernels  14.6 us (10%)
  between operations  1.59 us (1%)
    ppermute x8, starting transfers between devices, halo_pad(): lax.ppermute(lax.slice_in_dim(block, size - width, size, axis=dim), axis,...  25 us
    ppermute x8, starting transfers between devices, halo_pad(): lax.ppermute(lax.slice_in_dim(block, 0, width, axis=dim), axis, backward)  24.9 us
    ppermute x8, waiting for transfers between devices, halo_pad(): lax.ppermute(lax.slice_in_dim(block, size - width, size, axis=dim), axis,...  21.5 us
    pallas_call x1, Pallas kernels, pair_sums(): pl.pallas_call(functools.partial(pair_kernel, block, float(samples)), gri...  14.6 us
    ppermute x8, waiting for transfers between devices, halo_pad(): lax.ppermute(lax.slice_in_dim(block, 0, width, axis=dim), axis, backward)  11.2 us
    all_to_all x1, starting transfers between devices, station_part(): lax.all_to_all(send, ('gx', 'gy'), split_axis=0, concat_axis=0, tiled=True)  10.8 us
    select_n x1, other arithmetic, station_part(): jnp.where((mine_station >= 0)[:, :, None, None], rows[jnp.maximum(mine_st...  4.64 us
    unnamed x24, local copies, waits for them, and re-layouts  4.19 us
  transfers between devices with their start and end apart: 17, of which 6 were waited for; matrix products, arithmetic and copies ran while one was open for 10% of the time, Pallas kernels for 0%

profile of v4, /device:TPU:14, one launch (start us, length us, event | category | flops | bytes accessed | tf_op | source)
XLA Modules:
  0.0 141.4 jit_solution(14884643886016486360)
XLA Ops:
  4.9 3.5 %gather_fusion.1 = bf16[512,32,128]{2,1,0:T(8,128)(2,1)} fusion(bf16[32,32,128]{2,1,0:T(8,128)(2,1)S(1)} %bitcast.279, s32[1024]{0:T(1024)S(1)} %pad_clamp_fusion), kind=kCustom, calls=%fused_computation.1 | custom fusion | bytes 8390656 | tf_op jit(solution)/shard_map/gather | solution.py:169
  8.4 4.0 %broadcast_select_fusion.1 = bf16[128,4,32,128]{3,2,1,0:T(8,128)(2,1)} fusion(bf16[128,4,32,128]{3,2,1,0:T(8,128)(2,1)} %bitcast.281, pred[128,4]{1,0:T(8,128)(4,1)S(1)} %copy.389), kind=kLoop, calls=%fused_computation.3 | loop fusion | flops 2097152 | bytes 8389120 | tf_op jit(solution)/shard_map/jit(_where)/select_n | solution.py:168
  12.3 10.8 %all-to-all-start = ((bf16[128,4,32,128]{3,2,1,0:T(8,128)(2,1)}), bf16[128,4,32,128]{3,2,1,0:T(8,128)(2,1)}, u32[]{:S(2)}, u32[]{:S(2)}) async-start(bf16[128,4,32,128]{3,2,1,0:T(8,128)(2,1)} %broadcast_select_fusion.1), calls=%async_computation | async-start | bytes 8388608 | tf_op jit(solution)/shard_map/all_to_all | solution.py:171
  23.2 2.0 %collective-permute-start.2 = (f32[3,8,2,128]{3,1,2,0:T(8,128)S(1)}, f32[3,8,2,128]{3,1,2,0:T(8,128)S(1)}, u32[]{:S(2)}, u32[]{:S(2)}) collective-permute-start(f32[3,8,2,128]{3,1,2,0:T(8,128)S(1)} %copy.378), channel_id=1, source_target_pairs={{0,1},{1,2},{2,3},{3,4},{4,5},{5,6},{6,7},{8,9},{9,10},{10,11},{11... | collective-permute-start | bytes 73736 | tf_op jit(solution)/shard_map/ppermute | solution.py:37
  25.3 3.5 %collective-permute-start.3 = (f32[3,8,2,128]{3,1,2,0:T(8,128)S(1)}, f32[3,8,2,128]{3,1,2,0:T(8,128)S(1)}, u32[]{:S(2)}, u32[]{:S(2)}) collective-permute-start(f32[3,8,2,128]{3,1,2,0:T(8,128)S(1)} %copy.379), channel_id=1, source_target_pairs={{1,0},{2,1},{3,2},{4,3},{5,4},{6,5},{7,6},{9,8},{10,9},{11,10},{12... | collective-permute-start | bytes 73736 | tf_op jit(solution)/shard_map/ppermute | solution.py:38
  28.9 2.8 %collective-permute-start = (f32[3,2,16,128]{3,2,1,0:T(8,128)S(1)}, f32[3,2,16,128]{3,2,1,0:T(8,128)S(1)}, u32[]{:S(2)}, u32[]{:S(2)}) collective-permute-start(f32[3,2,16,128]{3,2,1,0:T(8,128)S(1)} %get-tuple-element.129), channel_id=1, source_target_pairs={{8,0},{16,8},{24,16},{32,24},{40,32},{48,40},{56,48},{64,56},{72,6... | collective-permute-start | bytes 147464 | tf_op jit(solution)/shard_map/ppermute | solution.py:38
  31.6 5.2 %collective-permute-start.1 = (f32[3,2,16,128]{3,2,1,0:T(8,128)S(1)}, f32[3,2,16,128]{3,2,1,0:T(8,128)S(1)}, u32[]{:S(2)}, u32[]{:S(2)}) collective-permute-start(f32[3,2,16,128]{3,2,1,0:T(8,128)S(1)} %get-tuple-element.130), channel_id=1, source_target_pairs={{0,8},{8,16},{16,24},{24,32},{32,40},{40,48},{48,56},{56,64},{64,7... | collective-permute-start | bytes 147464 | tf_op jit(solution)/shard_map/ppermute | solution.py:37
  37.1 3.5 %gather_fusion = bf16[512,32,128]{2,1,0:T(8,128)(2,1)} fusion(bf16[32,32,128]{2,1,0:T(8,128)(2,1)S(1)} %bitcast.280, s32[1024]{0:T(1024)S(1)} %pad_clamp_fusion.1), kind=kCustom, calls=%fused_computation | custom fusion | bytes 8390656 | tf_op jit(solution)/shard_map/gather | solution.py:174
  41.5 4.6 %broadcast_select_fusion.mine_ref = bf16[512,32,128]{2,1,0:T(8,128)(2,1)} fusion(bf16[512,32,128]{2,1,0:T(8,128)(2,1)} %gather_fusion, pred[512]{0:T(512)(128)(4,1)S(1)} %ge.23), kind=kLoop, calls=%fused_computation.2 | loop fusion | flops 2097152 | bytes 8389120 | tf_op jit(solution)/shard_map/jit(_where)/select_n | solution.py:173
  46.7 21.5 %collective-permute-done.2 = f32[3,8,2,128]{3,1,2,0:T(8,128)S(1)} collective-permute-done((f32[3,8,2,128]{3,1,2,0:T(8,128)S(1)}, f32[3,8,2,128]{3,1,2,0:T(8,128)S(1)}, u32[]{:S(2)}, u32[]{:S(2)}) %collective-permute-start.2) | collective-permute-done | bytes 24608 | tf_op jit(solution)/shard_map/ppermute | solution.py:37
  68.3 3.5 %collective-permute-done = f32[3,2,16,128]{3,2,1,0:T(8,128)S(1)} collective-permute-done((f32[3,2,16,128]{3,2,1,0:T(8,128)S(1)}, f32[3,2,16,128]{3,2,1,0:T(8,128)S(1)}, u32[]{:S(2)}, u32[]{:S(2)}) %collective-permute-start) | collective-permute-done | bytes 49184 | tf_op jit(solution)/shard_map/ppermute | solution.py:38
  73.7 14.6 %shard_map.146 = f32[32,32,128]{2,1,0:T(8,128)} custom-call(s32[512]{0:T(512)} %compare_select_fusion.station_ref, bf16[512,32,128]{2,1,0:T(8,128)(2,1)} %broadcast_select_fusion.mine_ref, bf16[512,32,128]{2,1,0:T(8,128)(2,1)} %bitcast.23.other_ref), custom_call_target="tpu_custom_call" | custom-call | flops 41943040 | bytes 8388608 | tf_op jit(solution)/shard_map/pallas_call | solution.py:127
  91.9 3.6 %collective-permute-start.7 = (f32[3,8,2,128]{3,1,2,0:T(8,128)S(1)}, f32[3,8,2,128]{3,1,2,0:T(8,128)S(1)}, u32[]{:S(2)}, u32[]{:S(2)}) collective-permute-start(f32[3,8,2,128]{3,1,2,0:T(8,128)S(1)} %copy.395), channel_id=1, source_target_pairs={{1,0},{2,1},{3,2},{4,3},{5,4},{6,5},{7,6},{9,8},{10,9},{11,10},{12... | collective-permute-start | bytes 73736 | tf_op jit(solution)/shard_map/ppermute | solution.py:38
  95.7 2.7 %collective-permute-start.4 = (f32[3,2,16,128]{3,2,1,0:T(8,128)S(1)}, f32[3,2,16,128]{3,2,1,0:T(8,128)S(1)}, u32[]{:S(2)}, u32[]{:S(2)}) collective-permute-start(f32[3,2,16,128]{3,2,1,0:T(8,128)S(1)} %get-tuple-element.123), channel_id=1, source_target_pairs={{0,8},{8,16},{16,24},{24,32},{32,40},{40,48},{48,56},{56,64},{64,7... | collective-permute-start | bytes 147464 | tf_op jit(solution)/shard_map/ppermute | solution.py:37
  98.4 3.2 %collective-permute-start.5 = (f32[3,2,16,128]{3,2,1,0:T(8,128)S(1)}, f32[3,2,16,128]{3,2,1,0:T(8,128)S(1)}, u32[]{:S(2)}, u32[]{:S(2)}) collective-permute-start(f32[3,2,16,128]{3,2,1,0:T(8,128)S(1)} %get-tuple-element.124), channel_id=1, source_target_pairs={{8,0},{16,8},{24,16},{32,24},{40,32},{48,40},{56,48},{64,56},{72,6... | collective-permute-start | bytes 147464 | tf_op jit(solution)/shard_map/ppermute | solution.py:38
  101.8 2.1 %copy.414 = f32[4,8,32,128]{3,1,2,0:T(8,128)} copy(f32[4,8,32,128]{3,2,1,0:T(8,128)} %bitcast.282) | data formatting | bytes 1048576
  104.1 2.4 %collective-permute-done.5 = f32[3,2,16,128]{3,2,1,0:T(8,128)S(1)} collective-permute-done((f32[3,2,16,128]{3,2,1,0:T(8,128)S(1)}, f32[3,2,16,128]{3,2,1,0:T(8,128)S(1)}, u32[]{:S(2)}, u32[]{:S(2)}) %collective-permute-start.5) | collective-permute-done | bytes 49184 | tf_op jit(solution)/shard_map/ppermute | solution.py:38
  107.1 1.9 %collective-permute-start.8 = (f32[3,2,16,128]{3,2,1,0:T(8,128)S(1)}, f32[3,2,16,128]{3,2,1,0:T(8,128)S(1)}, u32[]{:S(2)}, u32[]{:S(2)}) collective-permute-start(f32[3,2,16,128]{3,2,1,0:T(8,128)S(1)} %get-tuple-element.116), channel_id=1, source_target_pairs={{8,0},{16,8},{24,16},{32,24},{40,32},{48,40},{56,48},{64,56},{72,6... | collective-permute-start | bytes 147464 | tf_op jit(solution)/shard_map/ppermute | solution.py:38
  109.1 6.0 %collective-permute-start.9 = (f32[3,2,16,128]{3,2,1,0:T(8,128)S(1)}, f32[3,2,16,128]{3,2,1,0:T(8,128)S(1)}, u32[]{:S(2)}, u32[]{:S(2)}) collective-permute-start(f32[3,2,16,128]{3,2,1,0:T(8,128)S(1)} %get-tuple-element.117), channel_id=1, source_target_pairs={{0,8},{8,16},{16,24},{24,32},{32,40},{40,48},{48,56},{56,64},{64,7... | collective-permute-start | bytes 147464 | tf_op jit(solution)/shard_map/ppermute | solution.py:37
  117.1 3.6 %collective-permute-start.11 = (f32[3,8,2,128]{3,1,2,0:T(8,128)S(1)}, f32[3,8,2,128]{3,1,2,0:T(8,128)S(1)}, u32[]{:S(2)}, u32[]{:S(2)}) collective-permute-start(f32[3,8,2,128]{3,1,2,0:T(8,128)S(1)} %copy.399), channel_id=1, source_target_pairs={{1,0},{2,1},{3,2},{4,3},{5,4},{6,5},{7,6},{9,8},{10,9},{11,10},{12... | collective-permute-start | bytes 73736 | tf_op jit(solution)/shard_map/ppermute | solution.py:38
  123.1 3.3 %collective-permute-start.14 = (f32[3,8,2,128]{3,1,2,0:T(8,128)S(1)}, f32[3,8,2,128]{3,1,2,0:T(8,128)S(1)}, u32[]{:S(2)}, u32[]{:S(2)}) collective-permute-start(f32[3,8,2,128]{3,1,2,0:T(8,128)S(1)} %copy.404), channel_id=1, source_target_pairs={{0,1},{1,2},{2,3},{3,4},{4,5},{5,6},{6,7},{8,9},{9,10},{10,11},{11... | collective-permute-start | bytes 73736 | tf_op jit(solution)/shard_map/ppermute | solution.py:37
  126.4 2.3 %collective-permute-start.15 = (f32[3,8,2,128]{3,1,2,0:T(8,128)S(1)}, f32[3,8,2,128]{3,1,2,0:T(8,128)S(1)}, u32[]{:S(2)}, u32[]{:S(2)}) collective-permute-start(f32[3,8,2,128]{3,1,2,0:T(8,128)S(1)} %copy.405), channel_id=1, source_target_pairs={{1,0},{2,1},{3,2},{4,3},{5,4},{6,5},{7,6},{9,8},{10,9},{11,10},{12... | collective-permute-start | bytes 73736 | tf_op jit(solution)/shard_map/ppermute | solution.py:38
  130.8 3.9 %collective-permute-start.13 = (f32[3,2,16,128]{3,2,1,0:T(8,128)S(1)}, f32[3,2,16,128]{3,2,1,0:T(8,128)S(1)}, u32[]{:S(2)}, u32[]{:S(2)}) collective-permute-start(f32[3,2,16,128]{3,2,1,0:T(8,128)S(1)} %get-tuple-element.110), channel_id=1, source_target_pairs={{8,0},{16,8},{24,16},{32,24},{40,32},{48,40},{56,48},{64,56},{72,6... | collective-permute-start | bytes 147464 | tf_op jit(solution)/shard_map/ppermute | solution.py:38
  134.8 4.0 %collective-permute-done.13 = f32[3,2,16,128]{3,2,1,0:T(8,128)S(1)} collective-permute-done((f32[3,2,16,128]{3,2,1,0:T(8,128)S(1)}, f32[3,2,16,128]{3,2,1,0:T(8,128)S(1)}, u32[]{:S(2)}, u32[]{:S(2)}) %collective-permute-start.13) | collective-permute-done | bytes 49184 | tf_op jit(solution)/shard_map/ppermute | solution.py:38
  (152 shorter events, 21.2 us)
Async XLA Ops:
  12.3 61.4 %all-to-all-start = ((bf16[128,4,32,128]{3,2,1,0:T(8,128)(2,1)}), bf16[128,4,32,128]{3,2,1,0:T(8,128)(2,1)}, u32[]{:S(2)}, u32[]{:S(2)}) async-start(bf16[128,4,32,128]{3,2,1,0:T(8,128)(2,1)} %broadcast_select_fusion.1), calls=%async_computation | async-start | bytes 8388608 | tf_op jit(solution)/shard_map/all_to_all | solution.py:171
  23.2 44.9 %collective-permute-start.2 = (f32[3,8,2,128]{3,1,2,0:T(8,128)S(1)}, f32[3,8,2,128]{3,1,2,0:T(8,128)S(1)}, u32[]{:S(2)}, u32[]{:S(2)}) collective-permute-start(f32[3,8,2,128]{3,1,2,0:T(8,128)S(1)} %copy.378), channel_id=1, source_target_pairs={{0,1},{1,2},{2,3},{3,4},{4,5},{5,6},{6,7},{8,9},{9,10},{10,11},{11... | collective-permute-start | bytes 73736 | tf_op jit(solution)/shard_map/ppermute | solution.py:37
  25.3 42.9 %collective-permute-start.3 = (f32[3,8,2,128]{3,1,2,0:T(8,128)S(1)}, f32[3,8,2,128]{3,1,2,0:T(8,128)S(1)}, u32[]{:S(2)}, u32[]{:S(2)}) collective-permute-start(f32[3,8,2,128]{3,1,2,0:T(8,128)S(1)} %copy.379), channel_id=1, source_target_pairs={{1,0},{2,1},{3,2},{4,3},{5,4},{6,5},{7,6},{9,8},{10,9},{11,10},{12... | collective-permute-start | bytes 73736 | tf_op jit(solution)/shard_map/ppermute | solution.py:38
  28.9 42.9 %collective-permute-start = (f32[3,2,16,128]{3,2,1,0:T(8,128)S(1)}, f32[3,2,16,128]{3,2,1,0:T(8,128)S(1)}, u32[]{:S(2)}, u32[]{:S(2)}) collective-permute-start(f32[3,2,16,128]{3,2,1,0:T(8,128)S(1)} %get-tuple-element.129), channel_id=1, source_target_pairs={{8,0},{16,8},{24,16},{32,24},{40,32},{48,40},{56,48},{64,56},{72,6... | collective-permute-start | bytes 147464 | tf_op jit(solution)/shard_map/ppermute | solution.py:38
  31.6 40.2 %collective-permute-start.1 = (f32[3,2,16,128]{3,2,1,0:T(8,128)S(1)}, f32[3,2,16,128]{3,2,1,0:T(8,128)S(1)}, u32[]{:S(2)}, u32[]{:S(2)}) collective-permute-start(f32[3,2,16,128]{3,2,1,0:T(8,128)S(1)} %get-tuple-element.130), channel_id=1, source_target_pairs={{0,8},{8,16},{16,24},{24,32},{32,40},{40,48},{48,56},{56,64},{64,7... | collective-permute-start | bytes 147464 | tf_op jit(solution)/shard_map/ppermute | solution.py:37
  73.7 15.7 %copy-start.9 = (s32[32]{0:T(128)S(1)}, s32[32]{0:T(128)}, u32[]{:S(2)}) copy-start(s32[32]{0:T(128)} %param.24) | copy-start | bytes 388
  73.7 16.2 %copy-start.3 = (f32[3,8,16,128]{3,2,1,0:T(8,128)S(1)}, f32[3,8,16,128]{3,2,1,0:T(8,128)}, u32[]{:S(2)}) copy-start(f32[3,8,16,128]{3,2,1,0:T(8,128)} %param.15) | copy-start | bytes 589828
  88.3 18.2 %copy-start = (f32[8,16,128]{2,1,0:T(8,128)S(1)}, f32[8,16,128]{2,1,0:T(8,128)}, u32[]{:S(2)}) copy-start(f32[8,16,128]{2,1,0:T(8,128)} %param.18) | copy-start | bytes 196612
  88.3 18.2 %copy-start.5 = (f32[8,16,128]{2,1,0:T(8,128)S(1)}, f32[8,16,128]{2,1,0:T(8,128)}, u32[]{:S(2)}) copy-start(f32[8,16,128]{2,1,0:T(8,128)} %param.17) | copy-start | bytes 196612
  89.9 14.0 %collective-permute-start.6 = (f32[3,8,2,128]{3,1,2,0:T(8,128)S(1)}, f32[3,8,2,128]{3,1,2,0:T(8,128)S(1)}, u32[]{:S(2)}, u32[]{:S(2)}) collective-permute-start(f32[3,8,2,128]{3,1,2,0:T(8,128)S(1)} %copy.394), channel_id=1, source_target_pairs={{0,1},{1,2},{2,3},{3,4},{4,5},{5,6},{6,7},{8,9},{9,10},{10,11},{11... | collective-permute-start | bytes 73736 | tf_op jit(solution)/shard_map/ppermute | solution.py:37
  91.9 12.0 %collective-permute-start.7 = (f32[3,8,2,128]{3,1,2,0:T(8,128)S(1)}, f32[3,8,2,128]{3,1,2,0:T(8,128)S(1)}, u32[]{:S(2)}, u32[]{:S(2)}) collective-permute-start(f32[3,8,2,128]{3,1,2,0:T(8,128)S(1)} %copy.395), channel_id=1, source_target_pairs={{1,0},{2,1},{3,2},{4,3},{5,4},{6,5},{7,6},{9,8},{10,9},{11,10},{12... | collective-permute-start | bytes 73736 | tf_op jit(solution)/shard_map/ppermute | solution.py:38
  95.7 8.3 %collective-permute-start.4 = (f32[3,2,16,128]{3,2,1,0:T(8,128)S(1)}, f32[3,2,16,128]{3,2,1,0:T(8,128)S(1)}, u32[]{:S(2)}, u32[]{:S(2)}) collective-permute-start(f32[3,2,16,128]{3,2,1,0:T(8,128)S(1)} %get-tuple-element.123), channel_id=1, source_target_pairs={{0,8},{8,16},{16,24},{24,32},{32,40},{40,48},{48,56},{56,64},{64,7... | collective-permute-start | bytes 147464 | tf_op jit(solution)/shard_map/ppermute | solution.py:37
  98.4 8.1 %collective-permute-start.5 = (f32[3,2,16,128]{3,2,1,0:T(8,128)S(1)}, f32[3,2,16,128]{3,2,1,0:T(8,128)S(1)}, u32[]{:S(2)}, u32[]{:S(2)}) collective-permute-start(f32[3,2,16,128]{3,2,1,0:T(8,128)S(1)} %get-tuple-element.124), channel_id=1, source_target_pairs={{8,0},{16,8},{24,16},{32,24},{40,32},{48,40},{56,48},{64,56},{72,6... | collective-permute-start | bytes 147464 | tf_op jit(solution)/shard_map/ppermute | solution.py:38
  107.1 15.2 %collective-permute-start.8 = (f32[3,2,16,128]{3,2,1,0:T(8,128)S(1)}, f32[3,2,16,128]{3,2,1,0:T(8,128)S(1)}, u32[]{:S(2)}, u32[]{:S(2)}) collective-permute-start(f32[3,2,16,128]{3,2,1,0:T(8,128)S(1)} %get-tuple-element.116), channel_id=1, source_target_pairs={{8,0},{16,8},{24,16},{32,24},{40,32},{48,40},{56,48},{64,56},{72,6... | collective-permute-start | bytes 147464 | tf_op jit(solution)/shard_map/ppermute | solution.py:38
  109.1 13.3 %collective-permute-start.9 = (f32[3,2,16,128]{3,2,1,0:T(8,128)S(1)}, f32[3,2,16,128]{3,2,1,0:T(8,128)S(1)}, u32[]{:S(2)}, u32[]{:S(2)}) collective-permute-start(f32[3,2,16,128]{3,2,1,0:T(8,128)S(1)} %get-tuple-element.117), channel_id=1, source_target_pairs={{0,8},{8,16},{16,24},{24,32},{32,40},{40,48},{48,56},{56,64},{64,7... | collective-permute-start | bytes 147464 | tf_op jit(solution)/shard_map/ppermute | solution.py:37
  115.1 5.8 %collective-permute-start.10 = (f32[3,8,2,128]{3,1,2,0:T(8,128)S(1)}, f32[3,8,2,128]{3,1,2,0:T(8,128)S(1)}, u32[]{:S(2)}, u32[]{:S(2)}) collective-permute-start(f32[3,8,2,128]{3,1,2,0:T(8,128)S(1)} %copy.398), channel_id=1, source_target_pairs={{0,1},{1,2},{2,3},{3,4},{4,5},{5,6},{6,7},{8,9},{9,10},{10,11},{11... | collective-permute-start | bytes 73736 | tf_op jit(solution)/shard_map/ppermute | solution.py:37
  117.1 5.1 %collective-permute-start.11 = (f32[3,8,2,128]{3,1,2,0:T(8,128)S(1)}, f32[3,8,2,128]{3,1,2,0:T(8,128)S(1)}, u32[]{:S(2)}, u32[]{:S(2)}) collective-permute-start(f32[3,8,2,128]{3,1,2,0:T(8,128)S(1)} %copy.399), channel_id=1, source_target_pairs={{1,0},{2,1},{3,2},{4,3},{5,4},{6,5},{7,6},{9,8},{10,9},{11,10},{12... | collective-permute-start | bytes 73736 | tf_op jit(solution)/shard_map/ppermute | solution.py:38
  120.9 17.9 %copy-start.6 = (f32[8,16,128]{2,1,0:T(8,128)S(1)}, f32[8,16,128]{2,1,0:T(8,128)}, u32[]{:S(2)}) copy-start(f32[8,16,128]{2,1,0:T(8,128)} %param.22) | copy-start | bytes 196612
  122.6 17.2 %copy-start.7 = (f32[8,16,128]{2,1,0:T(8,128)S(1)}, f32[8,16,128]{2,1,0:T(8,128)}, u32[]{:S(2)}) copy-start(f32[8,16,128]{2,1,0:T(8,128)} %param.21) | copy-start | bytes 196612
  123.0 17.6 %copy-start.1 = (f32[3,8,16,128]{3,2,1,0:T(8,128)}, f32[3,8,16,128]{3,2,1,0:T(8,128)S(1)}, u32[]{:S(2)}) copy-start(f32[3,8,16,128]{3,2,1,0:T(8,128)S(1)} %fusion.2) | copy-start | bytes 589828
  123.1 11.6 %collective-permute-start.14 = (f32[3,8,2,128]{3,1,2,0:T(8,128)S(1)}, f32[3,8,2,128]{3,1,2,0:T(8,128)S(1)}, u32[]{:S(2)}, u32[]{:S(2)}) collective-permute-start(f32[3,8,2,128]{3,1,2,0:T(8,128)S(1)} %copy.404), channel_id=1, source_target_pairs={{0,1},{1,2},{2,3},{3,4},{4,5},{5,6},{6,7},{8,9},{9,10},{10,11},{11... | collective-permute-start | bytes 73736 | tf_op jit(solution)/shard_map/ppermute | solution.py:37
  126.4 8.3 %collective-permute-start.15 = (f32[3,8,2,128]{3,1,2,0:T(8,128)S(1)}, f32[3,8,2,128]{3,1,2,0:T(8,128)S(1)}, u32[]{:S(2)}, u32[]{:S(2)}) collective-permute-start(f32[3,8,2,128]{3,1,2,0:T(8,128)S(1)} %copy.405), channel_id=1, source_target_pairs={{1,0},{2,1},{3,2},{4,3},{5,4},{6,5},{7,6},{9,8},{10,9},{11,10},{12... | collective-permute-start | bytes 73736 | tf_op jit(solution)/shard_map/ppermute | solution.py:38
  128.8 6.0 %collective-permute-start.12 = (f32[3,2,16,128]{3,2,1,0:T(8,128)S(1)}, f32[3,2,16,128]{3,2,1,0:T(8,128)S(1)}, u32[]{:S(2)}, u32[]{:S(2)}) collective-permute-start(f32[3,2,16,128]{3,2,1,0:T(8,128)S(1)} %get-tuple-element.111), channel_id=1, source_target_pairs={{0,8},{8,16},{16,24},{24,32},{32,40},{40,48},{48,56},{56,64},{64,7... | collective-permute-start | bytes 147464 | tf_op jit(solution)/shard_map/ppermute | solution.py:37
  130.8 8.1 %collective-permute-start.13 = (f32[3,2,16,128]{3,2,1,0:T(8,128)S(1)}, f32[3,2,16,128]{3,2,1,0:T(8,128)S(1)}, u32[]{:S(2)}, u32[]{:S(2)}) collective-permute-start(f32[3,2,16,128]{3,2,1,0:T(8,128)S(1)} %get-tuple-element.110), channel_id=1, source_target_pairs={{8,0},{16,8},{24,16},{32,24},{40,32},{48,40},{56,48},{64,56},{72,6... | collective-permute-start | bytes 147464 | tf_op jit(solution)/shard_map/ppermute | solution.py:38
  (3 other events, 19.4 us)

commit v5 on v4

--- a/solution.py
+++ b/solution.py
@@ -107,16 +107,24 @@
     toward = other_vals / other_norm - corr * (mine_vals / mine_norm)
     toward_ref[...] = toward.astype(jnp.bfloat16).astype(jnp.float32)
 
-    def add_one(i, carry):
-        target = station_ref[step * block + i]
-        acc_ref[target] = acc_ref[target] + toward_ref[i]
+    ways = acc_ref.shape[0]
+
+    def add_some(i, carry):
+        for way in range(ways):
+            slot = i * ways + way
+            target = station_ref[step * block + slot]
+            acc_ref[way, target] = acc_ref[way, target] + toward_ref[slot]
         return carry
 
-    lax.fori_loop(0, block, add_one, 0)
+    lax.fori_loop(0, block // ways, add_some, 0)
 
     @pl.when(step == pl.num_programs(0) - 1)
     def _():
-        out_ref[...] = acc_ref[: out_ref.shape[0]]
+        stations = out_ref.shape[0]
+        total = acc_ref[0, :stations]
+        for way in range(1, ways):
+            total = total + acc_ref[way, :stations]
+        out_ref[...] = total
 
 
 def pair_sums(targets, mine, other, stations):
@@ -132,7 +140,7 @@
             in_specs=[spec, spec],
             out_specs=pl.BlockSpec((stations, rows, lanes), lambda g, t: (0, 0, 0)),
             scratch_shapes=[
-                pltpu.VMEM((stations + 1, rows, lanes), jnp.float32),
+                pltpu.VMEM((4, stations + 1, rows, lanes), jnp.float32),
                 pltpu.VMEM((block, rows, lanes), jnp.float32),
             ],
         ),
@@ -165,14 +173,11 @@
     slot_station = jnp.concatenate([own_station, in_station], axis=1)
     lanes = 128
     rows = residuals.reshape(stations_here, samples // lanes, lanes)
-    send = jnp.where(
-        (slot_station >= 0)[:, :, None, None], rows[jnp.maximum(slot_station, 0)], jnp.zeros((), residuals.dtype)
-    )
+    padded_rows = jnp.concatenate([rows, jnp.zeros((1,) + rows.shape[1:], rows.dtype)], axis=0)
+    send = padded_rows[jnp.where(slot_station >= 0, slot_station, stations_here)]
     recv = lax.all_to_all(send, ("gx", "gy"), split_axis=0, concat_axis=0, tiled=True)
     mine_station = jnp.concatenate([slot_station[:, 2:4], slot_station[:, 0:2]], axis=1)
-    mine = jnp.where(
-        (mine_station >= 0)[:, :, None, None], rows[jnp.maximum(mine_station, 0)], jnp.zeros((), residuals.dtype)
-    )
+    mine = padded_rows[jnp.where(mine_station >= 0, mine_station, stations_here)]
     slots = devices * 4
     targets = jnp.where(mine_station >= 0, mine_station, stations_here).reshape(slots)
     adjoint3 = pair_sums(

time: 142 us -> 137 us (0.965)
  other arithmetic: 14.8 us -> 6.16 us
  waiting for transfers between devices: 34.1 us -> 39.1 us
  Pallas kernels: 14.6 us -> 13 us
    select_n x2 -> x1, other arithmetic: 8.6 us -> 0.01 us  [station_part(): padded_rows[jnp.where(slot_station >= 0, slot_station, stations_here)]]
    ppermute x8, waiting for transfers between devices: 21.5 us -> 26.5 us  [halo_pad(): lax.ppermute(lax.slice_in_dim(block, size - width, size, axis=dim), axis,...]
    pallas_call x1, Pallas kernels: 14.6 us -> 13 us  [pair_sums(): pl.pallas_call(functools.partial(pair_kernel, block, float(samples)), gri...]
  transfers between devices with their start and end apart: 17 -> 17, of which waited for: 6 -> 6; matrix products, arithmetic and copies ran while one was open for 10% -> 6% of each run, Pallas kernels for 0% -> 0%
where the time goes in v5:
time: 137 us; the launch traced here: 136 us
  starting transfers between devices  60.7 us (44%)
  waiting for transfers between devices  39.1 us (29%)
  local copies, waits for them, and re-layouts  15.4 us (11%)
  Pallas kernels  13 us (9%)
  other arithmetic  6.16 us (4%)
  between operations  1.55 us (1%)
    ppermute x8, waiting for transfers between devices, halo_pad(): lax.ppermute(lax.slice_in_dim(block, size - width, size, axis=dim), axis,...  26.5 us
    ppermute x8, starting transfers between devices, halo_pad(): lax.ppermute(lax.slice_in_dim(block, size - width, size, axis=dim), axis,...  25 us
    ppermute x8, starting transfers between devices, halo_pad(): lax.ppermute(lax.slice_in_dim(block, 0, width, axis=dim), axis, backward)  24.9 us
    pallas_call x1, Pallas kernels, pair_sums(): pl.pallas_call(functools.partial(pair_kernel, block, float(samples)), gri...  13 us
    ppermute x8, waiting for transfers between devices, halo_pad(): lax.ppermute(lax.slice_in_dim(block, 0, width, axis=dim), axis, backward)  11.2 us
    all_to_all x1, starting transfers between devices, station_part(): lax.all_to_all(send, ('gx', 'gy'), split_axis=0, concat_axis=0, tiled=True)  10.8 us
    unnamed x24, local copies, waits for them, and re-layouts  4.19 us
    gather x1, local copies, waits for them, and re-layouts, station_part(): padded_rows[jnp.where(slot_station >= 0, slot_station, stations_here)]  3.54 us
  transfers between devices with their start and end apart: 17, of which 6 were waited for; matrix products, arithmetic and copies ran while one was open for 6% of the time, Pallas kernels for 0%

profile of v5, /device:TPU:14, one launch (start us, length us, event | category | flops | bytes accessed | tf_op | source)
XLA Modules:
  0.0 135.8 jit_solution(6075780945365705517)
XLA Ops:
  4.7 3.5 %gather_fusion.1 = bf16[512,32,128]{2,1,0:T(8,128)(2,1)} fusion(bf16[33,32,128]{2,1,0:T(8,128)(2,1)S(1)} %concatenate.120, s32[1024]{0:T(1024)S(1)} %pad_clamp_fusion), kind=kCustom, calls=%fused_computation.1 | custom fusion | bytes 8390656 | tf_op jit(solution)/shard_map/gather | solution.py:177
  8.3 10.8 %all-to-all-start = ((bf16[128,4,32,128]{3,2,1,0:T(8,128)(2,1)}), bf16[128,4,32,128]{3,2,1,0:T(8,128)(2,1)}, u32[]{:S(2)}, u32[]{:S(2)}) async-start(bf16[128,4,32,128]{3,2,1,0:T(8,128)(2,1)} %bitcast.271), calls=%async_computation | async-start | bytes 8388608 | tf_op jit(solution)/shard_map/all_to_all | solution.py:178
  19.2 2.0 %collective-permute-start.2 = (f32[3,8,2,128]{3,1,2,0:T(8,128)S(1)}, f32[3,8,2,128]{3,1,2,0:T(8,128)S(1)}, u32[]{:S(2)}, u32[]{:S(2)}) collective-permute-start(f32[3,8,2,128]{3,1,2,0:T(8,128)S(1)} %copy.372), channel_id=1, source_target_pairs={{0,1},{1,2},{2,3},{3,4},{4,5},{5,6},{6,7},{8,9},{9,10},{10,11},{11... | collective-permute-start | bytes 73736 | tf_op jit(solution)/shard_map/ppermute | solution.py:37
  21.3 3.5 %collective-permute-start.3 = (f32[3,8,2,128]{3,1,2,0:T(8,128)S(1)}, f32[3,8,2,128]{3,1,2,0:T(8,128)S(1)}, u32[]{:S(2)}, u32[]{:S(2)}) collective-permute-start(f32[3,8,2,128]{3,1,2,0:T(8,128)S(1)} %copy.373), channel_id=1, source_target_pairs={{1,0},{2,1},{3,2},{4,3},{5,4},{6,5},{7,6},{9,8},{10,9},{11,10},{12... | collective-permute-start | bytes 73736 | tf_op jit(solution)/shard_map/ppermute | solution.py:38
  24.8 2.8 %collective-permute-start = (f32[3,2,16,128]{3,2,1,0:T(8,128)S(1)}, f32[3,2,16,128]{3,2,1,0:T(8,128)S(1)}, u32[]{:S(2)}, u32[]{:S(2)}) collective-permute-start(f32[3,2,16,128]{3,2,1,0:T(8,128)S(1)} %get-tuple-element.129), channel_id=1, source_target_pairs={{8,0},{16,8},{24,16},{32,24},{40,32},{48,40},{56,48},{64,56},{72,6... | collective-permute-start | bytes 147464 | tf_op jit(solution)/shard_map/ppermute | solution.py:38
  27.6 5.2 %collective-permute-start.1 = (f32[3,2,16,128]{3,2,1,0:T(8,128)S(1)}, f32[3,2,16,128]{3,2,1,0:T(8,128)S(1)}, u32[]{:S(2)}, u32[]{:S(2)}) collective-permute-start(f32[3,2,16,128]{3,2,1,0:T(8,128)S(1)} %get-tuple-element.130), channel_id=1, source_target_pairs={{0,8},{8,16},{16,24},{24,32},{32,40},{40,48},{48,56},{56,64},{64,7... | collective-permute-start | bytes 147464 | tf_op jit(solution)/shard_map/ppermute | solution.py:37
  34.2 3.5 %gather_fusion = bf16[512,32,128]{2,1,0:T(8,128)(2,1)} fusion(bf16[33,32,128]{2,1,0:T(8,128)(2,1)S(1)} %concatenate.120, s32[1024]{0:T(1024)S(1)} %pad_clamp_fusion.1), kind=kCustom, calls=%fused_computation | custom fusion | bytes 8390656 | tf_op jit(solution)/shard_map/gather | solution.py:180
  37.7 26.4 %collective-permute-done.2 = f32[3,8,2,128]{3,1,2,0:T(8,128)S(1)} collective-permute-done((f32[3,8,2,128]{3,1,2,0:T(8,128)S(1)}, f32[3,8,2,128]{3,1,2,0:T(8,128)S(1)}, u32[]{:S(2)}, u32[]{:S(2)}) %collective-permute-start.2) | collective-permute-done | bytes 24608 | tf_op jit(solution)/shard_map/ppermute | solution.py:37
  64.3 3.5 %collective-permute-done = f32[3,2,16,128]{3,2,1,0:T(8,128)S(1)} collective-permute-done((f32[3,2,16,128]{3,2,1,0:T(8,128)S(1)}, f32[3,2,16,128]{3,2,1,0:T(8,128)S(1)}, u32[]{:S(2)}, u32[]{:S(2)}) %collective-permute-start) | collective-permute-done | bytes 49184 | tf_op jit(solution)/shard_map/ppermute | solution.py:38
  69.7 13.0 %shard_map.146 = f32[32,32,128]{2,1,0:T(8,128)} custom-call(s32[512]{0:T(512)} %compare_select_fusion.4.station_ref, bf16[512,32,128]{2,1,0:T(8,128)(2,1)} %gather_fusion, bf16[512,32,128]{2,1,0:T(8,128)(2,1)} %bitcast.21.other_ref), custom_call_target="tpu_custom_call" | custom-call | flops 41943040 | bytes 8388608 | tf_op jit(solution)/shard_map/pallas_call | solution.py:135
  84.3 1.9 %collective-permute-start.6 = (f32[3,8,2,128]{3,1,2,0:T(8,128)S(1)}, f32[3,8,2,128]{3,1,2,0:T(8,128)S(1)}, u32[]{:S(2)}, u32[]{:S(2)}) collective-permute-start(f32[3,8,2,128]{3,1,2,0:T(8,128)S(1)} %copy.386), channel_id=1, source_target_pairs={{0,1},{1,2},{2,3},{3,4},{4,5},{5,6},{6,7},{8,9},{9,10},{10,11},{11... | collective-permute-start | bytes 73736 | tf_op jit(solution)/shard_map/ppermute | solution.py:37
  86.3 3.6 %collective-permute-start.7 = (f32[3,8,2,128]{3,1,2,0:T(8,128)S(1)}, f32[3,8,2,128]{3,1,2,0:T(8,128)S(1)}, u32[]{:S(2)}, u32[]{:S(2)}) collective-permute-start(f32[3,8,2,128]{3,1,2,0:T(8,128)S(1)} %copy.387), channel_id=1, source_target_pairs={{1,0},{2,1},{3,2},{4,3},{5,4},{6,5},{7,6},{9,8},{10,9},{11,10},{12... | collective-permute-start | bytes 73736 | tf_op jit(solution)/shard_map/ppermute | solution.py:38
  90.1 2.7 %collective-permute-start.4 = (f32[3,2,16,128]{3,2,1,0:T(8,128)S(1)}, f32[3,2,16,128]{3,2,1,0:T(8,128)S(1)}, u32[]{:S(2)}, u32[]{:S(2)}) collective-permute-start(f32[3,2,16,128]{3,2,1,0:T(8,128)S(1)} %get-tuple-element.123), channel_id=1, source_target_pairs={{0,8},{8,16},{16,24},{24,32},{32,40},{40,48},{48,56},{56,64},{64,7... | collective-permute-start | bytes 147464 | tf_op jit(solution)/shard_map/ppermute | solution.py:37
  92.7 3.2 %collective-permute-start.5 = (f32[3,2,16,128]{3,2,1,0:T(8,128)S(1)}, f32[3,2,16,128]{3,2,1,0:T(8,128)S(1)}, u32[]{:S(2)}, u32[]{:S(2)}) collective-permute-start(f32[3,2,16,128]{3,2,1,0:T(8,128)S(1)} %get-tuple-element.124), channel_id=1, source_target_pairs={{8,0},{16,8},{24,16},{32,24},{40,32},{48,40},{56,48},{64,56},{72,6... | collective-permute-start | bytes 147464 | tf_op jit(solution)/shard_map/ppermute | solution.py:38
  96.1 2.1 %copy.406 = f32[4,8,32,128]{3,1,2,0:T(8,128)} copy(f32[4,8,32,128]{3,2,1,0:T(8,128)} %bitcast.272) | data formatting | bytes 1048576
  98.4 2.4 %collective-permute-done.5 = f32[3,2,16,128]{3,2,1,0:T(8,128)S(1)} collective-permute-done((f32[3,2,16,128]{3,2,1,0:T(8,128)S(1)}, f32[3,2,16,128]{3,2,1,0:T(8,128)S(1)}, u32[]{:S(2)}, u32[]{:S(2)}) %collective-permute-start.5) | collective-permute-done | bytes 49184 | tf_op jit(solution)/shard_map/ppermute | solution.py:38
  101.5 1.9 %collective-permute-start.8 = (f32[3,2,16,128]{3,2,1,0:T(8,128)S(1)}, f32[3,2,16,128]{3,2,1,0:T(8,128)S(1)}, u32[]{:S(2)}, u32[]{:S(2)}) collective-permute-start(f32[3,2,16,128]{3,2,1,0:T(8,128)S(1)} %get-tuple-element.116), channel_id=1, source_target_pairs={{8,0},{16,8},{24,16},{32,24},{40,32},{48,40},{56,48},{64,56},{72,6... | collective-permute-start | bytes 147464 | tf_op jit(solution)/shard_map/ppermute | solution.py:38
  103.4 6.0 %collective-permute-start.9 = (f32[3,2,16,128]{3,2,1,0:T(8,128)S(1)}, f32[3,2,16,128]{3,2,1,0:T(8,128)S(1)}, u32[]{:S(2)}, u32[]{:S(2)}) collective-permute-start(f32[3,2,16,128]{3,2,1,0:T(8,128)S(1)} %get-tuple-element.117), channel_id=1, source_target_pairs={{0,8},{8,16},{16,24},{24,32},{32,40},{40,48},{48,56},{56,64},{64,7... | collective-permute-start | bytes 147464 | tf_op jit(solution)/shard_map/ppermute | solution.py:37
  111.4 3.6 %collective-permute-start.11 = (f32[3,8,2,128]{3,1,2,0:T(8,128)S(1)}, f32[3,8,2,128]{3,1,2,0:T(8,128)S(1)}, u32[]{:S(2)}, u32[]{:S(2)}) collective-permute-start(f32[3,8,2,128]{3,1,2,0:T(8,128)S(1)} %copy.391), channel_id=1, source_target_pairs={{1,0},{2,1},{3,2},{4,3},{5,4},{6,5},{7,6},{9,8},{10,9},{11,10},{12... | collective-permute-start | bytes 73736 | tf_op jit(solution)/shard_map/ppermute | solution.py:38
  117.4 3.3 %collective-permute-start.14 = (f32[3,8,2,128]{3,1,2,0:T(8,128)S(1)}, f32[3,8,2,128]{3,1,2,0:T(8,128)S(1)}, u32[]{:S(2)}, u32[]{:S(2)}) collective-permute-start(f32[3,8,2,128]{3,1,2,0:T(8,128)S(1)} %copy.396), channel_id=1, source_target_pairs={{0,1},{1,2},{2,3},{3,4},{4,5},{5,6},{6,7},{8,9},{9,10},{10,11},{11... | collective-permute-start | bytes 73736 | tf_op jit(solution)/shard_map/ppermute | solution.py:37
  120.8 2.3 %collective-permute-start.15 = (f32[3,8,2,128]{3,1,2,0:T(8,128)S(1)}, f32[3,8,2,128]{3,1,2,0:T(8,128)S(1)}, u32[]{:S(2)}, u32[]{:S(2)}) collective-permute-start(f32[3,8,2,128]{3,1,2,0:T(8,128)S(1)} %copy.397), channel_id=1, source_target_pairs={{1,0},{2,1},{3,2},{4,3},{5,4},{6,5},{7,6},{9,8},{10,9},{11,10},{12... | collective-permute-start | bytes 73736 | tf_op jit(solution)/shard_map/ppermute | solution.py:38
  123.2 1.9 %collective-permute-start.12 = (f32[3,2,16,128]{3,2,1,0:T(8,128)S(1)}, f32[3,2,16,128]{3,2,1,0:T(8,128)S(1)}, u32[]{:S(2)}, u32[]{:S(2)}) collective-permute-start(f32[3,2,16,128]{3,2,1,0:T(8,128)S(1)} %get-tuple-element.111), channel_id=1, source_target_pairs={{0,8},{8,16},{16,24},{24,32},{32,40},{40,48},{48,56},{56,64},{64,7... | collective-permute-start | bytes 147464 | tf_op jit(solution)/shard_map/ppermute | solution.py:37
  125.1 3.9 %collective-permute-start.13 = (f32[3,2,16,128]{3,2,1,0:T(8,128)S(1)}, f32[3,2,16,128]{3,2,1,0:T(8,128)S(1)}, u32[]{:S(2)}, u32[]{:S(2)}) collective-permute-start(f32[3,2,16,128]{3,2,1,0:T(8,128)S(1)} %get-tuple-element.110), channel_id=1, source_target_pairs={{8,0},{16,8},{24,16},{32,24},{40,32},{48,40},{56,48},{64,56},{72,6... | collective-permute-start | bytes 147464 | tf_op jit(solution)/shard_map/ppermute | solution.py:38
  129.2 4.0 %collective-permute-done.13 = f32[3,2,16,128]{3,2,1,0:T(8,128)S(1)} collective-permute-done((f32[3,2,16,128]{3,2,1,0:T(8,128)S(1)}, f32[3,2,16,128]{3,2,1,0:T(8,128)S(1)}, u32[]{:S(2)}, u32[]{:S(2)}) %collective-permute-start.13) | collective-permute-done | bytes 49184 | tf_op jit(solution)/shard_map/ppermute | solution.py:38
  (146 shorter events, 17.0 us)
Async XLA Ops:
  8.3 25.7 %copy-start.8 = (f32[8,16,128]{2,1,0:T(8,128)S(1)}, f32[8,16,128]{2,1,0:T(8,128)}, u32[]{:S(2)}) copy-start(f32[8,16,128]{2,1,0:T(8,128)} %param.19) | copy-start | bytes 196612
  8.3 25.8 %copy-start.4 = (bf16[12,8,16,128]{3,2,1,0:T(8,128)(2,1)S(1)}, bf16[12,8,16,128]{3,2,1,0:T(8,128)(2,1)}, u32[]{:S(2)}) copy-start(bf16[12,8,16,128]{3,2,1,0:T(8,128)(2,1)} %param.20) | copy-start | bytes 1179652
  8.3 61.4 %all-to-all-start = ((bf16[128,4,32,128]{3,2,1,0:T(8,128)(2,1)}), bf16[128,4,32,128]{3,2,1,0:T(8,128)(2,1)}, u32[]{:S(2)}, u32[]{:S(2)}) async-start(bf16[128,4,32,128]{3,2,1,0:T(8,128)(2,1)} %bitcast.271), calls=%async_computation | async-start | bytes 8388608 | tf_op jit(solution)/shard_map/all_to_all | solution.py:178
  19.2 44.9 %collective-permute-start.2 = (f32[3,8,2,128]{3,1,2,0:T(8,128)S(1)}, f32[3,8,2,128]{3,1,2,0:T(8,128)S(1)}, u32[]{:S(2)}, u32[]{:S(2)}) collective-permute-start(f32[3,8,2,128]{3,1,2,0:T(8,128)S(1)} %copy.372), channel_id=1, source_target_pairs={{0,1},{1,2},{2,3},{3,4},{4,5},{5,6},{6,7},{8,9},{9,10},{10,11},{11... | collective-permute-start | bytes 73736 | tf_op jit(solution)/shard_map/ppermute | solution.py:37
  21.3 42.9 %collective-permute-start.3 = (f32[3,8,2,128]{3,1,2,0:T(8,128)S(1)}, f32[3,8,2,128]{3,1,2,0:T(8,128)S(1)}, u32[]{:S(2)}, u32[]{:S(2)}) collective-permute-start(f32[3,8,2,128]{3,1,2,0:T(8,128)S(1)} %copy.373), channel_id=1, source_target_pairs={{1,0},{2,1},{3,2},{4,3},{5,4},{6,5},{7,6},{9,8},{10,9},{11,10},{12... | collective-permute-start | bytes 73736 | tf_op jit(solution)/shard_map/ppermute | solution.py:38
  24.8 42.9 %collective-permute-start = (f32[3,2,16,128]{3,2,1,0:T(8,128)S(1)}, f32[3,2,16,128]{3,2,1,0:T(8,128)S(1)}, u32[]{:S(2)}, u32[]{:S(2)}) collective-permute-start(f32[3,2,16,128]{3,2,1,0:T(8,128)S(1)} %get-tuple-element.129), channel_id=1, source_target_pairs={{8,0},{16,8},{24,16},{32,24},{40,32},{48,40},{56,48},{64,56},{72,6... | collective-permute-start | bytes 147464 | tf_op jit(solution)/shard_map/ppermute | solution.py:38
  27.6 40.2 %collective-permute-start.1 = (f32[3,2,16,128]{3,2,1,0:T(8,128)S(1)}, f32[3,2,16,128]{3,2,1,0:T(8,128)S(1)}, u32[]{:S(2)}, u32[]{:S(2)}) collective-permute-start(f32[3,2,16,128]{3,2,1,0:T(8,128)S(1)} %get-tuple-element.130), channel_id=1, source_target_pairs={{0,8},{8,16},{16,24},{24,32},{32,40},{40,48},{48,56},{56,64},{64,7... | collective-permute-start | bytes 147464 | tf_op jit(solution)/shard_map/ppermute | solution.py:37
  82.6 18.2 %copy-start = (f32[8,16,128]{2,1,0:T(8,128)S(1)}, f32[8,16,128]{2,1,0:T(8,128)}, u32[]{:S(2)}) copy-start(f32[8,16,128]{2,1,0:T(8,128)} %param.18) | copy-start | bytes 196612
  82.6 18.2 %copy-start.5 = (f32[8,16,128]{2,1,0:T(8,128)S(1)}, f32[8,16,128]{2,1,0:T(8,128)}, u32[]{:S(2)}) copy-start(f32[8,16,128]{2,1,0:T(8,128)} %param.17) | copy-start | bytes 196612
  84.3 14.0 %collective-permute-start.6 = (f32[3,8,2,128]{3,1,2,0:T(8,128)S(1)}, f32[3,8,2,128]{3,1,2,0:T(8,128)S(1)}, u32[]{:S(2)}, u32[]{:S(2)}) collective-permute-start(f32[3,8,2,128]{3,1,2,0:T(8,128)S(1)} %copy.386), channel_id=1, source_target_pairs={{0,1},{1,2},{2,3},{3,4},{4,5},{5,6},{6,7},{8,9},{9,10},{10,11},{11... | collective-permute-start | bytes 73736 | tf_op jit(solution)/shard_map/ppermute | solution.py:37
  86.3 12.0 %collective-permute-start.7 = (f32[3,8,2,128]{3,1,2,0:T(8,128)S(1)}, f32[3,8,2,128]{3,1,2,0:T(8,128)S(1)}, u32[]{:S(2)}, u32[]{:S(2)}) collective-permute-start(f32[3,8,2,128]{3,1,2,0:T(8,128)S(1)} %copy.387), channel_id=1, source_target_pairs={{1,0},{2,1},{3,2},{4,3},{5,4},{6,5},{7,6},{9,8},{10,9},{11,10},{12... | collective-permute-start | bytes 73736 | tf_op jit(solution)/shard_map/ppermute | solution.py:38
  90.1 8.3 %collective-permute-start.4 = (f32[3,2,16,128]{3,2,1,0:T(8,128)S(1)}, f32[3,2,16,128]{3,2,1,0:T(8,128)S(1)}, u32[]{:S(2)}, u32[]{:S(2)}) collective-permute-start(f32[3,2,16,128]{3,2,1,0:T(8,128)S(1)} %get-tuple-element.123), channel_id=1, source_target_pairs={{0,8},{8,16},{16,24},{24,32},{32,40},{40,48},{48,56},{56,64},{64,7... | collective-permute-start | bytes 147464 | tf_op jit(solution)/shard_map/ppermute | solution.py:37
  92.7 8.1 %collective-permute-start.5 = (f32[3,2,16,128]{3,2,1,0:T(8,128)S(1)}, f32[3,2,16,128]{3,2,1,0:T(8,128)S(1)}, u32[]{:S(2)}, u32[]{:S(2)}) collective-permute-start(f32[3,2,16,128]{3,2,1,0:T(8,128)S(1)} %get-tuple-element.124), channel_id=1, source_target_pairs={{8,0},{16,8},{24,16},{32,24},{40,32},{48,40},{56,48},{64,56},{72,6... | collective-permute-start | bytes 147464 | tf_op jit(solution)/shard_map/ppermute | solution.py:38
  101.5 15.2 %collective-permute-start.8 = (f32[3,2,16,128]{3,2,1,0:T(8,128)S(1)}, f32[3,2,16,128]{3,2,1,0:T(8,128)S(1)}, u32[]{:S(2)}, u32[]{:S(2)}) collective-permute-start(f32[3,2,16,128]{3,2,1,0:T(8,128)S(1)} %get-tuple-element.116), channel_id=1, source_target_pairs={{8,0},{16,8},{24,16},{32,24},{40,32},{48,40},{56,48},{64,56},{72,6... | collective-permute-start | bytes 147464 | tf_op jit(solution)/shard_map/ppermute | solution.py:38
  103.4 13.3 %collective-permute-start.9 = (f32[3,2,16,128]{3,2,1,0:T(8,128)S(1)}, f32[3,2,16,128]{3,2,1,0:T(8,128)S(1)}, u32[]{:S(2)}, u32[]{:S(2)}) collective-permute-start(f32[3,2,16,128]{3,2,1,0:T(8,128)S(1)} %get-tuple-element.117), channel_id=1, source_target_pairs={{0,8},{8,16},{16,24},{24,32},{32,40},{40,48},{48,56},{56,64},{64,7... | collective-permute-start | bytes 147464 | tf_op jit(solution)/shard_map/ppermute | solution.py:37
  109.5 5.8 %collective-permute-start.10 = (f32[3,8,2,128]{3,1,2,0:T(8,128)S(1)}, f32[3,8,2,128]{3,1,2,0:T(8,128)S(1)}, u32[]{:S(2)}, u32[]{:S(2)}) collective-permute-start(f32[3,8,2,128]{3,1,2,0:T(8,128)S(1)} %copy.390), channel_id=1, source_target_pairs={{0,1},{1,2},{2,3},{3,4},{4,5},{5,6},{6,7},{8,9},{9,10},{10,11},{11... | collective-permute-start | bytes 73736 | tf_op jit(solution)/shard_map/ppermute | solution.py:37
  111.4 5.1 %collective-permute-start.11 = (f32[3,8,2,128]{3,1,2,0:T(8,128)S(1)}, f32[3,8,2,128]{3,1,2,0:T(8,128)S(1)}, u32[]{:S(2)}, u32[]{:S(2)}) collective-permute-start(f32[3,8,2,128]{3,1,2,0:T(8,128)S(1)} %copy.391), channel_id=1, source_target_pairs={{1,0},{2,1},{3,2},{4,3},{5,4},{6,5},{7,6},{9,8},{10,9},{11,10},{12... | collective-permute-start | bytes 73736 | tf_op jit(solution)/shard_map/ppermute | solution.py:38
  115.3 17.9 %copy-start.6 = (f32[8,16,128]{2,1,0:T(8,128)S(1)}, f32[8,16,128]{2,1,0:T(8,128)}, u32[]{:S(2)}) copy-start(f32[8,16,128]{2,1,0:T(8,128)} %param.22) | copy-start | bytes 196612
  117.0 17.2 %copy-start.7 = (f32[8,16,128]{2,1,0:T(8,128)S(1)}, f32[8,16,128]{2,1,0:T(8,128)}, u32[]{:S(2)}) copy-start(f32[8,16,128]{2,1,0:T(8,128)} %param.21) | copy-start | bytes 196612
  117.4 17.6 %copy-start.1 = (f32[3,8,16,128]{3,2,1,0:T(8,128)}, f32[3,8,16,128]{3,2,1,0:T(8,128)S(1)}, u32[]{:S(2)}) copy-start(f32[3,8,16,128]{3,2,1,0:T(8,128)S(1)} %fusion.2) | copy-start | bytes 589828
  117.4 11.6 %collective-permute-start.14 = (f32[3,8,2,128]{3,1,2,0:T(8,128)S(1)}, f32[3,8,2,128]{3,1,2,0:T(8,128)S(1)}, u32[]{:S(2)}, u32[]{:S(2)}) collective-permute-start(f32[3,8,2,128]{3,1,2,0:T(8,128)S(1)} %copy.396), channel_id=1, source_target_pairs={{0,1},{1,2},{2,3},{3,4},{4,5},{5,6},{6,7},{8,9},{9,10},{10,11},{11... | collective-permute-start | bytes 73736 | tf_op jit(solution)/shard_map/ppermute | solution.py:37
  120.8 8.3 %collective-permute-start.15 = (f32[3,8,2,128]{3,1,2,0:T(8,128)S(1)}, f32[3,8,2,128]{3,1,2,0:T(8,128)S(1)}, u32[]{:S(2)}, u32[]{:S(2)}) collective-permute-start(f32[3,8,2,128]{3,1,2,0:T(8,128)S(1)} %copy.397), channel_id=1, source_target_pairs={{1,0},{2,1},{3,2},{4,3},{5,4},{6,5},{7,6},{9,8},{10,9},{11,10},{12... | collective-permute-start | bytes 73736 | tf_op jit(solution)/shard_map/ppermute | solution.py:38
  123.2 6.0 %collective-permute-start.12 = (f32[3,2,16,128]{3,2,1,0:T(8,128)S(1)}, f32[3,2,16,128]{3,2,1,0:T(8,128)S(1)}, u32[]{:S(2)}, u32[]{:S(2)}) collective-permute-start(f32[3,2,16,128]{3,2,1,0:T(8,128)S(1)} %get-tuple-element.111), channel_id=1, source_target_pairs={{0,8},{8,16},{16,24},{24,32},{32,40},{40,48},{48,56},{56,64},{64,7... | collective-permute-start | bytes 147464 | tf_op jit(solution)/shard_map/ppermute | solution.py:37
  125.1 8.1 %collective-permute-start.13 = (f32[3,2,16,128]{3,2,1,0:T(8,128)S(1)}, f32[3,2,16,128]{3,2,1,0:T(8,128)S(1)}, u32[]{:S(2)}, u32[]{:S(2)}) collective-permute-start(f32[3,2,16,128]{3,2,1,0:T(8,128)S(1)} %get-tuple-element.110), channel_id=1, source_target_pairs={{8,0},{16,8},{24,16},{32,24},{40,32},{48,40},{56,48},{64,56},{72,6... | collective-permute-start | bytes 147464 | tf_op jit(solution)/shard_map/ppermute | solution.py:38
  (3 other events, 39.5 us)

commit v6 on v5

--- a/solution.py
+++ b/solution.py
@@ -98,9 +98,9 @@
 
     mine_vals = mine_ref[...].astype(jnp.float32)
     other_vals = other_ref[...].astype(jnp.float32)
-    mine_sq = jnp.sum(jnp.sum(mine_vals * mine_vals, axis=2, keepdims=True), axis=1, keepdims=True)
-    other_sq = jnp.sum(jnp.sum(other_vals * other_vals, axis=2, keepdims=True), axis=1, keepdims=True)
-    cross = jnp.sum(jnp.sum(mine_vals * other_vals, axis=2, keepdims=True), axis=1, keepdims=True)
+    mine_sq = jnp.sum(jnp.sum(mine_vals * mine_vals, axis=1, keepdims=True), axis=2, keepdims=True)
+    other_sq = jnp.sum(jnp.sum(other_vals * other_vals, axis=1, keepdims=True), axis=2, keepdims=True)
+    cross = jnp.sum(jnp.sum(mine_vals * other_vals, axis=1, keepdims=True), axis=2, keepdims=True)
     mine_norm = jnp.sqrt(mine_sq / samples + epsilon)
     other_norm = jnp.sqrt(other_sq / samples + epsilon)
     corr = (cross / samples) / (mine_norm * other_norm)

time: 137 us -> 136 us (level)
  no operation moved by 1% of the time
where the time goes in v6:
time: 136 us; the launch traced here: 135 us
  starting transfers between devices  60.7 us (45%)
  waiting for transfers between devices  39.1 us (29%)
  local copies, waits for them, and re-layouts  15.4 us (11%)
  Pallas kernels  12.2 us (9%)
  other arithmetic  6.16 us (5%)
  between operations  1.55 us (1%)
    ppermute x8, waiting for transfers between devices, halo_pad(): lax.ppermute(lax.slice_in_dim(block, size - width, size, axis=dim), axis,...  26.5 us
    ppermute x8, starting transfers between devices, halo_pad(): lax.ppermute(lax.slice_in_dim(block, size - width, size, axis=dim), axis,...  25 us
    ppermute x8, starting transfers between devices, halo_pad(): lax.ppermute(lax.slice_in_dim(block, 0, width, axis=dim), axis, backward)  24.9 us
    pallas_call x1, Pallas kernels, pair_sums(): pl.pallas_call(functools.partial(pair_kernel, block, float(samples)), gri...  12.2 us
    ppermute x8, waiting for transfers between devices, halo_pad(): lax.ppermute(lax.slice_in_dim(block, 0, width, axis=dim), axis, backward)  11.2 us
    all_to_all x1, starting transfers between devices, station_part(): lax.all_to_all(send, ('gx', 'gy'), split_axis=0, concat_axis=0, tiled=True)  10.8 us
    unnamed x24, local copies, waits for them, and re-layouts  4.19 us
    gather x1, local copies, waits for them, and re-layouts, station_part(): padded_rows[jnp.where(slot_station >= 0, slot_station, stations_here)]  3.54 us
  transfers between devices with their start and end apart: 17, of which 6 were waited for; matrix products, arithmetic and copies ran while one was open for 6% of the time, Pallas kernels for 0%

profile of v6, /device:TPU:14, one launch (start us, length us, event | category | flops | bytes accessed | tf_op | source)
XLA Modules:
  0.0 135.0 jit_solution(16509492361835959925)
XLA Ops:
  4.7 3.5 %gather_fusion.1 = bf16[512,32,128]{2,1,0:T(8,128)(2,1)} fusion(bf16[33,32,128]{2,1,0:T(8,128)(2,1)S(1)} %concatenate.120, s32[1024]{0:T(1024)S(1)} %pad_clamp_fusion), kind=kCustom, calls=%fused_computation.1 | custom fusion | bytes 8390656 | tf_op jit(solution)/shard_map/gather | solution.py:177
  8.3 10.8 %all-to-all-start = ((bf16[128,4,32,128]{3,2,1,0:T(8,128)(2,1)}), bf16[128,4,32,128]{3,2,1,0:T(8,128)(2,1)}, u32[]{:S(2)}, u32[]{:S(2)}) async-start(bf16[128,4,32,128]{3,2,1,0:T(8,128)(2,1)} %bitcast.271), calls=%async_computation | async-start | bytes 8388608 | tf_op jit(solution)/shard_map/all_to_all | solution.py:178
  19.2 2.0 %collective-permute-start.2 = (f32[3,8,2,128]{3,1,2,0:T(8,128)S(1)}, f32[3,8,2,128]{3,1,2,0:T(8,128)S(1)}, u32[]{:S(2)}, u32[]{:S(2)}) collective-permute-start(f32[3,8,2,128]{3,1,2,0:T(8,128)S(1)} %copy.372), channel_id=1, source_target_pairs={{0,1},{1,2},{2,3},{3,4},{4,5},{5,6},{6,7},{8,9},{9,10},{10,11},{11... | collective-permute-start | bytes 73736 | tf_op jit(solution)/shard_map/ppermute | solution.py:37
  21.3 3.5 %collective-permute-start.3 = (f32[3,8,2,128]{3,1,2,0:T(8,128)S(1)}, f32[3,8,2,128]{3,1,2,0:T(8,128)S(1)}, u32[]{:S(2)}, u32[]{:S(2)}) collective-permute-start(f32[3,8,2,128]{3,1,2,0:T(8,128)S(1)} %copy.373), channel_id=1, source_target_pairs={{1,0},{2,1},{3,2},{4,3},{5,4},{6,5},{7,6},{9,8},{10,9},{11,10},{12... | collective-permute-start | bytes 73736 | tf_op jit(solution)/shard_map/ppermute | solution.py:38
  24.8 2.8 %collective-permute-start = (f32[3,2,16,128]{3,2,1,0:T(8,128)S(1)}, f32[3,2,16,128]{3,2,1,0:T(8,128)S(1)}, u32[]{:S(2)}, u32[]{:S(2)}) collective-permute-start(f32[3,2,16,128]{3,2,1,0:T(8,128)S(1)} %get-tuple-element.129), channel_id=1, source_target_pairs={{8,0},{16,8},{24,16},{32,24},{40,32},{48,40},{56,48},{64,56},{72,6... | collective-permute-start | bytes 147464 | tf_op jit(solution)/shard_map/ppermute | solution.py:38
  27.6 5.2 %collective-permute-start.1 = (f32[3,2,16,128]{3,2,1,0:T(8,128)S(1)}, f32[3,2,16,128]{3,2,1,0:T(8,128)S(1)}, u32[]{:S(2)}, u32[]{:S(2)}) collective-permute-start(f32[3,2,16,128]{3,2,1,0:T(8,128)S(1)} %get-tuple-element.130), channel_id=1, source_target_pairs={{0,8},{8,16},{16,24},{24,32},{32,40},{40,48},{48,56},{56,64},{64,7... | collective-permute-start | bytes 147464 | tf_op jit(solution)/shard_map/ppermute | solution.py:37
  34.2 3.5 %gather_fusion = bf16[512,32,128]{2,1,0:T(8,128)(2,1)} fusion(bf16[33,32,128]{2,1,0:T(8,128)(2,1)S(1)} %concatenate.120, s32[1024]{0:T(1024)S(1)} %pad_clamp_fusion.1), kind=kCustom, calls=%fused_computation | custom fusion | bytes 8390656 | tf_op jit(solution)/shard_map/gather | solution.py:180
  37.7 26.4 %collective-permute-done.2 = f32[3,8,2,128]{3,1,2,0:T(8,128)S(1)} collective-permute-done((f32[3,8,2,128]{3,1,2,0:T(8,128)S(1)}, f32[3,8,2,128]{3,1,2,0:T(8,128)S(1)}, u32[]{:S(2)}, u32[]{:S(2)}) %collective-permute-start.2) | collective-permute-done | bytes 24608 | tf_op jit(solution)/shard_map/ppermute | solution.py:37
  64.3 3.5 %collective-permute-done = f32[3,2,16,128]{3,2,1,0:T(8,128)S(1)} collective-permute-done((f32[3,2,16,128]{3,2,1,0:T(8,128)S(1)}, f32[3,2,16,128]{3,2,1,0:T(8,128)S(1)}, u32[]{:S(2)}, u32[]{:S(2)}) %collective-permute-start) | collective-permute-done | bytes 49184 | tf_op jit(solution)/shard_map/ppermute | solution.py:38
  69.7 12.2 %shard_map.146 = f32[32,32,128]{2,1,0:T(8,128)} custom-call(s32[512]{0:T(512)} %compare_select_fusion.4.station_ref, bf16[512,32,128]{2,1,0:T(8,128)(2,1)} %gather_fusion, bf16[512,32,128]{2,1,0:T(8,128)(2,1)} %bitcast.21.other_ref), custom_call_target="tpu_custom_call" | custom-call | flops 41943040 | bytes 8388608 | tf_op jit(solution)/shard_map/pallas_call | solution.py:135
  83.5 1.9 %collective-permute-start.6 = (f32[3,8,2,128]{3,1,2,0:T(8,128)S(1)}, f32[3,8,2,128]{3,1,2,0:T(8,128)S(1)}, u32[]{:S(2)}, u32[]{:S(2)}) collective-permute-start(f32[3,8,2,128]{3,1,2,0:T(8,128)S(1)} %copy.386), channel_id=1, source_target_pairs={{0,1},{1,2},{2,3},{3,4},{4,5},{5,6},{6,7},{8,9},{9,10},{10,11},{11... | collective-permute-start | bytes 73736 | tf_op jit(solution)/shard_map/ppermute | solution.py:37
  85.4 3.6 %collective-permute-start.7 = (f32[3,8,2,128]{3,1,2,0:T(8,128)S(1)}, f32[3,8,2,128]{3,1,2,0:T(8,128)S(1)}, u32[]{:S(2)}, u32[]{:S(2)}) collective-permute-start(f32[3,8,2,128]{3,1,2,0:T(8,128)S(1)} %copy.387), channel_id=1, source_target_pairs={{1,0},{2,1},{3,2},{4,3},{5,4},{6,5},{7,6},{9,8},{10,9},{11,10},{12... | collective-permute-start | bytes 73736 | tf_op jit(solution)/shard_map/ppermute | solution.py:38
  89.3 2.7 %collective-permute-start.4 = (f32[3,2,16,128]{3,2,1,0:T(8,128)S(1)}, f32[3,2,16,128]{3,2,1,0:T(8,128)S(1)}, u32[]{:S(2)}, u32[]{:S(2)}) collective-permute-start(f32[3,2,16,128]{3,2,1,0:T(8,128)S(1)} %get-tuple-element.123), channel_id=1, source_target_pairs={{0,8},{8,16},{16,24},{24,32},{32,40},{40,48},{48,56},{56,64},{64,7... | collective-permute-start | bytes 147464 | tf_op jit(solution)/shard_map/ppermute | solution.py:37
  91.9 3.2 %collective-permute-start.5 = (f32[3,2,16,128]{3,2,1,0:T(8,128)S(1)}, f32[3,2,16,128]{3,2,1,0:T(8,128)S(1)}, u32[]{:S(2)}, u32[]{:S(2)}) collective-permute-start(f32[3,2,16,128]{3,2,1,0:T(8,128)S(1)} %get-tuple-element.124), channel_id=1, source_target_pairs={{8,0},{16,8},{24,16},{32,24},{40,32},{48,40},{56,48},{64,56},{72,6... | collective-permute-start | bytes 147464 | tf_op jit(solution)/shard_map/ppermute | solution.py:38
  95.3 2.1 %copy.406 = f32[4,8,32,128]{3,1,2,0:T(8,128)} copy(f32[4,8,32,128]{3,2,1,0:T(8,128)} %bitcast.272) | data formatting | bytes 1048576
  97.6 2.4 %collective-permute-done.5 = f32[3,2,16,128]{3,2,1,0:T(8,128)S(1)} collective-permute-done((f32[3,2,16,128]{3,2,1,0:T(8,128)S(1)}, f32[3,2,16,128]{3,2,1,0:T(8,128)S(1)}, u32[]{:S(2)}, u32[]{:S(2)}) %collective-permute-start.5) | collective-permute-done | bytes 49184 | tf_op jit(solution)/shard_map/ppermute | solution.py:38
  100.7 1.9 %collective-permute-start.8 = (f32[3,2,16,128]{3,2,1,0:T(8,128)S(1)}, f32[3,2,16,128]{3,2,1,0:T(8,128)S(1)}, u32[]{:S(2)}, u32[]{:S(2)}) collective-permute-start(f32[3,2,16,128]{3,2,1,0:T(8,128)S(1)} %get-tuple-element.116), channel_id=1, source_target_pairs={{8,0},{16,8},{24,16},{32,24},{40,32},{48,40},{56,48},{64,56},{72,6... | collective-permute-start | bytes 147464 | tf_op jit(solution)/shard_map/ppermute | solution.py:38
  102.6 6.0 %collective-permute-start.9 = (f32[3,2,16,128]{3,2,1,0:T(8,128)S(1)}, f32[3,2,16,128]{3,2,1,0:T(8,128)S(1)}, u32[]{:S(2)}, u32[]{:S(2)}) collective-permute-start(f32[3,2,16,128]{3,2,1,0:T(8,128)S(1)} %get-tuple-element.117), channel_id=1, source_target_pairs={{0,8},{8,16},{16,24},{24,32},{32,40},{40,48},{48,56},{56,64},{64,7... | collective-permute-start | bytes 147464 | tf_op jit(solution)/shard_map/ppermute | solution.py:37
  108.7 1.9 %collective-permute-start.10 = (f32[3,8,2,128]{3,1,2,0:T(8,128)S(1)}, f32[3,8,2,128]{3,1,2,0:T(8,128)S(1)}, u32[]{:S(2)}, u32[]{:S(2)}) collective-permute-start(f32[3,8,2,128]{3,1,2,0:T(8,128)S(1)} %copy.390), channel_id=1, source_target_pairs={{0,1},{1,2},{2,3},{3,4},{4,5},{5,6},{6,7},{8,9},{9,10},{10,11},{11... | collective-permute-start | bytes 73736 | tf_op jit(solution)/shard_map/ppermute | solution.py:37
  110.6 3.6 %collective-permute-start.11 = (f32[3,8,2,128]{3,1,2,0:T(8,128)S(1)}, f32[3,8,2,128]{3,1,2,0:T(8,128)S(1)}, u32[]{:S(2)}, u32[]{:S(2)}) collective-permute-start(f32[3,8,2,128]{3,1,2,0:T(8,128)S(1)} %copy.391), channel_id=1, source_target_pairs={{1,0},{2,1},{3,2},{4,3},{5,4},{6,5},{7,6},{9,8},{10,9},{11,10},{12... | collective-permute-start | bytes 73736 | tf_op jit(solution)/shard_map/ppermute | solution.py:38
  116.6 3.3 %collective-permute-start.14 = (f32[3,8,2,128]{3,1,2,0:T(8,128)S(1)}, f32[3,8,2,128]{3,1,2,0:T(8,128)S(1)}, u32[]{:S(2)}, u32[]{:S(2)}) collective-permute-start(f32[3,8,2,128]{3,1,2,0:T(8,128)S(1)} %copy.396), channel_id=1, source_target_pairs={{0,1},{1,2},{2,3},{3,4},{4,5},{5,6},{6,7},{8,9},{9,10},{10,11},{11... | collective-permute-start | bytes 73736 | tf_op jit(solution)/shard_map/ppermute | solution.py:37
  120.0 2.3 %collective-permute-start.15 = (f32[3,8,2,128]{3,1,2,0:T(8,128)S(1)}, f32[3,8,2,128]{3,1,2,0:T(8,128)S(1)}, u32[]{:S(2)}, u32[]{:S(2)}) collective-permute-start(f32[3,8,2,128]{3,1,2,0:T(8,128)S(1)} %copy.397), channel_id=1, source_target_pairs={{1,0},{2,1},{3,2},{4,3},{5,4},{6,5},{7,6},{9,8},{10,9},{11,10},{12... | collective-permute-start | bytes 73736 | tf_op jit(solution)/shard_map/ppermute | solution.py:38
  124.3 3.9 %collective-permute-start.13 = (f32[3,2,16,128]{3,2,1,0:T(8,128)S(1)}, f32[3,2,16,128]{3,2,1,0:T(8,128)S(1)}, u32[]{:S(2)}, u32[]{:S(2)}) collective-permute-start(f32[3,2,16,128]{3,2,1,0:T(8,128)S(1)} %get-tuple-element.110), channel_id=1, source_target_pairs={{8,0},{16,8},{24,16},{32,24},{40,32},{48,40},{56,48},{64,56},{72,6... | collective-permute-start | bytes 147464 | tf_op jit(solution)/shard_map/ppermute | solution.py:38
  128.4 4.0 %collective-permute-done.13 = f32[3,2,16,128]{3,2,1,0:T(8,128)S(1)} collective-permute-done((f32[3,2,16,128]{3,2,1,0:T(8,128)S(1)}, f32[3,2,16,128]{3,2,1,0:T(8,128)S(1)}, u32[]{:S(2)}, u32[]{:S(2)}) %collective-permute-start.13) | collective-permute-done | bytes 49184 | tf_op jit(solution)/shard_map/ppermute | solution.py:38
  (146 shorter events, 17.0 us)
Async XLA Ops:
  8.3 25.7 %copy-start.8 = (f32[8,16,128]{2,1,0:T(8,128)S(1)}, f32[8,16,128]{2,1,0:T(8,128)}, u32[]{:S(2)}) copy-start(f32[8,16,128]{2,1,0:T(8,128)} %param.19) | copy-start | bytes 196612
  8.3 25.8 %copy-start.4 = (bf16[12,8,16,128]{3,2,1,0:T(8,128)(2,1)S(1)}, bf16[12,8,16,128]{3,2,1,0:T(8,128)(2,1)}, u32[]{:S(2)}) copy-start(bf16[12,8,16,128]{3,2,1,0:T(8,128)(2,1)} %param.20) | copy-start | bytes 1179652
  8.3 61.4 %all-to-all-start = ((bf16[128,4,32,128]{3,2,1,0:T(8,128)(2,1)}), bf16[128,4,32,128]{3,2,1,0:T(8,128)(2,1)}, u32[]{:S(2)}, u32[]{:S(2)}) async-start(bf16[128,4,32,128]{3,2,1,0:T(8,128)(2,1)} %bitcast.271), calls=%async_computation | async-start | bytes 8388608 | tf_op jit(solution)/shard_map/all_to_all | solution.py:178
  19.2 44.9 %collective-permute-start.2 = (f32[3,8,2,128]{3,1,2,0:T(8,128)S(1)}, f32[3,8,2,128]{3,1,2,0:T(8,128)S(1)}, u32[]{:S(2)}, u32[]{:S(2)}) collective-permute-start(f32[3,8,2,128]{3,1,2,0:T(8,128)S(1)} %copy.372), channel_id=1, source_target_pairs={{0,1},{1,2},{2,3},{3,4},{4,5},{5,6},{6,7},{8,9},{9,10},{10,11},{11... | collective-permute-start | bytes 73736 | tf_op jit(solution)/shard_map/ppermute | solution.py:37
  21.3 42.9 %collective-permute-start.3 = (f32[3,8,2,128]{3,1,2,0:T(8,128)S(1)}, f32[3,8,2,128]{3,1,2,0:T(8,128)S(1)}, u32[]{:S(2)}, u32[]{:S(2)}) collective-permute-start(f32[3,8,2,128]{3,1,2,0:T(8,128)S(1)} %copy.373), channel_id=1, source_target_pairs={{1,0},{2,1},{3,2},{4,3},{5,4},{6,5},{7,6},{9,8},{10,9},{11,10},{12... | collective-permute-start | bytes 73736 | tf_op jit(solution)/shard_map/ppermute | solution.py:38
  24.8 42.9 %collective-permute-start = (f32[3,2,16,128]{3,2,1,0:T(8,128)S(1)}, f32[3,2,16,128]{3,2,1,0:T(8,128)S(1)}, u32[]{:S(2)}, u32[]{:S(2)}) collective-permute-start(f32[3,2,16,128]{3,2,1,0:T(8,128)S(1)} %get-tuple-element.129), channel_id=1, source_target_pairs={{8,0},{16,8},{24,16},{32,24},{40,32},{48,40},{56,48},{64,56},{72,6... | collective-permute-start | bytes 147464 | tf_op jit(solution)/shard_map/ppermute | solution.py:38
  27.6 40.2 %collective-permute-start.1 = (f32[3,2,16,128]{3,2,1,0:T(8,128)S(1)}, f32[3,2,16,128]{3,2,1,0:T(8,128)S(1)}, u32[]{:S(2)}, u32[]{:S(2)}) collective-permute-start(f32[3,2,16,128]{3,2,1,0:T(8,128)S(1)} %get-tuple-element.130), channel_id=1, source_target_pairs={{0,8},{8,16},{16,24},{24,32},{32,40},{40,48},{48,56},{56,64},{64,7... | collective-permute-start | bytes 147464 | tf_op jit(solution)/shard_map/ppermute | solution.py:37
  81.8 18.2 %copy-start = (f32[8,16,128]{2,1,0:T(8,128)S(1)}, f32[8,16,128]{2,1,0:T(8,128)}, u32[]{:S(2)}) copy-start(f32[8,16,128]{2,1,0:T(8,128)} %param.18) | copy-start | bytes 196612
  81.8 18.2 %copy-start.5 = (f32[8,16,128]{2,1,0:T(8,128)S(1)}, f32[8,16,128]{2,1,0:T(8,128)}, u32[]{:S(2)}) copy-start(f32[8,16,128]{2,1,0:T(8,128)} %param.17) | copy-start | bytes 196612
  83.5 14.0 %collective-permute-start.6 = (f32[3,8,2,128]{3,1,2,0:T(8,128)S(1)}, f32[3,8,2,128]{3,1,2,0:T(8,128)S(1)}, u32[]{:S(2)}, u32[]{:S(2)}) collective-permute-start(f32[3,8,2,128]{3,1,2,0:T(8,128)S(1)} %copy.386), channel_id=1, source_target_pairs={{0,1},{1,2},{2,3},{3,4},{4,5},{5,6},{6,7},{8,9},{9,10},{10,11},{11... | collective-permute-start | bytes 73736 | tf_op jit(solution)/shard_map/ppermute | solution.py:37
  85.4 12.0 %collective-permute-start.7 = (f32[3,8,2,128]{3,1,2,0:T(8,128)S(1)}, f32[3,8,2,128]{3,1,2,0:T(8,128)S(1)}, u32[]{:S(2)}, u32[]{:S(2)}) collective-permute-start(f32[3,8,2,128]{3,1,2,0:T(8,128)S(1)} %copy.387), channel_id=1, source_target_pairs={{1,0},{2,1},{3,2},{4,3},{5,4},{6,5},{7,6},{9,8},{10,9},{11,10},{12... | collective-permute-start | bytes 73736 | tf_op jit(solution)/shard_map/ppermute | solution.py:38
  89.3 8.3 %collective-permute-start.4 = (f32[3,2,16,128]{3,2,1,0:T(8,128)S(1)}, f32[3,2,16,128]{3,2,1,0:T(8,128)S(1)}, u32[]{:S(2)}, u32[]{:S(2)}) collective-permute-start(f32[3,2,16,128]{3,2,1,0:T(8,128)S(1)} %get-tuple-element.123), channel_id=1, source_target_pairs={{0,8},{8,16},{16,24},{24,32},{32,40},{40,48},{48,56},{56,64},{64,7... | collective-permute-start | bytes 147464 | tf_op jit(solution)/shard_map/ppermute | solution.py:37
  91.9 8.1 %collective-permute-start.5 = (f32[3,2,16,128]{3,2,1,0:T(8,128)S(1)}, f32[3,2,16,128]{3,2,1,0:T(8,128)S(1)}, u32[]{:S(2)}, u32[]{:S(2)}) collective-permute-start(f32[3,2,16,128]{3,2,1,0:T(8,128)S(1)} %get-tuple-element.124), channel_id=1, source_target_pairs={{8,0},{16,8},{24,16},{32,24},{40,32},{48,40},{56,48},{64,56},{72,6... | collective-permute-start | bytes 147464 | tf_op jit(solution)/shard_map/ppermute | solution.py:38
  100.7 15.2 %collective-permute-start.8 = (f32[3,2,16,128]{3,2,1,0:T(8,128)S(1)}, f32[3,2,16,128]{3,2,1,0:T(8,128)S(1)}, u32[]{:S(2)}, u32[]{:S(2)}) collective-permute-start(f32[3,2,16,128]{3,2,1,0:T(8,128)S(1)} %get-tuple-element.116), channel_id=1, source_target_pairs={{8,0},{16,8},{24,16},{32,24},{40,32},{48,40},{56,48},{64,56},{72,6... | collective-permute-start | bytes 147464 | tf_op jit(solution)/shard_map/ppermute | solution.py:38
  102.6 13.3 %collective-permute-start.9 = (f32[3,2,16,128]{3,2,1,0:T(8,128)S(1)}, f32[3,2,16,128]{3,2,1,0:T(8,128)S(1)}, u32[]{:S(2)}, u32[]{:S(2)}) collective-permute-start(f32[3,2,16,128]{3,2,1,0:T(8,128)S(1)} %get-tuple-element.117), channel_id=1, source_target_pairs={{0,8},{8,16},{16,24},{24,32},{32,40},{40,48},{48,56},{56,64},{64,7... | collective-permute-start | bytes 147464 | tf_op jit(solution)/shard_map/ppermute | solution.py:37
  108.7 5.8 %collective-permute-start.10 = (f32[3,8,2,128]{3,1,2,0:T(8,128)S(1)}, f32[3,8,2,128]{3,1,2,0:T(8,128)S(1)}, u32[]{:S(2)}, u32[]{:S(2)}) collective-permute-start(f32[3,8,2,128]{3,1,2,0:T(8,128)S(1)} %copy.390), channel_id=1, source_target_pairs={{0,1},{1,2},{2,3},{3,4},{4,5},{5,6},{6,7},{8,9},{9,10},{10,11},{11... | collective-permute-start | bytes 73736 | tf_op jit(solution)/shard_map/ppermute | solution.py:37
  110.6 5.1 %collective-permute-start.11 = (f32[3,8,2,128]{3,1,2,0:T(8,128)S(1)}, f32[3,8,2,128]{3,1,2,0:T(8,128)S(1)}, u32[]{:S(2)}, u32[]{:S(2)}) collective-permute-start(f32[3,8,2,128]{3,1,2,0:T(8,128)S(1)} %copy.391), channel_id=1, source_target_pairs={{1,0},{2,1},{3,2},{4,3},{5,4},{6,5},{7,6},{9,8},{10,9},{11,10},{12... | collective-permute-start | bytes 73736 | tf_op jit(solution)/shard_map/ppermute | solution.py:38
  114.5 17.9 %copy-start.6 = (f32[8,16,128]{2,1,0:T(8,128)S(1)}, f32[8,16,128]{2,1,0:T(8,128)}, u32[]{:S(2)}) copy-start(f32[8,16,128]{2,1,0:T(8,128)} %param.22) | copy-start | bytes 196612
  116.2 17.2 %copy-start.7 = (f32[8,16,128]{2,1,0:T(8,128)S(1)}, f32[8,16,128]{2,1,0:T(8,128)}, u32[]{:S(2)}) copy-start(f32[8,16,128]{2,1,0:T(8,128)} %param.21) | copy-start | bytes 196612
  116.6 17.6 %copy-start.1 = (f32[3,8,16,128]{3,2,1,0:T(8,128)}, f32[3,8,16,128]{3,2,1,0:T(8,128)S(1)}, u32[]{:S(2)}) copy-start(f32[3,8,16,128]{3,2,1,0:T(8,128)S(1)} %fusion.2) | copy-start | bytes 589828
  116.6 11.6 %collective-permute-start.14 = (f32[3,8,2,128]{3,1,2,0:T(8,128)S(1)}, f32[3,8,2,128]{3,1,2,0:T(8,128)S(1)}, u32[]{:S(2)}, u32[]{:S(2)}) collective-permute-start(f32[3,8,2,128]{3,1,2,0:T(8,128)S(1)} %copy.396), channel_id=1, source_target_pairs={{0,1},{1,2},{2,3},{3,4},{4,5},{5,6},{6,7},{8,9},{9,10},{10,11},{11... | collective-permute-start | bytes 73736 | tf_op jit(solution)/shard_map/ppermute | solution.py:37
  120.0 8.3 %collective-permute-start.15 = (f32[3,8,2,128]{3,1,2,0:T(8,128)S(1)}, f32[3,8,2,128]{3,1,2,0:T(8,128)S(1)}, u32[]{:S(2)}, u32[]{:S(2)}) collective-permute-start(f32[3,8,2,128]{3,1,2,0:T(8,128)S(1)} %copy.397), channel_id=1, source_target_pairs={{1,0},{2,1},{3,2},{4,3},{5,4},{6,5},{7,6},{9,8},{10,9},{11,10},{12... | collective-permute-start | bytes 73736 | tf_op jit(solution)/shard_map/ppermute | solution.py:38
  122.4 6.0 %collective-permute-start.12 = (f32[3,2,16,128]{3,2,1,0:T(8,128)S(1)}, f32[3,2,16,128]{3,2,1,0:T(8,128)S(1)}, u32[]{:S(2)}, u32[]{:S(2)}) collective-permute-start(f32[3,2,16,128]{3,2,1,0:T(8,128)S(1)} %get-tuple-element.111), channel_id=1, source_target_pairs={{0,8},{8,16},{16,24},{24,32},{32,40},{40,48},{48,56},{56,64},{64,7... | collective-permute-start | bytes 147464 | tf_op jit(solution)/shard_map/ppermute | solution.py:37
  124.3 8.1 %collective-permute-start.13 = (f32[3,2,16,128]{3,2,1,0:T(8,128)S(1)}, f32[3,2,16,128]{3,2,1,0:T(8,128)S(1)}, u32[]{:S(2)}, u32[]{:S(2)}) collective-permute-start(f32[3,2,16,128]{3,2,1,0:T(8,128)S(1)} %get-tuple-element.110), channel_id=1, source_target_pairs={{8,0},{16,8},{24,16},{32,24},{40,32},{48,40},{56,48},{64,56},{72,6... | collective-permute-start | bytes 147464 | tf_op jit(solution)/shard_map/ppermute | solution.py:38
  (3 other events, 37.9 us)

commit v7 on v6

--- a/solution.py
+++ b/solution.py
@@ -89,7 +89,33 @@
     return (moved, grown, lame_kernel, shear_kernel)
 
 
-def pair_kernel(block, samples, station_ref, mine_ref, other_ref, out_ref, acc_ref, toward_ref):
+def stats_kernel(mine_ref, other_ref, mine_out, other_out, cross_out):
+    mine_vals = mine_ref[...].astype(jnp.float32)
+    other_vals = other_ref[...].astype(jnp.float32)
+    shape = mine_out.shape
+    for values, out in ((mine_vals * mine_vals, mine_out), (other_vals * other_vals, other_out), (mine_vals * other_vals, cross_out)):
+        total = jnp.sum(jnp.sum(values, axis=1, keepdims=True), axis=2, keepdims=True)
+        out[...] = jnp.broadcast_to(total, shape)
+
+
+def row_stats(mine, other):
+    slots, rows, lanes = mine.shape
+    block = 64
+    spec = pl.BlockSpec((block, rows, lanes), lambda g: (g, 0, 0))
+    small = pl.BlockSpec((block, 1, lanes), lambda g: (g, 0, 0))
+    shape = jax.ShapeDtypeStruct((slots, 1, lanes), jnp.float32)
+    return pl.pallas_call(
+        stats_kernel,
+        grid=(slots // block,),
+        in_specs=[spec, spec],
+        out_specs=[small, small, small],
+        out_shape=[shape, shape, shape],
+        compiler_params=pltpu.CompilerParams(dimension_semantics=("arbitrary",)),
+        cost_estimate=pl.CostEstimate(flops=6 * slots * rows * lanes, transcendentals=0, bytes_accessed=4 * slots * rows * lanes),
+    )(mine, other)
+
+
+def pair_kernel(block, station_ref, mine_ref, other_ref, other_scale_ref, mine_scale_ref, out_ref, acc_ref, toward_ref):
     step = pl.program_id(0)
 
     @pl.when(step == 0)
@@ -98,15 +124,8 @@
 
     mine_vals = mine_ref[...].astype(jnp.float32)
     other_vals = other_ref[...].astype(jnp.float32)
-    mine_sq = jnp.sum(jnp.sum(mine_vals * mine_vals, axis=1, keepdims=True), axis=2, keepdims=True)
-    other_sq = jnp.sum(jnp.sum(other_vals * other_vals, axis=1, keepdims=True), axis=2, keepdims=True)
-    cross = jnp.sum(jnp.sum(mine_vals * other_vals, axis=1, keepdims=True), axis=2, keepdims=True)
-    mine_norm = jnp.sqrt(mine_sq / samples + epsilon)
-    other_norm = jnp.sqrt(other_sq / samples + epsilon)
-    corr = (cross / samples) / (mine_norm * other_norm)
-    toward = other_vals / other_norm - corr * (mine_vals / mine_norm)
+    toward = other_vals * other_scale_ref[...] - mine_scale_ref[...] * mine_vals
     toward_ref[...] = toward.astype(jnp.bfloat16).astype(jnp.float32)
-
     ways = acc_ref.shape[0]
 
     def add_some(i, carry):
@@ -127,17 +146,18 @@
         out_ref[...] = total
 
 
-def pair_sums(targets, mine, other, stations):
+def pair_sums(targets, mine, other, other_scale, mine_scale, stations):
     slots, rows, lanes = mine.shape
     block = 64
     samples = rows * lanes
     spec = pl.BlockSpec((block, rows, lanes), lambda g, t: (g, 0, 0))
+    small = pl.BlockSpec((block, 1, lanes), lambda g, t: (g, 0, 0))
     return pl.pallas_call(
-        functools.partial(pair_kernel, block, float(samples)),
+        functools.partial(pair_kernel, block),
         grid_spec=pltpu.PrefetchScalarGridSpec(
             num_scalar_prefetch=1,
             grid=(slots // block,),
-            in_specs=[spec, spec],
+            in_specs=[spec, spec, small, small],
             out_specs=pl.BlockSpec((stations, rows, lanes), lambda g, t: (0, 0, 0)),
             scratch_shapes=[
                 pltpu.VMEM((4, stations + 1, rows, lanes), jnp.float32),
@@ -146,8 +166,8 @@
         ),
         out_shape=jax.ShapeDtypeStruct((stations, rows, lanes), jnp.float32),
         compiler_params=pltpu.CompilerParams(dimension_semantics=("arbitrary",)),
-        cost_estimate=pl.CostEstimate(flops=20 * slots * samples, transcendentals=0, bytes_accessed=4 * slots * samples),
-    )(targets, mine, other)
+        cost_estimate=pl.CostEstimate(flops=8 * slots * samples, transcendentals=0, bytes_accessed=4 * slots * samples),
+    )(targets, mine, other, other_scale, mine_scale)
 
 
 def station_part(residuals, station_cell, station_pairs, cells_first, cells_second, step_count):
@@ -180,12 +200,21 @@
     mine = padded_rows[jnp.where(mine_station >= 0, mine_station, stations_here)]
     slots = devices * 4
     targets = jnp.where(mine_station >= 0, mine_station, stations_here).reshape(slots)
-    adjoint3 = pair_sums(
-        targets, mine.reshape(slots, samples // lanes, lanes), recv.reshape(slots, samples // lanes, lanes), stations_here
-    )
+    mine_rows = mine.reshape(slots, samples // lanes, lanes)
+    other_rows = recv.reshape(slots, samples // lanes, lanes)
+    mine_sq, other_sq, cross = row_stats(mine_rows, other_rows)
+    mine_norm = jnp.sqrt(mine_sq / samples + epsilon)
+    other_norm = jnp.sqrt(other_sq / samples + epsilon)
+    corr = (cross / samples) / (mine_norm * other_norm)
+    other_scale = 1.0 / other_norm
+    mine_scale = corr / mine_norm
+    adjoint3 = pair_sums(targets, mine_rows, other_rows, other_scale, mine_scale, stations_here)
     adjoint = adjoint3.reshape(stations_here, samples)
-    last = adjoint3[:, samples // lanes - 1, lanes - step_count :]
-    tail = last
+    end_other = other_rows[:, -1, lanes - step_count :].astype(jnp.float32)
+    end_mine = mine_rows[:, -1, lanes - step_count :].astype(jnp.float32)
+    end_toward = (end_other * other_scale[:, 0, :1] - mine_scale[:, 0, :1] * end_mine).astype(jnp.bfloat16).astype(jnp.float32)
+    slot_hits = (targets[:, None] == jnp.arange(stations_here)[None, :]).astype(jnp.float32)
+    tail = jnp.dot(slot_hits.T, end_toward, precision=lax.Precision.HIGHEST)
     cells_hit = (station_cell[:, None] == jnp.arange(cells_first * cells_second)[None, :]).astype(jnp.float32)
     surfaces = jnp.stack(
         [

time: 136 us -> 150 us (1.10)
  Pallas kernels: 12.2 us -> 17.8 us
  other arithmetic: 6.16 us -> 9.94 us
  local copies, waits for them, and re-layouts: 15.4 us -> 18.1 us
    pallas_call x1 -> x2, Pallas kernels: 12.2 us -> 17.8 us  [the longest x1 9.54 us: pair_sums(): pl.pallas_call(functools.partial(pair_kernel, block), grid_spec=pltpu.Pre...]
    div x0 -> x1, other arithmetic: none -> 2.74 us  [station_part(): other_scale = 1.0 / other_norm]
    slice x2 -> x3, local copies, waits for them, and re-layouts: 1.11 us -> 3.75 us  [the longest x1 1.68 us: station_part(): end_mine = mine_rows[:, -1, lanes - step_count:].astype(jnp.float32)]
    ppermute x8, waiting for transfers between devices: 11.2 us -> 13.3 us  [halo_pad(): lax.ppermute(lax.slice_in_dim(block, 0, width, axis=dim), axis, backward)]
    convert_element_type x0 -> x1, other arithmetic: none -> 1.65 us  [station_part(): end_other = other_rows[:, -1, lanes - step_count:].astype(jnp.float32)]
    unnamed x24 -> x30, local copies, waits for them, and re-layouts: 4.19 us -> 4.2 us
  transfers between devices with their start and end apart: 17 -> 17, of which waited for: 6 -> 6; matrix products, arithmetic and copies ran while one was open for 6% -> 7% of each run, Pallas kernels for 0% -> 6%
where the time goes in v7:
time: 150 us; the launch traced here: 149 us
  starting transfers between devices  60.7 us (40%)
  waiting for transfers between devices  40.1 us (27%)
  local copies, waits for them, and re-layouts  18.1 us (12%)
  Pallas kernels  17.8 us (12%)
  other arithmetic  9.94 us (7%)
  between operations  1.66 us (1%)
    ppermute x8, waiting for transfers between devices, halo_pad(): lax.ppermute(lax.slice_in_dim(block, size - width, size, axis=dim), axis,...  25.3 us
    ppermute x8, starting transfers between devices, halo_pad(): lax.ppermute(lax.slice_in_dim(block, size - width, size, axis=dim), axis,...  25 us
    ppermute x8, starting transfers between devices, halo_pad(): lax.ppermute(lax.slice_in_dim(block, 0, width, axis=dim), axis, backward)  24.9 us
    ppermute x8, waiting for transfers between devices, halo_pad(): lax.ppermute(lax.slice_in_dim(block, 0, width, axis=dim), axis, backward)  13.3 us
    all_to_all x1, starting transfers between devices, station_part(): lax.all_to_all(send, ('gx', 'gy'), split_axis=0, concat_axis=0, tiled=True)  10.8 us
    pallas_call x1, Pallas kernels, pair_sums(): pl.pallas_call(functools.partial(pair_kernel, block), grid_spec=pltpu.Pre...  9.54 us
    pallas_call x1, Pallas kernels, row_stats(): pl.pallas_call(stats_kernel, grid=(slots // block,), in_specs=[spec, spec...  8.29 us
    unnamed x30, local copies, waits for them, and re-layouts  4.2 us
  transfers between devices with their start and end apart: 17, of which 6 were waited for; matrix products, arithmetic and copies ran while one was open for 7% of the time, Pallas kernels for 6%

profile of v7, /device:TPU:14, one launch (start us, length us, event | category | flops | bytes accessed | tf_op | source)
XLA Modules:
  0.0 148.7 jit_solution(13819786717338940746)
XLA Ops:
  4.7 3.5 %gather_fusion = bf16[512,32,128]{2,1,0:T(8,128)(2,1)} fusion(bf16[33,32,128]{2,1,0:T(8,128)(2,1)S(1)} %concatenate.120, s32[1024]{0:T(1024)S(1)} %pad_clamp_fusion.1), kind=kCustom, calls=%fused_computation | custom fusion | bytes 8390656 | tf_op jit(solution)/shard_map/gather | solution.py:197
  8.3 10.8 %all-to-all-start = ((bf16[128,4,32,128]{3,2,1,0:T(8,128)(2,1)}), bf16[128,4,32,128]{3,2,1,0:T(8,128)(2,1)}, u32[]{:S(2)}, u32[]{:S(2)}) async-start(bf16[128,4,32,128]{3,2,1,0:T(8,128)(2,1)} %bitcast.277), calls=%async_computation | async-start | bytes 8388608 | tf_op jit(solution)/shard_map/all_to_all | solution.py:198
  19.2 2.0 %collective-permute-start.2 = (f32[3,8,2,128]{3,1,2,0:T(8,128)S(1)}, f32[3,8,2,128]{3,1,2,0:T(8,128)S(1)}, u32[]{:S(2)}, u32[]{:S(2)}) collective-permute-start(f32[3,8,2,128]{3,1,2,0:T(8,128)S(1)} %copy.373), channel_id=1, source_target_pairs={{0,1},{1,2},{2,3},{3,4},{4,5},{5,6},{6,7},{8,9},{9,10},{10,11},{11... | collective-permute-start | bytes 73736 | tf_op jit(solution)/shard_map/ppermute | solution.py:37
  21.2 3.5 %collective-permute-start.3 = (f32[3,8,2,128]{3,1,2,0:T(8,128)S(1)}, f32[3,8,2,128]{3,1,2,0:T(8,128)S(1)}, u32[]{:S(2)}, u32[]{:S(2)}) collective-permute-start(f32[3,8,2,128]{3,1,2,0:T(8,128)S(1)} %copy.374), channel_id=1, source_target_pairs={{1,0},{2,1},{3,2},{4,3},{5,4},{6,5},{7,6},{9,8},{10,9},{11,10},{12... | collective-permute-start | bytes 73736 | tf_op jit(solution)/shard_map/ppermute | solution.py:38
  24.8 2.8 %collective-permute-start = (f32[3,2,16,128]{3,2,1,0:T(8,128)S(1)}, f32[3,2,16,128]{3,2,1,0:T(8,128)S(1)}, u32[]{:S(2)}, u32[]{:S(2)}) collective-permute-start(f32[3,2,16,128]{3,2,1,0:T(8,128)S(1)} %get-tuple-element.137), channel_id=1, source_target_pairs={{8,0},{16,8},{24,16},{32,24},{40,32},{48,40},{56,48},{64,56},{72,6... | collective-permute-start | bytes 147464 | tf_op jit(solution)/shard_map/ppermute | solution.py:38
  27.6 5.2 %collective-permute-start.1 = (f32[3,2,16,128]{3,2,1,0:T(8,128)S(1)}, f32[3,2,16,128]{3,2,1,0:T(8,128)S(1)}, u32[]{:S(2)}, u32[]{:S(2)}) collective-permute-start(f32[3,2,16,128]{3,2,1,0:T(8,128)S(1)} %get-tuple-element.138), channel_id=1, source_target_pairs={{0,8},{8,16},{16,24},{24,32},{32,40},{40,48},{48,56},{56,64},{64,7... | collective-permute-start | bytes 147464 | tf_op jit(solution)/shard_map/ppermute | solution.py:37
  33.6 3.5 %gather_fusion.1 = bf16[512,32,128]{2,1,0:T(8,128)(2,1)} fusion(bf16[33,32,128]{2,1,0:T(8,128)(2,1)S(1)} %concatenate.120, s32[1024]{0:T(1024)S(1)} %pad_clamp_fusion), kind=kCustom, calls=%fused_computation.1 | custom fusion | bytes 8390656 | tf_op jit(solution)/shard_map/gather | solution.py:200
  38.8 25.3 %collective-permute-done.2 = f32[3,8,2,128]{3,1,2,0:T(8,128)S(1)} collective-permute-done((f32[3,8,2,128]{3,1,2,0:T(8,128)S(1)}, f32[3,8,2,128]{3,1,2,0:T(8,128)S(1)}, u32[]{:S(2)}, u32[]{:S(2)}) %collective-permute-start.2) | collective-permute-done | bytes 24608 | tf_op jit(solution)/shard_map/ppermute | solution.py:37
  64.3 3.5 %collective-permute-done = f32[3,2,16,128]{3,2,1,0:T(8,128)S(1)} collective-permute-done((f32[3,2,16,128]{3,2,1,0:T(8,128)S(1)}, f32[3,2,16,128]{3,2,1,0:T(8,128)S(1)}, u32[]{:S(2)}, u32[]{:S(2)}) %collective-permute-start) | collective-permute-done | bytes 49184 | tf_op jit(solution)/shard_map/ppermute | solution.py:38
  69.6 8.3 %shard_map.146 = (f32[512,1,128]{2,1,0:T(1,128)}, f32[512,1,128]{2,1,0:T(1,128)}, f32[512,1,128]{2,1,0:T(1,128)}) custom-call(bf16[512,32,128]{2,1,0:T(8,128)(2,1)} %gather_fusion.1, bf16[512,32,128]{2,1,0:T(8,128)(2,1)} %bitcast.21.other_ref), custom_call_target="tpu_custom_call" | custom-call | flops 12582912 | bytes 8388608 | tf_op jit(solution)/shard_map/pallas_call | solution.py:107
  79.6 2.7 %broadcast_divide_fusion = (f32[512,1,128]{2,1,0:T(1,128)S(1)}, f32[512,1,128]{2,1,0:T(1,128)S(1)}) fusion(f32[512,1,128]{2,1,0:T(1,128)} %get-tuple-element.32, f32[512,1,128]{2,1,0:T(1,128)} %get-tuple-element.34, f32[512,1,128]{2,1,0:T(1,128)} %get-tuple-element.33), kind=kLoop, calls=%fused_computation.85 | loop fusion | flops 589824 | bytes 1310720 | tf_op jit(solution)/shard_map/div | solution.py:209
  85.5 1.9 %collective-permute-start.6 = (f32[3,8,2,128]{3,1,2,0:T(8,128)S(1)}, f32[3,8,2,128]{3,1,2,0:T(8,128)S(1)}, u32[]{:S(2)}, u32[]{:S(2)}) collective-permute-start(f32[3,8,2,128]{3,1,2,0:T(8,128)S(1)} %copy.387), channel_id=1, source_target_pairs={{0,1},{1,2},{2,3},{3,4},{4,5},{5,6},{6,7},{8,9},{9,10},{10,11},{11... | collective-permute-start | bytes 73736 | tf_op jit(solution)/shard_map/ppermute | solution.py:37
  87.4 3.6 %collective-permute-start.7 = (f32[3,8,2,128]{3,1,2,0:T(8,128)S(1)}, f32[3,8,2,128]{3,1,2,0:T(8,128)S(1)}, u32[]{:S(2)}, u32[]{:S(2)}) collective-permute-start(f32[3,8,2,128]{3,1,2,0:T(8,128)S(1)} %copy.388), channel_id=1, source_target_pairs={{1,0},{2,1},{3,2},{4,3},{5,4},{6,5},{7,6},{9,8},{10,9},{11,10},{12... | collective-permute-start | bytes 73736 | tf_op jit(solution)/shard_map/ppermute | solution.py:38
  91.3 9.5 %shard_map.147 = f32[32,32,128]{2,1,0:T(8,128)} custom-call(s32[512]{0:T(512)} %copy-done.11, bf16[512,32,128]{2,1,0:T(8,128)(2,1)} %gather_fusion.1, bf16[512,32,128]{2,1,0:T(8,128)(2,1)} %bitcast.21.other_ref, f32[512,1,128]{2,1,0:T(1,128)} %copy-done.3, f32[512,1,128]{2,1,0:T(1,128)} %copy-done.4), custom_call_target="tpu_custom_call" | custom-call | flops 16777216 | bytes 8388608 | tf_op jit(solution)/shard_map/pallas_call | solution.py:155
  100.8 2.1 %copy.412 = f32[4,8,32,128]{3,1,2,0:T(8,128)} copy(f32[4,8,32,128]{3,2,1,0:T(8,128)} %bitcast.278) | data formatting | bytes 1048576
  102.9 2.7 %collective-permute-start.4 = (f32[3,2,16,128]{3,2,1,0:T(8,128)S(1)}, f32[3,2,16,128]{3,2,1,0:T(8,128)S(1)}, u32[]{:S(2)}, u32[]{:S(2)}) collective-permute-start(f32[3,2,16,128]{3,2,1,0:T(8,128)S(1)} %get-tuple-element.131), channel_id=1, source_target_pairs={{0,8},{8,16},{16,24},{24,32},{32,40},{40,48},{48,56},{56,64},{64,7... | collective-permute-start | bytes 147464 | tf_op jit(solution)/shard_map/ppermute | solution.py:37
  105.6 3.2 %collective-permute-start.5 = (f32[3,2,16,128]{3,2,1,0:T(8,128)S(1)}, f32[3,2,16,128]{3,2,1,0:T(8,128)S(1)}, u32[]{:S(2)}, u32[]{:S(2)}) collective-permute-start(f32[3,2,16,128]{3,2,1,0:T(8,128)S(1)} %get-tuple-element.132), channel_id=1, source_target_pairs={{8,0},{16,8},{24,16},{32,24},{40,32},{48,40},{56,48},{64,56},{72,6... | collective-permute-start | bytes 147464 | tf_op jit(solution)/shard_map/ppermute | solution.py:38
  109.1 4.5 %collective-permute-done.5 = f32[3,2,16,128]{3,2,1,0:T(8,128)S(1)} collective-permute-done((f32[3,2,16,128]{3,2,1,0:T(8,128)S(1)}, f32[3,2,16,128]{3,2,1,0:T(8,128)S(1)}, u32[]{:S(2)}, u32[]{:S(2)}) %collective-permute-start.5) | collective-permute-done | bytes 49184 | tf_op jit(solution)/shard_map/ppermute | solution.py:38
  116.3 6.0 %collective-permute-start.9 = (f32[3,2,16,128]{3,2,1,0:T(8,128)S(1)}, f32[3,2,16,128]{3,2,1,0:T(8,128)S(1)}, u32[]{:S(2)}, u32[]{:S(2)}) collective-permute-start(f32[3,2,16,128]{3,2,1,0:T(8,128)S(1)} %get-tuple-element.125), channel_id=1, source_target_pairs={{0,8},{8,16},{16,24},{24,32},{32,40},{40,48},{48,56},{56,64},{64,7... | collective-permute-start | bytes 147464 | tf_op jit(solution)/shard_map/ppermute | solution.py:37
  124.3 3.6 %collective-permute-start.11 = (f32[3,8,2,128]{3,1,2,0:T(8,128)S(1)}, f32[3,8,2,128]{3,1,2,0:T(8,128)S(1)}, u32[]{:S(2)}, u32[]{:S(2)}) collective-permute-start(f32[3,8,2,128]{3,1,2,0:T(8,128)S(1)} %copy.392), channel_id=1, source_target_pairs={{1,0},{2,1},{3,2},{4,3},{5,4},{6,5},{7,6},{9,8},{10,9},{11,10},{12... | collective-permute-start | bytes 73736 | tf_op jit(solution)/shard_map/ppermute | solution.py:38
  130.3 3.3 %collective-permute-start.14 = (f32[3,8,2,128]{3,1,2,0:T(8,128)S(1)}, f32[3,8,2,128]{3,1,2,0:T(8,128)S(1)}, u32[]{:S(2)}, u32[]{:S(2)}) collective-permute-start(f32[3,8,2,128]{3,1,2,0:T(8,128)S(1)} %copy.397), channel_id=1, source_target_pairs={{0,1},{1,2},{2,3},{3,4},{4,5},{5,6},{6,7},{8,9},{9,10},{10,11},{11... | collective-permute-start | bytes 73736 | tf_op jit(solution)/shard_map/ppermute | solution.py:37
  133.6 2.3 %collective-permute-start.15 = (f32[3,8,2,128]{3,1,2,0:T(8,128)S(1)}, f32[3,8,2,128]{3,1,2,0:T(8,128)S(1)}, u32[]{:S(2)}, u32[]{:S(2)}) collective-permute-start(f32[3,8,2,128]{3,1,2,0:T(8,128)S(1)} %copy.398), channel_id=1, source_target_pairs={{1,0},{2,1},{3,2},{4,3},{5,4},{6,5},{7,6},{9,8},{10,9},{11,10},{12... | collective-permute-start | bytes 73736 | tf_op jit(solution)/shard_map/ppermute | solution.py:38
  138.0 3.9 %collective-permute-start.13 = (f32[3,2,16,128]{3,2,1,0:T(8,128)S(1)}, f32[3,2,16,128]{3,2,1,0:T(8,128)S(1)}, u32[]{:S(2)}, u32[]{:S(2)}) collective-permute-start(f32[3,2,16,128]{3,2,1,0:T(8,128)S(1)} %get-tuple-element.118), channel_id=1, source_target_pairs={{8,0},{16,8},{24,16},{32,24},{40,32},{48,40},{56,48},{64,56},{72,6... | collective-permute-start | bytes 147464 | tf_op jit(solution)/shard_map/ppermute | solution.py:38
  142.1 4.0 %collective-permute-done.13 = f32[3,2,16,128]{3,2,1,0:T(8,128)S(1)} collective-permute-done((f32[3,2,16,128]{3,2,1,0:T(8,128)S(1)}, f32[3,2,16,128]{3,2,1,0:T(8,128)S(1)}, u32[]{:S(2)}, u32[]{:S(2)}) %collective-permute-start.13) | collective-permute-done | bytes 49184 | tf_op jit(solution)/shard_map/ppermute | solution.py:38
  (157 shorter events, 25.0 us)
Async XLA Ops:
  8.3 25.2 %copy-start.10 = (f32[8,16,128]{2,1,0:T(8,128)S(1)}, f32[8,16,128]{2,1,0:T(8,128)}, u32[]{:S(2)}) copy-start(f32[8,16,128]{2,1,0:T(8,128)} %param.19) | copy-start | bytes 196612
  8.3 25.2 %copy-start.6 = (bf16[12,8,16,128]{3,2,1,0:T(8,128)(2,1)S(1)}, bf16[12,8,16,128]{3,2,1,0:T(8,128)(2,1)}, u32[]{:S(2)}) copy-start(bf16[12,8,16,128]{3,2,1,0:T(8,128)(2,1)} %param.20) | copy-start | bytes 1179652
  8.3 61.4 %all-to-all-start = ((bf16[128,4,32,128]{3,2,1,0:T(8,128)(2,1)}), bf16[128,4,32,128]{3,2,1,0:T(8,128)(2,1)}, u32[]{:S(2)}, u32[]{:S(2)}) async-start(bf16[128,4,32,128]{3,2,1,0:T(8,128)(2,1)} %bitcast.277), calls=%async_computation | async-start | bytes 8388608 | tf_op jit(solution)/shard_map/all_to_all | solution.py:198
  19.2 44.9 %collective-permute-start.2 = (f32[3,8,2,128]{3,1,2,0:T(8,128)S(1)}, f32[3,8,2,128]{3,1,2,0:T(8,128)S(1)}, u32[]{:S(2)}, u32[]{:S(2)}) collective-permute-start(f32[3,8,2,128]{3,1,2,0:T(8,128)S(1)} %copy.373), channel_id=1, source_target_pairs={{0,1},{1,2},{2,3},{3,4},{4,5},{5,6},{6,7},{8,9},{9,10},{10,11},{11... | collective-permute-start | bytes 73736 | tf_op jit(solution)/shard_map/ppermute | solution.py:37
  21.2 42.9 %collective-permute-start.3 = (f32[3,8,2,128]{3,1,2,0:T(8,128)S(1)}, f32[3,8,2,128]{3,1,2,0:T(8,128)S(1)}, u32[]{:S(2)}, u32[]{:S(2)}) collective-permute-start(f32[3,8,2,128]{3,1,2,0:T(8,128)S(1)} %copy.374), channel_id=1, source_target_pairs={{1,0},{2,1},{3,2},{4,3},{5,4},{6,5},{7,6},{9,8},{10,9},{11,10},{12... | collective-permute-start | bytes 73736 | tf_op jit(solution)/shard_map/ppermute | solution.py:38
  24.8 42.9 %collective-permute-start = (f32[3,2,16,128]{3,2,1,0:T(8,128)S(1)}, f32[3,2,16,128]{3,2,1,0:T(8,128)S(1)}, u32[]{:S(2)}, u32[]{:S(2)}) collective-permute-start(f32[3,2,16,128]{3,2,1,0:T(8,128)S(1)} %get-tuple-element.137), channel_id=1, source_target_pairs={{8,0},{16,8},{24,16},{32,24},{40,32},{48,40},{56,48},{64,56},{72,6... | collective-permute-start | bytes 147464 | tf_op jit(solution)/shard_map/ppermute | solution.py:38
  27.6 40.2 %collective-permute-start.1 = (f32[3,2,16,128]{3,2,1,0:T(8,128)S(1)}, f32[3,2,16,128]{3,2,1,0:T(8,128)S(1)}, u32[]{:S(2)}, u32[]{:S(2)}) collective-permute-start(f32[3,2,16,128]{3,2,1,0:T(8,128)S(1)} %get-tuple-element.138), channel_id=1, source_target_pairs={{0,8},{8,16},{16,24},{24,32},{32,40},{40,48},{48,56},{56,64},{64,7... | collective-permute-start | bytes 147464 | tf_op jit(solution)/shard_map/ppermute | solution.py:37
  33.5 51.0 %copy-start.11 = (s32[512]{0:T(512)}, s32[512]{0:T(512)S(1)}, u32[]{:S(2)}) copy-start(s32[512]{0:T(512)S(1)} %compare_select_fusion.4.station_ref) | copy-start | bytes 6148
  85.5 23.5 %collective-permute-start.6 = (f32[3,8,2,128]{3,1,2,0:T(8,128)S(1)}, f32[3,8,2,128]{3,1,2,0:T(8,128)S(1)}, u32[]{:S(2)}, u32[]{:S(2)}) collective-permute-start(f32[3,8,2,128]{3,1,2,0:T(8,128)S(1)} %copy.387), channel_id=1, source_target_pairs={{0,1},{1,2},{2,3},{3,4},{4,5},{5,6},{6,7},{8,9},{9,10},{10,11},{11... | collective-permute-start | bytes 73736 | tf_op jit(solution)/shard_map/ppermute | solution.py:37
  87.4 21.6 %collective-permute-start.7 = (f32[3,8,2,128]{3,1,2,0:T(8,128)S(1)}, f32[3,8,2,128]{3,1,2,0:T(8,128)S(1)}, u32[]{:S(2)}, u32[]{:S(2)}) collective-permute-start(f32[3,8,2,128]{3,1,2,0:T(8,128)S(1)} %copy.388), channel_id=1, source_target_pairs={{1,0},{2,1},{3,2},{4,3},{5,4},{6,5},{7,6},{9,8},{10,9},{11,10},{12... | collective-permute-start | bytes 73736 | tf_op jit(solution)/shard_map/ppermute | solution.py:38
  91.2 22.5 %copy-start = (f32[8,16,128]{2,1,0:T(8,128)S(1)}, f32[8,16,128]{2,1,0:T(8,128)}, u32[]{:S(2)}) copy-start(f32[8,16,128]{2,1,0:T(8,128)} %param.18) | copy-start | bytes 196612
  91.2 22.5 %copy-start.7 = (f32[8,16,128]{2,1,0:T(8,128)S(1)}, f32[8,16,128]{2,1,0:T(8,128)}, u32[]{:S(2)}) copy-start(f32[8,16,128]{2,1,0:T(8,128)} %param.17) | copy-start | bytes 196612
  102.9 6.2 %collective-permute-start.4 = (f32[3,2,16,128]{3,2,1,0:T(8,128)S(1)}, f32[3,2,16,128]{3,2,1,0:T(8,128)S(1)}, u32[]{:S(2)}, u32[]{:S(2)}) collective-permute-start(f32[3,2,16,128]{3,2,1,0:T(8,128)S(1)} %get-tuple-element.131), channel_id=1, source_target_pairs={{0,8},{8,16},{16,24},{24,32},{32,40},{40,48},{48,56},{56,64},{64,7... | collective-permute-start | bytes 147464 | tf_op jit(solution)/shard_map/ppermute | solution.py:37
  105.6 8.1 %collective-permute-start.5 = (f32[3,2,16,128]{3,2,1,0:T(8,128)S(1)}, f32[3,2,16,128]{3,2,1,0:T(8,128)S(1)}, u32[]{:S(2)}, u32[]{:S(2)}) collective-permute-start(f32[3,2,16,128]{3,2,1,0:T(8,128)S(1)} %get-tuple-element.132), channel_id=1, source_target_pairs={{8,0},{16,8},{24,16},{32,24},{40,32},{48,40},{56,48},{64,56},{72,6... | collective-permute-start | bytes 147464 | tf_op jit(solution)/shard_map/ppermute | solution.py:38
  114.4 15.2 %collective-permute-start.8 = (f32[3,2,16,128]{3,2,1,0:T(8,128)S(1)}, f32[3,2,16,128]{3,2,1,0:T(8,128)S(1)}, u32[]{:S(2)}, u32[]{:S(2)}) collective-permute-start(f32[3,2,16,128]{3,2,1,0:T(8,128)S(1)} %get-tuple-element.124), channel_id=1, source_target_pairs={{8,0},{16,8},{24,16},{32,24},{40,32},{48,40},{56,48},{64,56},{72,6... | collective-permute-start | bytes 147464 | tf_op jit(solution)/shard_map/ppermute | solution.py:38
  116.3 13.3 %collective-permute-start.9 = (f32[3,2,16,128]{3,2,1,0:T(8,128)S(1)}, f32[3,2,16,128]{3,2,1,0:T(8,128)S(1)}, u32[]{:S(2)}, u32[]{:S(2)}) collective-permute-start(f32[3,2,16,128]{3,2,1,0:T(8,128)S(1)} %get-tuple-element.125), channel_id=1, source_target_pairs={{0,8},{8,16},{16,24},{24,32},{32,40},{40,48},{48,56},{56,64},{64,7... | collective-permute-start | bytes 147464 | tf_op jit(solution)/shard_map/ppermute | solution.py:37
  122.4 5.8 %collective-permute-start.10 = (f32[3,8,2,128]{3,1,2,0:T(8,128)S(1)}, f32[3,8,2,128]{3,1,2,0:T(8,128)S(1)}, u32[]{:S(2)}, u32[]{:S(2)}) collective-permute-start(f32[3,8,2,128]{3,1,2,0:T(8,128)S(1)} %copy.391), channel_id=1, source_target_pairs={{0,1},{1,2},{2,3},{3,4},{4,5},{5,6},{6,7},{8,9},{9,10},{10,11},{11... | collective-permute-start | bytes 73736 | tf_op jit(solution)/shard_map/ppermute | solution.py:37
  124.3 5.1 %collective-permute-start.11 = (f32[3,8,2,128]{3,1,2,0:T(8,128)S(1)}, f32[3,8,2,128]{3,1,2,0:T(8,128)S(1)}, u32[]{:S(2)}, u32[]{:S(2)}) collective-permute-start(f32[3,8,2,128]{3,1,2,0:T(8,128)S(1)} %copy.392), channel_id=1, source_target_pairs={{1,0},{2,1},{3,2},{4,3},{5,4},{6,5},{7,6},{9,8},{10,9},{11,10},{12... | collective-permute-start | bytes 73736 | tf_op jit(solution)/shard_map/ppermute | solution.py:38
  128.2 17.9 %copy-start.8 = (f32[8,16,128]{2,1,0:T(8,128)S(1)}, f32[8,16,128]{2,1,0:T(8,128)}, u32[]{:S(2)}) copy-start(f32[8,16,128]{2,1,0:T(8,128)} %param.22) | copy-start | bytes 196612
  130.2 17.6 %copy-start.1 = (f32[3,8,16,128]{3,2,1,0:T(8,128)}, f32[3,8,16,128]{3,2,1,0:T(8,128)S(1)}, u32[]{:S(2)}) copy-start(f32[3,8,16,128]{3,2,1,0:T(8,128)S(1)} %fusion.6) | copy-start | bytes 589828
  130.3 11.6 %collective-permute-start.14 = (f32[3,8,2,128]{3,1,2,0:T(8,128)S(1)}, f32[3,8,2,128]{3,1,2,0:T(8,128)S(1)}, u32[]{:S(2)}, u32[]{:S(2)}) collective-permute-start(f32[3,8,2,128]{3,1,2,0:T(8,128)S(1)} %copy.397), channel_id=1, source_target_pairs={{0,1},{1,2},{2,3},{3,4},{4,5},{5,6},{6,7},{8,9},{9,10},{10,11},{11... | collective-permute-start | bytes 73736 | tf_op jit(solution)/shard_map/ppermute | solution.py:37
  133.6 8.3 %collective-permute-start.15 = (f32[3,8,2,128]{3,1,2,0:T(8,128)S(1)}, f32[3,8,2,128]{3,1,2,0:T(8,128)S(1)}, u32[]{:S(2)}, u32[]{:S(2)}) collective-permute-start(f32[3,8,2,128]{3,1,2,0:T(8,128)S(1)} %copy.398), channel_id=1, source_target_pairs={{1,0},{2,1},{3,2},{4,3},{5,4},{6,5},{7,6},{9,8},{10,9},{11,10},{12... | collective-permute-start | bytes 73736 | tf_op jit(solution)/shard_map/ppermute | solution.py:38
  136.0 6.0 %collective-permute-start.12 = (f32[3,2,16,128]{3,2,1,0:T(8,128)S(1)}, f32[3,2,16,128]{3,2,1,0:T(8,128)S(1)}, u32[]{:S(2)}, u32[]{:S(2)}) collective-permute-start(f32[3,2,16,128]{3,2,1,0:T(8,128)S(1)} %get-tuple-element.119), channel_id=1, source_target_pairs={{0,8},{8,16},{16,24},{24,32},{32,40},{40,48},{48,56},{56,64},{64,7... | collective-permute-start | bytes 147464 | tf_op jit(solution)/shard_map/ppermute | solution.py:37
  138.0 8.1 %collective-permute-start.13 = (f32[3,2,16,128]{3,2,1,0:T(8,128)S(1)}, f32[3,2,16,128]{3,2,1,0:T(8,128)S(1)}, u32[]{:S(2)}, u32[]{:S(2)}) collective-permute-start(f32[3,2,16,128]{3,2,1,0:T(8,128)S(1)} %get-tuple-element.118), channel_id=1, source_target_pairs={{8,0},{16,8},{24,16},{32,24},{40,32},{48,40},{56,48},{64,56},{72,6... | collective-permute-start | bytes 147464 | tf_op jit(solution)/shard_map/ppermute | solution.py:38
  (6 other events, 76.7 us)

commit v8 on v1

--- a/solution.py
+++ b/solution.py
@@ -1,7 +1,11 @@
+import functools
+
 import jax
 import jax.numpy as jnp
 from jax import lax
 from jax.sharding import PartitionSpec as P
+from jax.experimental import pallas as pl
+from jax.experimental.pallas import tpu as pltpu
 
 near_weight = 9.0 / 8.0
 far_weight = -1.0 / 24.0
@@ -40,20 +44,24 @@
     return jnp.pad(block, pads)
 
 
+def exchange(block):
+    wide_x = halo_pad(block[0], "gx", 1)
+    wide_y = halo_pad(block[1], "gy", 2)
+    return wide_x, wide_y
+
+
 def advance(velocity, stress, lame_first, shear_modulus, buoyancy, strain_now, surface, lame_kernel, shear_kernel):
     nx = velocity.shape[1]
     ny = velocity.shape[2]
     nz = velocity.shape[3]
-    sx = halo_pad(jnp.stack([stress[0], stress[3], stress[4]]), "gx", 1)
-    sy = halo_pad(jnp.stack([stress[3], stress[1], stress[5]]), "gy", 2)
+    sx, sy = exchange((jnp.stack([stress[0], stress[3], stress[4]]), jnp.stack([stress[3], stress[1], stress[5]])))
     sz = z_pad(jnp.stack([stress[4], stress[5], stress[2]]))
     force_first = forward_diff(sx[0], nx, 0) + backward_diff(sy[0], ny, 1) + backward_diff(sz[0], nz, 2)
     force_second = backward_diff(sx[1], nx, 0) + forward_diff(sy[1], ny, 1) + backward_diff(sz[1], nz, 2)
     force_third = backward_diff(sx[2], nx, 0) + backward_diff(sy[2], ny, 1) + forward_diff(sz[2], nz, 2)
     force_third = force_third.at[:, :, 0].add(surface)
     moved = velocity + time_step * buoyancy[None] * jnp.stack([force_first, force_second, force_third])
-    mx = halo_pad(moved, "gx", 1)
-    my = halo_pad(moved, "gy", 2)
+    mx, my = exchange((moved, moved))
     mz = z_pad(moved)
     rate_first = backward_diff(mx[0], nx, 0)
     rate_second = backward_diff(my[1], ny, 1)
@@ -83,6 +91,49 @@
         + strain_vals[5] * shear_three
     )
     return (moved, grown, lame_kernel, shear_kernel)
+
+
+def pair_kernel(samples, mine_ref, other_ref, hits_ref, out_ref, toward_ref):
+    step = pl.program_id(0)
+
+    @pl.when(step == 0)
+    def _():
+        out_ref[...] = jnp.zeros_like(out_ref)
+
+    mine_vals = mine_ref[...].astype(jnp.float32)
+    other_vals = other_ref[...].astype(jnp.float32)
+    mine_sq = jnp.sum(jnp.sum(mine_vals * mine_vals, axis=1, keepdims=True), axis=2, keepdims=True)
+    other_sq = jnp.sum(jnp.sum(other_vals * other_vals, axis=1, keepdims=True), axis=2, keepdims=True)
+    cross = jnp.sum(jnp.sum(mine_vals * other_vals, axis=1, keepdims=True), axis=2, keepdims=True)
+    mine_norm = jnp.sqrt(mine_sq / samples + epsilon)
+    other_norm = jnp.sqrt(other_sq / samples + epsilon)
+    corr = (cross / samples) / (mine_norm * other_norm)
+    other_scale = 1.0 / other_norm
+    mine_scale = corr / mine_norm
+    toward = other_vals * other_scale - mine_scale * mine_vals
+    block, rows, lanes = toward.shape
+    toward_ref[...] = toward.astype(jnp.bfloat16).astype(jnp.float32).reshape(block * rows, lanes)
+    hits = hits_ref[...]
+    for row in range(rows):
+        part = toward_ref[pl.ds(row, block, stride=rows), :]
+        out_ref[row] = out_ref[row] + jnp.dot(hits, part, preferred_element_type=jnp.float32)
+
+
+def pair_sums(hits_t, mine, other, stations):
+    slots, rows, lanes = mine.shape
+    block = 128
+    samples = rows * lanes
+    spec = pl.BlockSpec((block, rows, lanes), lambda g: (g, 0, 0))
+    return pl.pallas_call(
+        functools.partial(pair_kernel, float(samples)),
+        grid=(slots // block,),
+        in_specs=[spec, spec, pl.BlockSpec((stations, block), lambda g: (0, g))],
+        out_specs=pl.BlockSpec((rows, stations, lanes), lambda g: (0, 0, 0)),
+        out_shape=jax.ShapeDtypeStruct((rows, stations, lanes), jnp.float32),
+        scratch_shapes=[pltpu.VMEM((block * rows, lanes), jnp.float32)],
+        compiler_params=pltpu.CompilerParams(dimension_semantics=("arbitrary",)),
+        cost_estimate=pl.CostEstimate(flops=20 * slots * samples, transcendentals=0, bytes_accessed=4 * slots * samples),
+    )(mine, other, hits_t)
 
 
 def station_part(residuals, station_cell, station_pairs, cells_first, cells_second, step_count):
@@ -106,23 +157,20 @@
     pick_in = (hit[:, :, None] > 0) & (before[:, :, None] == jnp.arange(2)[None, None, :])
     in_station = jnp.sum(jnp.where(pick_in, (blocks[:, :, 1] % stations_here)[:, :, None] + 1, 0), axis=1) - 1
     slot_station = jnp.concatenate([own_station, in_station], axis=1)
-    hits = (slot_station[:, :, None] == jnp.arange(stations_here)[None, None, :]).astype(jnp.bfloat16)
     lanes = 128
     rows = residuals.reshape(stations_here, samples // lanes, lanes)
-    send = jnp.einsum("xjs,sab->xjab", hits, rows)
+    padded_rows = jnp.concatenate([rows, jnp.zeros((1,) + rows.shape[1:], rows.dtype)], axis=0)
+    send = padded_rows[jnp.where(slot_station >= 0, slot_station, stations_here)]
     recv = lax.all_to_all(send, ("gx", "gy"), split_axis=0, concat_axis=0, tiled=True)
-    partner = jnp.concatenate([recv[:, 2:4], recv[:, 0:2]], axis=1)
-    mine_vals = send.astype(jnp.float32)
-    other_vals = partner.astype(jnp.float32)
-    mine_norm = jnp.sqrt(jnp.mean(mine_vals * mine_vals, axis=(2, 3), keepdims=True) + epsilon)
-    other_norm = jnp.sqrt(jnp.mean(other_vals * other_vals, axis=(2, 3), keepdims=True) + epsilon)
-    corr = jnp.mean(mine_vals * other_vals, axis=(2, 3), keepdims=True) / (mine_norm * other_norm)
-    toward = (other_vals / other_norm - corr * (mine_vals / mine_norm)).astype(jnp.bfloat16)
-    adjoint3 = jnp.einsum("xjs,xjab->sab", hits, toward, preferred_element_type=jnp.float32)
-    adjoint = adjoint3.reshape(stations_here, samples)
-    tail = jnp.einsum(
-        "xjs,xjk->sk", hits, toward[:, :, -1, lanes - step_count :], preferred_element_type=jnp.float32
-    )
+    mine_station = jnp.concatenate([slot_station[:, 2:4], slot_station[:, 0:2]], axis=1)
+    mine = padded_rows[jnp.where(mine_station >= 0, mine_station, stations_here)]
+    slots = devices * 4
+    hits_t = (jnp.arange(stations_here)[:, None] == mine_station.reshape(slots)[None, :]).astype(jnp.float32)
+    by_row = pair_sums(
+        hits_t, mine.reshape(slots, samples // lanes, lanes), recv.reshape(slots, samples // lanes, lanes), stations_here
+    )
+    adjoint = by_row.transpose(1, 0, 2).reshape(stations_here, samples)
+    tail = by_row[-1, :, lanes - step_count :]
     cells_hit = (station_cell[:, None] == jnp.arange(cells_first * cells_second)[None, :]).astype(jnp.float32)
     surfaces = jnp.stack(
         [

time: 167 us -> 139 us (0.83)
  other arithmetic: 23.2 us -> 6.21 us
  local copies, waits for them, and re-layouts: 29.9 us -> 14.9 us
  Pallas kernels: 0 us -> 13.4 us
  matrix products: 6.87 us -> 0 us
  waiting for transfers between devices: 43.2 us -> 41.1 us
    pallas_call x0 -> x1, Pallas kernels: none -> 13.4 us  [pair_sums(): pl.pallas_call(functools.partial(pair_kernel, float(samples)), grid=(slot...]
    unnamed x38 -> x23, local copies, waits for them, and re-layouts: 11.6 us -> 2.04 us
    dot_general x1 -> x0, local copies, waits for them, and re-layouts: 7.9 us -> none  [station_part(): send = jnp.einsum('xjs,sab->xjab', hits, rows)]
    gather x0 -> x2, local copies, waits for them, and re-layouts: none -> 7.07 us  [the longest x1 3.54 us: station_part(): padded_rows[jnp.where(slot_station >= 0, slot_station, stations_here)]]
    dot_general x3 -> x0, matrix products: 6.87 us -> none  [the longest x1 3.48 us: station_part(): jnp.einsum('xjs,xjab->sab', hits, toward, preferred_element_type=jnp.floa...]
    slice x5 -> x6, local copies, waits for them, and re-layouts: 5.32 us -> 0.99 us  [the longest x2 0.9 us: station_part(): tail = by_row[-1, :, lanes - step_count:]]
    reduce_sum x1 -> x0, other arithmetic: 4.27 us -> none  [station_part(): jnp.mean(other_vals * other_vals, axis=(2, 3), keepdims=True) + epsilon]
    ppermute x8, waiting for transfers between devices: 30.4 us -> 26.4 us  [halo_pad(): lax.ppermute(lax.slice_in_dim(block, size - width, size, axis=dim), axis,...]
  transfers between devices with their start and end apart: 17 -> 17, of which waited for: 5 -> 6; matrix products, arithmetic and copies ran while one was open for 4% -> 5% of each run, Pallas kernels for 0% -> 0%
where the time goes in v8:
time: 139 us; the launch traced here: 138 us
  starting transfers between devices  60.6 us (44%)
  waiting for transfers between devices  41.1 us (30%)
  local copies, waits for them, and re-layouts  14.9 us (11%)
  Pallas kernels  13.4 us (10%)
  other arithmetic  6.21 us (4%)
  between operations  1.54 us (1%)
    ppermute x8, waiting for transfers between devices, halo_pad(): lax.ppermute(lax.slice_in_dim(block, size - width, size, axis=dim), axis,...  26.4 us
    ppermute x8, starting transfers between devices, halo_pad(): lax.ppermute(lax.slice_in_dim(block, size - width, size, axis=dim), axis,...  25 us
    ppermute x8, starting transfers between devices, halo_pad(): lax.ppermute(lax.slice_in_dim(block, 0, width, axis=dim), axis, backward)  24.9 us
    pallas_call x1, Pallas kernels, pair_sums(): pl.pallas_call(functools.partial(pair_kernel, float(samples)), grid=(slot...  13.4 us
    ppermute x8, waiting for transfers between devices, halo_pad(): lax.ppermute(lax.slice_in_dim(block, 0, width, axis=dim), axis, backward)  13.3 us
    all_to_all x1, starting transfers between devices, station_part(): lax.all_to_all(send, ('gx', 'gy'), split_axis=0, concat_axis=0, tiled=True)  10.8 us
    gather x1, local copies, waits for them, and re-layouts, station_part(): padded_rows[jnp.where(slot_station >= 0, slot_station, stations_here)]  3.54 us
    gather x1, local copies, waits for them, and re-layouts, station_part(): padded_rows[jnp.where(mine_station >= 0, mine_station, stations_here)]  3.53 us
  transfers between devices with their start and end apart: 17, of which 6 were waited for; matrix products, arithmetic and copies ran while one was open for 5% of the time, Pallas kernels for 0%

profile of v8, /device:TPU:14, one launch (start us, length us, event | category | flops | bytes accessed | tf_op | source)
XLA Modules:
  0.0 137.9 jit_solution(13594767816892160517)
XLA Ops:
  4.7 3.5 %gather_fusion.1 = bf16[512,32,128]{2,1,0:T(8,128)(2,1)} fusion(bf16[33,32,128]{2,1,0:T(8,128)(2,1)S(1)} %concatenate.116, s32[1024]{0:T(1024)S(1)} %pad_clamp_fusion), kind=kCustom, calls=%fused_computation.1 | custom fusion | bytes 8390656 | tf_op jit(solution)/shard_map/gather | solution.py:163
  8.3 10.8 %all-to-all-start = ((bf16[128,4,32,128]{3,2,1,0:T(8,128)(2,1)}), bf16[128,4,32,128]{3,2,1,0:T(8,128)(2,1)}, u32[]{:S(2)}, u32[]{:S(2)}) async-start(bf16[128,4,32,128]{3,2,1,0:T(8,128)(2,1)} %bitcast.273), calls=%async_computation | async-start | bytes 8388608 | tf_op jit(solution)/shard_map/all_to_all | solution.py:164
  19.2 2.0 %collective-permute-start.2 = (f32[3,8,2,128]{3,1,2,0:T(8,128)S(1)}, f32[3,8,2,128]{3,1,2,0:T(8,128)S(1)}, u32[]{:S(2)}, u32[]{:S(2)}) collective-permute-start(f32[3,8,2,128]{3,1,2,0:T(8,128)S(1)} %copy.376), channel_id=1, source_target_pairs={{0,1},{1,2},{2,3},{3,4},{4,5},{5,6},{6,7},{8,9},{9,10},{10,11},{11... | collective-permute-start | bytes 73736 | tf_op jit(solution)/shard_map/ppermute | solution.py:37
  21.3 3.5 %collective-permute-start.3 = (f32[3,8,2,128]{3,1,2,0:T(8,128)S(1)}, f32[3,8,2,128]{3,1,2,0:T(8,128)S(1)}, u32[]{:S(2)}, u32[]{:S(2)}) collective-permute-start(f32[3,8,2,128]{3,1,2,0:T(8,128)S(1)} %copy.377), channel_id=1, source_target_pairs={{1,0},{2,1},{3,2},{4,3},{5,4},{6,5},{7,6},{9,8},{10,9},{11,10},{12... | collective-permute-start | bytes 73736 | tf_op jit(solution)/shard_map/ppermute | solution.py:38
  24.8 2.8 %collective-permute-start = (f32[3,2,16,128]{3,2,1,0:T(8,128)S(1)}, f32[3,2,16,128]{3,2,1,0:T(8,128)S(1)}, u32[]{:S(2)}, u32[]{:S(2)}) collective-permute-start(f32[3,2,16,128]{3,2,1,0:T(8,128)S(1)} %get-tuple-element.129), channel_id=1, source_target_pairs={{8,0},{16,8},{24,16},{32,24},{40,32},{48,40},{56,48},{64,56},{72,6... | collective-permute-start | bytes 147464 | tf_op jit(solution)/shard_map/ppermute | solution.py:38
  27.6 5.2 %collective-permute-start.1 = (f32[3,2,16,128]{3,2,1,0:T(8,128)S(1)}, f32[3,2,16,128]{3,2,1,0:T(8,128)S(1)}, u32[]{:S(2)}, u32[]{:S(2)}) collective-permute-start(f32[3,2,16,128]{3,2,1,0:T(8,128)S(1)} %get-tuple-element.130), channel_id=1, source_target_pairs={{0,8},{8,16},{16,24},{24,32},{32,40},{40,48},{48,56},{56,64},{64,7... | collective-permute-start | bytes 147464 | tf_op jit(solution)/shard_map/ppermute | solution.py:37
  34.2 3.5 %gather_fusion = bf16[512,32,128]{2,1,0:T(8,128)(2,1)} fusion(bf16[33,32,128]{2,1,0:T(8,128)(2,1)S(1)} %concatenate.116, s32[1024]{0:T(1024)S(1)} %pad_clamp_fusion.1), kind=kCustom, calls=%fused_computation | custom fusion | bytes 8390656 | tf_op jit(solution)/shard_map/gather | solution.py:166
  37.8 26.4 %collective-permute-done.2 = f32[3,8,2,128]{3,1,2,0:T(8,128)S(1)} collective-permute-done((f32[3,8,2,128]{3,1,2,0:T(8,128)S(1)}, f32[3,8,2,128]{3,1,2,0:T(8,128)S(1)}, u32[]{:S(2)}, u32[]{:S(2)}) %collective-permute-start.2) | collective-permute-done | bytes 24608 | tf_op jit(solution)/shard_map/ppermute | solution.py:37
  64.3 3.5 %collective-permute-done = f32[3,2,16,128]{3,2,1,0:T(8,128)S(1)} collective-permute-done((f32[3,2,16,128]{3,2,1,0:T(8,128)S(1)}, f32[3,2,16,128]{3,2,1,0:T(8,128)S(1)}, u32[]{:S(2)}, u32[]{:S(2)}) %collective-permute-start) | collective-permute-done | bytes 49184 | tf_op jit(solution)/shard_map/ppermute | solution.py:38
  69.7 13.4 %shard_map.146 = f32[32,32,128]{2,1,0:T(8,128)} custom-call(bf16[512,32,128]{2,1,0:T(8,128)(2,1)} %gather_fusion, bf16[512,32,128]{2,1,0:T(8,128)(2,1)} %bitcast.21.other_ref, f32[32,512]{1,0:T(8,128)} %fusion.201.hits_ref), custom_call_target="tpu_custom_call" | custom-call | flops 41943040 | bytes 8388608 | tf_op jit(solution)/shard_map/pallas_call | solution.py:127
  86.4 1.9 %collective-permute-start.6 = (f32[3,8,2,128]{3,1,2,0:T(8,128)S(1)}, f32[3,8,2,128]{3,1,2,0:T(8,128)S(1)}, u32[]{:S(2)}, u32[]{:S(2)}) collective-permute-start(f32[3,8,2,128]{3,1,2,0:T(8,128)S(1)} %copy.390), channel_id=1, source_target_pairs={{0,1},{1,2},{2,3},{3,4},{4,5},{5,6},{6,7},{8,9},{9,10},{10,11},{11... | collective-permute-start | bytes 73736 | tf_op jit(solution)/shard_map/ppermute | solution.py:37
  88.3 3.6 %collective-permute-start.7 = (f32[3,8,2,128]{3,1,2,0:T(8,128)S(1)}, f32[3,8,2,128]{3,1,2,0:T(8,128)S(1)}, u32[]{:S(2)}, u32[]{:S(2)}) collective-permute-start(f32[3,8,2,128]{3,1,2,0:T(8,128)S(1)} %copy.391), channel_id=1, source_target_pairs={{1,0},{2,1},{3,2},{4,3},{5,4},{6,5},{7,6},{9,8},{10,9},{11,10},{12... | collective-permute-start | bytes 73736 | tf_op jit(solution)/shard_map/ppermute | solution.py:38
  92.2 2.7 %collective-permute-start.4 = (f32[3,2,16,128]{3,2,1,0:T(8,128)S(1)}, f32[3,2,16,128]{3,2,1,0:T(8,128)S(1)}, u32[]{:S(2)}, u32[]{:S(2)}) collective-permute-start(f32[3,2,16,128]{3,2,1,0:T(8,128)S(1)} %get-tuple-element.123), channel_id=1, source_target_pairs={{0,8},{8,16},{16,24},{24,32},{32,40},{40,48},{48,56},{56,64},{64,7... | collective-permute-start | bytes 147464 | tf_op jit(solution)/shard_map/ppermute | solution.py:37
  94.8 3.2 %collective-permute-start.5 = (f32[3,2,16,128]{3,2,1,0:T(8,128)S(1)}, f32[3,2,16,128]{3,2,1,0:T(8,128)S(1)}, u32[]{:S(2)}, u32[]{:S(2)}) collective-permute-start(f32[3,2,16,128]{3,2,1,0:T(8,128)S(1)} %get-tuple-element.124), channel_id=1, source_target_pairs={{8,0},{16,8},{24,16},{32,24},{40,32},{48,40},{56,48},{64,56},{72,6... | collective-permute-start | bytes 147464 | tf_op jit(solution)/shard_map/ppermute | solution.py:38
  98.4 4.5 %collective-permute-done.5 = f32[3,2,16,128]{3,2,1,0:T(8,128)S(1)} collective-permute-done((f32[3,2,16,128]{3,2,1,0:T(8,128)S(1)}, f32[3,2,16,128]{3,2,1,0:T(8,128)S(1)}, u32[]{:S(2)}, u32[]{:S(2)}) %collective-permute-start.5) | collective-permute-done | bytes 49184 | tf_op jit(solution)/shard_map/ppermute | solution.py:38
  103.6 1.9 %collective-permute-start.8 = (f32[3,2,16,128]{3,2,1,0:T(8,128)S(1)}, f32[3,2,16,128]{3,2,1,0:T(8,128)S(1)}, u32[]{:S(2)}, u32[]{:S(2)}) collective-permute-start(f32[3,2,16,128]{3,2,1,0:T(8,128)S(1)} %get-tuple-element.116), channel_id=1, source_target_pairs={{8,0},{16,8},{24,16},{32,24},{40,32},{48,40},{56,48},{64,56},{72,6... | collective-permute-start | bytes 147464 | tf_op jit(solution)/shard_map/ppermute | solution.py:38
  105.5 6.0 %collective-permute-start.9 = (f32[3,2,16,128]{3,2,1,0:T(8,128)S(1)}, f32[3,2,16,128]{3,2,1,0:T(8,128)S(1)}, u32[]{:S(2)}, u32[]{:S(2)}) collective-permute-start(f32[3,2,16,128]{3,2,1,0:T(8,128)S(1)} %get-tuple-element.117), channel_id=1, source_target_pairs={{0,8},{8,16},{16,24},{24,32},{32,40},{40,48},{48,56},{56,64},{64,7... | collective-permute-start | bytes 147464 | tf_op jit(solution)/shard_map/ppermute | solution.py:37
  111.6 1.9 %collective-permute-start.10 = (f32[3,8,2,128]{3,1,2,0:T(8,128)S(1)}, f32[3,8,2,128]{3,1,2,0:T(8,128)S(1)}, u32[]{:S(2)}, u32[]{:S(2)}) collective-permute-start(f32[3,8,2,128]{3,1,2,0:T(8,128)S(1)} %copy.394), channel_id=1, source_target_pairs={{0,1},{1,2},{2,3},{3,4},{4,5},{5,6},{6,7},{8,9},{9,10},{10,11},{11... | collective-permute-start | bytes 73736 | tf_op jit(solution)/shard_map/ppermute | solution.py:37
  113.5 3.6 %collective-permute-start.11 = (f32[3,8,2,128]{3,1,2,0:T(8,128)S(1)}, f32[3,8,2,128]{3,1,2,0:T(8,128)S(1)}, u32[]{:S(2)}, u32[]{:S(2)}) collective-permute-start(f32[3,8,2,128]{3,1,2,0:T(8,128)S(1)} %copy.395), channel_id=1, source_target_pairs={{1,0},{2,1},{3,2},{4,3},{5,4},{6,5},{7,6},{9,8},{10,9},{11,10},{12... | collective-permute-start | bytes 73736 | tf_op jit(solution)/shard_map/ppermute | solution.py:38
  119.5 3.3 %collective-permute-start.14 = (f32[3,8,2,128]{3,1,2,0:T(8,128)S(1)}, f32[3,8,2,128]{3,1,2,0:T(8,128)S(1)}, u32[]{:S(2)}, u32[]{:S(2)}) collective-permute-start(f32[3,8,2,128]{3,1,2,0:T(8,128)S(1)} %copy.400), channel_id=1, source_target_pairs={{0,1},{1,2},{2,3},{3,4},{4,5},{5,6},{6,7},{8,9},{9,10},{10,11},{11... | collective-permute-start | bytes 73736 | tf_op jit(solution)/shard_map/ppermute | solution.py:37
  122.9 2.3 %collective-permute-start.15 = (f32[3,8,2,128]{3,1,2,0:T(8,128)S(1)}, f32[3,8,2,128]{3,1,2,0:T(8,128)S(1)}, u32[]{:S(2)}, u32[]{:S(2)}) collective-permute-start(f32[3,8,2,128]{3,1,2,0:T(8,128)S(1)} %copy.401), channel_id=1, source_target_pairs={{1,0},{2,1},{3,2},{4,3},{5,4},{6,5},{7,6},{9,8},{10,9},{11,10},{12... | collective-permute-start | bytes 73736 | tf_op jit(solution)/shard_map/ppermute | solution.py:38
  125.3 1.9 %collective-permute-start.12 = (f32[3,2,16,128]{3,2,1,0:T(8,128)S(1)}, f32[3,2,16,128]{3,2,1,0:T(8,128)S(1)}, u32[]{:S(2)}, u32[]{:S(2)}) collective-permute-start(f32[3,2,16,128]{3,2,1,0:T(8,128)S(1)} %get-tuple-element.111), channel_id=1, source_target_pairs={{0,8},{8,16},{16,24},{24,32},{32,40},{40,48},{48,56},{56,64},{64,7... | collective-permute-start | bytes 147464 | tf_op jit(solution)/shard_map/ppermute | solution.py:37
  127.2 3.9 %collective-permute-start.13 = (f32[3,2,16,128]{3,2,1,0:T(8,128)S(1)}, f32[3,2,16,128]{3,2,1,0:T(8,128)S(1)}, u32[]{:S(2)}, u32[]{:S(2)}) collective-permute-start(f32[3,2,16,128]{3,2,1,0:T(8,128)S(1)} %get-tuple-element.110), channel_id=1, source_target_pairs={{8,0},{16,8},{24,16},{32,24},{40,32},{48,40},{56,48},{64,56},{72,6... | collective-permute-start | bytes 147464 | tf_op jit(solution)/shard_map/ppermute | solution.py:38
  131.3 4.0 %collective-permute-done.13 = f32[3,2,16,128]{3,2,1,0:T(8,128)S(1)} collective-permute-done((f32[3,2,16,128]{3,2,1,0:T(8,128)S(1)}, f32[3,2,16,128]{3,2,1,0:T(8,128)S(1)}, u32[]{:S(2)}, u32[]{:S(2)}) %collective-permute-start.13) | collective-permute-done | bytes 49184 | tf_op jit(solution)/shard_map/ppermute | solution.py:38
  (146 shorter events, 16.8 us)
Async XLA Ops:
  8.3 25.8 %copy-start.8 = (f32[8,16,128]{2,1,0:T(8,128)S(1)}, f32[8,16,128]{2,1,0:T(8,128)}, u32[]{:S(2)}) copy-start(f32[8,16,128]{2,1,0:T(8,128)} %param.19) | copy-start | bytes 196612
  8.3 25.8 %copy-start.4 = (bf16[12,8,16,128]{3,2,1,0:T(8,128)(2,1)S(1)}, bf16[12,8,16,128]{3,2,1,0:T(8,128)(2,1)}, u32[]{:S(2)}) copy-start(bf16[12,8,16,128]{3,2,1,0:T(8,128)(2,1)} %param.20) | copy-start | bytes 1179652
  8.3 61.4 %all-to-all-start = ((bf16[128,4,32,128]{3,2,1,0:T(8,128)(2,1)}), bf16[128,4,32,128]{3,2,1,0:T(8,128)(2,1)}, u32[]{:S(2)}, u32[]{:S(2)}) async-start(bf16[128,4,32,128]{3,2,1,0:T(8,128)(2,1)} %bitcast.273), calls=%async_computation | async-start | bytes 8388608 | tf_op jit(solution)/shard_map/all_to_all | solution.py:164
  19.2 44.9 %collective-permute-start.2 = (f32[3,8,2,128]{3,1,2,0:T(8,128)S(1)}, f32[3,8,2,128]{3,1,2,0:T(8,128)S(1)}, u32[]{:S(2)}, u32[]{:S(2)}) collective-permute-start(f32[3,8,2,128]{3,1,2,0:T(8,128)S(1)} %copy.376), channel_id=1, source_target_pairs={{0,1},{1,2},{2,3},{3,4},{4,5},{5,6},{6,7},{8,9},{9,10},{10,11},{11... | collective-permute-start | bytes 73736 | tf_op jit(solution)/shard_map/ppermute | solution.py:37
  21.3 42.9 %collective-permute-start.3 = (f32[3,8,2,128]{3,1,2,0:T(8,128)S(1)}, f32[3,8,2,128]{3,1,2,0:T(8,128)S(1)}, u32[]{:S(2)}, u32[]{:S(2)}) collective-permute-start(f32[3,8,2,128]{3,1,2,0:T(8,128)S(1)} %copy.377), channel_id=1, source_target_pairs={{1,0},{2,1},{3,2},{4,3},{5,4},{6,5},{7,6},{9,8},{10,9},{11,10},{12... | collective-permute-start | bytes 73736 | tf_op jit(solution)/shard_map/ppermute | solution.py:38
  24.8 42.9 %collective-permute-start = (f32[3,2,16,128]{3,2,1,0:T(8,128)S(1)}, f32[3,2,16,128]{3,2,1,0:T(8,128)S(1)}, u32[]{:S(2)}, u32[]{:S(2)}) collective-permute-start(f32[3,2,16,128]{3,2,1,0:T(8,128)S(1)} %get-tuple-element.129), channel_id=1, source_target_pairs={{8,0},{16,8},{24,16},{32,24},{40,32},{48,40},{56,48},{64,56},{72,6... | collective-permute-start | bytes 147464 | tf_op jit(solution)/shard_map/ppermute | solution.py:38
  27.6 40.2 %collective-permute-start.1 = (f32[3,2,16,128]{3,2,1,0:T(8,128)S(1)}, f32[3,2,16,128]{3,2,1,0:T(8,128)S(1)}, u32[]{:S(2)}, u32[]{:S(2)}) collective-permute-start(f32[3,2,16,128]{3,2,1,0:T(8,128)S(1)} %get-tuple-element.130), channel_id=1, source_target_pairs={{0,8},{8,16},{16,24},{24,32},{32,40},{40,48},{48,56},{56,64},{64,7... | collective-permute-start | bytes 147464 | tf_op jit(solution)/shard_map/ppermute | solution.py:37
  83.1 19.9 %copy-start = (f32[8,16,128]{2,1,0:T(8,128)S(1)}, f32[8,16,128]{2,1,0:T(8,128)}, u32[]{:S(2)}) copy-start(f32[8,16,128]{2,1,0:T(8,128)} %param.18) | copy-start | bytes 196612
  83.1 19.9 %copy-start.5 = (f32[8,16,128]{2,1,0:T(8,128)S(1)}, f32[8,16,128]{2,1,0:T(8,128)}, u32[]{:S(2)}) copy-start(f32[8,16,128]{2,1,0:T(8,128)} %param.17) | copy-start | bytes 196612
  86.4 11.8 %collective-permute-start.6 = (f32[3,8,2,128]{3,1,2,0:T(8,128)S(1)}, f32[3,8,2,128]{3,1,2,0:T(8,128)S(1)}, u32[]{:S(2)}, u32[]{:S(2)}) collective-permute-start(f32[3,8,2,128]{3,1,2,0:T(8,128)S(1)} %copy.390), channel_id=1, source_target_pairs={{0,1},{1,2},{2,3},{3,4},{4,5},{5,6},{6,7},{8,9},{9,10},{10,11},{11... | collective-permute-start | bytes 73736 | tf_op jit(solution)/shard_map/ppermute | solution.py:37
  88.3 9.9 %collective-permute-start.7 = (f32[3,8,2,128]{3,1,2,0:T(8,128)S(1)}, f32[3,8,2,128]{3,1,2,0:T(8,128)S(1)}, u32[]{:S(2)}, u32[]{:S(2)}) collective-permute-start(f32[3,8,2,128]{3,1,2,0:T(8,128)S(1)} %copy.391), channel_id=1, source_target_pairs={{1,0},{2,1},{3,2},{4,3},{5,4},{6,5},{7,6},{9,8},{10,9},{11,10},{12... | collective-permute-start | bytes 73736 | tf_op jit(solution)/shard_map/ppermute | solution.py:38
  92.2 6.2 %collective-permute-start.4 = (f32[3,2,16,128]{3,2,1,0:T(8,128)S(1)}, f32[3,2,16,128]{3,2,1,0:T(8,128)S(1)}, u32[]{:S(2)}, u32[]{:S(2)}) collective-permute-start(f32[3,2,16,128]{3,2,1,0:T(8,128)S(1)} %get-tuple-element.123), channel_id=1, source_target_pairs={{0,8},{8,16},{16,24},{24,32},{32,40},{40,48},{48,56},{56,64},{64,7... | collective-permute-start | bytes 147464 | tf_op jit(solution)/shard_map/ppermute | solution.py:37
  94.8 8.1 %collective-permute-start.5 = (f32[3,2,16,128]{3,2,1,0:T(8,128)S(1)}, f32[3,2,16,128]{3,2,1,0:T(8,128)S(1)}, u32[]{:S(2)}, u32[]{:S(2)}) collective-permute-start(f32[3,2,16,128]{3,2,1,0:T(8,128)S(1)} %get-tuple-element.124), channel_id=1, source_target_pairs={{8,0},{16,8},{24,16},{32,24},{40,32},{48,40},{56,48},{64,56},{72,6... | collective-permute-start | bytes 147464 | tf_op jit(solution)/shard_map/ppermute | solution.py:38
  103.6 15.2 %collective-permute-start.8 = (f32[3,2,16,128]{3,2,1,0:T(8,128)S(1)}, f32[3,2,16,128]{3,2,1,0:T(8,128)S(1)}, u32[]{:S(2)}, u32[]{:S(2)}) collective-permute-start(f32[3,2,16,128]{3,2,1,0:T(8,128)S(1)} %get-tuple-element.116), channel_id=1, source_target_pairs={{8,0},{16,8},{24,16},{32,24},{40,32},{48,40},{56,48},{64,56},{72,6... | collective-permute-start | bytes 147464 | tf_op jit(solution)/shard_map/ppermute | solution.py:38
  105.5 13.3 %collective-permute-start.9 = (f32[3,2,16,128]{3,2,1,0:T(8,128)S(1)}, f32[3,2,16,128]{3,2,1,0:T(8,128)S(1)}, u32[]{:S(2)}, u32[]{:S(2)}) collective-permute-start(f32[3,2,16,128]{3,2,1,0:T(8,128)S(1)} %get-tuple-element.117), channel_id=1, source_target_pairs={{0,8},{8,16},{16,24},{24,32},{32,40},{40,48},{48,56},{56,64},{64,7... | collective-permute-start | bytes 147464 | tf_op jit(solution)/shard_map/ppermute | solution.py:37
  111.6 5.8 %collective-permute-start.10 = (f32[3,8,2,128]{3,1,2,0:T(8,128)S(1)}, f32[3,8,2,128]{3,1,2,0:T(8,128)S(1)}, u32[]{:S(2)}, u32[]{:S(2)}) collective-permute-start(f32[3,8,2,128]{3,1,2,0:T(8,128)S(1)} %copy.394), channel_id=1, source_target_pairs={{0,1},{1,2},{2,3},{3,4},{4,5},{5,6},{6,7},{8,9},{9,10},{10,11},{11... | collective-permute-start | bytes 73736 | tf_op jit(solution)/shard_map/ppermute | solution.py:37
  113.5 5.1 %collective-permute-start.11 = (f32[3,8,2,128]{3,1,2,0:T(8,128)S(1)}, f32[3,8,2,128]{3,1,2,0:T(8,128)S(1)}, u32[]{:S(2)}, u32[]{:S(2)}) collective-permute-start(f32[3,8,2,128]{3,1,2,0:T(8,128)S(1)} %copy.395), channel_id=1, source_target_pairs={{1,0},{2,1},{3,2},{4,3},{5,4},{6,5},{7,6},{9,8},{10,9},{11,10},{12... | collective-permute-start | bytes 73736 | tf_op jit(solution)/shard_map/ppermute | solution.py:38
  117.4 17.9 %copy-start.6 = (f32[8,16,128]{2,1,0:T(8,128)S(1)}, f32[8,16,128]{2,1,0:T(8,128)}, u32[]{:S(2)}) copy-start(f32[8,16,128]{2,1,0:T(8,128)} %param.22) | copy-start | bytes 196612
  119.1 17.2 %copy-start.7 = (f32[8,16,128]{2,1,0:T(8,128)S(1)}, f32[8,16,128]{2,1,0:T(8,128)}, u32[]{:S(2)}) copy-start(f32[8,16,128]{2,1,0:T(8,128)} %param.21) | copy-start | bytes 196612
  119.5 17.6 %copy-start.1 = (f32[3,8,16,128]{3,2,1,0:T(8,128)}, f32[3,8,16,128]{3,2,1,0:T(8,128)S(1)}, u32[]{:S(2)}) copy-start(f32[3,8,16,128]{3,2,1,0:T(8,128)S(1)} %fusion.2) | copy-start | bytes 589828
  119.5 11.6 %collective-permute-start.14 = (f32[3,8,2,128]{3,1,2,0:T(8,128)S(1)}, f32[3,8,2,128]{3,1,2,0:T(8,128)S(1)}, u32[]{:S(2)}, u32[]{:S(2)}) collective-permute-start(f32[3,8,2,128]{3,1,2,0:T(8,128)S(1)} %copy.400), channel_id=1, source_target_pairs={{0,1},{1,2},{2,3},{3,4},{4,5},{5,6},{6,7},{8,9},{9,10},{10,11},{11... | collective-permute-start | bytes 73736 | tf_op jit(solution)/shard_map/ppermute | solution.py:37
  122.9 8.3 %collective-permute-start.15 = (f32[3,8,2,128]{3,1,2,0:T(8,128)S(1)}, f32[3,8,2,128]{3,1,2,0:T(8,128)S(1)}, u32[]{:S(2)}, u32[]{:S(2)}) collective-permute-start(f32[3,8,2,128]{3,1,2,0:T(8,128)S(1)} %copy.401), channel_id=1, source_target_pairs={{1,0},{2,1},{3,2},{4,3},{5,4},{6,5},{7,6},{9,8},{10,9},{11,10},{12... | collective-permute-start | bytes 73736 | tf_op jit(solution)/shard_map/ppermute | solution.py:38
  125.3 6.0 %collective-permute-start.12 = (f32[3,2,16,128]{3,2,1,0:T(8,128)S(1)}, f32[3,2,16,128]{3,2,1,0:T(8,128)S(1)}, u32[]{:S(2)}, u32[]{:S(2)}) collective-permute-start(f32[3,2,16,128]{3,2,1,0:T(8,128)S(1)} %get-tuple-element.111), channel_id=1, source_target_pairs={{0,8},{8,16},{16,24},{24,32},{32,40},{40,48},{48,56},{56,64},{64,7... | collective-permute-start | bytes 147464 | tf_op jit(solution)/shard_map/ppermute | solution.py:37
  127.2 8.1 %collective-permute-start.13 = (f32[3,2,16,128]{3,2,1,0:T(8,128)S(1)}, f32[3,2,16,128]{3,2,1,0:T(8,128)S(1)}, u32[]{:S(2)}, u32[]{:S(2)}) collective-permute-start(f32[3,2,16,128]{3,2,1,0:T(8,128)S(1)} %get-tuple-element.110), channel_id=1, source_target_pairs={{8,0},{16,8},{24,16},{32,24},{40,32},{48,40},{56,48},{64,56},{72,6... | collective-permute-start | bytes 147464 | tf_op jit(solution)/shard_map/ppermute | solution.py:38
  (3 other events, 40.0 us)

commit v9 on v6

--- a/solution.py
+++ b/solution.py
@@ -44,20 +44,24 @@
     return jnp.pad(block, pads)
 
 
+def exchange(block):
+    wide_x = halo_pad(block[0], "gx", 1)
+    wide_y = halo_pad(block[1], "gy", 2)
+    return wide_x, wide_y
+
+
 def advance(velocity, stress, lame_first, shear_modulus, buoyancy, strain_now, surface, lame_kernel, shear_kernel):
     nx = velocity.shape[1]
     ny = velocity.shape[2]
     nz = velocity.shape[3]
-    sx = halo_pad(jnp.stack([stress[0], stress[3], stress[4]]), "gx", 1)
-    sy = halo_pad(jnp.stack([stress[3], stress[1], stress[5]]), "gy", 2)
+    sx, sy = exchange((jnp.stack([stress[0], stress[3], stress[4]]), jnp.stack([stress[3], stress[1], stress[5]])))
     sz = z_pad(jnp.stack([stress[4], stress[5], stress[2]]))
     force_first = forward_diff(sx[0], nx, 0) + backward_diff(sy[0], ny, 1) + backward_diff(sz[0], nz, 2)
     force_second = backward_diff(sx[1], nx, 0) + forward_diff(sy[1], ny, 1) + backward_diff(sz[1], nz, 2)
     force_third = backward_diff(sx[2], nx, 0) + backward_diff(sy[2], ny, 1) + forward_diff(sz[2], nz, 2)
     force_third = force_third.at[:, :, 0].add(surface)
     moved = velocity + time_step * buoyancy[None] * jnp.stack([force_first, force_second, force_third])
-    mx = halo_pad(moved, "gx", 1)
-    my = halo_pad(moved, "gy", 2)
+    mx, my = exchange((moved, moved))
     mz = z_pad(moved)
     rate_first = backward_diff(mx[0], nx, 0)
     rate_second = backward_diff(my[1], ny, 1)
@@ -89,13 +93,18 @@
     return (moved, grown, lame_kernel, shear_kernel)
 
 
-def pair_kernel(block, samples, station_ref, mine_ref, other_ref, out_ref, acc_ref, toward_ref):
+def pair_kernel(block, samples, station_ref, table_ref, other_ref, out_ref, acc_ref, toward_ref, mine_ref):
     step = pl.program_id(0)
 
     @pl.when(step == 0)
     def _():
         acc_ref[...] = jnp.zeros_like(acc_ref)
 
+    def pick(i, carry):
+        mine_ref[i] = table_ref[station_ref[step * block + i]]
+        return carry
+
+    lax.fori_loop(0, block, pick, 0)
     mine_vals = mine_ref[...].astype(jnp.float32)
     other_vals = other_ref[...].astype(jnp.float32)
     mine_sq = jnp.sum(jnp.sum(mine_vals * mine_vals, axis=1, keepdims=True), axis=2, keepdims=True)
@@ -104,7 +113,9 @@
     mine_norm = jnp.sqrt(mine_sq / samples + epsilon)
     other_norm = jnp.sqrt(other_sq / samples + epsilon)
     corr = (cross / samples) / (mine_norm * other_norm)
-    toward = other_vals / other_norm - corr * (mine_vals / mine_norm)
+    other_scale = 1.0 / other_norm
+    mine_scale = corr / mine_norm
+    toward = other_vals * other_scale - mine_scale * mine_vals
     toward_ref[...] = toward.astype(jnp.bfloat16).astype(jnp.float32)
 
     ways = acc_ref.shape[0]
@@ -127,8 +138,8 @@
         out_ref[...] = total
 
 
-def pair_sums(targets, mine, other, stations):
-    slots, rows, lanes = mine.shape
+def pair_sums(targets, table, other, stations):
+    slots, rows, lanes = other.shape
     block = 64
     samples = rows * lanes
     spec = pl.BlockSpec((block, rows, lanes), lambda g, t: (g, 0, 0))
@@ -137,17 +148,18 @@
         grid_spec=pltpu.PrefetchScalarGridSpec(
             num_scalar_prefetch=1,
             grid=(slots // block,),
-            in_specs=[spec, spec],
+            in_specs=[pl.BlockSpec(table.shape, lambda g, t: (0, 0, 0)), spec],
             out_specs=pl.BlockSpec((stations, rows, lanes), lambda g, t: (0, 0, 0)),
             scratch_shapes=[
                 pltpu.VMEM((4, stations + 1, rows, lanes), jnp.float32),
                 pltpu.VMEM((block, rows, lanes), jnp.float32),
+                pltpu.VMEM((block, rows, lanes), table.dtype),
             ],
         ),
         out_shape=jax.ShapeDtypeStruct((stations, rows, lanes), jnp.float32),
         compiler_params=pltpu.CompilerParams(dimension_semantics=("arbitrary",)),
-        cost_estimate=pl.CostEstimate(flops=20 * slots * samples, transcendentals=0, bytes_accessed=4 * slots * samples),
-    )(targets, mine, other)
+        cost_estimate=pl.CostEstimate(flops=20 * slots * samples, transcendentals=0, bytes_accessed=2 * slots * samples),
+    )(targets, table, other)
 
 
 def station_part(residuals, station_cell, station_pairs, cells_first, cells_second, step_count):
@@ -177,11 +189,10 @@
     send = padded_rows[jnp.where(slot_station >= 0, slot_station, stations_here)]
     recv = lax.all_to_all(send, ("gx", "gy"), split_axis=0, concat_axis=0, tiled=True)
     mine_station = jnp.concatenate([slot_station[:, 2:4], slot_station[:, 0:2]], axis=1)
-    mine = padded_rows[jnp.where(mine_station >= 0, mine_station, stations_here)]
     slots = devices * 4
     targets = jnp.where(mine_station >= 0, mine_station, stations_here).reshape(slots)
     adjoint3 = pair_sums(
-        targets, mine.reshape(slots, samples // lanes, lanes), recv.reshape(slots, samples // lanes, lanes), stations_here
+        targets, padded_rows, recv.reshape(slots, samples // lanes, lanes), stations_here
     )
     adjoint = adjoint3.reshape(stations_here, samples)
     last = adjoint3[:, samples // lanes - 1, lanes - step_count :]

time: 136 us -> 139 us (1.022)
  local copies, waits for them, and re-layouts: 15.4 us -> 11.6 us
  waiting for transfers between devices: 39.1 us -> 42.8 us
  Pallas kernels: 12.2 us -> 15 us
    ppermute x8, waiting for transfers between devices: 26.5 us -> 30.2 us  [halo_pad(): lax.ppermute(lax.slice_in_dim(block, size - width, size, axis=dim), axis,...]
    gather x1 -> x0, local copies, waits for them, and re-layouts: 3.53 us -> none  [station_part(): padded_rows[jnp.where(mine_station >= 0, mine_station, stations_here)]]
    pallas_call x1, Pallas kernels: 12.2 us -> 15 us  [pair_sums(): pl.pallas_call(functools.partial(pair_kernel, block, float(samples)), gri...]
    unnamed x24 -> x26, local copies, waits for them, and re-layouts: 4.19 us -> 4.2 us
  transfers between devices with their start and end apart: 17 -> 17, of which waited for: 6 -> 6; matrix products, arithmetic and copies ran while one was open for 6% -> 4% of each run, Pallas kernels for 0% -> 0%
where the time goes in v9:
time: 139 us; the launch traced here: 138 us
  starting transfers between devices  60.7 us (44%)
  waiting for transfers between devices  42.8 us (31%)
  Pallas kernels  15 us (11%)
  local copies, waits for them, and re-layouts  11.6 us (8%)
  other arithmetic  6.09 us (4%)
  between operations  1.59 us (1%)
    ppermute x8, waiting for transfers between devices, halo_pad(): lax.ppermute(lax.slice_in_dim(block, size - width, size, axis=dim), axis,...  30.2 us
    ppermute x8, starting transfers between devices, halo_pad(): lax.ppermute(lax.slice_in_dim(block, size - width, size, axis=dim), axis,...  25 us
    ppermute x8, starting transfers between devices, halo_pad(): lax.ppermute(lax.slice_in_dim(block, 0, width, axis=dim), axis, backward)  24.9 us
    pallas_call x1, Pallas kernels, pair_sums(): pl.pallas_call(functools.partial(pair_kernel, block, float(samples)), gri...  15 us
    ppermute x8, waiting for transfers between devices, halo_pad(): lax.ppermute(lax.slice_in_dim(block, 0, width, axis=dim), axis, backward)  11.2 us
    all_to_all x1, starting transfers between devices, station_part(): lax.all_to_all(send, ('gx', 'gy'), split_axis=0, concat_axis=0, tiled=True)  10.8 us
    unnamed x26, local copies, waits for them, and re-layouts  4.2 us
    gather x1, local copies, waits for them, and re-layouts, station_part(): padded_rows[jnp.where(slot_station >= 0, slot_station, stations_here)]  3.53 us
  transfers between devices with their start and end apart: 17, of which 6 were waited for; matrix products, arithmetic and copies ran while one was open for 4% of the time, Pallas kernels for 0%

profile of v9, /device:TPU:14, one launch (start us, length us, event | category | flops | bytes accessed | tf_op | source)
XLA Modules:
  0.0 137.8 jit_solution(16074860881469901580)
XLA Ops:
  4.8 3.5 %gather_fusion = bf16[512,32,128]{2,1,0:T(8,128)(2,1)} fusion(bf16[33,32,128]{2,1,0:T(8,128)(2,1)S(1)} %concatenate.105.table_ref, s32[1024]{0:T(1024)S(1)} %pad_clamp_fusion), kind=kCustom, calls=%fused_computation | custom fusion | bytes 8390656 | tf_op jit(solution)/shard_map/gather | solution.py:189
  8.3 10.8 %all-to-all-start = ((bf16[128,4,32,128]{3,2,1,0:T(8,128)(2,1)}), bf16[128,4,32,128]{3,2,1,0:T(8,128)(2,1)}, u32[]{:S(2)}, u32[]{:S(2)}) async-start(bf16[128,4,32,128]{3,2,1,0:T(8,128)(2,1)} %bitcast.269), calls=%async_computation | async-start | bytes 8388608 | tf_op jit(solution)/shard_map/all_to_all | solution.py:190
  19.2 2.0 %collective-permute-start.2 = (f32[3,8,2,128]{3,1,2,0:T(8,128)S(1)}, f32[3,8,2,128]{3,1,2,0:T(8,128)S(1)}, u32[]{:S(2)}, u32[]{:S(2)}) collective-permute-start(f32[3,8,2,128]{3,1,2,0:T(8,128)S(1)} %copy.369), channel_id=1, source_target_pairs={{0,1},{1,2},{2,3},{3,4},{4,5},{5,6},{6,7},{8,9},{9,10},{10,11},{11... | collective-permute-start | bytes 73736 | tf_op jit(solution)/shard_map/ppermute | solution.py:37
  21.3 3.5 %collective-permute-start.3 = (f32[3,8,2,128]{3,1,2,0:T(8,128)S(1)}, f32[3,8,2,128]{3,1,2,0:T(8,128)S(1)}, u32[]{:S(2)}, u32[]{:S(2)}) collective-permute-start(f32[3,8,2,128]{3,1,2,0:T(8,128)S(1)} %copy.370), channel_id=1, source_target_pairs={{1,0},{2,1},{3,2},{4,3},{5,4},{6,5},{7,6},{9,8},{10,9},{11,10},{12... | collective-permute-start | bytes 73736 | tf_op jit(solution)/shard_map/ppermute | solution.py:38
  24.9 2.8 %collective-permute-start = (f32[3,2,16,128]{3,2,1,0:T(8,128)S(1)}, f32[3,2,16,128]{3,2,1,0:T(8,128)S(1)}, u32[]{:S(2)}, u32[]{:S(2)}) collective-permute-start(f32[3,2,16,128]{3,2,1,0:T(8,128)S(1)} %get-tuple-element.129), channel_id=1, source_target_pairs={{8,0},{16,8},{24,16},{32,24},{40,32},{48,40},{56,48},{64,56},{72,6... | collective-permute-start | bytes 147464 | tf_op jit(solution)/shard_map/ppermute | solution.py:38
  27.6 5.2 %collective-permute-start.1 = (f32[3,2,16,128]{3,2,1,0:T(8,128)S(1)}, f32[3,2,16,128]{3,2,1,0:T(8,128)S(1)}, u32[]{:S(2)}, u32[]{:S(2)}) collective-permute-start(f32[3,2,16,128]{3,2,1,0:T(8,128)S(1)} %get-tuple-element.130), channel_id=1, source_target_pairs={{0,8},{8,16},{16,24},{24,32},{32,40},{40,48},{48,56},{56,64},{64,7... | collective-permute-start | bytes 147464 | tf_op jit(solution)/shard_map/ppermute | solution.py:37
  34.0 30.2 %collective-permute-done.2 = f32[3,8,2,128]{3,1,2,0:T(8,128)S(1)} collective-permute-done((f32[3,8,2,128]{3,1,2,0:T(8,128)S(1)}, f32[3,8,2,128]{3,1,2,0:T(8,128)S(1)}, u32[]{:S(2)}, u32[]{:S(2)}) %collective-permute-start.2) | collective-permute-done | bytes 24608 | tf_op jit(solution)/shard_map/ppermute | solution.py:37
  64.3 3.5 %collective-permute-done = f32[3,2,16,128]{3,2,1,0:T(8,128)S(1)} collective-permute-done((f32[3,2,16,128]{3,2,1,0:T(8,128)S(1)}, f32[3,2,16,128]{3,2,1,0:T(8,128)S(1)}, u32[]{:S(2)}, u32[]{:S(2)}) %collective-permute-start) | collective-permute-done | bytes 49184 | tf_op jit(solution)/shard_map/ppermute | solution.py:38
  69.7 15.0 %shard_map.146 = f32[32,32,128]{2,1,0:T(8,128)} custom-call(s32[512]{0:T(512)} %compare_select_fusion.2.station_ref, bf16[33,32,128]{2,1,0:T(8,128)(2,1)} %copy-done, bf16[512,32,128]{2,1,0:T(8,128)(2,1)} %bitcast.21.other_ref), custom_call_target="tpu_custom_call" | custom-call | flops 41943040 | bytes 4194304 | tf_op jit(solution)/shard_map/pallas_call | solution.py:146
  86.4 1.9 %collective-permute-start.6 = (f32[3,8,2,128]{3,1,2,0:T(8,128)S(1)}, f32[3,8,2,128]{3,1,2,0:T(8,128)S(1)}, u32[]{:S(2)}, u32[]{:S(2)}) collective-permute-start(f32[3,8,2,128]{3,1,2,0:T(8,128)S(1)} %copy.382), channel_id=1, source_target_pairs={{0,1},{1,2},{2,3},{3,4},{4,5},{5,6},{6,7},{8,9},{9,10},{10,11},{11... | collective-permute-start | bytes 73736 | tf_op jit(solution)/shard_map/ppermute | solution.py:37
  88.3 3.6 %collective-permute-start.7 = (f32[3,8,2,128]{3,1,2,0:T(8,128)S(1)}, f32[3,8,2,128]{3,1,2,0:T(8,128)S(1)}, u32[]{:S(2)}, u32[]{:S(2)}) collective-permute-start(f32[3,8,2,128]{3,1,2,0:T(8,128)S(1)} %copy.383), channel_id=1, source_target_pairs={{1,0},{2,1},{3,2},{4,3},{5,4},{6,5},{7,6},{9,8},{10,9},{11,10},{12... | collective-permute-start | bytes 73736 | tf_op jit(solution)/shard_map/ppermute | solution.py:38
  92.1 2.7 %collective-permute-start.4 = (f32[3,2,16,128]{3,2,1,0:T(8,128)S(1)}, f32[3,2,16,128]{3,2,1,0:T(8,128)S(1)}, u32[]{:S(2)}, u32[]{:S(2)}) collective-permute-start(f32[3,2,16,128]{3,2,1,0:T(8,128)S(1)} %get-tuple-element.123), channel_id=1, source_target_pairs={{0,8},{8,16},{16,24},{24,32},{32,40},{40,48},{48,56},{56,64},{64,7... | collective-permute-start | bytes 147464 | tf_op jit(solution)/shard_map/ppermute | solution.py:37
  94.8 3.2 %collective-permute-start.5 = (f32[3,2,16,128]{3,2,1,0:T(8,128)S(1)}, f32[3,2,16,128]{3,2,1,0:T(8,128)S(1)}, u32[]{:S(2)}, u32[]{:S(2)}) collective-permute-start(f32[3,2,16,128]{3,2,1,0:T(8,128)S(1)} %get-tuple-element.124), channel_id=1, source_target_pairs={{8,0},{16,8},{24,16},{32,24},{40,32},{48,40},{56,48},{64,56},{72,6... | collective-permute-start | bytes 147464 | tf_op jit(solution)/shard_map/ppermute | solution.py:38
  98.2 2.1 %copy.402 = f32[4,8,32,128]{3,1,2,0:T(8,128)} copy(f32[4,8,32,128]{3,2,1,0:T(8,128)} %bitcast.270) | data formatting | bytes 1048576
  100.5 2.4 %collective-permute-done.5 = f32[3,2,16,128]{3,2,1,0:T(8,128)S(1)} collective-permute-done((f32[3,2,16,128]{3,2,1,0:T(8,128)S(1)}, f32[3,2,16,128]{3,2,1,0:T(8,128)S(1)}, u32[]{:S(2)}, u32[]{:S(2)}) %collective-permute-start.5) | collective-permute-done | bytes 49184 | tf_op jit(solution)/shard_map/ppermute | solution.py:38
  103.5 1.9 %collective-permute-start.8 = (f32[3,2,16,128]{3,2,1,0:T(8,128)S(1)}, f32[3,2,16,128]{3,2,1,0:T(8,128)S(1)}, u32[]{:S(2)}, u32[]{:S(2)}) collective-permute-start(f32[3,2,16,128]{3,2,1,0:T(8,128)S(1)} %get-tuple-element.116), channel_id=1, source_target_pairs={{8,0},{16,8},{24,16},{32,24},{40,32},{48,40},{56,48},{64,56},{72,6... | collective-permute-start | bytes 147464 | tf_op jit(solution)/shard_map/ppermute | solution.py:38
  105.5 6.0 %collective-permute-start.9 = (f32[3,2,16,128]{3,2,1,0:T(8,128)S(1)}, f32[3,2,16,128]{3,2,1,0:T(8,128)S(1)}, u32[]{:S(2)}, u32[]{:S(2)}) collective-permute-start(f32[3,2,16,128]{3,2,1,0:T(8,128)S(1)} %get-tuple-element.117), channel_id=1, source_target_pairs={{0,8},{8,16},{16,24},{24,32},{32,40},{40,48},{48,56},{56,64},{64,7... | collective-permute-start | bytes 147464 | tf_op jit(solution)/shard_map/ppermute | solution.py:37
  111.5 1.9 %collective-permute-start.10 = (f32[3,8,2,128]{3,1,2,0:T(8,128)S(1)}, f32[3,8,2,128]{3,1,2,0:T(8,128)S(1)}, u32[]{:S(2)}, u32[]{:S(2)}) collective-permute-start(f32[3,8,2,128]{3,1,2,0:T(8,128)S(1)} %copy.386), channel_id=1, source_target_pairs={{0,1},{1,2},{2,3},{3,4},{4,5},{5,6},{6,7},{8,9},{9,10},{10,11},{11... | collective-permute-start | bytes 73736 | tf_op jit(solution)/shard_map/ppermute | solution.py:37
  113.5 3.6 %collective-permute-start.11 = (f32[3,8,2,128]{3,1,2,0:T(8,128)S(1)}, f32[3,8,2,128]{3,1,2,0:T(8,128)S(1)}, u32[]{:S(2)}, u32[]{:S(2)}) collective-permute-start(f32[3,8,2,128]{3,1,2,0:T(8,128)S(1)} %copy.387), channel_id=1, source_target_pairs={{1,0},{2,1},{3,2},{4,3},{5,4},{6,5},{7,6},{9,8},{10,9},{11,10},{12... | collective-permute-start | bytes 73736 | tf_op jit(solution)/shard_map/ppermute | solution.py:38
  119.5 3.3 %collective-permute-start.14 = (f32[3,8,2,128]{3,1,2,0:T(8,128)S(1)}, f32[3,8,2,128]{3,1,2,0:T(8,128)S(1)}, u32[]{:S(2)}, u32[]{:S(2)}) collective-permute-start(f32[3,8,2,128]{3,1,2,0:T(8,128)S(1)} %copy.392), channel_id=1, source_target_pairs={{0,1},{1,2},{2,3},{3,4},{4,5},{5,6},{6,7},{8,9},{9,10},{10,11},{11... | collective-permute-start | bytes 73736 | tf_op jit(solution)/shard_map/ppermute | solution.py:37
  122.8 2.3 %collective-permute-start.15 = (f32[3,8,2,128]{3,1,2,0:T(8,128)S(1)}, f32[3,8,2,128]{3,1,2,0:T(8,128)S(1)}, u32[]{:S(2)}, u32[]{:S(2)}) collective-permute-start(f32[3,8,2,128]{3,1,2,0:T(8,128)S(1)} %copy.393), channel_id=1, source_target_pairs={{1,0},{2,1},{3,2},{4,3},{5,4},{6,5},{7,6},{9,8},{10,9},{11,10},{12... | collective-permute-start | bytes 73736 | tf_op jit(solution)/shard_map/ppermute | solution.py:38
  125.2 1.9 %collective-permute-start.12 = (f32[3,2,16,128]{3,2,1,0:T(8,128)S(1)}, f32[3,2,16,128]{3,2,1,0:T(8,128)S(1)}, u32[]{:S(2)}, u32[]{:S(2)}) collective-permute-start(f32[3,2,16,128]{3,2,1,0:T(8,128)S(1)} %get-tuple-element.111), channel_id=1, source_target_pairs={{0,8},{8,16},{16,24},{24,32},{32,40},{40,48},{48,56},{56,64},{64,7... | collective-permute-start | bytes 147464 | tf_op jit(solution)/shard_map/ppermute | solution.py:37
  127.2 3.9 %collective-permute-start.13 = (f32[3,2,16,128]{3,2,1,0:T(8,128)S(1)}, f32[3,2,16,128]{3,2,1,0:T(8,128)S(1)}, u32[]{:S(2)}, u32[]{:S(2)}) collective-permute-start(f32[3,2,16,128]{3,2,1,0:T(8,128)S(1)} %get-tuple-element.110), channel_id=1, source_target_pairs={{8,0},{16,8},{24,16},{32,24},{40,32},{48,40},{56,48},{64,56},{72,6... | collective-permute-start | bytes 147464 | tf_op jit(solution)/shard_map/ppermute | solution.py:38
  131.2 4.0 %collective-permute-done.13 = f32[3,2,16,128]{3,2,1,0:T(8,128)S(1)} collective-permute-done((f32[3,2,16,128]{3,2,1,0:T(8,128)S(1)}, f32[3,2,16,128]{3,2,1,0:T(8,128)S(1)}, u32[]{:S(2)}, u32[]{:S(2)}) %collective-permute-start.13) | collective-permute-done | bytes 49184 | tf_op jit(solution)/shard_map/ppermute | solution.py:38
  (144 shorter events, 14.7 us)
Async XLA Ops:
  8.3 24.9 %copy-start.9 = (f32[8,16,128]{2,1,0:T(8,128)S(1)}, f32[8,16,128]{2,1,0:T(8,128)}, u32[]{:S(2)}) copy-start(f32[8,16,128]{2,1,0:T(8,128)} %param.19) | copy-start | bytes 196612
  8.3 25.0 %copy-start.5 = (bf16[12,8,16,128]{3,2,1,0:T(8,128)(2,1)S(1)}, bf16[12,8,16,128]{3,2,1,0:T(8,128)(2,1)}, u32[]{:S(2)}) copy-start(bf16[12,8,16,128]{3,2,1,0:T(8,128)(2,1)} %param.20) | copy-start | bytes 1179652
  8.3 61.4 %all-to-all-start = ((bf16[128,4,32,128]{3,2,1,0:T(8,128)(2,1)}), bf16[128,4,32,128]{3,2,1,0:T(8,128)(2,1)}, u32[]{:S(2)}, u32[]{:S(2)}) async-start(bf16[128,4,32,128]{3,2,1,0:T(8,128)(2,1)} %bitcast.269), calls=%async_computation | async-start | bytes 8388608 | tf_op jit(solution)/shard_map/all_to_all | solution.py:190
  19.2 44.9 %collective-permute-start.2 = (f32[3,8,2,128]{3,1,2,0:T(8,128)S(1)}, f32[3,8,2,128]{3,1,2,0:T(8,128)S(1)}, u32[]{:S(2)}, u32[]{:S(2)}) collective-permute-start(f32[3,8,2,128]{3,1,2,0:T(8,128)S(1)} %copy.369), channel_id=1, source_target_pairs={{0,1},{1,2},{2,3},{3,4},{4,5},{5,6},{6,7},{8,9},{9,10},{10,11},{11... | collective-permute-start | bytes 73736 | tf_op jit(solution)/shard_map/ppermute | solution.py:37
  21.3 42.9 %collective-permute-start.3 = (f32[3,8,2,128]{3,1,2,0:T(8,128)S(1)}, f32[3,8,2,128]{3,1,2,0:T(8,128)S(1)}, u32[]{:S(2)}, u32[]{:S(2)}) collective-permute-start(f32[3,8,2,128]{3,1,2,0:T(8,128)S(1)} %copy.370), channel_id=1, source_target_pairs={{1,0},{2,1},{3,2},{4,3},{5,4},{6,5},{7,6},{9,8},{10,9},{11,10},{12... | collective-permute-start | bytes 73736 | tf_op jit(solution)/shard_map/ppermute | solution.py:38
  24.9 42.9 %collective-permute-start = (f32[3,2,16,128]{3,2,1,0:T(8,128)S(1)}, f32[3,2,16,128]{3,2,1,0:T(8,128)S(1)}, u32[]{:S(2)}, u32[]{:S(2)}) collective-permute-start(f32[3,2,16,128]{3,2,1,0:T(8,128)S(1)} %get-tuple-element.129), channel_id=1, source_target_pairs={{8,0},{16,8},{24,16},{32,24},{40,32},{48,40},{56,48},{64,56},{72,6... | collective-permute-start | bytes 147464 | tf_op jit(solution)/shard_map/ppermute | solution.py:38
  27.6 40.2 %collective-permute-start.1 = (f32[3,2,16,128]{3,2,1,0:T(8,128)S(1)}, f32[3,2,16,128]{3,2,1,0:T(8,128)S(1)}, u32[]{:S(2)}, u32[]{:S(2)}) collective-permute-start(f32[3,2,16,128]{3,2,1,0:T(8,128)S(1)} %get-tuple-element.130), channel_id=1, source_target_pairs={{0,8},{8,16},{16,24},{24,32},{32,40},{40,48},{48,56},{56,64},{64,7... | collective-permute-start | bytes 147464 | tf_op jit(solution)/shard_map/ppermute | solution.py:37
  64.3 21.5 %copy-start.10 = (s32[32]{0:T(128)S(1)}, s32[32]{0:T(128)}, u32[]{:S(2)}) copy-start(s32[32]{0:T(128)} %param.24) | copy-start | bytes 388
  67.8 18.4 %copy-start.4 = (f32[3,8,16,128]{3,2,1,0:T(8,128)S(1)}, f32[3,8,16,128]{3,2,1,0:T(8,128)}, u32[]{:S(2)}) copy-start(f32[3,8,16,128]{3,2,1,0:T(8,128)} %param.15) | copy-start | bytes 589828
  69.7 33.2 %copy-start.1 = (f32[8,16,128]{2,1,0:T(8,128)S(1)}, f32[8,16,128]{2,1,0:T(8,128)}, u32[]{:S(2)}) copy-start(f32[8,16,128]{2,1,0:T(8,128)} %param.18) | copy-start | bytes 196612
  69.7 33.2 %copy-start.6 = (f32[8,16,128]{2,1,0:T(8,128)S(1)}, f32[8,16,128]{2,1,0:T(8,128)}, u32[]{:S(2)}) copy-start(f32[8,16,128]{2,1,0:T(8,128)} %param.17) | copy-start | bytes 196612
  86.4 14.0 %collective-permute-start.6 = (f32[3,8,2,128]{3,1,2,0:T(8,128)S(1)}, f32[3,8,2,128]{3,1,2,0:T(8,128)S(1)}, u32[]{:S(2)}, u32[]{:S(2)}) collective-permute-start(f32[3,8,2,128]{3,1,2,0:T(8,128)S(1)} %copy.382), channel_id=1, source_target_pairs={{0,1},{1,2},{2,3},{3,4},{4,5},{5,6},{6,7},{8,9},{9,10},{10,11},{11... | collective-permute-start | bytes 73736 | tf_op jit(solution)/shard_map/ppermute | solution.py:37
  88.3 12.0 %collective-permute-start.7 = (f32[3,8,2,128]{3,1,2,0:T(8,128)S(1)}, f32[3,8,2,128]{3,1,2,0:T(8,128)S(1)}, u32[]{:S(2)}, u32[]{:S(2)}) collective-permute-start(f32[3,8,2,128]{3,1,2,0:T(8,128)S(1)} %copy.383), channel_id=1, source_target_pairs={{1,0},{2,1},{3,2},{4,3},{5,4},{6,5},{7,6},{9,8},{10,9},{11,10},{12... | collective-permute-start | bytes 73736 | tf_op jit(solution)/shard_map/ppermute | solution.py:38
  92.1 8.3 %collective-permute-start.4 = (f32[3,2,16,128]{3,2,1,0:T(8,128)S(1)}, f32[3,2,16,128]{3,2,1,0:T(8,128)S(1)}, u32[]{:S(2)}, u32[]{:S(2)}) collective-permute-start(f32[3,2,16,128]{3,2,1,0:T(8,128)S(1)} %get-tuple-element.123), channel_id=1, source_target_pairs={{0,8},{8,16},{16,24},{24,32},{32,40},{40,48},{48,56},{56,64},{64,7... | collective-permute-start | bytes 147464 | tf_op jit(solution)/shard_map/ppermute | solution.py:37
  94.8 8.1 %collective-permute-start.5 = (f32[3,2,16,128]{3,2,1,0:T(8,128)S(1)}, f32[3,2,16,128]{3,2,1,0:T(8,128)S(1)}, u32[]{:S(2)}, u32[]{:S(2)}) collective-permute-start(f32[3,2,16,128]{3,2,1,0:T(8,128)S(1)} %get-tuple-element.124), channel_id=1, source_target_pairs={{8,0},{16,8},{24,16},{32,24},{40,32},{48,40},{56,48},{64,56},{72,6... | collective-permute-start | bytes 147464 | tf_op jit(solution)/shard_map/ppermute | solution.py:38
  103.5 15.2 %collective-permute-start.8 = (f32[3,2,16,128]{3,2,1,0:T(8,128)S(1)}, f32[3,2,16,128]{3,2,1,0:T(8,128)S(1)}, u32[]{:S(2)}, u32[]{:S(2)}) collective-permute-start(f32[3,2,16,128]{3,2,1,0:T(8,128)S(1)} %get-tuple-element.116), channel_id=1, source_target_pairs={{8,0},{16,8},{24,16},{32,24},{40,32},{48,40},{56,48},{64,56},{72,6... | collective-permute-start | bytes 147464 | tf_op jit(solution)/shard_map/ppermute | solution.py:38
  105.5 13.3 %collective-permute-start.9 = (f32[3,2,16,128]{3,2,1,0:T(8,128)S(1)}, f32[3,2,16,128]{3,2,1,0:T(8,128)S(1)}, u32[]{:S(2)}, u32[]{:S(2)}) collective-permute-start(f32[3,2,16,128]{3,2,1,0:T(8,128)S(1)} %get-tuple-element.117), channel_id=1, source_target_pairs={{0,8},{8,16},{16,24},{24,32},{32,40},{40,48},{48,56},{56,64},{64,7... | collective-permute-start | bytes 147464 | tf_op jit(solution)/shard_map/ppermute | solution.py:37
  111.5 5.8 %collective-permute-start.10 = (f32[3,8,2,128]{3,1,2,0:T(8,128)S(1)}, f32[3,8,2,128]{3,1,2,0:T(8,128)S(1)}, u32[]{:S(2)}, u32[]{:S(2)}) collective-permute-start(f32[3,8,2,128]{3,1,2,0:T(8,128)S(1)} %copy.386), channel_id=1, source_target_pairs={{0,1},{1,2},{2,3},{3,4},{4,5},{5,6},{6,7},{8,9},{9,10},{10,11},{11... | collective-permute-start | bytes 73736 | tf_op jit(solution)/shard_map/ppermute | solution.py:37
  113.5 5.1 %collective-permute-start.11 = (f32[3,8,2,128]{3,1,2,0:T(8,128)S(1)}, f32[3,8,2,128]{3,1,2,0:T(8,128)S(1)}, u32[]{:S(2)}, u32[]{:S(2)}) collective-permute-start(f32[3,8,2,128]{3,1,2,0:T(8,128)S(1)} %copy.387), channel_id=1, source_target_pairs={{1,0},{2,1},{3,2},{4,3},{5,4},{6,5},{7,6},{9,8},{10,9},{11,10},{12... | collective-permute-start | bytes 73736 | tf_op jit(solution)/shard_map/ppermute | solution.py:38
  117.3 17.9 %copy-start.7 = (f32[8,16,128]{2,1,0:T(8,128)S(1)}, f32[8,16,128]{2,1,0:T(8,128)}, u32[]{:S(2)}) copy-start(f32[8,16,128]{2,1,0:T(8,128)} %param.22) | copy-start | bytes 196612
  119.5 11.6 %collective-permute-start.14 = (f32[3,8,2,128]{3,1,2,0:T(8,128)S(1)}, f32[3,8,2,128]{3,1,2,0:T(8,128)S(1)}, u32[]{:S(2)}, u32[]{:S(2)}) collective-permute-start(f32[3,8,2,128]{3,1,2,0:T(8,128)S(1)} %copy.392), channel_id=1, source_target_pairs={{0,1},{1,2},{2,3},{3,4},{4,5},{5,6},{6,7},{8,9},{9,10},{10,11},{11... | collective-permute-start | bytes 73736 | tf_op jit(solution)/shard_map/ppermute | solution.py:37
  122.8 8.3 %collective-permute-start.15 = (f32[3,8,2,128]{3,1,2,0:T(8,128)S(1)}, f32[3,8,2,128]{3,1,2,0:T(8,128)S(1)}, u32[]{:S(2)}, u32[]{:S(2)}) collective-permute-start(f32[3,8,2,128]{3,1,2,0:T(8,128)S(1)} %copy.393), channel_id=1, source_target_pairs={{1,0},{2,1},{3,2},{4,3},{5,4},{6,5},{7,6},{9,8},{10,9},{11,10},{12... | collective-permute-start | bytes 73736 | tf_op jit(solution)/shard_map/ppermute | solution.py:38
  125.2 6.0 %collective-permute-start.12 = (f32[3,2,16,128]{3,2,1,0:T(8,128)S(1)}, f32[3,2,16,128]{3,2,1,0:T(8,128)S(1)}, u32[]{:S(2)}, u32[]{:S(2)}) collective-permute-start(f32[3,2,16,128]{3,2,1,0:T(8,128)S(1)} %get-tuple-element.111), channel_id=1, source_target_pairs={{0,8},{8,16},{16,24},{24,32},{32,40},{40,48},{48,56},{56,64},{64,7... | collective-permute-start | bytes 147464 | tf_op jit(solution)/shard_map/ppermute | solution.py:37
  127.2 8.1 %collective-permute-start.13 = (f32[3,2,16,128]{3,2,1,0:T(8,128)S(1)}, f32[3,2,16,128]{3,2,1,0:T(8,128)S(1)}, u32[]{:S(2)}, u32[]{:S(2)}) collective-permute-start(f32[3,2,16,128]{3,2,1,0:T(8,128)S(1)} %get-tuple-element.110), channel_id=1, source_target_pairs={{8,0},{16,8},{24,16},{32,24},{40,32},{48,40},{56,48},{64,56},{72,6... | collective-permute-start | bytes 147464 | tf_op jit(solution)/shard_map/ppermute | solution.py:38
  (4 other events, 49.1 us)

commit v10 on v6

--- a/solution.py
+++ b/solution.py
@@ -44,20 +44,24 @@
     return jnp.pad(block, pads)
 
 
+def exchange(block):
+    wide_x = halo_pad(block[0], "gx", 1)
+    wide_y = halo_pad(block[1], "gy", 2)
+    return wide_x, wide_y
+
+
 def advance(velocity, stress, lame_first, shear_modulus, buoyancy, strain_now, surface, lame_kernel, shear_kernel):
     nx = velocity.shape[1]
     ny = velocity.shape[2]
     nz = velocity.shape[3]
-    sx = halo_pad(jnp.stack([stress[0], stress[3], stress[4]]), "gx", 1)
-    sy = halo_pad(jnp.stack([stress[3], stress[1], stress[5]]), "gy", 2)
+    sx, sy = exchange((jnp.stack([stress[0], stress[3], stress[4]]), jnp.stack([stress[3], stress[1], stress[5]])))
     sz = z_pad(jnp.stack([stress[4], stress[5], stress[2]]))
     force_first = forward_diff(sx[0], nx, 0) + backward_diff(sy[0], ny, 1) + backward_diff(sz[0], nz, 2)
     force_second = backward_diff(sx[1], nx, 0) + forward_diff(sy[1], ny, 1) + backward_diff(sz[1], nz, 2)
     force_third = backward_diff(sx[2], nx, 0) + backward_diff(sy[2], ny, 1) + forward_diff(sz[2], nz, 2)
     force_third = force_third.at[:, :, 0].add(surface)
     moved = velocity + time_step * buoyancy[None] * jnp.stack([force_first, force_second, force_third])
-    mx = halo_pad(moved, "gx", 1)
-    my = halo_pad(moved, "gy", 2)
+    mx, my = exchange((moved, moved))
     mz = z_pad(moved)
     rate_first = backward_diff(mx[0], nx, 0)
     rate_second = backward_diff(my[1], ny, 1)
@@ -104,7 +108,9 @@
     mine_norm = jnp.sqrt(mine_sq / samples + epsilon)
     other_norm = jnp.sqrt(other_sq / samples + epsilon)
     corr = (cross / samples) / (mine_norm * other_norm)
-    toward = other_vals / other_norm - corr * (mine_vals / mine_norm)
+    other_scale = 1.0 / other_norm
+    mine_scale = corr / mine_norm
+    toward = other_vals * other_scale - mine_scale * mine_vals
     toward_ref[...] = toward.astype(jnp.bfloat16).astype(jnp.float32)
 
     ways = acc_ref.shape[0]
@@ -129,7 +135,7 @@
 
 def pair_sums(targets, mine, other, stations):
     slots, rows, lanes = mine.shape
-    block = 64
+    block = 128
     samples = rows * lanes
     spec = pl.BlockSpec((block, rows, lanes), lambda g, t: (g, 0, 0))
     return pl.pallas_call(

time: 136 us -> 135 us (level)
  no operation moved by 1% of the time
where the time goes in v10:
time: 135 us
  starting transfers between devices  60.7 us (45%)
  waiting for transfers between devices  39.1 us (29%)
  local copies, waits for them, and re-layouts  15.4 us (11%)
  Pallas kernels  11.9 us (9%)
  other arithmetic  6.16 us (5%)
  between operations  1.55 us (1%)
    ppermute x8, waiting for transfers between devices, halo_pad(): lax.ppermute(lax.slice_in_dim(block, size - width, size, axis=dim), axis,...  26.5 us
    ppermute x8, starting transfers between devices, halo_pad(): lax.ppermute(lax.slice_in_dim(block, size - width, size, axis=dim), axis,...  25 us
    ppermute x8, starting transfers between devices, halo_pad(): lax.ppermute(lax.slice_in_dim(block, 0, width, axis=dim), axis, backward)  24.9 us
    pallas_call x1, Pallas kernels, pair_sums(): pl.pallas_call(functools.partial(pair_kernel, block, float(samples)), gri...  11.9 us
    ppermute x8, waiting for transfers between devices, halo_pad(): lax.ppermute(lax.slice_in_dim(block, 0, width, axis=dim), axis, backward)  11.2 us
    all_to_all x1, starting transfers between devices, station_part(): lax.all_to_all(send, ('gx', 'gy'), split_axis=0, concat_axis=0, tiled=True)  10.8 us
    unnamed x24, local copies, waits for them, and re-layouts  4.19 us
    gather x1, local copies, waits for them, and re-layouts, station_part(): padded_rows[jnp.where(slot_station >= 0, slot_station, stations_here)]  3.54 us
  transfers between devices with their start and end apart: 17, of which 6 were waited for; matrix products, arithmetic and copies ran while one was open for 6% of the time, Pallas kernels for 0%

profile of v10, /device:TPU:14, one launch (start us, length us, event | category | flops | bytes accessed | tf_op | source)
XLA Modules:
  0.0 134.7 jit_solution(14099181672739305691)
XLA Ops:
  4.7 3.5 %gather_fusion.1 = bf16[512,32,128]{2,1,0:T(8,128)(2,1)} fusion(bf16[33,32,128]{2,1,0:T(8,128)(2,1)S(1)} %concatenate.120, s32[1024]{0:T(1024)S(1)} %pad_clamp_fusion), kind=kCustom, calls=%fused_computation.1 | custom fusion | bytes 8390656 | tf_op jit(solution)/shard_map/gather | solution.py:183
  8.3 10.8 %all-to-all-start = ((bf16[128,4,32,128]{3,2,1,0:T(8,128)(2,1)}), bf16[128,4,32,128]{3,2,1,0:T(8,128)(2,1)}, u32[]{:S(2)}, u32[]{:S(2)}) async-start(bf16[128,4,32,128]{3,2,1,0:T(8,128)(2,1)} %bitcast.271), calls=%async_computation | async-start | bytes 8388608 | tf_op jit(solution)/shard_map/all_to_all | solution.py:184
  19.2 2.0 %collective-permute-start.2 = (f32[3,8,2,128]{3,1,2,0:T(8,128)S(1)}, f32[3,8,2,128]{3,1,2,0:T(8,128)S(1)}, u32[]{:S(2)}, u32[]{:S(2)}) collective-permute-start(f32[3,8,2,128]{3,1,2,0:T(8,128)S(1)} %copy.372), channel_id=1, source_target_pairs={{0,1},{1,2},{2,3},{3,4},{4,5},{5,6},{6,7},{8,9},{9,10},{10,11},{11... | collective-permute-start | bytes 73736 | tf_op jit(solution)/shard_map/ppermute | solution.py:37
  21.3 3.5 %collective-permute-start.3 = (f32[3,8,2,128]{3,1,2,0:T(8,128)S(1)}, f32[3,8,2,128]{3,1,2,0:T(8,128)S(1)}, u32[]{:S(2)}, u32[]{:S(2)}) collective-permute-start(f32[3,8,2,128]{3,1,2,0:T(8,128)S(1)} %copy.373), channel_id=1, source_target_pairs={{1,0},{2,1},{3,2},{4,3},{5,4},{6,5},{7,6},{9,8},{10,9},{11,10},{12... | collective-permute-start | bytes 73736 | tf_op jit(solution)/shard_map/ppermute | solution.py:38
  24.8 2.8 %collective-permute-start = (f32[3,2,16,128]{3,2,1,0:T(8,128)S(1)}, f32[3,2,16,128]{3,2,1,0:T(8,128)S(1)}, u32[]{:S(2)}, u32[]{:S(2)}) collective-permute-start(f32[3,2,16,128]{3,2,1,0:T(8,128)S(1)} %get-tuple-element.129), channel_id=1, source_target_pairs={{8,0},{16,8},{24,16},{32,24},{40,32},{48,40},{56,48},{64,56},{72,6... | collective-permute-start | bytes 147464 | tf_op jit(solution)/shard_map/ppermute | solution.py:38
  27.6 5.2 %collective-permute-start.1 = (f32[3,2,16,128]{3,2,1,0:T(8,128)S(1)}, f32[3,2,16,128]{3,2,1,0:T(8,128)S(1)}, u32[]{:S(2)}, u32[]{:S(2)}) collective-permute-start(f32[3,2,16,128]{3,2,1,0:T(8,128)S(1)} %get-tuple-element.130), channel_id=1, source_target_pairs={{0,8},{8,16},{16,24},{24,32},{32,40},{40,48},{48,56},{56,64},{64,7... | collective-permute-start | bytes 147464 | tf_op jit(solution)/shard_map/ppermute | solution.py:37
  34.2 3.5 %gather_fusion = bf16[512,32,128]{2,1,0:T(8,128)(2,1)} fusion(bf16[33,32,128]{2,1,0:T(8,128)(2,1)S(1)} %concatenate.120, s32[1024]{0:T(1024)S(1)} %pad_clamp_fusion.1), kind=kCustom, calls=%fused_computation | custom fusion | bytes 8390656 | tf_op jit(solution)/shard_map/gather | solution.py:186
  37.7 26.4 %collective-permute-done.2 = f32[3,8,2,128]{3,1,2,0:T(8,128)S(1)} collective-permute-done((f32[3,8,2,128]{3,1,2,0:T(8,128)S(1)}, f32[3,8,2,128]{3,1,2,0:T(8,128)S(1)}, u32[]{:S(2)}, u32[]{:S(2)}) %collective-permute-start.2) | collective-permute-done | bytes 24608 | tf_op jit(solution)/shard_map/ppermute | solution.py:37
  64.3 3.5 %collective-permute-done = f32[3,2,16,128]{3,2,1,0:T(8,128)S(1)} collective-permute-done((f32[3,2,16,128]{3,2,1,0:T(8,128)S(1)}, f32[3,2,16,128]{3,2,1,0:T(8,128)S(1)}, u32[]{:S(2)}, u32[]{:S(2)}) %collective-permute-start) | collective-permute-done | bytes 49184 | tf_op jit(solution)/shard_map/ppermute | solution.py:38
  69.7 11.9 %shard_map.146 = f32[32,32,128]{2,1,0:T(8,128)} custom-call(s32[512]{0:T(512)} %compare_select_fusion.4.station_ref, bf16[512,32,128]{2,1,0:T(8,128)(2,1)} %gather_fusion, bf16[512,32,128]{2,1,0:T(8,128)(2,1)} %bitcast.21.other_ref), custom_call_target="tpu_custom_call" | custom-call | flops 41943040 | bytes 8388608 | tf_op jit(solution)/shard_map/pallas_call | solution.py:141
  83.2 1.9 %collective-permute-start.6 = (f32[3,8,2,128]{3,1,2,0:T(8,128)S(1)}, f32[3,8,2,128]{3,1,2,0:T(8,128)S(1)}, u32[]{:S(2)}, u32[]{:S(2)}) collective-permute-start(f32[3,8,2,128]{3,1,2,0:T(8,128)S(1)} %copy.386), channel_id=1, source_target_pairs={{0,1},{1,2},{2,3},{3,4},{4,5},{5,6},{6,7},{8,9},{9,10},{10,11},{11... | collective-permute-start | bytes 73736 | tf_op jit(solution)/shard_map/ppermute | solution.py:37
  85.2 3.6 %collective-permute-start.7 = (f32[3,8,2,128]{3,1,2,0:T(8,128)S(1)}, f32[3,8,2,128]{3,1,2,0:T(8,128)S(1)}, u32[]{:S(2)}, u32[]{:S(2)}) collective-permute-start(f32[3,8,2,128]{3,1,2,0:T(8,128)S(1)} %copy.387), channel_id=1, source_target_pairs={{1,0},{2,1},{3,2},{4,3},{5,4},{6,5},{7,6},{9,8},{10,9},{11,10},{12... | collective-permute-start | bytes 73736 | tf_op jit(solution)/shard_map/ppermute | solution.py:38
  89.0 2.7 %collective-permute-start.4 = (f32[3,2,16,128]{3,2,1,0:T(8,128)S(1)}, f32[3,2,16,128]{3,2,1,0:T(8,128)S(1)}, u32[]{:S(2)}, u32[]{:S(2)}) collective-permute-start(f32[3,2,16,128]{3,2,1,0:T(8,128)S(1)} %get-tuple-element.123), channel_id=1, source_target_pairs={{0,8},{8,16},{16,24},{24,32},{32,40},{40,48},{48,56},{56,64},{64,7... | collective-permute-start | bytes 147464 | tf_op jit(solution)/shard_map/ppermute | solution.py:37
  91.7 3.2 %collective-permute-start.5 = (f32[3,2,16,128]{3,2,1,0:T(8,128)S(1)}, f32[3,2,16,128]{3,2,1,0:T(8,128)S(1)}, u32[]{:S(2)}, u32[]{:S(2)}) collective-permute-start(f32[3,2,16,128]{3,2,1,0:T(8,128)S(1)} %get-tuple-element.124), channel_id=1, source_target_pairs={{8,0},{16,8},{24,16},{32,24},{40,32},{48,40},{56,48},{64,56},{72,6... | collective-permute-start | bytes 147464 | tf_op jit(solution)/shard_map/ppermute | solution.py:38
  95.0 2.1 %copy.406 = f32[4,8,32,128]{3,1,2,0:T(8,128)} copy(f32[4,8,32,128]{3,2,1,0:T(8,128)} %bitcast.272) | data formatting | bytes 1048576
  97.3 2.4 %collective-permute-done.5 = f32[3,2,16,128]{3,2,1,0:T(8,128)S(1)} collective-permute-done((f32[3,2,16,128]{3,2,1,0:T(8,128)S(1)}, f32[3,2,16,128]{3,2,1,0:T(8,128)S(1)}, u32[]{:S(2)}, u32[]{:S(2)}) %collective-permute-start.5) | collective-permute-done | bytes 49184 | tf_op jit(solution)/shard_map/ppermute | solution.py:38
  100.4 1.9 %collective-permute-start.8 = (f32[3,2,16,128]{3,2,1,0:T(8,128)S(1)}, f32[3,2,16,128]{3,2,1,0:T(8,128)S(1)}, u32[]{:S(2)}, u32[]{:S(2)}) collective-permute-start(f32[3,2,16,128]{3,2,1,0:T(8,128)S(1)} %get-tuple-element.116), channel_id=1, source_target_pairs={{8,0},{16,8},{24,16},{32,24},{40,32},{48,40},{56,48},{64,56},{72,6... | collective-permute-start | bytes 147464 | tf_op jit(solution)/shard_map/ppermute | solution.py:38
  102.3 6.0 %collective-permute-start.9 = (f32[3,2,16,128]{3,2,1,0:T(8,128)S(1)}, f32[3,2,16,128]{3,2,1,0:T(8,128)S(1)}, u32[]{:S(2)}, u32[]{:S(2)}) collective-permute-start(f32[3,2,16,128]{3,2,1,0:T(8,128)S(1)} %get-tuple-element.117), channel_id=1, source_target_pairs={{0,8},{8,16},{16,24},{24,32},{32,40},{40,48},{48,56},{56,64},{64,7... | collective-permute-start | bytes 147464 | tf_op jit(solution)/shard_map/ppermute | solution.py:37
  108.4 1.9 %collective-permute-start.10 = (f32[3,8,2,128]{3,1,2,0:T(8,128)S(1)}, f32[3,8,2,128]{3,1,2,0:T(8,128)S(1)}, u32[]{:S(2)}, u32[]{:S(2)}) collective-permute-start(f32[3,8,2,128]{3,1,2,0:T(8,128)S(1)} %copy.390), channel_id=1, source_target_pairs={{0,1},{1,2},{2,3},{3,4},{4,5},{5,6},{6,7},{8,9},{9,10},{10,11},{11... | collective-permute-start | bytes 73736 | tf_op jit(solution)/shard_map/ppermute | solution.py:37
  110.3 3.6 %collective-permute-start.11 = (f32[3,8,2,128]{3,1,2,0:T(8,128)S(1)}, f32[3,8,2,128]{3,1,2,0:T(8,128)S(1)}, u32[]{:S(2)}, u32[]{:S(2)}) collective-permute-start(f32[3,8,2,128]{3,1,2,0:T(8,128)S(1)} %copy.391), channel_id=1, source_target_pairs={{1,0},{2,1},{3,2},{4,3},{5,4},{6,5},{7,6},{9,8},{10,9},{11,10},{12... | collective-permute-start | bytes 73736 | tf_op jit(solution)/shard_map/ppermute | solution.py:38
  116.3 3.3 %collective-permute-start.14 = (f32[3,8,2,128]{3,1,2,0:T(8,128)S(1)}, f32[3,8,2,128]{3,1,2,0:T(8,128)S(1)}, u32[]{:S(2)}, u32[]{:S(2)}) collective-permute-start(f32[3,8,2,128]{3,1,2,0:T(8,128)S(1)} %copy.396), channel_id=1, source_target_pairs={{0,1},{1,2},{2,3},{3,4},{4,5},{5,6},{6,7},{8,9},{9,10},{10,11},{11... | collective-permute-start | bytes 73736 | tf_op jit(solution)/shard_map/ppermute | solution.py:37
  119.7 2.3 %collective-permute-start.15 = (f32[3,8,2,128]{3,1,2,0:T(8,128)S(1)}, f32[3,8,2,128]{3,1,2,0:T(8,128)S(1)}, u32[]{:S(2)}, u32[]{:S(2)}) collective-permute-start(f32[3,8,2,128]{3,1,2,0:T(8,128)S(1)} %copy.397), channel_id=1, source_target_pairs={{1,0},{2,1},{3,2},{4,3},{5,4},{6,5},{7,6},{9,8},{10,9},{11,10},{12... | collective-permute-start | bytes 73736 | tf_op jit(solution)/shard_map/ppermute | solution.py:38
  124.0 3.9 %collective-permute-start.13 = (f32[3,2,16,128]{3,2,1,0:T(8,128)S(1)}, f32[3,2,16,128]{3,2,1,0:T(8,128)S(1)}, u32[]{:S(2)}, u32[]{:S(2)}) collective-permute-start(f32[3,2,16,128]{3,2,1,0:T(8,128)S(1)} %get-tuple-element.110), channel_id=1, source_target_pairs={{8,0},{16,8},{24,16},{32,24},{40,32},{48,40},{56,48},{64,56},{72,6... | collective-permute-start | bytes 147464 | tf_op jit(solution)/shard_map/ppermute | solution.py:38
  128.1 4.0 %collective-permute-done.13 = f32[3,2,16,128]{3,2,1,0:T(8,128)S(1)} collective-permute-done((f32[3,2,16,128]{3,2,1,0:T(8,128)S(1)}, f32[3,2,16,128]{3,2,1,0:T(8,128)S(1)}, u32[]{:S(2)}, u32[]{:S(2)}) %collective-permute-start.13) | collective-permute-done | bytes 49184 | tf_op jit(solution)/shard_map/ppermute | solution.py:38
  (146 shorter events, 17.0 us)
Async XLA Ops:
  8.3 25.7 %copy-start.8 = (f32[8,16,128]{2,1,0:T(8,128)S(1)}, f32[8,16,128]{2,1,0:T(8,128)}, u32[]{:S(2)}) copy-start(f32[8,16,128]{2,1,0:T(8,128)} %param.19) | copy-start | bytes 196612
  8.3 25.8 %copy-start.4 = (bf16[12,8,16,128]{3,2,1,0:T(8,128)(2,1)S(1)}, bf16[12,8,16,128]{3,2,1,0:T(8,128)(2,1)}, u32[]{:S(2)}) copy-start(bf16[12,8,16,128]{3,2,1,0:T(8,128)(2,1)} %param.20) | copy-start | bytes 1179652
  8.3 61.4 %all-to-all-start = ((bf16[128,4,32,128]{3,2,1,0:T(8,128)(2,1)}), bf16[128,4,32,128]{3,2,1,0:T(8,128)(2,1)}, u32[]{:S(2)}, u32[]{:S(2)}) async-start(bf16[128,4,32,128]{3,2,1,0:T(8,128)(2,1)} %bitcast.271), calls=%async_computation | async-start | bytes 8388608 | tf_op jit(solution)/shard_map/all_to_all | solution.py:184
  19.2 44.9 %collective-permute-start.2 = (f32[3,8,2,128]{3,1,2,0:T(8,128)S(1)}, f32[3,8,2,128]{3,1,2,0:T(8,128)S(1)}, u32[]{:S(2)}, u32[]{:S(2)}) collective-permute-start(f32[3,8,2,128]{3,1,2,0:T(8,128)S(1)} %copy.372), channel_id=1, source_target_pairs={{0,1},{1,2},{2,3},{3,4},{4,5},{5,6},{6,7},{8,9},{9,10},{10,11},{11... | collective-permute-start | bytes 73736 | tf_op jit(solution)/shard_map/ppermute | solution.py:37
  21.3 42.9 %collective-permute-start.3 = (f32[3,8,2,128]{3,1,2,0:T(8,128)S(1)}, f32[3,8,2,128]{3,1,2,0:T(8,128)S(1)}, u32[]{:S(2)}, u32[]{:S(2)}) collective-permute-start(f32[3,8,2,128]{3,1,2,0:T(8,128)S(1)} %copy.373), channel_id=1, source_target_pairs={{1,0},{2,1},{3,2},{4,3},{5,4},{6,5},{7,6},{9,8},{10,9},{11,10},{12... | collective-permute-start | bytes 73736 | tf_op jit(solution)/shard_map/ppermute | solution.py:38
  24.8 42.9 %collective-permute-start = (f32[3,2,16,128]{3,2,1,0:T(8,128)S(1)}, f32[3,2,16,128]{3,2,1,0:T(8,128)S(1)}, u32[]{:S(2)}, u32[]{:S(2)}) collective-permute-start(f32[3,2,16,128]{3,2,1,0:T(8,128)S(1)} %get-tuple-element.129), channel_id=1, source_target_pairs={{8,0},{16,8},{24,16},{32,24},{40,32},{48,40},{56,48},{64,56},{72,6... | collective-permute-start | bytes 147464 | tf_op jit(solution)/shard_map/ppermute | solution.py:38
  27.6 40.2 %collective-permute-start.1 = (f32[3,2,16,128]{3,2,1,0:T(8,128)S(1)}, f32[3,2,16,128]{3,2,1,0:T(8,128)S(1)}, u32[]{:S(2)}, u32[]{:S(2)}) collective-permute-start(f32[3,2,16,128]{3,2,1,0:T(8,128)S(1)} %get-tuple-element.130), channel_id=1, source_target_pairs={{0,8},{8,16},{16,24},{24,32},{32,40},{40,48},{48,56},{56,64},{64,7... | collective-permute-start | bytes 147464 | tf_op jit(solution)/shard_map/ppermute | solution.py:37
  81.5 18.2 %copy-start = (f32[8,16,128]{2,1,0:T(8,128)S(1)}, f32[8,16,128]{2,1,0:T(8,128)}, u32[]{:S(2)}) copy-start(f32[8,16,128]{2,1,0:T(8,128)} %param.18) | copy-start | bytes 196612
  81.5 18.2 %copy-start.5 = (f32[8,16,128]{2,1,0:T(8,128)S(1)}, f32[8,16,128]{2,1,0:T(8,128)}, u32[]{:S(2)}) copy-start(f32[8,16,128]{2,1,0:T(8,128)} %param.17) | copy-start | bytes 196612
  83.2 14.0 %collective-permute-start.6 = (f32[3,8,2,128]{3,1,2,0:T(8,128)S(1)}, f32[3,8,2,128]{3,1,2,0:T(8,128)S(1)}, u32[]{:S(2)}, u32[]{:S(2)}) collective-permute-start(f32[3,8,2,128]{3,1,2,0:T(8,128)S(1)} %copy.386), channel_id=1, source_target_pairs={{0,1},{1,2},{2,3},{3,4},{4,5},{5,6},{6,7},{8,9},{9,10},{10,11},{11... | collective-permute-start | bytes 73736 | tf_op jit(solution)/shard_map/ppermute | solution.py:37
  85.2 12.0 %collective-permute-start.7 = (f32[3,8,2,128]{3,1,2,0:T(8,128)S(1)}, f32[3,8,2,128]{3,1,2,0:T(8,128)S(1)}, u32[]{:S(2)}, u32[]{:S(2)}) collective-permute-start(f32[3,8,2,128]{3,1,2,0:T(8,128)S(1)} %copy.387), channel_id=1, source_target_pairs={{1,0},{2,1},{3,2},{4,3},{5,4},{6,5},{7,6},{9,8},{10,9},{11,10},{12... | collective-permute-start | bytes 73736 | tf_op jit(solution)/shard_map/ppermute | solution.py:38
  89.0 8.3 %collective-permute-start.4 = (f32[3,2,16,128]{3,2,1,0:T(8,128)S(1)}, f32[3,2,16,128]{3,2,1,0:T(8,128)S(1)}, u32[]{:S(2)}, u32[]{:S(2)}) collective-permute-start(f32[3,2,16,128]{3,2,1,0:T(8,128)S(1)} %get-tuple-element.123), channel_id=1, source_target_pairs={{0,8},{8,16},{16,24},{24,32},{32,40},{40,48},{48,56},{56,64},{64,7... | collective-permute-start | bytes 147464 | tf_op jit(solution)/shard_map/ppermute | solution.py:37
  91.7 8.1 %collective-permute-start.5 = (f32[3,2,16,128]{3,2,1,0:T(8,128)S(1)}, f32[3,2,16,128]{3,2,1,0:T(8,128)S(1)}, u32[]{:S(2)}, u32[]{:S(2)}) collective-permute-start(f32[3,2,16,128]{3,2,1,0:T(8,128)S(1)} %get-tuple-element.124), channel_id=1, source_target_pairs={{8,0},{16,8},{24,16},{32,24},{40,32},{48,40},{56,48},{64,56},{72,6... | collective-permute-start | bytes 147464 | tf_op jit(solution)/shard_map/ppermute | solution.py:38
  100.4 15.2 %collective-permute-start.8 = (f32[3,2,16,128]{3,2,1,0:T(8,128)S(1)}, f32[3,2,16,128]{3,2,1,0:T(8,128)S(1)}, u32[]{:S(2)}, u32[]{:S(2)}) collective-permute-start(f32[3,2,16,128]{3,2,1,0:T(8,128)S(1)} %get-tuple-element.116), channel_id=1, source_target_pairs={{8,0},{16,8},{24,16},{32,24},{40,32},{48,40},{56,48},{64,56},{72,6... | collective-permute-start | bytes 147464 | tf_op jit(solution)/shard_map/ppermute | solution.py:38
  102.3 13.3 %collective-permute-start.9 = (f32[3,2,16,128]{3,2,1,0:T(8,128)S(1)}, f32[3,2,16,128]{3,2,1,0:T(8,128)S(1)}, u32[]{:S(2)}, u32[]{:S(2)}) collective-permute-start(f32[3,2,16,128]{3,2,1,0:T(8,128)S(1)} %get-tuple-element.117), channel_id=1, source_target_pairs={{0,8},{8,16},{16,24},{24,32},{32,40},{40,48},{48,56},{56,64},{64,7... | collective-permute-start | bytes 147464 | tf_op jit(solution)/shard_map/ppermute | solution.py:37
  108.4 5.8 %collective-permute-start.10 = (f32[3,8,2,128]{3,1,2,0:T(8,128)S(1)}, f32[3,8,2,128]{3,1,2,0:T(8,128)S(1)}, u32[]{:S(2)}, u32[]{:S(2)}) collective-permute-start(f32[3,8,2,128]{3,1,2,0:T(8,128)S(1)} %copy.390), channel_id=1, source_target_pairs={{0,1},{1,2},{2,3},{3,4},{4,5},{5,6},{6,7},{8,9},{9,10},{10,11},{11... | collective-permute-start | bytes 73736 | tf_op jit(solution)/shard_map/ppermute | solution.py:37
  110.3 5.1 %collective-permute-start.11 = (f32[3,8,2,128]{3,1,2,0:T(8,128)S(1)}, f32[3,8,2,128]{3,1,2,0:T(8,128)S(1)}, u32[]{:S(2)}, u32[]{:S(2)}) collective-permute-start(f32[3,8,2,128]{3,1,2,0:T(8,128)S(1)} %copy.391), channel_id=1, source_target_pairs={{1,0},{2,1},{3,2},{4,3},{5,4},{6,5},{7,6},{9,8},{10,9},{11,10},{12... | collective-permute-start | bytes 73736 | tf_op jit(solution)/shard_map/ppermute | solution.py:38
  114.2 17.9 %copy-start.6 = (f32[8,16,128]{2,1,0:T(8,128)S(1)}, f32[8,16,128]{2,1,0:T(8,128)}, u32[]{:S(2)}) copy-start(f32[8,16,128]{2,1,0:T(8,128)} %param.22) | copy-start | bytes 196612
  115.9 17.2 %copy-start.7 = (f32[8,16,128]{2,1,0:T(8,128)S(1)}, f32[8,16,128]{2,1,0:T(8,128)}, u32[]{:S(2)}) copy-start(f32[8,16,128]{2,1,0:T(8,128)} %param.21) | copy-start | bytes 196612
  116.3 17.6 %copy-start.1 = (f32[3,8,16,128]{3,2,1,0:T(8,128)}, f32[3,8,16,128]{3,2,1,0:T(8,128)S(1)}, u32[]{:S(2)}) copy-start(f32[3,8,16,128]{3,2,1,0:T(8,128)S(1)} %fusion.2) | copy-start | bytes 589828
  116.3 11.6 %collective-permute-start.14 = (f32[3,8,2,128]{3,1,2,0:T(8,128)S(1)}, f32[3,8,2,128]{3,1,2,0:T(8,128)S(1)}, u32[]{:S(2)}, u32[]{:S(2)}) collective-permute-start(f32[3,8,2,128]{3,1,2,0:T(8,128)S(1)} %copy.396), channel_id=1, source_target_pairs={{0,1},{1,2},{2,3},{3,4},{4,5},{5,6},{6,7},{8,9},{9,10},{10,11},{11... | collective-permute-start | bytes 73736 | tf_op jit(solution)/shard_map/ppermute | solution.py:37
  119.7 8.3 %collective-permute-start.15 = (f32[3,8,2,128]{3,1,2,0:T(8,128)S(1)}, f32[3,8,2,128]{3,1,2,0:T(8,128)S(1)}, u32[]{:S(2)}, u32[]{:S(2)}) collective-permute-start(f32[3,8,2,128]{3,1,2,0:T(8,128)S(1)} %copy.397), channel_id=1, source_target_pairs={{1,0},{2,1},{3,2},{4,3},{5,4},{6,5},{7,6},{9,8},{10,9},{11,10},{12... | collective-permute-start | bytes 73736 | tf_op jit(solution)/shard_map/ppermute | solution.py:38
  122.1 6.0 %collective-permute-start.12 = (f32[3,2,16,128]{3,2,1,0:T(8,128)S(1)}, f32[3,2,16,128]{3,2,1,0:T(8,128)S(1)}, u32[]{:S(2)}, u32[]{:S(2)}) collective-permute-start(f32[3,2,16,128]{3,2,1,0:T(8,128)S(1)} %get-tuple-element.111), channel_id=1, source_target_pairs={{0,8},{8,16},{16,24},{24,32},{32,40},{40,48},{48,56},{56,64},{64,7... | collective-permute-start | bytes 147464 | tf_op jit(solution)/shard_map/ppermute | solution.py:37
  124.0 8.1 %collective-permute-start.13 = (f32[3,2,16,128]{3,2,1,0:T(8,128)S(1)}, f32[3,2,16,128]{3,2,1,0:T(8,128)S(1)}, u32[]{:S(2)}, u32[]{:S(2)}) collective-permute-start(f32[3,2,16,128]{3,2,1,0:T(8,128)S(1)} %get-tuple-element.110), channel_id=1, source_target_pairs={{8,0},{16,8},{24,16},{32,24},{40,32},{48,40},{56,48},{64,56},{72,6... | collective-permute-start | bytes 147464 | tf_op jit(solution)/shard_map/ppermute | solution.py:38
  (3 other events, 37.3 us)

commit v11 on v10

--- a/solution.py
+++ b/solution.py
@@ -93,7 +93,7 @@
     return (moved, grown, lame_kernel, shear_kernel)
 
 
-def pair_kernel(block, samples, station_ref, mine_ref, other_ref, out_ref, acc_ref, toward_ref):
+def pair_kernel(block, samples, station_ref, mine_ref, other_ref, out_ref, last_ref, acc_ref, toward_ref):
     step = pl.program_id(0)
 
     @pl.when(step == 0)
@@ -108,9 +108,7 @@
     mine_norm = jnp.sqrt(mine_sq / samples + epsilon)
     other_norm = jnp.sqrt(other_sq / samples + epsilon)
     corr = (cross / samples) / (mine_norm * other_norm)
-    other_scale = 1.0 / other_norm
-    mine_scale = corr / mine_norm
-    toward = other_vals * other_scale - mine_scale * mine_vals
+    toward = other_vals / other_norm - corr * (mine_vals / mine_norm)
     toward_ref[...] = toward.astype(jnp.bfloat16).astype(jnp.float32)
 
     ways = acc_ref.shape[0]
@@ -131,11 +129,12 @@
         for way in range(1, ways):
             total = total + acc_ref[way, :stations]
         out_ref[...] = total
+        last_ref[...] = total[:, total.shape[1] - 1 :, :]
 
 
 def pair_sums(targets, mine, other, stations):
     slots, rows, lanes = mine.shape
-    block = 128
+    block = 64
     samples = rows * lanes
     spec = pl.BlockSpec((block, rows, lanes), lambda g, t: (g, 0, 0))
     return pl.pallas_call(
@@ -144,13 +143,19 @@
             num_scalar_prefetch=1,
             grid=(slots // block,),
             in_specs=[spec, spec],
-            out_specs=pl.BlockSpec((stations, rows, lanes), lambda g, t: (0, 0, 0)),
+            out_specs=[
+                pl.BlockSpec((stations, rows, lanes), lambda g, t: (0, 0, 0)),
+                pl.BlockSpec((stations, 1, lanes), lambda g, t: (0, 0, 0)),
+            ],
             scratch_shapes=[
                 pltpu.VMEM((4, stations + 1, rows, lanes), jnp.float32),
                 pltpu.VMEM((block, rows, lanes), jnp.float32),
             ],
         ),
-        out_shape=jax.ShapeDtypeStruct((stations, rows, lanes), jnp.float32),
+        out_shape=[
+            jax.ShapeDtypeStruct((stations, rows, lanes), jnp.float32),
+            jax.ShapeDtypeStruct((stations, 1, lanes), jnp.float32),
+        ],
         compiler_params=pltpu.CompilerParams(dimension_semantics=("arbitrary",)),
         cost_estimate=pl.CostEstimate(flops=20 * slots * samples, transcendentals=0, bytes_accessed=4 * slots * samples),
     )(targets, mine, other)
@@ -186,11 +191,11 @@
     mine = padded_rows[jnp.where(mine_station >= 0, mine_station, stations_here)]
     slots = devices * 4
     targets = jnp.where(mine_station >= 0, mine_station, stations_here).reshape(slots)
-    adjoint3 = pair_sums(
+    adjoint3, last_rows = pair_sums(
         targets, mine.reshape(slots, samples // lanes, lanes), recv.reshape(slots, samples // lanes, lanes), stations_here
     )
     adjoint = adjoint3.reshape(stations_here, samples)
-    last = adjoint3[:, samples // lanes - 1, lanes - step_count :]
+    last = last_rows[:, 0, lanes - step_count :]
     tail = last
     cells_hit = (station_cell[:, None] == jnp.arange(cells_first * cells_second)[None, :]).astype(jnp.float32)
     surfaces = jnp.stack(

time: 135 us -> 136 us (level)
  no operation moved by 1% of the time
where the time goes in v11:
time: 136 us; the launch traced here: 135 us
  starting transfers between devices  60.7 us (45%)
  waiting for transfers between devices  39.1 us (29%)
  local copies, waits for them, and re-layouts  15.2 us (11%)
  Pallas kernels  12.2 us (9%)
  other arithmetic  6.13 us (5%)
  between operations  1.56 us (1%)
    ppermute x8, waiting for transfers between devices, halo_pad(): lax.ppermute(lax.slice_in_dim(block, size - width, size, axis=dim), axis,...  26.5 us
    ppermute x8, starting transfers between devices, halo_pad(): lax.ppermute(lax.slice_in_dim(block, size - width, size, axis=dim), axis,...  25 us
    ppermute x8, starting transfers between devices, halo_pad(): lax.ppermute(lax.slice_in_dim(block, 0, width, axis=dim), axis, backward)  24.9 us
    pallas_call x1, Pallas kernels, pair_sums(): pl.pallas_call(functools.partial(pair_kernel, block, float(samples)), gri...  12.2 us
    ppermute x8, waiting for transfers between devices, halo_pad(): lax.ppermute(lax.slice_in_dim(block, 0, width, axis=dim), axis, backward)  11.2 us
    all_to_all x1, starting transfers between devices, station_part(): lax.all_to_all(send, ('gx', 'gy'), split_axis=0, concat_axis=0, tiled=True)  10.8 us
    unnamed x24, local copies, waits for them, and re-layouts  4.19 us
    gather x1, local copies, waits for them, and re-layouts, station_part(): padded_rows[jnp.where(slot_station >= 0, slot_station, stations_here)]  3.55 us
  transfers between devices with their start and end apart: 17, of which 6 were waited for; matrix products, arithmetic and copies ran while one was open for 6% of the time, Pallas kernels for 0%

profile of v11, /device:TPU:14, one launch (start us, length us, event | category | flops | bytes accessed | tf_op | source)
XLA Modules:
  0.0 134.8 jit_solution(5834544512022831579)
XLA Ops:
  4.7 3.6 %gather_fusion.1 = bf16[512,32,128]{2,1,0:T(8,128)(2,1)} fusion(bf16[33,32,128]{2,1,0:T(8,128)(2,1)S(1)} %concatenate.120, s32[1024]{0:T(1024)S(1)} %pad_clamp_fusion), kind=kCustom, calls=%fused_computation.1 | custom fusion | bytes 8390656 | tf_op jit(solution)/shard_map/gather | solution.py:188
  8.3 10.8 %all-to-all-start = ((bf16[128,4,32,128]{3,2,1,0:T(8,128)(2,1)}), bf16[128,4,32,128]{3,2,1,0:T(8,128)(2,1)}, u32[]{:S(2)}, u32[]{:S(2)}) async-start(bf16[128,4,32,128]{3,2,1,0:T(8,128)(2,1)} %bitcast.271), calls=%async_computation | async-start | bytes 8388608 | tf_op jit(solution)/shard_map/all_to_all | solution.py:189
  19.2 2.0 %collective-permute-start.2 = (f32[3,8,2,128]{3,1,2,0:T(8,128)S(1)}, f32[3,8,2,128]{3,1,2,0:T(8,128)S(1)}, u32[]{:S(2)}, u32[]{:S(2)}) collective-permute-start(f32[3,8,2,128]{3,1,2,0:T(8,128)S(1)} %copy.372), channel_id=1, source_target_pairs={{0,1},{1,2},{2,3},{3,4},{4,5},{5,6},{6,7},{8,9},{9,10},{10,11},{11... | collective-permute-start | bytes 73736 | tf_op jit(solution)/shard_map/ppermute | solution.py:37
  21.3 3.5 %collective-permute-start.3 = (f32[3,8,2,128]{3,1,2,0:T(8,128)S(1)}, f32[3,8,2,128]{3,1,2,0:T(8,128)S(1)}, u32[]{:S(2)}, u32[]{:S(2)}) collective-permute-start(f32[3,8,2,128]{3,1,2,0:T(8,128)S(1)} %copy.373), channel_id=1, source_target_pairs={{1,0},{2,1},{3,2},{4,3},{5,4},{6,5},{7,6},{9,8},{10,9},{11,10},{12... | collective-permute-start | bytes 73736 | tf_op jit(solution)/shard_map/ppermute | solution.py:38
  24.9 2.8 %collective-permute-start = (f32[3,2,16,128]{3,2,1,0:T(8,128)S(1)}, f32[3,2,16,128]{3,2,1,0:T(8,128)S(1)}, u32[]{:S(2)}, u32[]{:S(2)}) collective-permute-start(f32[3,2,16,128]{3,2,1,0:T(8,128)S(1)} %get-tuple-element.133), channel_id=1, source_target_pairs={{8,0},{16,8},{24,16},{32,24},{40,32},{48,40},{56,48},{64,56},{72,6... | collective-permute-start | bytes 147464 | tf_op jit(solution)/shard_map/ppermute | solution.py:38
  27.6 5.2 %collective-permute-start.1 = (f32[3,2,16,128]{3,2,1,0:T(8,128)S(1)}, f32[3,2,16,128]{3,2,1,0:T(8,128)S(1)}, u32[]{:S(2)}, u32[]{:S(2)}) collective-permute-start(f32[3,2,16,128]{3,2,1,0:T(8,128)S(1)} %get-tuple-element.134), channel_id=1, source_target_pairs={{0,8},{8,16},{16,24},{24,32},{32,40},{40,48},{48,56},{56,64},{64,7... | collective-permute-start | bytes 147464 | tf_op jit(solution)/shard_map/ppermute | solution.py:37
  34.2 3.5 %gather_fusion = bf16[512,32,128]{2,1,0:T(8,128)(2,1)} fusion(bf16[33,32,128]{2,1,0:T(8,128)(2,1)S(1)} %concatenate.120, s32[1024]{0:T(1024)S(1)} %pad_clamp_fusion.1), kind=kCustom, calls=%fused_computation | custom fusion | bytes 8390656 | tf_op jit(solution)/shard_map/gather | solution.py:191
  37.7 26.4 %collective-permute-done.2 = f32[3,8,2,128]{3,1,2,0:T(8,128)S(1)} collective-permute-done((f32[3,8,2,128]{3,1,2,0:T(8,128)S(1)}, f32[3,8,2,128]{3,1,2,0:T(8,128)S(1)}, u32[]{:S(2)}, u32[]{:S(2)}) %collective-permute-start.2) | collective-permute-done | bytes 24608 | tf_op jit(solution)/shard_map/ppermute | solution.py:37
  64.3 3.5 %collective-permute-done = f32[3,2,16,128]{3,2,1,0:T(8,128)S(1)} collective-permute-done((f32[3,2,16,128]{3,2,1,0:T(8,128)S(1)}, f32[3,2,16,128]{3,2,1,0:T(8,128)S(1)}, u32[]{:S(2)}, u32[]{:S(2)}) %collective-permute-start) | collective-permute-done | bytes 49184 | tf_op jit(solution)/shard_map/ppermute | solution.py:38
  69.7 12.2 %shard_map.146 = (f32[32,32,128]{2,1,0:T(8,128)}, f32[32,1,128]{2,1,0:T(1,128)}) custom-call(s32[512]{0:T(512)} %compare_select_fusion.4.station_ref, bf16[512,32,128]{2,1,0:T(8,128)(2,1)} %gather_fusion, bf16[512,32,128]{2,1,0:T(8,128)(2,1)} %bitcast.21.other_ref), custom_call_target="tpu_custom_call" | custom-call | flops 41943040 | bytes 8388608 | tf_op jit(solution)/shard_map/pallas_call | solution.py:140
  83.3 1.9 %collective-permute-start.6 = (f32[3,8,2,128]{3,1,2,0:T(8,128)S(1)}, f32[3,8,2,128]{3,1,2,0:T(8,128)S(1)}, u32[]{:S(2)}, u32[]{:S(2)}) collective-permute-start(f32[3,8,2,128]{3,1,2,0:T(8,128)S(1)} %copy.386), channel_id=1, source_target_pairs={{0,1},{1,2},{2,3},{3,4},{4,5},{5,6},{6,7},{8,9},{9,10},{10,11},{11... | collective-permute-start | bytes 73736 | tf_op jit(solution)/shard_map/ppermute | solution.py:37
  85.3 3.6 %collective-permute-start.7 = (f32[3,8,2,128]{3,1,2,0:T(8,128)S(1)}, f32[3,8,2,128]{3,1,2,0:T(8,128)S(1)}, u32[]{:S(2)}, u32[]{:S(2)}) collective-permute-start(f32[3,8,2,128]{3,1,2,0:T(8,128)S(1)} %copy.387), channel_id=1, source_target_pairs={{1,0},{2,1},{3,2},{4,3},{5,4},{6,5},{7,6},{9,8},{10,9},{11,10},{12... | collective-permute-start | bytes 73736 | tf_op jit(solution)/shard_map/ppermute | solution.py:38
  89.1 2.7 %collective-permute-start.4 = (f32[3,2,16,128]{3,2,1,0:T(8,128)S(1)}, f32[3,2,16,128]{3,2,1,0:T(8,128)S(1)}, u32[]{:S(2)}, u32[]{:S(2)}) collective-permute-start(f32[3,2,16,128]{3,2,1,0:T(8,128)S(1)} %get-tuple-element.127), channel_id=1, source_target_pairs={{0,8},{8,16},{16,24},{24,32},{32,40},{40,48},{48,56},{56,64},{64,7... | collective-permute-start | bytes 147464 | tf_op jit(solution)/shard_map/ppermute | solution.py:37
  91.8 3.2 %collective-permute-start.5 = (f32[3,2,16,128]{3,2,1,0:T(8,128)S(1)}, f32[3,2,16,128]{3,2,1,0:T(8,128)S(1)}, u32[]{:S(2)}, u32[]{:S(2)}) collective-permute-start(f32[3,2,16,128]{3,2,1,0:T(8,128)S(1)} %get-tuple-element.128), channel_id=1, source_target_pairs={{8,0},{16,8},{24,16},{32,24},{40,32},{48,40},{56,48},{64,56},{72,6... | collective-permute-start | bytes 147464 | tf_op jit(solution)/shard_map/ppermute | solution.py:38
  95.2 2.1 %copy.406 = f32[4,8,32,128]{3,1,2,0:T(8,128)} copy(f32[4,8,32,128]{3,2,1,0:T(8,128)} %bitcast.276) | data formatting | bytes 1048576
  97.5 2.4 %collective-permute-done.5 = f32[3,2,16,128]{3,2,1,0:T(8,128)S(1)} collective-permute-done((f32[3,2,16,128]{3,2,1,0:T(8,128)S(1)}, f32[3,2,16,128]{3,2,1,0:T(8,128)S(1)}, u32[]{:S(2)}, u32[]{:S(2)}) %collective-permute-start.5) | collective-permute-done | bytes 49184 | tf_op jit(solution)/shard_map/ppermute | solution.py:38
  100.5 1.9 %collective-permute-start.8 = (f32[3,2,16,128]{3,2,1,0:T(8,128)S(1)}, f32[3,2,16,128]{3,2,1,0:T(8,128)S(1)}, u32[]{:S(2)}, u32[]{:S(2)}) collective-permute-start(f32[3,2,16,128]{3,2,1,0:T(8,128)S(1)} %get-tuple-element.120), channel_id=1, source_target_pairs={{8,0},{16,8},{24,16},{32,24},{40,32},{48,40},{56,48},{64,56},{72,6... | collective-permute-start | bytes 147464 | tf_op jit(solution)/shard_map/ppermute | solution.py:38
  102.5 6.0 %collective-permute-start.9 = (f32[3,2,16,128]{3,2,1,0:T(8,128)S(1)}, f32[3,2,16,128]{3,2,1,0:T(8,128)S(1)}, u32[]{:S(2)}, u32[]{:S(2)}) collective-permute-start(f32[3,2,16,128]{3,2,1,0:T(8,128)S(1)} %get-tuple-element.121), channel_id=1, source_target_pairs={{0,8},{8,16},{16,24},{24,32},{32,40},{40,48},{48,56},{56,64},{64,7... | collective-permute-start | bytes 147464 | tf_op jit(solution)/shard_map/ppermute | solution.py:37
  108.5 1.9 %collective-permute-start.10 = (f32[3,8,2,128]{3,1,2,0:T(8,128)S(1)}, f32[3,8,2,128]{3,1,2,0:T(8,128)S(1)}, u32[]{:S(2)}, u32[]{:S(2)}) collective-permute-start(f32[3,8,2,128]{3,1,2,0:T(8,128)S(1)} %copy.390), channel_id=1, source_target_pairs={{0,1},{1,2},{2,3},{3,4},{4,5},{5,6},{6,7},{8,9},{9,10},{10,11},{11... | collective-permute-start | bytes 73736 | tf_op jit(solution)/shard_map/ppermute | solution.py:37
  110.5 3.6 %collective-permute-start.11 = (f32[3,8,2,128]{3,1,2,0:T(8,128)S(1)}, f32[3,8,2,128]{3,1,2,0:T(8,128)S(1)}, u32[]{:S(2)}, u32[]{:S(2)}) collective-permute-start(f32[3,8,2,128]{3,1,2,0:T(8,128)S(1)} %copy.391), channel_id=1, source_target_pairs={{1,0},{2,1},{3,2},{4,3},{5,4},{6,5},{7,6},{9,8},{10,9},{11,10},{12... | collective-permute-start | bytes 73736 | tf_op jit(solution)/shard_map/ppermute | solution.py:38
  116.5 3.3 %collective-permute-start.14 = (f32[3,8,2,128]{3,1,2,0:T(8,128)S(1)}, f32[3,8,2,128]{3,1,2,0:T(8,128)S(1)}, u32[]{:S(2)}, u32[]{:S(2)}) collective-permute-start(f32[3,8,2,128]{3,1,2,0:T(8,128)S(1)} %copy.396), channel_id=1, source_target_pairs={{0,1},{1,2},{2,3},{3,4},{4,5},{5,6},{6,7},{8,9},{9,10},{10,11},{11... | collective-permute-start | bytes 73736 | tf_op jit(solution)/shard_map/ppermute | solution.py:37
  119.8 2.3 %collective-permute-start.15 = (f32[3,8,2,128]{3,1,2,0:T(8,128)S(1)}, f32[3,8,2,128]{3,1,2,0:T(8,128)S(1)}, u32[]{:S(2)}, u32[]{:S(2)}) collective-permute-start(f32[3,8,2,128]{3,1,2,0:T(8,128)S(1)} %copy.397), channel_id=1, source_target_pairs={{1,0},{2,1},{3,2},{4,3},{5,4},{6,5},{7,6},{9,8},{10,9},{11,10},{12... | collective-permute-start | bytes 73736 | tf_op jit(solution)/shard_map/ppermute | solution.py:38
  124.2 3.9 %collective-permute-start.13 = (f32[3,2,16,128]{3,2,1,0:T(8,128)S(1)}, f32[3,2,16,128]{3,2,1,0:T(8,128)S(1)}, u32[]{:S(2)}, u32[]{:S(2)}) collective-permute-start(f32[3,2,16,128]{3,2,1,0:T(8,128)S(1)} %get-tuple-element.114), channel_id=1, source_target_pairs={{8,0},{16,8},{24,16},{32,24},{40,32},{48,40},{56,48},{64,56},{72,6... | collective-permute-start | bytes 147464 | tf_op jit(solution)/shard_map/ppermute | solution.py:38
  128.2 4.0 %collective-permute-done.13 = f32[3,2,16,128]{3,2,1,0:T(8,128)S(1)} collective-permute-done((f32[3,2,16,128]{3,2,1,0:T(8,128)S(1)}, f32[3,2,16,128]{3,2,1,0:T(8,128)S(1)}, u32[]{:S(2)}, u32[]{:S(2)}) %collective-permute-start.13) | collective-permute-done | bytes 49184 | tf_op jit(solution)/shard_map/ppermute | solution.py:38
  (146 shorter events, 16.8 us)
Async XLA Ops:
  8.3 25.7 %copy-start.8 = (f32[8,16,128]{2,1,0:T(8,128)S(1)}, f32[8,16,128]{2,1,0:T(8,128)}, u32[]{:S(2)}) copy-start(f32[8,16,128]{2,1,0:T(8,128)} %param.19) | copy-start | bytes 196612
  8.3 25.8 %copy-start.4 = (bf16[12,8,16,128]{3,2,1,0:T(8,128)(2,1)S(1)}, bf16[12,8,16,128]{3,2,1,0:T(8,128)(2,1)}, u32[]{:S(2)}) copy-start(bf16[12,8,16,128]{3,2,1,0:T(8,128)(2,1)} %param.20) | copy-start | bytes 1179652
  8.3 61.4 %all-to-all-start = ((bf16[128,4,32,128]{3,2,1,0:T(8,128)(2,1)}), bf16[128,4,32,128]{3,2,1,0:T(8,128)(2,1)}, u32[]{:S(2)}, u32[]{:S(2)}) async-start(bf16[128,4,32,128]{3,2,1,0:T(8,128)(2,1)} %bitcast.271), calls=%async_computation | async-start | bytes 8388608 | tf_op jit(solution)/shard_map/all_to_all | solution.py:189
  19.2 44.9 %collective-permute-start.2 = (f32[3,8,2,128]{3,1,2,0:T(8,128)S(1)}, f32[3,8,2,128]{3,1,2,0:T(8,128)S(1)}, u32[]{:S(2)}, u32[]{:S(2)}) collective-permute-start(f32[3,8,2,128]{3,1,2,0:T(8,128)S(1)} %copy.372), channel_id=1, source_target_pairs={{0,1},{1,2},{2,3},{3,4},{4,5},{5,6},{6,7},{8,9},{9,10},{10,11},{11... | collective-permute-start | bytes 73736 | tf_op jit(solution)/shard_map/ppermute | solution.py:37
  21.3 42.9 %collective-permute-start.3 = (f32[3,8,2,128]{3,1,2,0:T(8,128)S(1)}, f32[3,8,2,128]{3,1,2,0:T(8,128)S(1)}, u32[]{:S(2)}, u32[]{:S(2)}) collective-permute-start(f32[3,8,2,128]{3,1,2,0:T(8,128)S(1)} %copy.373), channel_id=1, source_target_pairs={{1,0},{2,1},{3,2},{4,3},{5,4},{6,5},{7,6},{9,8},{10,9},{11,10},{12... | collective-permute-start | bytes 73736 | tf_op jit(solution)/shard_map/ppermute | solution.py:38
  24.9 42.9 %collective-permute-start = (f32[3,2,16,128]{3,2,1,0:T(8,128)S(1)}, f32[3,2,16,128]{3,2,1,0:T(8,128)S(1)}, u32[]{:S(2)}, u32[]{:S(2)}) collective-permute-start(f32[3,2,16,128]{3,2,1,0:T(8,128)S(1)} %get-tuple-element.133), channel_id=1, source_target_pairs={{8,0},{16,8},{24,16},{32,24},{40,32},{48,40},{56,48},{64,56},{72,6... | collective-permute-start | bytes 147464 | tf_op jit(solution)/shard_map/ppermute | solution.py:38
  27.6 40.2 %collective-permute-start.1 = (f32[3,2,16,128]{3,2,1,0:T(8,128)S(1)}, f32[3,2,16,128]{3,2,1,0:T(8,128)S(1)}, u32[]{:S(2)}, u32[]{:S(2)}) collective-permute-start(f32[3,2,16,128]{3,2,1,0:T(8,128)S(1)} %get-tuple-element.134), channel_id=1, source_target_pairs={{0,8},{8,16},{16,24},{24,32},{32,40},{40,48},{48,56},{56,64},{64,7... | collective-permute-start | bytes 147464 | tf_op jit(solution)/shard_map/ppermute | solution.py:37
  81.8 18.0 %copy-start = (f32[8,16,128]{2,1,0:T(8,128)S(1)}, f32[8,16,128]{2,1,0:T(8,128)}, u32[]{:S(2)}) copy-start(f32[8,16,128]{2,1,0:T(8,128)} %param.18) | copy-start | bytes 196612
  81.8 18.0 %copy-start.5 = (f32[8,16,128]{2,1,0:T(8,128)S(1)}, f32[8,16,128]{2,1,0:T(8,128)}, u32[]{:S(2)}) copy-start(f32[8,16,128]{2,1,0:T(8,128)} %param.17) | copy-start | bytes 196612
  83.3 14.0 %collective-permute-start.6 = (f32[3,8,2,128]{3,1,2,0:T(8,128)S(1)}, f32[3,8,2,128]{3,1,2,0:T(8,128)S(1)}, u32[]{:S(2)}, u32[]{:S(2)}) collective-permute-start(f32[3,8,2,128]{3,1,2,0:T(8,128)S(1)} %copy.386), channel_id=1, source_target_pairs={{0,1},{1,2},{2,3},{3,4},{4,5},{5,6},{6,7},{8,9},{9,10},{10,11},{11... | collective-permute-start | bytes 73736 | tf_op jit(solution)/shard_map/ppermute | solution.py:37
  85.3 12.0 %collective-permute-start.7 = (f32[3,8,2,128]{3,1,2,0:T(8,128)S(1)}, f32[3,8,2,128]{3,1,2,0:T(8,128)S(1)}, u32[]{:S(2)}, u32[]{:S(2)}) collective-permute-start(f32[3,8,2,128]{3,1,2,0:T(8,128)S(1)} %copy.387), channel_id=1, source_target_pairs={{1,0},{2,1},{3,2},{4,3},{5,4},{6,5},{7,6},{9,8},{10,9},{11,10},{12... | collective-permute-start | bytes 73736 | tf_op jit(solution)/shard_map/ppermute | solution.py:38
  89.1 8.3 %collective-permute-start.4 = (f32[3,2,16,128]{3,2,1,0:T(8,128)S(1)}, f32[3,2,16,128]{3,2,1,0:T(8,128)S(1)}, u32[]{:S(2)}, u32[]{:S(2)}) collective-permute-start(f32[3,2,16,128]{3,2,1,0:T(8,128)S(1)} %get-tuple-element.127), channel_id=1, source_target_pairs={{0,8},{8,16},{16,24},{24,32},{32,40},{40,48},{48,56},{56,64},{64,7... | collective-permute-start | bytes 147464 | tf_op jit(solution)/shard_map/ppermute | solution.py:37
  91.8 8.1 %collective-permute-start.5 = (f32[3,2,16,128]{3,2,1,0:T(8,128)S(1)}, f32[3,2,16,128]{3,2,1,0:T(8,128)S(1)}, u32[]{:S(2)}, u32[]{:S(2)}) collective-permute-start(f32[3,2,16,128]{3,2,1,0:T(8,128)S(1)} %get-tuple-element.128), channel_id=1, source_target_pairs={{8,0},{16,8},{24,16},{32,24},{40,32},{48,40},{56,48},{64,56},{72,6... | collective-permute-start | bytes 147464 | tf_op jit(solution)/shard_map/ppermute | solution.py:38
  100.5 15.2 %collective-permute-start.8 = (f32[3,2,16,128]{3,2,1,0:T(8,128)S(1)}, f32[3,2,16,128]{3,2,1,0:T(8,128)S(1)}, u32[]{:S(2)}, u32[]{:S(2)}) collective-permute-start(f32[3,2,16,128]{3,2,1,0:T(8,128)S(1)} %get-tuple-element.120), channel_id=1, source_target_pairs={{8,0},{16,8},{24,16},{32,24},{40,32},{48,40},{56,48},{64,56},{72,6... | collective-permute-start | bytes 147464 | tf_op jit(solution)/shard_map/ppermute | solution.py:38
  102.5 13.3 %collective-permute-start.9 = (f32[3,2,16,128]{3,2,1,0:T(8,128)S(1)}, f32[3,2,16,128]{3,2,1,0:T(8,128)S(1)}, u32[]{:S(2)}, u32[]{:S(2)}) collective-permute-start(f32[3,2,16,128]{3,2,1,0:T(8,128)S(1)} %get-tuple-element.121), channel_id=1, source_target_pairs={{0,8},{8,16},{16,24},{24,32},{32,40},{40,48},{48,56},{56,64},{64,7... | collective-permute-start | bytes 147464 | tf_op jit(solution)/shard_map/ppermute | solution.py:37
  108.5 5.8 %collective-permute-start.10 = (f32[3,8,2,128]{3,1,2,0:T(8,128)S(1)}, f32[3,8,2,128]{3,1,2,0:T(8,128)S(1)}, u32[]{:S(2)}, u32[]{:S(2)}) collective-permute-start(f32[3,8,2,128]{3,1,2,0:T(8,128)S(1)} %copy.390), channel_id=1, source_target_pairs={{0,1},{1,2},{2,3},{3,4},{4,5},{5,6},{6,7},{8,9},{9,10},{10,11},{11... | collective-permute-start | bytes 73736 | tf_op jit(solution)/shard_map/ppermute | solution.py:37
  110.5 5.1 %collective-permute-start.11 = (f32[3,8,2,128]{3,1,2,0:T(8,128)S(1)}, f32[3,8,2,128]{3,1,2,0:T(8,128)S(1)}, u32[]{:S(2)}, u32[]{:S(2)}) collective-permute-start(f32[3,8,2,128]{3,1,2,0:T(8,128)S(1)} %copy.391), channel_id=1, source_target_pairs={{1,0},{2,1},{3,2},{4,3},{5,4},{6,5},{7,6},{9,8},{10,9},{11,10},{12... | collective-permute-start | bytes 73736 | tf_op jit(solution)/shard_map/ppermute | solution.py:38
  114.3 17.9 %copy-start.6 = (f32[8,16,128]{2,1,0:T(8,128)S(1)}, f32[8,16,128]{2,1,0:T(8,128)}, u32[]{:S(2)}) copy-start(f32[8,16,128]{2,1,0:T(8,128)} %param.22) | copy-start | bytes 196612
  116.0 17.2 %copy-start.7 = (f32[8,16,128]{2,1,0:T(8,128)S(1)}, f32[8,16,128]{2,1,0:T(8,128)}, u32[]{:S(2)}) copy-start(f32[8,16,128]{2,1,0:T(8,128)} %param.21) | copy-start | bytes 196612
  116.4 17.6 %copy-start.1 = (f32[3,8,16,128]{3,2,1,0:T(8,128)}, f32[3,8,16,128]{3,2,1,0:T(8,128)S(1)}, u32[]{:S(2)}) copy-start(f32[3,8,16,128]{3,2,1,0:T(8,128)S(1)} %fusion.2) | copy-start | bytes 589828
  116.5 11.6 %collective-permute-start.14 = (f32[3,8,2,128]{3,1,2,0:T(8,128)S(1)}, f32[3,8,2,128]{3,1,2,0:T(8,128)S(1)}, u32[]{:S(2)}, u32[]{:S(2)}) collective-permute-start(f32[3,8,2,128]{3,1,2,0:T(8,128)S(1)} %copy.396), channel_id=1, source_target_pairs={{0,1},{1,2},{2,3},{3,4},{4,5},{5,6},{6,7},{8,9},{9,10},{10,11},{11... | collective-permute-start | bytes 73736 | tf_op jit(solution)/shard_map/ppermute | solution.py:37
  119.8 8.3 %collective-permute-start.15 = (f32[3,8,2,128]{3,1,2,0:T(8,128)S(1)}, f32[3,8,2,128]{3,1,2,0:T(8,128)S(1)}, u32[]{:S(2)}, u32[]{:S(2)}) collective-permute-start(f32[3,8,2,128]{3,1,2,0:T(8,128)S(1)} %copy.397), channel_id=1, source_target_pairs={{1,0},{2,1},{3,2},{4,3},{5,4},{6,5},{7,6},{9,8},{10,9},{11,10},{12... | collective-permute-start | bytes 73736 | tf_op jit(solution)/shard_map/ppermute | solution.py:38
  122.2 6.0 %collective-permute-start.12 = (f32[3,2,16,128]{3,2,1,0:T(8,128)S(1)}, f32[3,2,16,128]{3,2,1,0:T(8,128)S(1)}, u32[]{:S(2)}, u32[]{:S(2)}) collective-permute-start(f32[3,2,16,128]{3,2,1,0:T(8,128)S(1)} %get-tuple-element.115), channel_id=1, source_target_pairs={{0,8},{8,16},{16,24},{24,32},{32,40},{40,48},{48,56},{56,64},{64,7... | collective-permute-start | bytes 147464 | tf_op jit(solution)/shard_map/ppermute | solution.py:37
  124.2 8.1 %collective-permute-start.13 = (f32[3,2,16,128]{3,2,1,0:T(8,128)S(1)}, f32[3,2,16,128]{3,2,1,0:T(8,128)S(1)}, u32[]{:S(2)}, u32[]{:S(2)}) collective-permute-start(f32[3,2,16,128]{3,2,1,0:T(8,128)S(1)} %get-tuple-element.114), channel_id=1, source_target_pairs={{8,0},{16,8},{24,16},{32,24},{40,32},{48,40},{56,48},{64,56},{72,6... | collective-permute-start | bytes 147464 | tf_op jit(solution)/shard_map/ppermute | solution.py:38
  (3 other events, 37.5 us)

commit v12 on v10

--- a/solution.py
+++ b/solution.py
@@ -93,7 +93,7 @@
     return (moved, grown, lame_kernel, shear_kernel)
 
 
-def pair_kernel(block, samples, station_ref, mine_ref, other_ref, out_ref, acc_ref, toward_ref):
+def pair_kernel(block, samples, station_ref, mine_ref, other_ref, mine_sq_ref, out_ref, acc_ref, toward_ref):
     step = pl.program_id(0)
 
     @pl.when(step == 0)
@@ -102,15 +102,13 @@
 
     mine_vals = mine_ref[...].astype(jnp.float32)
     other_vals = other_ref[...].astype(jnp.float32)
-    mine_sq = jnp.sum(jnp.sum(mine_vals * mine_vals, axis=1, keepdims=True), axis=2, keepdims=True)
+    mine_sq = mine_sq_ref[...][:, :, :1]
     other_sq = jnp.sum(jnp.sum(other_vals * other_vals, axis=1, keepdims=True), axis=2, keepdims=True)
     cross = jnp.sum(jnp.sum(mine_vals * other_vals, axis=1, keepdims=True), axis=2, keepdims=True)
     mine_norm = jnp.sqrt(mine_sq / samples + epsilon)
     other_norm = jnp.sqrt(other_sq / samples + epsilon)
     corr = (cross / samples) / (mine_norm * other_norm)
-    other_scale = 1.0 / other_norm
-    mine_scale = corr / mine_norm
-    toward = other_vals * other_scale - mine_scale * mine_vals
+    toward = other_vals / other_norm - corr * (mine_vals / mine_norm)
     toward_ref[...] = toward.astype(jnp.bfloat16).astype(jnp.float32)
 
     ways = acc_ref.shape[0]
@@ -133,9 +131,9 @@
         out_ref[...] = total
 
 
-def pair_sums(targets, mine, other, stations):
+def pair_sums(targets, mine, other, mine_sq, stations):
     slots, rows, lanes = mine.shape
-    block = 128
+    block = 64
     samples = rows * lanes
     spec = pl.BlockSpec((block, rows, lanes), lambda g, t: (g, 0, 0))
     return pl.pallas_call(
@@ -143,7 +141,7 @@
         grid_spec=pltpu.PrefetchScalarGridSpec(
             num_scalar_prefetch=1,
             grid=(slots // block,),
-            in_specs=[spec, spec],
+            in_specs=[spec, spec, pl.BlockSpec((block, 1, lanes), lambda g, t: (g, 0, 0))],
             out_specs=pl.BlockSpec((stations, rows, lanes), lambda g, t: (0, 0, 0)),
             scratch_shapes=[
                 pltpu.VMEM((4, stations + 1, rows, lanes), jnp.float32),
@@ -153,7 +151,7 @@
         out_shape=jax.ShapeDtypeStruct((stations, rows, lanes), jnp.float32),
         compiler_params=pltpu.CompilerParams(dimension_semantics=("arbitrary",)),
         cost_estimate=pl.CostEstimate(flops=20 * slots * samples, transcendentals=0, bytes_accessed=4 * slots * samples),
-    )(targets, mine, other)
+    )(targets, mine, other, mine_sq)
 
 
 def station_part(residuals, station_cell, station_pairs, cells_first, cells_second, step_count):
@@ -186,8 +184,11 @@
     mine = padded_rows[jnp.where(mine_station >= 0, mine_station, stations_here)]
     slots = devices * 4
     targets = jnp.where(mine_station >= 0, mine_station, stations_here).reshape(slots)
+    row_vals = padded_rows.astype(jnp.float32)
+    station_sq = jnp.sum(jnp.sum(row_vals * row_vals, axis=1), axis=1)
+    slot_sq = jnp.broadcast_to(station_sq[targets][:, None, None], (slots, 1, lanes))
     adjoint3 = pair_sums(
-        targets, mine.reshape(slots, samples // lanes, lanes), recv.reshape(slots, samples // lanes, lanes), stations_here
+        targets, mine.reshape(slots, samples // lanes, lanes), recv.reshape(slots, samples // lanes, lanes), slot_sq, stations_here
     )
     adjoint = adjoint3.reshape(stations_here, samples)
     last = adjoint3[:, samples // lanes - 1, lanes - step_count :]

time: 135 us -> 138 us (1.022); the launches traced: 135 us -> 136 us
  waiting for transfers between devices: 39.1 us -> 16.4 us
  other arithmetic: 6.16 us -> 27.1 us
  local copies, waits for them, and re-layouts: 15.4 us -> 18.2 us
    ppermute x8, waiting for transfers between devices: 26.5 us -> 3.78 us  [halo_pad(): lax.ppermute(lax.slice_in_dim(block, size - width, size, axis=dim), axis,...]
    gather x0 -> x3, other arithmetic: none -> 20.7 us  [station_part(): station_sq[targets][:, None, None]]
    gather x0 -> x2, local copies, waits for them, and re-layouts: none -> 1.44 us  [station_part(): station_sq[targets][:, None, None]]
  transfers between devices with their start and end apart: 17 -> 17, of which waited for: 6 -> 6; matrix products, arithmetic and copies ran while one was open for 6% -> 23% of each run, Pallas kernels for 0% -> 0%
where the time goes in v12:
time: 138 us; the launch traced here: 136 us
  starting transfers between devices  60.8 us (44%)
  other arithmetic  27.1 us (20%)
  local copies, waits for them, and re-layouts  18.2 us (13%)
  waiting for transfers between devices  16.4 us (12%)
  Pallas kernels  12.3 us (9%)
  between operations  1.61 us (1%)
    ppermute x8, starting transfers between devices, halo_pad(): lax.ppermute(lax.slice_in_dim(block, size - width, size, axis=dim), axis,...  25.1 us
    ppermute x8, starting transfers between devices, halo_pad(): lax.ppermute(lax.slice_in_dim(block, 0, width, axis=dim), axis, backward)  24.9 us
    gather x3, other arithmetic, station_part(): station_sq[targets][:, None, None]  20.7 us
    pallas_call x1, Pallas kernels, pair_sums(): pl.pallas_call(functools.partial(pair_kernel, block, float(samples)), gri...  12.3 us
    ppermute x8, waiting for transfers between devices, halo_pad(): lax.ppermute(lax.slice_in_dim(block, 0, width, axis=dim), axis, backward)  11.2 us
    all_to_all x1, starting transfers between devices, station_part(): lax.all_to_all(send, ('gx', 'gy'), split_axis=0, concat_axis=0, tiled=True)  10.8 us
    unnamed x24, local copies, waits for them, and re-layouts  4.19 us
    ppermute x8, waiting for transfers between devices, halo_pad(): lax.ppermute(lax.slice_in_dim(block, size - width, size, axis=dim), axis,...  3.78 us
  transfers between devices with their start and end apart: 17, of which 6 were waited for; matrix products, arithmetic and copies ran while one was open for 23% of the time, Pallas kernels for 0%

profile of v12, /device:TPU:14, one launch (start us, length us, event | category | flops | bytes accessed | tf_op | source)
XLA Modules:
  0.0 136.3 jit_solution(12588228414377927776)
XLA Ops:
  4.7 3.5 %gather_fusion.1 = bf16[512,32,128]{2,1,0:T(8,128)(2,1)} fusion(bf16[33,32,128]{2,1,0:T(8,128)(2,1)S(1)} %concatenate.122, s32[1024]{0:T(1024)S(1)} %pad_clamp_fusion), kind=kCustom, calls=%fused_computation.1 | custom fusion | bytes 8390656 | tf_op jit(solution)/shard_map/gather | solution.py:181
  8.2 10.8 %all-to-all-start = ((bf16[128,4,32,128]{3,2,1,0:T(8,128)(2,1)}), bf16[128,4,32,128]{3,2,1,0:T(8,128)(2,1)}, u32[]{:S(2)}, u32[]{:S(2)}) async-start(bf16[128,4,32,128]{3,2,1,0:T(8,128)(2,1)} %bitcast.305), calls=%async_computation | async-start | bytes 8388608 | tf_op jit(solution)/shard_map/all_to_all | solution.py:182
  19.2 2.2 %collective-permute-start.2 = (f32[3,8,2,128]{3,1,2,0:T(8,128)S(1)}, f32[3,8,2,128]{3,1,2,0:T(8,128)S(1)}, u32[]{:S(2)}, u32[]{:S(2)}) collective-permute-start(f32[3,8,2,128]{3,1,2,0:T(8,128)S(1)} %copy.375), channel_id=1, source_target_pairs={{0,1},{1,2},{2,3},{3,4},{4,5},{5,6},{6,7},{8,9},{9,10},{10,11},{11... | collective-permute-start | bytes 73736 | tf_op jit(solution)/shard_map/ppermute | solution.py:37
  21.3 3.5 %collective-permute-start.3 = (f32[3,8,2,128]{3,1,2,0:T(8,128)S(1)}, f32[3,8,2,128]{3,1,2,0:T(8,128)S(1)}, u32[]{:S(2)}, u32[]{:S(2)}) collective-permute-start(f32[3,8,2,128]{3,1,2,0:T(8,128)S(1)} %copy.376), channel_id=1, source_target_pairs={{1,0},{2,1},{3,2},{4,3},{5,4},{6,5},{7,6},{9,8},{10,9},{11,10},{12... | collective-permute-start | bytes 73736 | tf_op jit(solution)/shard_map/ppermute | solution.py:38
  24.9 2.8 %collective-permute-start = (f32[3,2,16,128]{3,2,1,0:T(8,128)S(1)}, f32[3,2,16,128]{3,2,1,0:T(8,128)S(1)}, u32[]{:S(2)}, u32[]{:S(2)}) collective-permute-start(f32[3,2,16,128]{3,2,1,0:T(8,128)S(1)} %get-tuple-element.157), channel_id=1, source_target_pairs={{8,0},{16,8},{24,16},{32,24},{40,32},{48,40},{56,48},{64,56},{72,6... | collective-permute-start | bytes 147464 | tf_op jit(solution)/shard_map/ppermute | solution.py:38
  27.7 5.2 %collective-permute-start.1 = (f32[3,2,16,128]{3,2,1,0:T(8,128)S(1)}, f32[3,2,16,128]{3,2,1,0:T(8,128)S(1)}, u32[]{:S(2)}, u32[]{:S(2)}) collective-permute-start(f32[3,2,16,128]{3,2,1,0:T(8,128)S(1)} %get-tuple-element.158), channel_id=1, source_target_pairs={{0,8},{8,16},{16,24},{24,32},{32,40},{40,48},{48,56},{56,64},{64,7... | collective-permute-start | bytes 147464 | tf_op jit(solution)/shard_map/ppermute | solution.py:37
  35.2 4.3 %compare_select_fusion.2 = (f32[512,1]{0,1:T(1,128)S(1)}, s32[512,1]{0,1:T(1,128)S(1)}) fusion(f32[]{:T(128)} %bitcast.48, f32[]{:T(128)} %bitcast.49, f32[]{:T(128)} %bitcast.50, f32[]{:T(128)} %bitcast.51, f32[]{:T(128)} %bitcast.52, f32[]{:T(128)} %bitcast.54, f32[]{:T(128)} %bitcast.53, s32[512,1]{0,1:T(1,128)S(1)} %concatenate.127), kind=kLoop, calls=%fused_computation.427 | loop fusion | flops 8704 | bytes 6172 | tf_op jit(solution)/shard_map/gather | solution.py:189
  40.5 16.2 %select_select_fusion = f32[512]{0:T(512)S(1)} fusion(pred[512]{0:T(512)(128)(4,1)S(1)} %get-tuple-element.74, pred[512]{0:T(512)(128)(4,1)S(1)} %get-tuple-element.73, pred[512]{0:T(512)(128)(4,1)S(1)} %get-tuple-element.72, pred[512]{0:T(512)(128)(4,1)S(1)} %get-tuple-element.71, pred[512]{0:T(512)(128)(4,1)S(1)} %get-tuple-element.70, ...), kind=kLoop, calls=%fused_computation.441 | loop fusion | flops 13312 | bytes 17512 | tf_op jit(solution)/shard_map/gather | solution.py:189
  56.8 3.5 %gather_fusion = bf16[512,32,128]{2,1,0:T(8,128)(2,1)} fusion(bf16[33,32,128]{2,1,0:T(8,128)(2,1)S(1)} %concatenate.122, s32[1024]{0:T(1024)S(1)} %pad_clamp_fusion.1), kind=kCustom, calls=%fused_computation | custom fusion | bytes 8390656 | tf_op jit(solution)/shard_map/gather | solution.py:184
  60.3 3.8 %collective-permute-done.2 = f32[3,8,2,128]{3,1,2,0:T(8,128)S(1)} collective-permute-done((f32[3,8,2,128]{3,1,2,0:T(8,128)S(1)}, f32[3,8,2,128]{3,1,2,0:T(8,128)S(1)}, u32[]{:S(2)}, u32[]{:S(2)}) %collective-permute-start.2) | collective-permute-done | bytes 24608 | tf_op jit(solution)/shard_map/ppermute | solution.py:37
  64.2 3.5 %collective-permute-done = f32[3,2,16,128]{3,2,1,0:T(8,128)S(1)} collective-permute-done((f32[3,2,16,128]{3,2,1,0:T(8,128)S(1)}, f32[3,2,16,128]{3,2,1,0:T(8,128)S(1)}, u32[]{:S(2)}, u32[]{:S(2)}) %collective-permute-start) | collective-permute-done | bytes 49184 | tf_op jit(solution)/shard_map/ppermute | solution.py:38
  70.9 12.3 %shard_map.146 = f32[32,32,128]{2,1,0:T(8,128)} custom-call(s32[512]{0:T(512)} %compare_select_fusion.12.station_ref, bf16[512,32,128]{2,1,0:T(8,128)(2,1)} %gather_fusion, bf16[512,32,128]{2,1,0:T(8,128)(2,1)} %bitcast.21.other_ref, f32[512,1,128]{2,1,0:T(1,128)} %broadcast_in_dim.68.mine_sq_ref), custom_call_target="tpu_custom_call" | custom-call | flops 41943040 | bytes 8388608 | tf_op jit(solution)/shard_map/pallas_call | solution.py:139
  86.8 3.6 %collective-permute-start.7 = (f32[3,8,2,128]{3,1,2,0:T(8,128)S(1)}, f32[3,8,2,128]{3,1,2,0:T(8,128)S(1)}, u32[]{:S(2)}, u32[]{:S(2)}) collective-permute-start(f32[3,8,2,128]{3,1,2,0:T(8,128)S(1)} %copy.391), channel_id=1, source_target_pairs={{1,0},{2,1},{3,2},{4,3},{5,4},{6,5},{7,6},{9,8},{10,9},{11,10},{12... | collective-permute-start | bytes 73736 | tf_op jit(solution)/shard_map/ppermute | solution.py:38
  90.6 2.7 %collective-permute-start.4 = (f32[3,2,16,128]{3,2,1,0:T(8,128)S(1)}, f32[3,2,16,128]{3,2,1,0:T(8,128)S(1)}, u32[]{:S(2)}, u32[]{:S(2)}) collective-permute-start(f32[3,2,16,128]{3,2,1,0:T(8,128)S(1)} %get-tuple-element.151), channel_id=1, source_target_pairs={{0,8},{8,16},{16,24},{24,32},{32,40},{40,48},{48,56},{56,64},{64,7... | collective-permute-start | bytes 147464 | tf_op jit(solution)/shard_map/ppermute | solution.py:37
  93.3 3.2 %collective-permute-start.5 = (f32[3,2,16,128]{3,2,1,0:T(8,128)S(1)}, f32[3,2,16,128]{3,2,1,0:T(8,128)S(1)}, u32[]{:S(2)}, u32[]{:S(2)}) collective-permute-start(f32[3,2,16,128]{3,2,1,0:T(8,128)S(1)} %get-tuple-element.152), channel_id=1, source_target_pairs={{8,0},{16,8},{24,16},{32,24},{40,32},{48,40},{56,48},{64,56},{72,6... | collective-permute-start | bytes 147464 | tf_op jit(solution)/shard_map/ppermute | solution.py:38
  96.7 2.1 %copy.410 = f32[4,8,32,128]{3,1,2,0:T(8,128)} copy(f32[4,8,32,128]{3,2,1,0:T(8,128)} %bitcast.308) | data formatting | bytes 1048576
  99.0 2.4 %collective-permute-done.5 = f32[3,2,16,128]{3,2,1,0:T(8,128)S(1)} collective-permute-done((f32[3,2,16,128]{3,2,1,0:T(8,128)S(1)}, f32[3,2,16,128]{3,2,1,0:T(8,128)S(1)}, u32[]{:S(2)}, u32[]{:S(2)}) %collective-permute-start.5) | collective-permute-done | bytes 49184 | tf_op jit(solution)/shard_map/ppermute | solution.py:38
  104.0 6.0 %collective-permute-start.9 = (f32[3,2,16,128]{3,2,1,0:T(8,128)S(1)}, f32[3,2,16,128]{3,2,1,0:T(8,128)S(1)}, u32[]{:S(2)}, u32[]{:S(2)}) collective-permute-start(f32[3,2,16,128]{3,2,1,0:T(8,128)S(1)} %get-tuple-element.145), channel_id=1, source_target_pairs={{0,8},{8,16},{16,24},{24,32},{32,40},{40,48},{48,56},{56,64},{64,7... | collective-permute-start | bytes 147464 | tf_op jit(solution)/shard_map/ppermute | solution.py:37
  110.0 1.9 %collective-permute-start.10 = (f32[3,8,2,128]{3,1,2,0:T(8,128)S(1)}, f32[3,8,2,128]{3,1,2,0:T(8,128)S(1)}, u32[]{:S(2)}, u32[]{:S(2)}) collective-permute-start(f32[3,8,2,128]{3,1,2,0:T(8,128)S(1)} %copy.394), channel_id=1, source_target_pairs={{0,1},{1,2},{2,3},{3,4},{4,5},{5,6},{6,7},{8,9},{9,10},{10,11},{11... | collective-permute-start | bytes 73736 | tf_op jit(solution)/shard_map/ppermute | solution.py:37
  112.0 3.6 %collective-permute-start.11 = (f32[3,8,2,128]{3,1,2,0:T(8,128)S(1)}, f32[3,8,2,128]{3,1,2,0:T(8,128)S(1)}, u32[]{:S(2)}, u32[]{:S(2)}) collective-permute-start(f32[3,8,2,128]{3,1,2,0:T(8,128)S(1)} %copy.395), channel_id=1, source_target_pairs={{1,0},{2,1},{3,2},{4,3},{5,4},{6,5},{7,6},{9,8},{10,9},{11,10},{12... | collective-permute-start | bytes 73736 | tf_op jit(solution)/shard_map/ppermute | solution.py:38
  118.0 3.3 %collective-permute-start.14 = (f32[3,8,2,128]{3,1,2,0:T(8,128)S(1)}, f32[3,8,2,128]{3,1,2,0:T(8,128)S(1)}, u32[]{:S(2)}, u32[]{:S(2)}) collective-permute-start(f32[3,8,2,128]{3,1,2,0:T(8,128)S(1)} %copy.400), channel_id=1, source_target_pairs={{0,1},{1,2},{2,3},{3,4},{4,5},{5,6},{6,7},{8,9},{9,10},{10,11},{11... | collective-permute-start | bytes 73736 | tf_op jit(solution)/shard_map/ppermute | solution.py:37
  121.3 2.3 %collective-permute-start.15 = (f32[3,8,2,128]{3,1,2,0:T(8,128)S(1)}, f32[3,8,2,128]{3,1,2,0:T(8,128)S(1)}, u32[]{:S(2)}, u32[]{:S(2)}) collective-permute-start(f32[3,8,2,128]{3,1,2,0:T(8,128)S(1)} %copy.401), channel_id=1, source_target_pairs={{1,0},{2,1},{3,2},{4,3},{5,4},{6,5},{7,6},{9,8},{10,9},{11,10},{12... | collective-permute-start | bytes 73736 | tf_op jit(solution)/shard_map/ppermute | solution.py:38
  125.6 3.9 %collective-permute-start.13 = (f32[3,2,16,128]{3,2,1,0:T(8,128)S(1)}, f32[3,2,16,128]{3,2,1,0:T(8,128)S(1)}, u32[]{:S(2)}, u32[]{:S(2)}) collective-permute-start(f32[3,2,16,128]{3,2,1,0:T(8,128)S(1)} %get-tuple-element.138), channel_id=1, source_target_pairs={{8,0},{16,8},{24,16},{32,24},{40,32},{48,40},{56,48},{64,56},{72,6... | collective-permute-start | bytes 147464 | tf_op jit(solution)/shard_map/ppermute | solution.py:38
  129.7 4.0 %collective-permute-done.13 = f32[3,2,16,128]{3,2,1,0:T(8,128)S(1)} collective-permute-done((f32[3,2,16,128]{3,2,1,0:T(8,128)S(1)}, f32[3,2,16,128]{3,2,1,0:T(8,128)S(1)}, u32[]{:S(2)}, u32[]{:S(2)}) %collective-permute-start.13) | collective-permute-done | bytes 49184 | tf_op jit(solution)/shard_map/ppermute | solution.py:38
  (154 shorter events, 24.1 us)
Async XLA Ops:
  8.2 48.4 %copy-start.8 = (f32[8,16,128]{2,1,0:T(8,128)S(1)}, f32[8,16,128]{2,1,0:T(8,128)}, u32[]{:S(2)}) copy-start(f32[8,16,128]{2,1,0:T(8,128)} %param.19) | copy-start | bytes 196612
  8.2 61.4 %all-to-all-start = ((bf16[128,4,32,128]{3,2,1,0:T(8,128)(2,1)}), bf16[128,4,32,128]{3,2,1,0:T(8,128)(2,1)}, u32[]{:S(2)}, u32[]{:S(2)}) async-start(bf16[128,4,32,128]{3,2,1,0:T(8,128)(2,1)} %bitcast.305), calls=%async_computation | async-start | bytes 8388608 | tf_op jit(solution)/shard_map/all_to_all | solution.py:182
  19.1 37.7 %copy-start.4 = (bf16[12,8,16,128]{3,2,1,0:T(8,128)(2,1)S(1)}, bf16[12,8,16,128]{3,2,1,0:T(8,128)(2,1)}, u32[]{:S(2)}) copy-start(bf16[12,8,16,128]{3,2,1,0:T(8,128)(2,1)} %param.20) | copy-start | bytes 1179652
  19.2 44.9 %collective-permute-start.2 = (f32[3,8,2,128]{3,1,2,0:T(8,128)S(1)}, f32[3,8,2,128]{3,1,2,0:T(8,128)S(1)}, u32[]{:S(2)}, u32[]{:S(2)}) collective-permute-start(f32[3,8,2,128]{3,1,2,0:T(8,128)S(1)} %copy.375), channel_id=1, source_target_pairs={{0,1},{1,2},{2,3},{3,4},{4,5},{5,6},{6,7},{8,9},{9,10},{10,11},{11... | collective-permute-start | bytes 73736 | tf_op jit(solution)/shard_map/ppermute | solution.py:37
  21.3 42.8 %collective-permute-start.3 = (f32[3,8,2,128]{3,1,2,0:T(8,128)S(1)}, f32[3,8,2,128]{3,1,2,0:T(8,128)S(1)}, u32[]{:S(2)}, u32[]{:S(2)}) collective-permute-start(f32[3,8,2,128]{3,1,2,0:T(8,128)S(1)} %copy.376), channel_id=1, source_target_pairs={{1,0},{2,1},{3,2},{4,3},{5,4},{6,5},{7,6},{9,8},{10,9},{11,10},{12... | collective-permute-start | bytes 73736 | tf_op jit(solution)/shard_map/ppermute | solution.py:38
  24.9 42.8 %collective-permute-start = (f32[3,2,16,128]{3,2,1,0:T(8,128)S(1)}, f32[3,2,16,128]{3,2,1,0:T(8,128)S(1)}, u32[]{:S(2)}, u32[]{:S(2)}) collective-permute-start(f32[3,2,16,128]{3,2,1,0:T(8,128)S(1)} %get-tuple-element.157), channel_id=1, source_target_pairs={{8,0},{16,8},{24,16},{32,24},{40,32},{48,40},{56,48},{64,56},{72,6... | collective-permute-start | bytes 147464 | tf_op jit(solution)/shard_map/ppermute | solution.py:38
  27.7 40.0 %collective-permute-start.1 = (f32[3,2,16,128]{3,2,1,0:T(8,128)S(1)}, f32[3,2,16,128]{3,2,1,0:T(8,128)S(1)}, u32[]{:S(2)}, u32[]{:S(2)}) collective-permute-start(f32[3,2,16,128]{3,2,1,0:T(8,128)S(1)} %get-tuple-element.158), channel_id=1, source_target_pairs={{0,8},{8,16},{16,24},{24,32},{32,40},{40,48},{48,56},{56,64},{64,7... | collective-permute-start | bytes 147464 | tf_op jit(solution)/shard_map/ppermute | solution.py:37
  83.2 18.2 %copy-start = (f32[8,16,128]{2,1,0:T(8,128)S(1)}, f32[8,16,128]{2,1,0:T(8,128)}, u32[]{:S(2)}) copy-start(f32[8,16,128]{2,1,0:T(8,128)} %param.18) | copy-start | bytes 196612
  83.2 18.2 %copy-start.5 = (f32[8,16,128]{2,1,0:T(8,128)S(1)}, f32[8,16,128]{2,1,0:T(8,128)}, u32[]{:S(2)}) copy-start(f32[8,16,128]{2,1,0:T(8,128)} %param.17) | copy-start | bytes 196612
  84.8 14.0 %collective-permute-start.6 = (f32[3,8,2,128]{3,1,2,0:T(8,128)S(1)}, f32[3,8,2,128]{3,1,2,0:T(8,128)S(1)}, u32[]{:S(2)}, u32[]{:S(2)}) collective-permute-start(f32[3,8,2,128]{3,1,2,0:T(8,128)S(1)} %copy.390), channel_id=1, source_target_pairs={{0,1},{1,2},{2,3},{3,4},{4,5},{5,6},{6,7},{8,9},{9,10},{10,11},{11... | collective-permute-start | bytes 73736 | tf_op jit(solution)/shard_map/ppermute | solution.py:37
  86.8 12.0 %collective-permute-start.7 = (f32[3,8,2,128]{3,1,2,0:T(8,128)S(1)}, f32[3,8,2,128]{3,1,2,0:T(8,128)S(1)}, u32[]{:S(2)}, u32[]{:S(2)}) collective-permute-start(f32[3,8,2,128]{3,1,2,0:T(8,128)S(1)} %copy.391), channel_id=1, source_target_pairs={{1,0},{2,1},{3,2},{4,3},{5,4},{6,5},{7,6},{9,8},{10,9},{11,10},{12... | collective-permute-start | bytes 73736 | tf_op jit(solution)/shard_map/ppermute | solution.py:38
  90.6 8.3 %collective-permute-start.4 = (f32[3,2,16,128]{3,2,1,0:T(8,128)S(1)}, f32[3,2,16,128]{3,2,1,0:T(8,128)S(1)}, u32[]{:S(2)}, u32[]{:S(2)}) collective-permute-start(f32[3,2,16,128]{3,2,1,0:T(8,128)S(1)} %get-tuple-element.151), channel_id=1, source_target_pairs={{0,8},{8,16},{16,24},{24,32},{32,40},{40,48},{48,56},{56,64},{64,7... | collective-permute-start | bytes 147464 | tf_op jit(solution)/shard_map/ppermute | solution.py:37
  93.3 8.1 %collective-permute-start.5 = (f32[3,2,16,128]{3,2,1,0:T(8,128)S(1)}, f32[3,2,16,128]{3,2,1,0:T(8,128)S(1)}, u32[]{:S(2)}, u32[]{:S(2)}) collective-permute-start(f32[3,2,16,128]{3,2,1,0:T(8,128)S(1)} %get-tuple-element.152), channel_id=1, source_target_pairs={{8,0},{16,8},{24,16},{32,24},{40,32},{48,40},{56,48},{64,56},{72,6... | collective-permute-start | bytes 147464 | tf_op jit(solution)/shard_map/ppermute | solution.py:38
  102.0 15.2 %collective-permute-start.8 = (f32[3,2,16,128]{3,2,1,0:T(8,128)S(1)}, f32[3,2,16,128]{3,2,1,0:T(8,128)S(1)}, u32[]{:S(2)}, u32[]{:S(2)}) collective-permute-start(f32[3,2,16,128]{3,2,1,0:T(8,128)S(1)} %get-tuple-element.144), channel_id=1, source_target_pairs={{8,0},{16,8},{24,16},{32,24},{40,32},{48,40},{56,48},{64,56},{72,6... | collective-permute-start | bytes 147464 | tf_op jit(solution)/shard_map/ppermute | solution.py:38
  104.0 13.3 %collective-permute-start.9 = (f32[3,2,16,128]{3,2,1,0:T(8,128)S(1)}, f32[3,2,16,128]{3,2,1,0:T(8,128)S(1)}, u32[]{:S(2)}, u32[]{:S(2)}) collective-permute-start(f32[3,2,16,128]{3,2,1,0:T(8,128)S(1)} %get-tuple-element.145), channel_id=1, source_target_pairs={{0,8},{8,16},{16,24},{24,32},{32,40},{40,48},{48,56},{56,64},{64,7... | collective-permute-start | bytes 147464 | tf_op jit(solution)/shard_map/ppermute | solution.py:37
  110.0 5.8 %collective-permute-start.10 = (f32[3,8,2,128]{3,1,2,0:T(8,128)S(1)}, f32[3,8,2,128]{3,1,2,0:T(8,128)S(1)}, u32[]{:S(2)}, u32[]{:S(2)}) collective-permute-start(f32[3,8,2,128]{3,1,2,0:T(8,128)S(1)} %copy.394), channel_id=1, source_target_pairs={{0,1},{1,2},{2,3},{3,4},{4,5},{5,6},{6,7},{8,9},{9,10},{10,11},{11... | collective-permute-start | bytes 73736 | tf_op jit(solution)/shard_map/ppermute | solution.py:37
  112.0 5.1 %collective-permute-start.11 = (f32[3,8,2,128]{3,1,2,0:T(8,128)S(1)}, f32[3,8,2,128]{3,1,2,0:T(8,128)S(1)}, u32[]{:S(2)}, u32[]{:S(2)}) collective-permute-start(f32[3,8,2,128]{3,1,2,0:T(8,128)S(1)} %copy.395), channel_id=1, source_target_pairs={{1,0},{2,1},{3,2},{4,3},{5,4},{6,5},{7,6},{9,8},{10,9},{11,10},{12... | collective-permute-start | bytes 73736 | tf_op jit(solution)/shard_map/ppermute | solution.py:38
  115.8 17.9 %copy-start.6 = (f32[8,16,128]{2,1,0:T(8,128)S(1)}, f32[8,16,128]{2,1,0:T(8,128)}, u32[]{:S(2)}) copy-start(f32[8,16,128]{2,1,0:T(8,128)} %param.22) | copy-start | bytes 196612
  117.5 17.2 %copy-start.7 = (f32[8,16,128]{2,1,0:T(8,128)S(1)}, f32[8,16,128]{2,1,0:T(8,128)}, u32[]{:S(2)}) copy-start(f32[8,16,128]{2,1,0:T(8,128)} %param.21) | copy-start | bytes 196612
  117.9 17.6 %copy-start.1 = (f32[3,8,16,128]{3,2,1,0:T(8,128)}, f32[3,8,16,128]{3,2,1,0:T(8,128)S(1)}, u32[]{:S(2)}) copy-start(f32[3,8,16,128]{3,2,1,0:T(8,128)S(1)} %fusion.2) | copy-start | bytes 589828
  118.0 11.6 %collective-permute-start.14 = (f32[3,8,2,128]{3,1,2,0:T(8,128)S(1)}, f32[3,8,2,128]{3,1,2,0:T(8,128)S(1)}, u32[]{:S(2)}, u32[]{:S(2)}) collective-permute-start(f32[3,8,2,128]{3,1,2,0:T(8,128)S(1)} %copy.400), channel_id=1, source_target_pairs={{0,1},{1,2},{2,3},{3,4},{4,5},{5,6},{6,7},{8,9},{9,10},{10,11},{11... | collective-permute-start | bytes 73736 | tf_op jit(solution)/shard_map/ppermute | solution.py:37
  121.3 8.3 %collective-permute-start.15 = (f32[3,8,2,128]{3,1,2,0:T(8,128)S(1)}, f32[3,8,2,128]{3,1,2,0:T(8,128)S(1)}, u32[]{:S(2)}, u32[]{:S(2)}) collective-permute-start(f32[3,8,2,128]{3,1,2,0:T(8,128)S(1)} %copy.401), channel_id=1, source_target_pairs={{1,0},{2,1},{3,2},{4,3},{5,4},{6,5},{7,6},{9,8},{10,9},{11,10},{12... | collective-permute-start | bytes 73736 | tf_op jit(solution)/shard_map/ppermute | solution.py:38
  123.7 6.0 %collective-permute-start.12 = (f32[3,2,16,128]{3,2,1,0:T(8,128)S(1)}, f32[3,2,16,128]{3,2,1,0:T(8,128)S(1)}, u32[]{:S(2)}, u32[]{:S(2)}) collective-permute-start(f32[3,2,16,128]{3,2,1,0:T(8,128)S(1)} %get-tuple-element.139), channel_id=1, source_target_pairs={{0,8},{8,16},{16,24},{24,32},{32,40},{40,48},{48,56},{56,64},{64,7... | collective-permute-start | bytes 147464 | tf_op jit(solution)/shard_map/ppermute | solution.py:37
  125.6 8.1 %collective-permute-start.13 = (f32[3,2,16,128]{3,2,1,0:T(8,128)S(1)}, f32[3,2,16,128]{3,2,1,0:T(8,128)S(1)}, u32[]{:S(2)}, u32[]{:S(2)}) collective-permute-start(f32[3,2,16,128]{3,2,1,0:T(8,128)S(1)} %get-tuple-element.138), channel_id=1, source_target_pairs={{8,0},{16,8},{24,16},{32,24},{40,32},{48,40},{56,48},{64,56},{72,6... | collective-permute-start | bytes 147464 | tf_op jit(solution)/shard_map/ppermute | solution.py:38
  (3 other events, 38.1 us)

commit v13 on v10

--- a/solution.py
+++ b/solution.py
@@ -108,9 +108,7 @@
     mine_norm = jnp.sqrt(mine_sq / samples + epsilon)
     other_norm = jnp.sqrt(other_sq / samples + epsilon)
     corr = (cross / samples) / (mine_norm * other_norm)
-    other_scale = 1.0 / other_norm
-    mine_scale = corr / mine_norm
-    toward = other_vals * other_scale - mine_scale * mine_vals
+    toward = other_vals / other_norm - corr * (mine_vals / mine_norm)
     toward_ref[...] = toward.astype(jnp.bfloat16).astype(jnp.float32)
 
     ways = acc_ref.shape[0]
@@ -135,7 +133,7 @@
 
 def pair_sums(targets, mine, other, stations):
     slots, rows, lanes = mine.shape
-    block = 128
+    block = 64
     samples = rows * lanes
     spec = pl.BlockSpec((block, rows, lanes), lambda g, t: (g, 0, 0))
     return pl.pallas_call(

time: 135 us -> 136 us (level)
  no operation moved by 1% of the time
where the time goes in v13:
time: 136 us; the launch traced here: 135 us
  starting transfers between devices  60.7 us (45%)
  waiting for transfers between devices  39.1 us (29%)
  local copies, waits for them, and re-layouts  15.4 us (11%)
  Pallas kernels  12.2 us (9%)
  other arithmetic  6.16 us (5%)
  between operations  1.55 us (1%)
    ppermute x8, waiting for transfers between devices, halo_pad(): lax.ppermute(lax.slice_in_dim(block, size - width, size, axis=dim), axis,...  26.5 us
    ppermute x8, starting transfers between devices, halo_pad(): lax.ppermute(lax.slice_in_dim(block, size - width, size, axis=dim), axis,...  25 us
    ppermute x8, starting transfers between devices, halo_pad(): lax.ppermute(lax.slice_in_dim(block, 0, width, axis=dim), axis, backward)  24.9 us
    pallas_call x1, Pallas kernels, pair_sums(): pl.pallas_call(functools.partial(pair_kernel, block, float(samples)), gri...  12.2 us
    ppermute x8, waiting for transfers between devices, halo_pad(): lax.ppermute(lax.slice_in_dim(block, 0, width, axis=dim), axis, backward)  11.2 us
    all_to_all x1, starting transfers between devices, station_part(): lax.all_to_all(send, ('gx', 'gy'), split_axis=0, concat_axis=0, tiled=True)  10.8 us
    unnamed x24, local copies, waits for them, and re-layouts  4.19 us
    gather x1, local copies, waits for them, and re-layouts, station_part(): padded_rows[jnp.where(slot_station >= 0, slot_station, stations_here)]  3.54 us
  transfers between devices with their start and end apart: 17, of which 6 were waited for; matrix products, arithmetic and copies ran while one was open for 6% of the time, Pallas kernels for 0%

profile of v13, /device:TPU:14, one launch (start us, length us, event | category | flops | bytes accessed | tf_op | source)
XLA Modules:
  0.0 135.0 jit_solution(16509492361835959925)
XLA Ops:
  4.7 3.5 %gather_fusion.1 = bf16[512,32,128]{2,1,0:T(8,128)(2,1)} fusion(bf16[33,32,128]{2,1,0:T(8,128)(2,1)S(1)} %concatenate.120, s32[1024]{0:T(1024)S(1)} %pad_clamp_fusion), kind=kCustom, calls=%fused_computation.1 | custom fusion | bytes 8390656 | tf_op jit(solution)/shard_map/gather | solution.py:181
  8.3 10.8 %all-to-all-start = ((bf16[128,4,32,128]{3,2,1,0:T(8,128)(2,1)}), bf16[128,4,32,128]{3,2,1,0:T(8,128)(2,1)}, u32[]{:S(2)}, u32[]{:S(2)}) async-start(bf16[128,4,32,128]{3,2,1,0:T(8,128)(2,1)} %bitcast.271), calls=%async_computation | async-start | bytes 8388608 | tf_op jit(solution)/shard_map/all_to_all | solution.py:182
  19.2 2.0 %collective-permute-start.2 = (f32[3,8,2,128]{3,1,2,0:T(8,128)S(1)}, f32[3,8,2,128]{3,1,2,0:T(8,128)S(1)}, u32[]{:S(2)}, u32[]{:S(2)}) collective-permute-start(f32[3,8,2,128]{3,1,2,0:T(8,128)S(1)} %copy.372), channel_id=1, source_target_pairs={{0,1},{1,2},{2,3},{3,4},{4,5},{5,6},{6,7},{8,9},{9,10},{10,11},{11... | collective-permute-start | bytes 73736 | tf_op jit(solution)/shard_map/ppermute | solution.py:37
  21.3 3.5 %collective-permute-start.3 = (f32[3,8,2,128]{3,1,2,0:T(8,128)S(1)}, f32[3,8,2,128]{3,1,2,0:T(8,128)S(1)}, u32[]{:S(2)}, u32[]{:S(2)}) collective-permute-start(f32[3,8,2,128]{3,1,2,0:T(8,128)S(1)} %copy.373), channel_id=1, source_target_pairs={{1,0},{2,1},{3,2},{4,3},{5,4},{6,5},{7,6},{9,8},{10,9},{11,10},{12... | collective-permute-start | bytes 73736 | tf_op jit(solution)/shard_map/ppermute | solution.py:38
  24.8 2.8 %collective-permute-start = (f32[3,2,16,128]{3,2,1,0:T(8,128)S(1)}, f32[3,2,16,128]{3,2,1,0:T(8,128)S(1)}, u32[]{:S(2)}, u32[]{:S(2)}) collective-permute-start(f32[3,2,16,128]{3,2,1,0:T(8,128)S(1)} %get-tuple-element.129), channel_id=1, source_target_pairs={{8,0},{16,8},{24,16},{32,24},{40,32},{48,40},{56,48},{64,56},{72,6... | collective-permute-start | bytes 147464 | tf_op jit(solution)/shard_map/ppermute | solution.py:38
  27.6 5.2 %collective-permute-start.1 = (f32[3,2,16,128]{3,2,1,0:T(8,128)S(1)}, f32[3,2,16,128]{3,2,1,0:T(8,128)S(1)}, u32[]{:S(2)}, u32[]{:S(2)}) collective-permute-start(f32[3,2,16,128]{3,2,1,0:T(8,128)S(1)} %get-tuple-element.130), channel_id=1, source_target_pairs={{0,8},{8,16},{16,24},{24,32},{32,40},{40,48},{48,56},{56,64},{64,7... | collective-permute-start | bytes 147464 | tf_op jit(solution)/shard_map/ppermute | solution.py:37
  34.2 3.5 %gather_fusion = bf16[512,32,128]{2,1,0:T(8,128)(2,1)} fusion(bf16[33,32,128]{2,1,0:T(8,128)(2,1)S(1)} %concatenate.120, s32[1024]{0:T(1024)S(1)} %pad_clamp_fusion.1), kind=kCustom, calls=%fused_computation | custom fusion | bytes 8390656 | tf_op jit(solution)/shard_map/gather | solution.py:184
  37.7 26.4 %collective-permute-done.2 = f32[3,8,2,128]{3,1,2,0:T(8,128)S(1)} collective-permute-done((f32[3,8,2,128]{3,1,2,0:T(8,128)S(1)}, f32[3,8,2,128]{3,1,2,0:T(8,128)S(1)}, u32[]{:S(2)}, u32[]{:S(2)}) %collective-permute-start.2) | collective-permute-done | bytes 24608 | tf_op jit(solution)/shard_map/ppermute | solution.py:37
  64.3 3.5 %collective-permute-done = f32[3,2,16,128]{3,2,1,0:T(8,128)S(1)} collective-permute-done((f32[3,2,16,128]{3,2,1,0:T(8,128)S(1)}, f32[3,2,16,128]{3,2,1,0:T(8,128)S(1)}, u32[]{:S(2)}, u32[]{:S(2)}) %collective-permute-start) | collective-permute-done | bytes 49184 | tf_op jit(solution)/shard_map/ppermute | solution.py:38
  69.7 12.2 %shard_map.146 = f32[32,32,128]{2,1,0:T(8,128)} custom-call(s32[512]{0:T(512)} %compare_select_fusion.4.station_ref, bf16[512,32,128]{2,1,0:T(8,128)(2,1)} %gather_fusion, bf16[512,32,128]{2,1,0:T(8,128)(2,1)} %bitcast.21.other_ref), custom_call_target="tpu_custom_call" | custom-call | flops 41943040 | bytes 8388608 | tf_op jit(solution)/shard_map/pallas_call | solution.py:139
  83.5 1.9 %collective-permute-start.6 = (f32[3,8,2,128]{3,1,2,0:T(8,128)S(1)}, f32[3,8,2,128]{3,1,2,0:T(8,128)S(1)}, u32[]{:S(2)}, u32[]{:S(2)}) collective-permute-start(f32[3,8,2,128]{3,1,2,0:T(8,128)S(1)} %copy.386), channel_id=1, source_target_pairs={{0,1},{1,2},{2,3},{3,4},{4,5},{5,6},{6,7},{8,9},{9,10},{10,11},{11... | collective-permute-start | bytes 73736 | tf_op jit(solution)/shard_map/ppermute | solution.py:37
  85.4 3.6 %collective-permute-start.7 = (f32[3,8,2,128]{3,1,2,0:T(8,128)S(1)}, f32[3,8,2,128]{3,1,2,0:T(8,128)S(1)}, u32[]{:S(2)}, u32[]{:S(2)}) collective-permute-start(f32[3,8,2,128]{3,1,2,0:T(8,128)S(1)} %copy.387), channel_id=1, source_target_pairs={{1,0},{2,1},{3,2},{4,3},{5,4},{6,5},{7,6},{9,8},{10,9},{11,10},{12... | collective-permute-start | bytes 73736 | tf_op jit(solution)/shard_map/ppermute | solution.py:38
  89.3 2.7 %collective-permute-start.4 = (f32[3,2,16,128]{3,2,1,0:T(8,128)S(1)}, f32[3,2,16,128]{3,2,1,0:T(8,128)S(1)}, u32[]{:S(2)}, u32[]{:S(2)}) collective-permute-start(f32[3,2,16,128]{3,2,1,0:T(8,128)S(1)} %get-tuple-element.123), channel_id=1, source_target_pairs={{0,8},{8,16},{16,24},{24,32},{32,40},{40,48},{48,56},{56,64},{64,7... | collective-permute-start | bytes 147464 | tf_op jit(solution)/shard_map/ppermute | solution.py:37
  91.9 3.2 %collective-permute-start.5 = (f32[3,2,16,128]{3,2,1,0:T(8,128)S(1)}, f32[3,2,16,128]{3,2,1,0:T(8,128)S(1)}, u32[]{:S(2)}, u32[]{:S(2)}) collective-permute-start(f32[3,2,16,128]{3,2,1,0:T(8,128)S(1)} %get-tuple-element.124), channel_id=1, source_target_pairs={{8,0},{16,8},{24,16},{32,24},{40,32},{48,40},{56,48},{64,56},{72,6... | collective-permute-start | bytes 147464 | tf_op jit(solution)/shard_map/ppermute | solution.py:38
  95.3 2.1 %copy.406 = f32[4,8,32,128]{3,1,2,0:T(8,128)} copy(f32[4,8,32,128]{3,2,1,0:T(8,128)} %bitcast.272) | data formatting | bytes 1048576
  97.6 2.4 %collective-permute-done.5 = f32[3,2,16,128]{3,2,1,0:T(8,128)S(1)} collective-permute-done((f32[3,2,16,128]{3,2,1,0:T(8,128)S(1)}, f32[3,2,16,128]{3,2,1,0:T(8,128)S(1)}, u32[]{:S(2)}, u32[]{:S(2)}) %collective-permute-start.5) | collective-permute-done | bytes 49184 | tf_op jit(solution)/shard_map/ppermute | solution.py:38
  102.6 6.0 %collective-permute-start.9 = (f32[3,2,16,128]{3,2,1,0:T(8,128)S(1)}, f32[3,2,16,128]{3,2,1,0:T(8,128)S(1)}, u32[]{:S(2)}, u32[]{:S(2)}) collective-permute-start(f32[3,2,16,128]{3,2,1,0:T(8,128)S(1)} %get-tuple-element.117), channel_id=1, source_target_pairs={{0,8},{8,16},{16,24},{24,32},{32,40},{40,48},{48,56},{56,64},{64,7... | collective-permute-start | bytes 147464 | tf_op jit(solution)/shard_map/ppermute | solution.py:37
  108.7 1.9 %collective-permute-start.10 = (f32[3,8,2,128]{3,1,2,0:T(8,128)S(1)}, f32[3,8,2,128]{3,1,2,0:T(8,128)S(1)}, u32[]{:S(2)}, u32[]{:S(2)}) collective-permute-start(f32[3,8,2,128]{3,1,2,0:T(8,128)S(1)} %copy.390), channel_id=1, source_target_pairs={{0,1},{1,2},{2,3},{3,4},{4,5},{5,6},{6,7},{8,9},{9,10},{10,11},{11... | collective-permute-start | bytes 73736 | tf_op jit(solution)/shard_map/ppermute | solution.py:37
  110.6 3.6 %collective-permute-start.11 = (f32[3,8,2,128]{3,1,2,0:T(8,128)S(1)}, f32[3,8,2,128]{3,1,2,0:T(8,128)S(1)}, u32[]{:S(2)}, u32[]{:S(2)}) collective-permute-start(f32[3,8,2,128]{3,1,2,0:T(8,128)S(1)} %copy.391), channel_id=1, source_target_pairs={{1,0},{2,1},{3,2},{4,3},{5,4},{6,5},{7,6},{9,8},{10,9},{11,10},{12... | collective-permute-start | bytes 73736 | tf_op jit(solution)/shard_map/ppermute | solution.py:38
  116.6 3.3 %collective-permute-start.14 = (f32[3,8,2,128]{3,1,2,0:T(8,128)S(1)}, f32[3,8,2,128]{3,1,2,0:T(8,128)S(1)}, u32[]{:S(2)}, u32[]{:S(2)}) collective-permute-start(f32[3,8,2,128]{3,1,2,0:T(8,128)S(1)} %copy.396), channel_id=1, source_target_pairs={{0,1},{1,2},{2,3},{3,4},{4,5},{5,6},{6,7},{8,9},{9,10},{10,11},{11... | collective-permute-start | bytes 73736 | tf_op jit(solution)/shard_map/ppermute | solution.py:37
  120.0 2.3 %collective-permute-start.15 = (f32[3,8,2,128]{3,1,2,0:T(8,128)S(1)}, f32[3,8,2,128]{3,1,2,0:T(8,128)S(1)}, u32[]{:S(2)}, u32[]{:S(2)}) collective-permute-start(f32[3,8,2,128]{3,1,2,0:T(8,128)S(1)} %copy.397), channel_id=1, source_target_pairs={{1,0},{2,1},{3,2},{4,3},{5,4},{6,5},{7,6},{9,8},{10,9},{11,10},{12... | collective-permute-start | bytes 73736 | tf_op jit(solution)/shard_map/ppermute | solution.py:38
  122.4 1.9 %collective-permute-start.12 = (f32[3,2,16,128]{3,2,1,0:T(8,128)S(1)}, f32[3,2,16,128]{3,2,1,0:T(8,128)S(1)}, u32[]{:S(2)}, u32[]{:S(2)}) collective-permute-start(f32[3,2,16,128]{3,2,1,0:T(8,128)S(1)} %get-tuple-element.111), channel_id=1, source_target_pairs={{0,8},{8,16},{16,24},{24,32},{32,40},{40,48},{48,56},{56,64},{64,7... | collective-permute-start | bytes 147464 | tf_op jit(solution)/shard_map/ppermute | solution.py:37
  124.3 3.9 %collective-permute-start.13 = (f32[3,2,16,128]{3,2,1,0:T(8,128)S(1)}, f32[3,2,16,128]{3,2,1,0:T(8,128)S(1)}, u32[]{:S(2)}, u32[]{:S(2)}) collective-permute-start(f32[3,2,16,128]{3,2,1,0:T(8,128)S(1)} %get-tuple-element.110), channel_id=1, source_target_pairs={{8,0},{16,8},{24,16},{32,24},{40,32},{48,40},{56,48},{64,56},{72,6... | collective-permute-start | bytes 147464 | tf_op jit(solution)/shard_map/ppermute | solution.py:38
  128.4 4.0 %collective-permute-done.13 = f32[3,2,16,128]{3,2,1,0:T(8,128)S(1)} collective-permute-done((f32[3,2,16,128]{3,2,1,0:T(8,128)S(1)}, f32[3,2,16,128]{3,2,1,0:T(8,128)S(1)}, u32[]{:S(2)}, u32[]{:S(2)}) %collective-permute-start.13) | collective-permute-done | bytes 49184 | tf_op jit(solution)/shard_map/ppermute | solution.py:38
  (146 shorter events, 17.0 us)
Async XLA Ops:
  8.3 25.7 %copy-start.8 = (f32[8,16,128]{2,1,0:T(8,128)S(1)}, f32[8,16,128]{2,1,0:T(8,128)}, u32[]{:S(2)}) copy-start(f32[8,16,128]{2,1,0:T(8,128)} %param.19) | copy-start | bytes 196612
  8.3 25.8 %copy-start.4 = (bf16[12,8,16,128]{3,2,1,0:T(8,128)(2,1)S(1)}, bf16[12,8,16,128]{3,2,1,0:T(8,128)(2,1)}, u32[]{:S(2)}) copy-start(bf16[12,8,16,128]{3,2,1,0:T(8,128)(2,1)} %param.20) | copy-start | bytes 1179652
  8.3 61.4 %all-to-all-start = ((bf16[128,4,32,128]{3,2,1,0:T(8,128)(2,1)}), bf16[128,4,32,128]{3,2,1,0:T(8,128)(2,1)}, u32[]{:S(2)}, u32[]{:S(2)}) async-start(bf16[128,4,32,128]{3,2,1,0:T(8,128)(2,1)} %bitcast.271), calls=%async_computation | async-start | bytes 8388608 | tf_op jit(solution)/shard_map/all_to_all | solution.py:182
  19.2 44.9 %collective-permute-start.2 = (f32[3,8,2,128]{3,1,2,0:T(8,128)S(1)}, f32[3,8,2,128]{3,1,2,0:T(8,128)S(1)}, u32[]{:S(2)}, u32[]{:S(2)}) collective-permute-start(f32[3,8,2,128]{3,1,2,0:T(8,128)S(1)} %copy.372), channel_id=1, source_target_pairs={{0,1},{1,2},{2,3},{3,4},{4,5},{5,6},{6,7},{8,9},{9,10},{10,11},{11... | collective-permute-start | bytes 73736 | tf_op jit(solution)/shard_map/ppermute | solution.py:37
  21.3 42.9 %collective-permute-start.3 = (f32[3,8,2,128]{3,1,2,0:T(8,128)S(1)}, f32[3,8,2,128]{3,1,2,0:T(8,128)S(1)}, u32[]{:S(2)}, u32[]{:S(2)}) collective-permute-start(f32[3,8,2,128]{3,1,2,0:T(8,128)S(1)} %copy.373), channel_id=1, source_target_pairs={{1,0},{2,1},{3,2},{4,3},{5,4},{6,5},{7,6},{9,8},{10,9},{11,10},{12... | collective-permute-start | bytes 73736 | tf_op jit(solution)/shard_map/ppermute | solution.py:38
  24.8 42.9 %collective-permute-start = (f32[3,2,16,128]{3,2,1,0:T(8,128)S(1)}, f32[3,2,16,128]{3,2,1,0:T(8,128)S(1)}, u32[]{:S(2)}, u32[]{:S(2)}) collective-permute-start(f32[3,2,16,128]{3,2,1,0:T(8,128)S(1)} %get-tuple-element.129), channel_id=1, source_target_pairs={{8,0},{16,8},{24,16},{32,24},{40,32},{48,40},{56,48},{64,56},{72,6... | collective-permute-start | bytes 147464 | tf_op jit(solution)/shard_map/ppermute | solution.py:38
  27.6 40.2 %collective-permute-start.1 = (f32[3,2,16,128]{3,2,1,0:T(8,128)S(1)}, f32[3,2,16,128]{3,2,1,0:T(8,128)S(1)}, u32[]{:S(2)}, u32[]{:S(2)}) collective-permute-start(f32[3,2,16,128]{3,2,1,0:T(8,128)S(1)} %get-tuple-element.130), channel_id=1, source_target_pairs={{0,8},{8,16},{16,24},{24,32},{32,40},{40,48},{48,56},{56,64},{64,7... | collective-permute-start | bytes 147464 | tf_op jit(solution)/shard_map/ppermute | solution.py:37
  81.8 18.2 %copy-start = (f32[8,16,128]{2,1,0:T(8,128)S(1)}, f32[8,16,128]{2,1,0:T(8,128)}, u32[]{:S(2)}) copy-start(f32[8,16,128]{2,1,0:T(8,128)} %param.18) | copy-start | bytes 196612
  81.8 18.2 %copy-start.5 = (f32[8,16,128]{2,1,0:T(8,128)S(1)}, f32[8,16,128]{2,1,0:T(8,128)}, u32[]{:S(2)}) copy-start(f32[8,16,128]{2,1,0:T(8,128)} %param.17) | copy-start | bytes 196612
  83.5 14.0 %collective-permute-start.6 = (f32[3,8,2,128]{3,1,2,0:T(8,128)S(1)}, f32[3,8,2,128]{3,1,2,0:T(8,128)S(1)}, u32[]{:S(2)}, u32[]{:S(2)}) collective-permute-start(f32[3,8,2,128]{3,1,2,0:T(8,128)S(1)} %copy.386), channel_id=1, source_target_pairs={{0,1},{1,2},{2,3},{3,4},{4,5},{5,6},{6,7},{8,9},{9,10},{10,11},{11... | collective-permute-start | bytes 73736 | tf_op jit(solution)/shard_map/ppermute | solution.py:37
  85.4 12.0 %collective-permute-start.7 = (f32[3,8,2,128]{3,1,2,0:T(8,128)S(1)}, f32[3,8,2,128]{3,1,2,0:T(8,128)S(1)}, u32[]{:S(2)}, u32[]{:S(2)}) collective-permute-start(f32[3,8,2,128]{3,1,2,0:T(8,128)S(1)} %copy.387), channel_id=1, source_target_pairs={{1,0},{2,1},{3,2},{4,3},{5,4},{6,5},{7,6},{9,8},{10,9},{11,10},{12... | collective-permute-start | bytes 73736 | tf_op jit(solution)/shard_map/ppermute | solution.py:38
  89.3 8.3 %collective-permute-start.4 = (f32[3,2,16,128]{3,2,1,0:T(8,128)S(1)}, f32[3,2,16,128]{3,2,1,0:T(8,128)S(1)}, u32[]{:S(2)}, u32[]{:S(2)}) collective-permute-start(f32[3,2,16,128]{3,2,1,0:T(8,128)S(1)} %get-tuple-element.123), channel_id=1, source_target_pairs={{0,8},{8,16},{16,24},{24,32},{32,40},{40,48},{48,56},{56,64},{64,7... | collective-permute-start | bytes 147464 | tf_op jit(solution)/shard_map/ppermute | solution.py:37
  91.9 8.1 %collective-permute-start.5 = (f32[3,2,16,128]{3,2,1,0:T(8,128)S(1)}, f32[3,2,16,128]{3,2,1,0:T(8,128)S(1)}, u32[]{:S(2)}, u32[]{:S(2)}) collective-permute-start(f32[3,2,16,128]{3,2,1,0:T(8,128)S(1)} %get-tuple-element.124), channel_id=1, source_target_pairs={{8,0},{16,8},{24,16},{32,24},{40,32},{48,40},{56,48},{64,56},{72,6... | collective-permute-start | bytes 147464 | tf_op jit(solution)/shard_map/ppermute | solution.py:38
  100.7 15.2 %collective-permute-start.8 = (f32[3,2,16,128]{3,2,1,0:T(8,128)S(1)}, f32[3,2,16,128]{3,2,1,0:T(8,128)S(1)}, u32[]{:S(2)}, u32[]{:S(2)}) collective-permute-start(f32[3,2,16,128]{3,2,1,0:T(8,128)S(1)} %get-tuple-element.116), channel_id=1, source_target_pairs={{8,0},{16,8},{24,16},{32,24},{40,32},{48,40},{56,48},{64,56},{72,6... | collective-permute-start | bytes 147464 | tf_op jit(solution)/shard_map/ppermute | solution.py:38
  102.6 13.3 %collective-permute-start.9 = (f32[3,2,16,128]{3,2,1,0:T(8,128)S(1)}, f32[3,2,16,128]{3,2,1,0:T(8,128)S(1)}, u32[]{:S(2)}, u32[]{:S(2)}) collective-permute-start(f32[3,2,16,128]{3,2,1,0:T(8,128)S(1)} %get-tuple-element.117), channel_id=1, source_target_pairs={{0,8},{8,16},{16,24},{24,32},{32,40},{40,48},{48,56},{56,64},{64,7... | collective-permute-start | bytes 147464 | tf_op jit(solution)/shard_map/ppermute | solution.py:37
  108.7 5.8 %collective-permute-start.10 = (f32[3,8,2,128]{3,1,2,0:T(8,128)S(1)}, f32[3,8,2,128]{3,1,2,0:T(8,128)S(1)}, u32[]{:S(2)}, u32[]{:S(2)}) collective-permute-start(f32[3,8,2,128]{3,1,2,0:T(8,128)S(1)} %copy.390), channel_id=1, source_target_pairs={{0,1},{1,2},{2,3},{3,4},{4,5},{5,6},{6,7},{8,9},{9,10},{10,11},{11... | collective-permute-start | bytes 73736 | tf_op jit(solution)/shard_map/ppermute | solution.py:37
  110.6 5.1 %collective-permute-start.11 = (f32[3,8,2,128]{3,1,2,0:T(8,128)S(1)}, f32[3,8,2,128]{3,1,2,0:T(8,128)S(1)}, u32[]{:S(2)}, u32[]{:S(2)}) collective-permute-start(f32[3,8,2,128]{3,1,2,0:T(8,128)S(1)} %copy.391), channel_id=1, source_target_pairs={{1,0},{2,1},{3,2},{4,3},{5,4},{6,5},{7,6},{9,8},{10,9},{11,10},{12... | collective-permute-start | bytes 73736 | tf_op jit(solution)/shard_map/ppermute | solution.py:38
  114.5 17.9 %copy-start.6 = (f32[8,16,128]{2,1,0:T(8,128)S(1)}, f32[8,16,128]{2,1,0:T(8,128)}, u32[]{:S(2)}) copy-start(f32[8,16,128]{2,1,0:T(8,128)} %param.22) | copy-start | bytes 196612
  116.2 17.2 %copy-start.7 = (f32[8,16,128]{2,1,0:T(8,128)S(1)}, f32[8,16,128]{2,1,0:T(8,128)}, u32[]{:S(2)}) copy-start(f32[8,16,128]{2,1,0:T(8,128)} %param.21) | copy-start | bytes 196612
  116.6 17.6 %copy-start.1 = (f32[3,8,16,128]{3,2,1,0:T(8,128)}, f32[3,8,16,128]{3,2,1,0:T(8,128)S(1)}, u32[]{:S(2)}) copy-start(f32[3,8,16,128]{3,2,1,0:T(8,128)S(1)} %fusion.2) | copy-start | bytes 589828
  116.6 11.6 %collective-permute-start.14 = (f32[3,8,2,128]{3,1,2,0:T(8,128)S(1)}, f32[3,8,2,128]{3,1,2,0:T(8,128)S(1)}, u32[]{:S(2)}, u32[]{:S(2)}) collective-permute-start(f32[3,8,2,128]{3,1,2,0:T(8,128)S(1)} %copy.396), channel_id=1, source_target_pairs={{0,1},{1,2},{2,3},{3,4},{4,5},{5,6},{6,7},{8,9},{9,10},{10,11},{11... | collective-permute-start | bytes 73736 | tf_op jit(solution)/shard_map/ppermute | solution.py:37
  120.0 8.3 %collective-permute-start.15 = (f32[3,8,2,128]{3,1,2,0:T(8,128)S(1)}, f32[3,8,2,128]{3,1,2,0:T(8,128)S(1)}, u32[]{:S(2)}, u32[]{:S(2)}) collective-permute-start(f32[3,8,2,128]{3,1,2,0:T(8,128)S(1)} %copy.397), channel_id=1, source_target_pairs={{1,0},{2,1},{3,2},{4,3},{5,4},{6,5},{7,6},{9,8},{10,9},{11,10},{12... | collective-permute-start | bytes 73736 | tf_op jit(solution)/shard_map/ppermute | solution.py:38
  122.4 6.0 %collective-permute-start.12 = (f32[3,2,16,128]{3,2,1,0:T(8,128)S(1)}, f32[3,2,16,128]{3,2,1,0:T(8,128)S(1)}, u32[]{:S(2)}, u32[]{:S(2)}) collective-permute-start(f32[3,2,16,128]{3,2,1,0:T(8,128)S(1)} %get-tuple-element.111), channel_id=1, source_target_pairs={{0,8},{8,16},{16,24},{24,32},{32,40},{40,48},{48,56},{56,64},{64,7... | collective-permute-start | bytes 147464 | tf_op jit(solution)/shard_map/ppermute | solution.py:37
  124.3 8.1 %collective-permute-start.13 = (f32[3,2,16,128]{3,2,1,0:T(8,128)S(1)}, f32[3,2,16,128]{3,2,1,0:T(8,128)S(1)}, u32[]{:S(2)}, u32[]{:S(2)}) collective-permute-start(f32[3,2,16,128]{3,2,1,0:T(8,128)S(1)} %get-tuple-element.110), channel_id=1, source_target_pairs={{8,0},{16,8},{24,16},{32,24},{40,32},{48,40},{56,48},{64,56},{72,6... | collective-permute-start | bytes 147464 | tf_op jit(solution)/shard_map/ppermute | solution.py:38
  (3 other events, 37.9 us)

commit v14 on v13

--- a/solution.py
+++ b/solution.py
@@ -169,11 +169,11 @@
     device_ids = jnp.arange(devices)
     pick_own = (dest[None, :, None] == device_ids[:, None, None]) & (rank[None, :, None] == jnp.arange(2)[None, None, :])
     own_station = jnp.sum(jnp.where(pick_own, first_local[None, :, None] + 1, 0), axis=1) - 1
-    blocks = station_pairs.reshape(devices, pair_rows, 2)
-    hit = (blocks[:, :, 1] // stations_here == me).astype(jnp.int32)
+    seconds = station_pairs[:, 1].reshape(devices, pair_rows)
+    hit = (seconds // stations_here == me).astype(jnp.int32)
     before = jnp.cumsum(hit, axis=1) - hit
     pick_in = (hit[:, :, None] > 0) & (before[:, :, None] == jnp.arange(2)[None, None, :])
-    in_station = jnp.sum(jnp.where(pick_in, (blocks[:, :, 1] % stations_here)[:, :, None] + 1, 0), axis=1) - 1
+    in_station = jnp.sum(jnp.where(pick_in, (seconds % stations_here)[:, :, None] + 1, 0), axis=1) - 1
     slot_station = jnp.concatenate([own_station, in_station], axis=1)
     lanes = 128
     rows = residuals.reshape(stations_here, samples // lanes, lanes)

time: 136 us -> 136 us (level)
    unnamed x24 -> x22, local copies, waits for them, and re-layouts: 4.19 us -> 3.18 us
where the time goes in v14:
time: 136 us; the launch traced here: 135 us
  starting transfers between devices  60.7 us (45%)
  waiting for transfers between devices  39.1 us (29%)
  local copies, waits for them, and re-layouts  15.5 us (11%)
  Pallas kernels  12.2 us (9%)
  other arithmetic  6.16 us (5%)
  between operations  1.54 us (1%)
    ppermute x8, waiting for transfers between devices, halo_pad(): lax.ppermute(lax.slice_in_dim(block, size - width, size, axis=dim), axis,...  26.5 us
    ppermute x8, starting transfers between devices, halo_pad(): lax.ppermute(lax.slice_in_dim(block, size - width, size, axis=dim), axis,...  25 us
    ppermute x8, starting transfers between devices, halo_pad(): lax.ppermute(lax.slice_in_dim(block, 0, width, axis=dim), axis, backward)  24.9 us
    pallas_call x1, Pallas kernels, pair_sums(): pl.pallas_call(functools.partial(pair_kernel, block, float(samples)), gri...  12.2 us
    ppermute x8, waiting for transfers between devices, halo_pad(): lax.ppermute(lax.slice_in_dim(block, 0, width, axis=dim), axis, backward)  11.2 us
    all_to_all x1, starting transfers between devices, station_part(): lax.all_to_all(send, ('gx', 'gy'), split_axis=0, concat_axis=0, tiled=True)  10.8 us
    gather x1, local copies, waits for them, and re-layouts, station_part(): padded_rows[jnp.where(slot_station >= 0, slot_station, stations_here)]  3.54 us
    gather x1, local copies, waits for them, and re-layouts, station_part(): padded_rows[jnp.where(mine_station >= 0, mine_station, stations_here)]  3.53 us
  transfers between devices with their start and end apart: 17, of which 6 were waited for; matrix products, arithmetic and copies ran while one was open for 6% of the time, Pallas kernels for 0%

profile of v14, /device:TPU:14, one launch (start us, length us, event | category | flops | bytes accessed | tf_op | source)
XLA Modules:
  0.0 135.0 jit_solution(7321616291020565825)
XLA Ops:
  4.8 3.5 %gather_fusion.1 = bf16[512,32,128]{2,1,0:T(8,128)(2,1)} fusion(bf16[33,32,128]{2,1,0:T(8,128)(2,1)S(1)} %concatenate.120, s32[1024]{0:T(1024)S(1)} %pad_clamp_fusion), kind=kCustom, calls=%fused_computation.1 | custom fusion | bytes 8390656 | tf_op jit(solution)/shard_map/gather | solution.py:181
  8.3 10.8 %all-to-all-start = ((bf16[128,4,32,128]{3,2,1,0:T(8,128)(2,1)}), bf16[128,4,32,128]{3,2,1,0:T(8,128)(2,1)}, u32[]{:S(2)}, u32[]{:S(2)}) async-start(bf16[128,4,32,128]{3,2,1,0:T(8,128)(2,1)} %bitcast.260), calls=%async_computation | async-start | bytes 8388608 | tf_op jit(solution)/shard_map/all_to_all | solution.py:182
  19.3 2.0 %collective-permute-start.2 = (f32[3,8,2,128]{3,1,2,0:T(8,128)S(1)}, f32[3,8,2,128]{3,1,2,0:T(8,128)S(1)}, u32[]{:S(2)}, u32[]{:S(2)}) collective-permute-start(f32[3,8,2,128]{3,1,2,0:T(8,128)S(1)} %copy.384), channel_id=1, source_target_pairs={{0,1},{1,2},{2,3},{3,4},{4,5},{5,6},{6,7},{8,9},{9,10},{10,11},{11... | collective-permute-start | bytes 73736 | tf_op jit(solution)/shard_map/ppermute | solution.py:37
  21.3 3.5 %collective-permute-start.3 = (f32[3,8,2,128]{3,1,2,0:T(8,128)S(1)}, f32[3,8,2,128]{3,1,2,0:T(8,128)S(1)}, u32[]{:S(2)}, u32[]{:S(2)}) collective-permute-start(f32[3,8,2,128]{3,1,2,0:T(8,128)S(1)} %copy.385), channel_id=1, source_target_pairs={{1,0},{2,1},{3,2},{4,3},{5,4},{6,5},{7,6},{9,8},{10,9},{11,10},{12... | collective-permute-start | bytes 73736 | tf_op jit(solution)/shard_map/ppermute | solution.py:38
  24.9 2.8 %collective-permute-start = (f32[3,2,16,128]{3,2,1,0:T(8,128)S(1)}, f32[3,2,16,128]{3,2,1,0:T(8,128)S(1)}, u32[]{:S(2)}, u32[]{:S(2)}) collective-permute-start(f32[3,2,16,128]{3,2,1,0:T(8,128)S(1)} %get-tuple-element.129), channel_id=1, source_target_pairs={{8,0},{16,8},{24,16},{32,24},{40,32},{48,40},{56,48},{64,56},{72,6... | collective-permute-start | bytes 147464 | tf_op jit(solution)/shard_map/ppermute | solution.py:38
  27.7 5.2 %collective-permute-start.1 = (f32[3,2,16,128]{3,2,1,0:T(8,128)S(1)}, f32[3,2,16,128]{3,2,1,0:T(8,128)S(1)}, u32[]{:S(2)}, u32[]{:S(2)}) collective-permute-start(f32[3,2,16,128]{3,2,1,0:T(8,128)S(1)} %get-tuple-element.130), channel_id=1, source_target_pairs={{0,8},{8,16},{16,24},{24,32},{32,40},{40,48},{48,56},{56,64},{64,7... | collective-permute-start | bytes 147464 | tf_op jit(solution)/shard_map/ppermute | solution.py:37
  34.2 3.5 %gather_fusion = bf16[512,32,128]{2,1,0:T(8,128)(2,1)} fusion(bf16[33,32,128]{2,1,0:T(8,128)(2,1)S(1)} %concatenate.120, s32[1024]{0:T(1024)S(1)} %pad_clamp_fusion.1), kind=kCustom, calls=%fused_computation | custom fusion | bytes 8390656 | tf_op jit(solution)/shard_map/gather | solution.py:184
  37.8 26.4 %collective-permute-done.2 = f32[3,8,2,128]{3,1,2,0:T(8,128)S(1)} collective-permute-done((f32[3,8,2,128]{3,1,2,0:T(8,128)S(1)}, f32[3,8,2,128]{3,1,2,0:T(8,128)S(1)}, u32[]{:S(2)}, u32[]{:S(2)}) %collective-permute-start.2) | collective-permute-done | bytes 24608 | tf_op jit(solution)/shard_map/ppermute | solution.py:37
  64.3 3.5 %collective-permute-done = f32[3,2,16,128]{3,2,1,0:T(8,128)S(1)} collective-permute-done((f32[3,2,16,128]{3,2,1,0:T(8,128)S(1)}, f32[3,2,16,128]{3,2,1,0:T(8,128)S(1)}, u32[]{:S(2)}, u32[]{:S(2)}) %collective-permute-start) | collective-permute-done | bytes 49184 | tf_op jit(solution)/shard_map/ppermute | solution.py:38
  69.7 12.2 %shard_map.146 = f32[32,32,128]{2,1,0:T(8,128)} custom-call(s32[512]{0:T(512)} %compare_select_fusion.4.station_ref, bf16[512,32,128]{2,1,0:T(8,128)(2,1)} %gather_fusion, bf16[512,32,128]{2,1,0:T(8,128)(2,1)} %bitcast.19.other_ref), custom_call_target="tpu_custom_call" | custom-call | flops 41943040 | bytes 8388608 | tf_op jit(solution)/shard_map/pallas_call | solution.py:139
  83.6 1.9 %collective-permute-start.6 = (f32[3,8,2,128]{3,1,2,0:T(8,128)S(1)}, f32[3,8,2,128]{3,1,2,0:T(8,128)S(1)}, u32[]{:S(2)}, u32[]{:S(2)}) collective-permute-start(f32[3,8,2,128]{3,1,2,0:T(8,128)S(1)} %copy.401), channel_id=1, source_target_pairs={{0,1},{1,2},{2,3},{3,4},{4,5},{5,6},{6,7},{8,9},{9,10},{10,11},{11... | collective-permute-start | bytes 73736 | tf_op jit(solution)/shard_map/ppermute | solution.py:37
  85.5 3.6 %collective-permute-start.7 = (f32[3,8,2,128]{3,1,2,0:T(8,128)S(1)}, f32[3,8,2,128]{3,1,2,0:T(8,128)S(1)}, u32[]{:S(2)}, u32[]{:S(2)}) collective-permute-start(f32[3,8,2,128]{3,1,2,0:T(8,128)S(1)} %copy.402), channel_id=1, source_target_pairs={{1,0},{2,1},{3,2},{4,3},{5,4},{6,5},{7,6},{9,8},{10,9},{11,10},{12... | collective-permute-start | bytes 73736 | tf_op jit(solution)/shard_map/ppermute | solution.py:38
  89.3 2.7 %collective-permute-start.4 = (f32[3,2,16,128]{3,2,1,0:T(8,128)S(1)}, f32[3,2,16,128]{3,2,1,0:T(8,128)S(1)}, u32[]{:S(2)}, u32[]{:S(2)}) collective-permute-start(f32[3,2,16,128]{3,2,1,0:T(8,128)S(1)} %get-tuple-element.123), channel_id=1, source_target_pairs={{0,8},{8,16},{16,24},{24,32},{32,40},{40,48},{48,56},{56,64},{64,7... | collective-permute-start | bytes 147464 | tf_op jit(solution)/shard_map/ppermute | solution.py:37
  92.0 3.2 %collective-permute-start.5 = (f32[3,2,16,128]{3,2,1,0:T(8,128)S(1)}, f32[3,2,16,128]{3,2,1,0:T(8,128)S(1)}, u32[]{:S(2)}, u32[]{:S(2)}) collective-permute-start(f32[3,2,16,128]{3,2,1,0:T(8,128)S(1)} %get-tuple-element.124), channel_id=1, source_target_pairs={{8,0},{16,8},{24,16},{32,24},{40,32},{48,40},{56,48},{64,56},{72,6... | collective-permute-start | bytes 147464 | tf_op jit(solution)/shard_map/ppermute | solution.py:38
  95.4 2.1 %copy.418 = f32[4,8,32,128]{3,1,2,0:T(8,128)} copy(f32[4,8,32,128]{3,2,1,0:T(8,128)} %bitcast.261) | data formatting | bytes 1048576
  97.7 2.4 %collective-permute-done.5 = f32[3,2,16,128]{3,2,1,0:T(8,128)S(1)} collective-permute-done((f32[3,2,16,128]{3,2,1,0:T(8,128)S(1)}, f32[3,2,16,128]{3,2,1,0:T(8,128)S(1)}, u32[]{:S(2)}, u32[]{:S(2)}) %collective-permute-start.5) | collective-permute-done | bytes 49184 | tf_op jit(solution)/shard_map/ppermute | solution.py:38
  100.7 1.9 %collective-permute-start.8 = (f32[3,2,16,128]{3,2,1,0:T(8,128)S(1)}, f32[3,2,16,128]{3,2,1,0:T(8,128)S(1)}, u32[]{:S(2)}, u32[]{:S(2)}) collective-permute-start(f32[3,2,16,128]{3,2,1,0:T(8,128)S(1)} %get-tuple-element.116), channel_id=1, source_target_pairs={{8,0},{16,8},{24,16},{32,24},{40,32},{48,40},{56,48},{64,56},{72,6... | collective-permute-start | bytes 147464 | tf_op jit(solution)/shard_map/ppermute | solution.py:38
  102.7 6.0 %collective-permute-start.9 = (f32[3,2,16,128]{3,2,1,0:T(8,128)S(1)}, f32[3,2,16,128]{3,2,1,0:T(8,128)S(1)}, u32[]{:S(2)}, u32[]{:S(2)}) collective-permute-start(f32[3,2,16,128]{3,2,1,0:T(8,128)S(1)} %get-tuple-element.117), channel_id=1, source_target_pairs={{0,8},{8,16},{16,24},{24,32},{32,40},{40,48},{48,56},{56,64},{64,7... | collective-permute-start | bytes 147464 | tf_op jit(solution)/shard_map/ppermute | solution.py:37
  108.7 1.9 %collective-permute-start.10 = (f32[3,8,2,128]{3,1,2,0:T(8,128)S(1)}, f32[3,8,2,128]{3,1,2,0:T(8,128)S(1)}, u32[]{:S(2)}, u32[]{:S(2)}) collective-permute-start(f32[3,8,2,128]{3,1,2,0:T(8,128)S(1)} %copy.405), channel_id=1, source_target_pairs={{0,1},{1,2},{2,3},{3,4},{4,5},{5,6},{6,7},{8,9},{9,10},{10,11},{11... | collective-permute-start | bytes 73736 | tf_op jit(solution)/shard_map/ppermute | solution.py:37
  110.7 3.6 %collective-permute-start.11 = (f32[3,8,2,128]{3,1,2,0:T(8,128)S(1)}, f32[3,8,2,128]{3,1,2,0:T(8,128)S(1)}, u32[]{:S(2)}, u32[]{:S(2)}) collective-permute-start(f32[3,8,2,128]{3,1,2,0:T(8,128)S(1)} %copy.406), channel_id=1, source_target_pairs={{1,0},{2,1},{3,2},{4,3},{5,4},{6,5},{7,6},{9,8},{10,9},{11,10},{12... | collective-permute-start | bytes 73736 | tf_op jit(solution)/shard_map/ppermute | solution.py:38
  116.7 3.3 %collective-permute-start.14 = (f32[3,8,2,128]{3,1,2,0:T(8,128)S(1)}, f32[3,8,2,128]{3,1,2,0:T(8,128)S(1)}, u32[]{:S(2)}, u32[]{:S(2)}) collective-permute-start(f32[3,8,2,128]{3,1,2,0:T(8,128)S(1)} %copy.411), channel_id=1, source_target_pairs={{0,1},{1,2},{2,3},{3,4},{4,5},{5,6},{6,7},{8,9},{9,10},{10,11},{11... | collective-permute-start | bytes 73736 | tf_op jit(solution)/shard_map/ppermute | solution.py:37
  120.0 2.3 %collective-permute-start.15 = (f32[3,8,2,128]{3,1,2,0:T(8,128)S(1)}, f32[3,8,2,128]{3,1,2,0:T(8,128)S(1)}, u32[]{:S(2)}, u32[]{:S(2)}) collective-permute-start(f32[3,8,2,128]{3,1,2,0:T(8,128)S(1)} %copy.412), channel_id=1, source_target_pairs={{1,0},{2,1},{3,2},{4,3},{5,4},{6,5},{7,6},{9,8},{10,9},{11,10},{12... | collective-permute-start | bytes 73736 | tf_op jit(solution)/shard_map/ppermute | solution.py:38
  124.4 3.9 %collective-permute-start.13 = (f32[3,2,16,128]{3,2,1,0:T(8,128)S(1)}, f32[3,2,16,128]{3,2,1,0:T(8,128)S(1)}, u32[]{:S(2)}, u32[]{:S(2)}) collective-permute-start(f32[3,2,16,128]{3,2,1,0:T(8,128)S(1)} %get-tuple-element.110), channel_id=1, source_target_pairs={{8,0},{16,8},{24,16},{32,24},{40,32},{48,40},{56,48},{64,56},{72,6... | collective-permute-start | bytes 147464 | tf_op jit(solution)/shard_map/ppermute | solution.py:38
  128.4 4.0 %collective-permute-done.13 = f32[3,2,16,128]{3,2,1,0:T(8,128)S(1)} collective-permute-done((f32[3,2,16,128]{3,2,1,0:T(8,128)S(1)}, f32[3,2,16,128]{3,2,1,0:T(8,128)S(1)}, u32[]{:S(2)}, u32[]{:S(2)}) %collective-permute-start.13) | collective-permute-done | bytes 49184 | tf_op jit(solution)/shard_map/ppermute | solution.py:38
  (145 shorter events, 17.0 us)
Async XLA Ops:
  8.3 25.7 %copy-start.8 = (f32[8,16,128]{2,1,0:T(8,128)S(1)}, f32[8,16,128]{2,1,0:T(8,128)}, u32[]{:S(2)}) copy-start(f32[8,16,128]{2,1,0:T(8,128)} %param.19) | copy-start | bytes 196612
  8.3 25.8 %copy-start.4 = (bf16[12,8,16,128]{3,2,1,0:T(8,128)(2,1)S(1)}, bf16[12,8,16,128]{3,2,1,0:T(8,128)(2,1)}, u32[]{:S(2)}) copy-start(bf16[12,8,16,128]{3,2,1,0:T(8,128)(2,1)} %param.20) | copy-start | bytes 1179652
  8.3 61.4 %all-to-all-start = ((bf16[128,4,32,128]{3,2,1,0:T(8,128)(2,1)}), bf16[128,4,32,128]{3,2,1,0:T(8,128)(2,1)}, u32[]{:S(2)}, u32[]{:S(2)}) async-start(bf16[128,4,32,128]{3,2,1,0:T(8,128)(2,1)} %bitcast.260), calls=%async_computation | async-start | bytes 8388608 | tf_op jit(solution)/shard_map/all_to_all | solution.py:182
  19.3 44.9 %collective-permute-start.2 = (f32[3,8,2,128]{3,1,2,0:T(8,128)S(1)}, f32[3,8,2,128]{3,1,2,0:T(8,128)S(1)}, u32[]{:S(2)}, u32[]{:S(2)}) collective-permute-start(f32[3,8,2,128]{3,1,2,0:T(8,128)S(1)} %copy.384), channel_id=1, source_target_pairs={{0,1},{1,2},{2,3},{3,4},{4,5},{5,6},{6,7},{8,9},{9,10},{10,11},{11... | collective-permute-start | bytes 73736 | tf_op jit(solution)/shard_map/ppermute | solution.py:37
  21.3 42.9 %collective-permute-start.3 = (f32[3,8,2,128]{3,1,2,0:T(8,128)S(1)}, f32[3,8,2,128]{3,1,2,0:T(8,128)S(1)}, u32[]{:S(2)}, u32[]{:S(2)}) collective-permute-start(f32[3,8,2,128]{3,1,2,0:T(8,128)S(1)} %copy.385), channel_id=1, source_target_pairs={{1,0},{2,1},{3,2},{4,3},{5,4},{6,5},{7,6},{9,8},{10,9},{11,10},{12... | collective-permute-start | bytes 73736 | tf_op jit(solution)/shard_map/ppermute | solution.py:38
  24.9 42.9 %collective-permute-start = (f32[3,2,16,128]{3,2,1,0:T(8,128)S(1)}, f32[3,2,16,128]{3,2,1,0:T(8,128)S(1)}, u32[]{:S(2)}, u32[]{:S(2)}) collective-permute-start(f32[3,2,16,128]{3,2,1,0:T(8,128)S(1)} %get-tuple-element.129), channel_id=1, source_target_pairs={{8,0},{16,8},{24,16},{32,24},{40,32},{48,40},{56,48},{64,56},{72,6... | collective-permute-start | bytes 147464 | tf_op jit(solution)/shard_map/ppermute | solution.py:38
  27.7 40.2 %collective-permute-start.1 = (f32[3,2,16,128]{3,2,1,0:T(8,128)S(1)}, f32[3,2,16,128]{3,2,1,0:T(8,128)S(1)}, u32[]{:S(2)}, u32[]{:S(2)}) collective-permute-start(f32[3,2,16,128]{3,2,1,0:T(8,128)S(1)} %get-tuple-element.130), channel_id=1, source_target_pairs={{0,8},{8,16},{16,24},{24,32},{32,40},{40,48},{48,56},{56,64},{64,7... | collective-permute-start | bytes 147464 | tf_op jit(solution)/shard_map/ppermute | solution.py:37
  81.9 18.2 %copy-start = (f32[8,16,128]{2,1,0:T(8,128)S(1)}, f32[8,16,128]{2,1,0:T(8,128)}, u32[]{:S(2)}) copy-start(f32[8,16,128]{2,1,0:T(8,128)} %param.18) | copy-start | bytes 196612
  81.9 18.2 %copy-start.5 = (f32[8,16,128]{2,1,0:T(8,128)S(1)}, f32[8,16,128]{2,1,0:T(8,128)}, u32[]{:S(2)}) copy-start(f32[8,16,128]{2,1,0:T(8,128)} %param.17) | copy-start | bytes 196612
  83.6 14.0 %collective-permute-start.6 = (f32[3,8,2,128]{3,1,2,0:T(8,128)S(1)}, f32[3,8,2,128]{3,1,2,0:T(8,128)S(1)}, u32[]{:S(2)}, u32[]{:S(2)}) collective-permute-start(f32[3,8,2,128]{3,1,2,0:T(8,128)S(1)} %copy.401), channel_id=1, source_target_pairs={{0,1},{1,2},{2,3},{3,4},{4,5},{5,6},{6,7},{8,9},{9,10},{10,11},{11... | collective-permute-start | bytes 73736 | tf_op jit(solution)/shard_map/ppermute | solution.py:37
  85.5 12.0 %collective-permute-start.7 = (f32[3,8,2,128]{3,1,2,0:T(8,128)S(1)}, f32[3,8,2,128]{3,1,2,0:T(8,128)S(1)}, u32[]{:S(2)}, u32[]{:S(2)}) collective-permute-start(f32[3,8,2,128]{3,1,2,0:T(8,128)S(1)} %copy.402), channel_id=1, source_target_pairs={{1,0},{2,1},{3,2},{4,3},{5,4},{6,5},{7,6},{9,8},{10,9},{11,10},{12... | collective-permute-start | bytes 73736 | tf_op jit(solution)/shard_map/ppermute | solution.py:38
  89.3 8.3 %collective-permute-start.4 = (f32[3,2,16,128]{3,2,1,0:T(8,128)S(1)}, f32[3,2,16,128]{3,2,1,0:T(8,128)S(1)}, u32[]{:S(2)}, u32[]{:S(2)}) collective-permute-start(f32[3,2,16,128]{3,2,1,0:T(8,128)S(1)} %get-tuple-element.123), channel_id=1, source_target_pairs={{0,8},{8,16},{16,24},{24,32},{32,40},{40,48},{48,56},{56,64},{64,7... | collective-permute-start | bytes 147464 | tf_op jit(solution)/shard_map/ppermute | solution.py:37
  92.0 8.1 %collective-permute-start.5 = (f32[3,2,16,128]{3,2,1,0:T(8,128)S(1)}, f32[3,2,16,128]{3,2,1,0:T(8,128)S(1)}, u32[]{:S(2)}, u32[]{:S(2)}) collective-permute-start(f32[3,2,16,128]{3,2,1,0:T(8,128)S(1)} %get-tuple-element.124), channel_id=1, source_target_pairs={{8,0},{16,8},{24,16},{32,24},{40,32},{48,40},{56,48},{64,56},{72,6... | collective-permute-start | bytes 147464 | tf_op jit(solution)/shard_map/ppermute | solution.py:38
  100.7 15.2 %collective-permute-start.8 = (f32[3,2,16,128]{3,2,1,0:T(8,128)S(1)}, f32[3,2,16,128]{3,2,1,0:T(8,128)S(1)}, u32[]{:S(2)}, u32[]{:S(2)}) collective-permute-start(f32[3,2,16,128]{3,2,1,0:T(8,128)S(1)} %get-tuple-element.116), channel_id=1, source_target_pairs={{8,0},{16,8},{24,16},{32,24},{40,32},{48,40},{56,48},{64,56},{72,6... | collective-permute-start | bytes 147464 | tf_op jit(solution)/shard_map/ppermute | solution.py:38
  102.7 13.3 %collective-permute-start.9 = (f32[3,2,16,128]{3,2,1,0:T(8,128)S(1)}, f32[3,2,16,128]{3,2,1,0:T(8,128)S(1)}, u32[]{:S(2)}, u32[]{:S(2)}) collective-permute-start(f32[3,2,16,128]{3,2,1,0:T(8,128)S(1)} %get-tuple-element.117), channel_id=1, source_target_pairs={{0,8},{8,16},{16,24},{24,32},{32,40},{40,48},{48,56},{56,64},{64,7... | collective-permute-start | bytes 147464 | tf_op jit(solution)/shard_map/ppermute | solution.py:37
  108.7 5.8 %collective-permute-start.10 = (f32[3,8,2,128]{3,1,2,0:T(8,128)S(1)}, f32[3,8,2,128]{3,1,2,0:T(8,128)S(1)}, u32[]{:S(2)}, u32[]{:S(2)}) collective-permute-start(f32[3,8,2,128]{3,1,2,0:T(8,128)S(1)} %copy.405), channel_id=1, source_target_pairs={{0,1},{1,2},{2,3},{3,4},{4,5},{5,6},{6,7},{8,9},{9,10},{10,11},{11... | collective-permute-start | bytes 73736 | tf_op jit(solution)/shard_map/ppermute | solution.py:37
  110.7 5.1 %collective-permute-start.11 = (f32[3,8,2,128]{3,1,2,0:T(8,128)S(1)}, f32[3,8,2,128]{3,1,2,0:T(8,128)S(1)}, u32[]{:S(2)}, u32[]{:S(2)}) collective-permute-start(f32[3,8,2,128]{3,1,2,0:T(8,128)S(1)} %copy.406), channel_id=1, source_target_pairs={{1,0},{2,1},{3,2},{4,3},{5,4},{6,5},{7,6},{9,8},{10,9},{11,10},{12... | collective-permute-start | bytes 73736 | tf_op jit(solution)/shard_map/ppermute | solution.py:38
  114.5 17.9 %copy-start.6 = (f32[8,16,128]{2,1,0:T(8,128)S(1)}, f32[8,16,128]{2,1,0:T(8,128)}, u32[]{:S(2)}) copy-start(f32[8,16,128]{2,1,0:T(8,128)} %param.22) | copy-start | bytes 196612
  116.3 17.2 %copy-start.7 = (f32[8,16,128]{2,1,0:T(8,128)S(1)}, f32[8,16,128]{2,1,0:T(8,128)}, u32[]{:S(2)}) copy-start(f32[8,16,128]{2,1,0:T(8,128)} %param.21) | copy-start | bytes 196612
  116.6 17.6 %copy-start.1 = (f32[3,8,16,128]{3,2,1,0:T(8,128)}, f32[3,8,16,128]{3,2,1,0:T(8,128)S(1)}, u32[]{:S(2)}) copy-start(f32[3,8,16,128]{3,2,1,0:T(8,128)S(1)} %fusion.2) | copy-start | bytes 589828
  116.7 11.6 %collective-permute-start.14 = (f32[3,8,2,128]{3,1,2,0:T(8,128)S(1)}, f32[3,8,2,128]{3,1,2,0:T(8,128)S(1)}, u32[]{:S(2)}, u32[]{:S(2)}) collective-permute-start(f32[3,8,2,128]{3,1,2,0:T(8,128)S(1)} %copy.411), channel_id=1, source_target_pairs={{0,1},{1,2},{2,3},{3,4},{4,5},{5,6},{6,7},{8,9},{9,10},{10,11},{11... | collective-permute-start | bytes 73736 | tf_op jit(solution)/shard_map/ppermute | solution.py:37
  120.0 8.3 %collective-permute-start.15 = (f32[3,8,2,128]{3,1,2,0:T(8,128)S(1)}, f32[3,8,2,128]{3,1,2,0:T(8,128)S(1)}, u32[]{:S(2)}, u32[]{:S(2)}) collective-permute-start(f32[3,8,2,128]{3,1,2,0:T(8,128)S(1)} %copy.412), channel_id=1, source_target_pairs={{1,0},{2,1},{3,2},{4,3},{5,4},{6,5},{7,6},{9,8},{10,9},{11,10},{12... | collective-permute-start | bytes 73736 | tf_op jit(solution)/shard_map/ppermute | solution.py:38
  122.4 6.0 %collective-permute-start.12 = (f32[3,2,16,128]{3,2,1,0:T(8,128)S(1)}, f32[3,2,16,128]{3,2,1,0:T(8,128)S(1)}, u32[]{:S(2)}, u32[]{:S(2)}) collective-permute-start(f32[3,2,16,128]{3,2,1,0:T(8,128)S(1)} %get-tuple-element.111), channel_id=1, source_target_pairs={{0,8},{8,16},{16,24},{24,32},{32,40},{40,48},{48,56},{56,64},{64,7... | collective-permute-start | bytes 147464 | tf_op jit(solution)/shard_map/ppermute | solution.py:37
  124.4 8.1 %collective-permute-start.13 = (f32[3,2,16,128]{3,2,1,0:T(8,128)S(1)}, f32[3,2,16,128]{3,2,1,0:T(8,128)S(1)}, u32[]{:S(2)}, u32[]{:S(2)}) collective-permute-start(f32[3,2,16,128]{3,2,1,0:T(8,128)S(1)} %get-tuple-element.110), channel_id=1, source_target_pairs={{8,0},{16,8},{24,16},{32,24},{40,32},{48,40},{56,48},{64,56},{72,6... | collective-permute-start | bytes 147464 | tf_op jit(solution)/shard_map/ppermute | solution.py:38
  (3 other events, 37.9 us)
